TPU v7x, 32 devices: a whole 2x2x4 slice. The times are simulated.
32 devices in a mesh: groups: 2 (over y), enc: 4 (over z), mp: 4 (over x, core).
Axes of the slice: x: 2, y: 2, z: 4, core: 2. Of those that a mesh axis runs over, the one named last changes fastest.
Arguments:
- hidden: bfloat16 [131072, 1024], P(('groups', 'enc'), 'mp'), parts along dimension 0, may hold values from -6 to 6
- proj_w: bfloat16 [1024, 128], P('mp'), may hold values from -0.1875 to 0.1875
- queries: bfloat16 [256, 32, 128], P(('groups', 'enc', 'mp')), parts along dimension 0, may hold values from -208 to 208
- lengths: int32 [512], P('groups'), parts along dimension 0, may hold values from 193 to 256, as said below
- candidates: int32 [256, 16], P(('groups', 'enc', 'mp')), parts along dimension 0, may hold values from 0 to 1023, as said below
Outputs:
- losses: float32 [256], P(('groups', 'enc', 'mp')), parts along dimension 0
- grad_w: float32 [2048, 128], P(('groups', 'mp')), parts along dimension 0
There are 2 independent parts, one for each index of `groups`. A program takes and returns all parts, laid end to end along the dimension named above; an argument that names none is the same for every part. Nothing has to cross between parts.
Inputs may be any that keep to these rules, and one draw needn't show every extreme that they name: Entries are global block numbers of this part. Of the candidates of the 8 queries of one device (aligned rows), at most 16 lie in the 64 blocks of any one device along enc+mp, where device k holds blocks k * 64 to (k + 1) * 64 - 1; some device receives exactly 16 from every device. Blocks may repeat. `lengths`: some passage has 256 tokens and some has 193.
All inputs are finite; a program needn't handle non-finite values.
Results may differ from a plain program's by a relative error of at most 0.0013.
The roundings to bfloat16 on the way count: a program that leaves them out, or rounds other values in their place, can miss the bound.
Values may be sent and summed in bfloat16 or wider, within the bound.
No kernel may reach another device: no remote copies, remote signals or barrier semaphores. Data moves between devices by JAX's collectives and lax.ppermute only.
A program may use at most 128 MiB of HBM per device.

v0:
```python
import jax
import jax.numpy as jnp
from jax import lax
from jax.sharding import PartitionSpec as P

L = 256
BLK = 64


def block_valid(block_ids, lengths):
    per_passage = L // BLK
    passage = block_ids // per_passage
    within = block_ids % per_passage
    positions = within[..., None] * BLK + jnp.arange(BLK, dtype=jnp.int32)
    return positions < lengths[passage][..., None]


def soft_max_sim(sim_tile, valid_mask):
    masked = jnp.where(valid_mask, sim_tile, jnp.float32(-1e30))
    peak = jnp.max(masked, -1, keepdims=True)
    shifted = jnp.exp(masked - peak)
    running = jnp.sum(shifted, -1, keepdims=True)
    scores = jnp.mean(peak[..., 0] + jnp.log(running[..., 0]), -1)
    weights = (shifted / running).astype(jnp.bfloat16)
    return (scores, weights)


def loss_terms(scores):
    margins = scores[:, 1:] - scores[:, :1]
    losses = jnp.mean(jax.nn.softplus(margins), 1)
    slopes = jax.nn.sigmoid(margins) / (scores.shape[1] - 1)
    d_score = jnp.concatenate([-jnp.sum(slopes, 1, keepdims=True), slopes], 1)
    return (losses, d_score)


def left_product(left, right):
    return lax.dot_general(
        left, right, (((0,), (0,)), ((), ())), preferred_element_type=jnp.float32
    )


def local(hidden, proj_w, queries, lengths, candidates):
    mp_count = lax.axis_size("mp")
    owners = lax.axis_size("enc") * mp_count
    row_share = hidden.shape[0] // mp_count
    emb_width = proj_w.shape[1]
    qry_dev = queries.shape[0]
    query_len = queries.shape[1]
    cand_count = candidates.shape[1]
    blk_dev = row_share // BLK
    slot_count = qry_dev * cand_count
    capacity = 2 * slot_count // owners
    e_pre = lax.psum_scatter(
        jnp.dot(hidden, proj_w, preferred_element_type=jnp.float32),
        "mp",
        scatter_dimension=0,
        tiled=True,
    )
    scale = lax.rsqrt(jnp.sum(e_pre * e_pre, -1, keepdims=True) + 1e-06)
    embedded = (e_pre * scale).astype(jnp.bfloat16)
    local_blocks = embedded.reshape(blk_dev, BLK, emb_width)
    flat_cand = candidates.reshape(-1)
    owner_of = flat_cand // blk_dev
    slot_ids = jnp.arange(slot_count, dtype=jnp.int32)
    same_owner = owner_of[:, None] == owner_of[None, :]
    earlier = slot_ids[None, :] < slot_ids[:, None]
    rank_in = jnp.sum(jnp.where(same_owner & earlier, 1, 0), 1).astype(jnp.int32)
    dest = owner_of * capacity + rank_in
    wanted = jnp.zeros((owners * capacity,), jnp.int32).at[dest].set(flat_cand % blk_dev)
    served = lax.all_to_all(
        wanted.reshape(owners, capacity), ("enc", "mp"), split_axis=0, concat_axis=0, tiled=True
    ).reshape(-1)
    grad_emb = jnp.zeros((blk_dev, BLK, emb_width), jnp.float32)
    tiles = local_blocks[served].reshape(owners, capacity, BLK, emb_width)
    arrived = lax.all_to_all(tiles, ("enc", "mp"), split_axis=0, concat_axis=0, tiled=True).reshape(
        owners * capacity, BLK, emb_width
    )
    mine = arrived[dest].reshape(qry_dev, cand_count, BLK, emb_width)
    valid_mask = block_valid(candidates, lengths)
    sim_tile = jnp.einsum("qie,qcje->qcij", queries, mine, preferred_element_type=jnp.float32)
    scores, weights = soft_max_sim(sim_tile, valid_mask[:, :, None, :])
    losses, d_score = loss_terms(scores)
    occ_grad = jnp.einsum("qcij,qie->qcje", weights, queries, preferred_element_type=jnp.float32)
    occ_grad = (occ_grad * (d_score / query_len)[:, :, None, None]).astype(jnp.bfloat16)
    outgoing = jnp.zeros((owners * capacity, BLK, emb_width), jnp.bfloat16)
    outgoing = outgoing.at[dest].set(occ_grad.reshape(slot_count, BLK, emb_width))
    returned = lax.all_to_all(
        outgoing.reshape(owners, capacity, BLK, emb_width),
        ("enc", "mp"),
        split_axis=0,
        concat_axis=0,
        tiled=True,
    )
    grad_emb = grad_emb.at[served].add(returned.reshape(-1, BLK, emb_width).astype(jnp.float32))
    grad_flat = grad_emb.reshape(row_share, emb_width)
    dot_e = jnp.sum(e_pre * grad_flat, -1, keepdims=True)
    de_pre = (scale * grad_flat - e_pre * (scale * scale * scale) * dot_e).astype(jnp.bfloat16)
    partial_w = left_product(hidden, lax.all_gather(de_pre, "mp", axis=0, tiled=True))
    grad_w = lax.psum(partial_w, "enc")
    return (losses, grad_w)


def solution(mesh):
    return jax.shard_map(
        local,
        mesh=mesh,
        in_specs=(
            P(("groups", "enc"), "mp"),
            P("mp", None),
            P(("groups", "enc", "mp"), None, None),
            P("groups"),
            P(("groups", "enc", "mp"), None),
        ),
        out_specs=(P(("groups", "enc", "mp")), P(("groups", "mp"), None)),
        check_vma=False,
    )
```

profile of v0, /device:TPU:0, one launch (start us, length us, event | category | flops | bytes accessed | tf_op | source)
XLA Modules:
  0.0 446.6 jit_solution(9475051947328319691)
XLA Ops:
  7.2 0.8 copy-done
  8.0 8.9 %fusion.22 = f32[16384,128]{1,0:T(8,128)} fusion(bf16[16384,256]{1,0:T(8,128)(2,1)} %param.5, bf16[256,128]{1,0:T(8,128)(2,1)S(1)} %copy-done), kind=kOutput, calls=%fused_computation.74 | convolution fusion | flops 1073741824 | bytes 16842752 | tf_op jit(solution)/shard_map/dot_general | solution.py:54
  17.0 0.7 copy-done.6
  18.0 1.0 scatter_custom_fusion
  19.1 13.6 %all_to_all.19 = s32[16,1,16]{2,1,0:T(1,128)S(1)} all-to-all(s32[16,1,16]{2,1,0:T(1,128)S(1)} %all_to_all.12), channel_id=1, replica_groups=mesh['groups'=2,'enc'=4,'mp'=4] {'enc','mp'}, dimensions={0} | all-to-all | bytes 2048 | tf_op jit(solution)/shard_map/all_to_all | solution.py:70
  32.7 0.5 broadcast.263
  33.2 0.7 reduce.5
  33.9 57.6 %reduce-scatter.2.cloned.1.call-done = f32[4096,128]{1,0:T(8,128)} async-done(((f32[16384,128]{1,0:T(8,128)}), f32[4096,128]{1,0:T(8,128)}) %reduce-scatter.2.cloned.1.call-update) | async-done | bytes 2097168 | tf_op jit(solution)/shard_map/reduce_scatter | solution.py:53
  91.5 2.4 multiply_reduce_fusion
  93.9 0.7 multiply_convert_fusion.1
  94.6 3.1 gather_fusion.1
  97.7 4.8 %all-to-all-start.1 = ((bf16[16,16,64,128]{3,2,1,0:T(8,128)(2,1)}), bf16[16,16,64,128]{3,2,1,0:T(8,128)(2,1)}, u32[]{:S(2)}, u32[]{:S(2)}) async-start(bf16[16,16,64,128]{3,2,1,0:T(8,128)(2,1)} %bitcast.55), calls=%async_computation.2 | async-start | bytes 8388608 | tf_op jit(solution)/shard_map/all_to_all | solution.py:75
  102.7 0.5 copy-done.1
  103.2 1.3 gather_fusion
  104.7 75.5 %all-to-all-done.1 = bf16[16,16,64,128]{3,2,1,0:T(8,128)(2,1)} async-done(((bf16[16,16,64,128]{3,2,1,0:T(8,128)(2,1)}), bf16[16,16,64,128]{3,2,1,0:T(8,128)(2,1)}, u32[]{:S(2)}, u32[]{:S(2)}) %all-to-all-start.1) | async-done | bytes 4194336 | tf_op jit(solution)/shard_map/all_to_all | solution.py:75
  180.2 4.4 gather_fusion.2
  184.5 3.8 bitcast_reduce_fusion
  188.3 1.3 fusion.4
  190.3 4.4 multiply_convert_fusion
  194.7 3.0 broadcast_in_dim.32
  197.7 15.7 %scatter_fusion = bf16[256,64,128]{2,1,0:T(8,128)(2,1)} fusion(bf16[256,64,128]{2,1,0:T(8,128)(2,1)} %broadcast_in_dim.32, s32[128]{0:T(128)S(1)} %fusion.17, bf16[128,64,128]{2,1,0:T(8,128)(2,1)S(1)} %bitcast.57), kind=kCustom, calls=%fused_computation.4 | custom fusion | bytes 6291968 | tf_op jit(solution)/shard_map/scatter | solution.py:86
  213.4 111.9 %all_to_all.20 = bf16[16,16,64,128]{3,2,1,0:T(8,128)(2,1)S(1)} all-to-all(bf16[16,16,64,128]{3,2,1,0:T(8,128)(2,1)} %bitcast.53), channel_id=1, replica_groups=mesh['groups'=2,'enc'=4,'mp'=4] {'enc','mp'}, dimensions={0} | all-to-all | bytes 8388608 | tf_op jit(solution)/shard_map/all_to_all | solution.py:87
  325.3 4.5 %bitcast_convert_fusion = f32[256,64,128]{2,1,0:T(8,128)} fusion(bf16[16,16,64,128]{3,2,1,0:T(8,128)(2,1)S(1)} %all_to_all.20), kind=kLoop, calls=%fused_computation.6 | loop fusion | flops 2097152 | bytes 12582912 | tf_op jit(solution)/shard_map/convert_element_type | solution.py:94
  329.8 0.2 broadcast_in_dim.31
  330.1 26.2 %scatter_fusion.1 = f32[64,64,128]{2,1,0:T(8,128)S(1)} fusion(f32[64,64,128]{2,1,0:T(8,128)S(1)} %broadcast_in_dim.31, s32[256]{0:T(256)S(1)} %bitcast.59, f32[256,64,128]{2,1,0:T(8,128)} %bitcast_convert_fusion), kind=kCustom, calls=%fused_computation.5 | custom fusion | flops 2097152 | bytes 25166848 | tf_op jit(solution)/shard_map/scatter-add | solution.py:94
  356.3 2.4 fusion.2
  358.7 3.0 fusion.1
  361.8 35.2 %all-gather.2.cloned.1.call-done = bf16[16384,128]{1,0:T(8,128)(2,1)} async-done(((bf16[4096,128]{1,0:T(8,128)(2,1)}), bf16[16384,128]{1,0:T(8,128)(2,1)}) %all-gather.2.cloned.1.call-update) | async-done | bytes 4194320 | tf_op jit(solution)/shard_map/all_gather | solution.py:98
  397.0 6.8 %convolution_bitcast_fusion = f32[256,128]{0,1:T(8,128)} fusion(bf16[16384,128]{1,0:T(8,128)(2,1)} %all-gather.2.cloned.1.call-done, bf16[16384,256]{1,0:T(8,128)(2,1)} %param.5), kind=kOutput, calls=%fused_computation.20 | convolution fusion | flops 1073741824 | bytes 12713984 | tf_op jit(solution)/shard_map/dot_general | solution.py:37
  403.8 0.5 broadcast_multiply_fusion.1
  404.3 34.0 %all-reduce.2.cloned.1.call-done = f32[256,128]{0,1:T(8,128)} async-done(((f32[256,128]{0,1:T(8,128)}), f32[256,128]{0,1:T(8,128)}) %all-reduce.2.cloned.1.call-update) | async-done | bytes 131088 | tf_op jit(solution)/shard_map/psum | solution.py:99
  438.4 1.7 copy.16
  (40 shorter events, 1.6 us)
Async XLA Ops:
  7.2 0.8 copy-start
  7.2 84.4 %reduce-scatter.2.cloned.1.call-start = ((), (), s32[]{:S(2)}) async-start(), calls=%async_computation.4 | async-start | bytes 10485760 | tf_op jit(solution)/shard_map/reduce_scatter | solution.py:53
  16.9 0.7 copy-start.6
  91.5 2.4 copy-start.2
  97.7 82.5 %all-to-all-start.1 = ((bf16[16,16,64,128]{3,2,1,0:T(8,128)(2,1)}), bf16[16,16,64,128]{3,2,1,0:T(8,128)(2,1)}, u32[]{:S(2)}, u32[]{:S(2)}) async-start(bf16[16,16,64,128]{3,2,1,0:T(8,128)(2,1)} %bitcast.55), calls=%async_computation.2 | async-start | bytes 8388608 | tf_op jit(solution)/shard_map/all_to_all | solution.py:75
  102.5 0.7 copy-start.1
  102.5 294.4 %all-gather.2.cloned.1.call-start = ((), (), s32[]{:S(2)}) async-start(), calls=%async_computation.5 | async-start | bytes 5242880 | tf_op jit(solution)/shard_map/all_gather | solution.py:98
  180.2 4.4 copy-start.5
  194.7 3.0 copy-start.4
  356.3 2.4 copy-start.3
  361.7 76.7 %all-reduce.2.cloned.1.call-start = ((), (), s32[]{:S(2)}) async-start(), calls=%async_computation.6 | async-start | bytes 262144 | tf_op jit(solution)/shard_map/psum | solution.py:99
Sparse Core Ops, SparseCore 0:
  17.1 74.3 reduce-scatter.1
  361.8 35.0 all-gather.1
  403.9 34.3 all-reduce.1
where the time goes:
time: 448 us; the launch traced here: 447 us
  waiting for transfers between devices  202 us (45%)
  blocking collectives  125 us (28%)
  other arithmetic  42.4 us (9%)
  local copies, waits for them, and re-layouts  33.4 us (7%)
  matrix products  24 us (5%)
  between operations  14 us (3%)
  starting transfers between devices  4.9 us (1%)
    all_to_all x1, blocking collectives, local(): lax.all_to_all(outgoing.reshape(owners, capacity, BLK, emb_width), ('enc'...  112 us
    all_to_all x1, waiting for transfers between devices, local(): lax.all_to_all(tiles, ('enc', 'mp'), split_axis=0, concat_axis=0, tiled=T...  75.5 us
    reduce_scatter x1, waiting for transfers between devices, local(): lax.psum_scatter(jnp.dot(hidden, proj_w, preferred_element_type=jnp.float...  57.6 us
    all_gather x1, waiting for transfers between devices, local(): lax.all_gather(de_pre, 'mp', axis=0, tiled=True)  35.2 us
    psum x1, waiting for transfers between devices, local(): grad_w = lax.psum(partial_w, 'enc')  34 us
    scatter-add x1, other arithmetic, local(): grad_emb.at[served]  26.2 us
    scatter x1, local copies, waits for them, and re-layouts, local(): outgoing.at[dest].set(occ_grad.reshape(slot_count, BLK, emb_width))  15.7 us
    all_to_all x1, blocking collectives, local(): lax.all_to_all(wanted.reshape(owners, capacity), ('enc', 'mp'), split_axi...  13.6 us
  transfers between devices with their start and end apart: 4, of which 4 were waited for; matrix products, arithmetic and copies ran while one was open for 1% of the time, Pallas kernels for 0%

commit v1 on v0

--- a/solution.py
+++ b/solution.py
@@ -50,6 +50,12 @@
     blk_dev = row_share // BLK
     slot_count = qry_dev * cand_count
     capacity = 2 * slot_count // owners
+    me = lax.axis_index("enc") * mp_count + lax.axis_index("mp")
+
+    all_queries = lax.all_gather(queries, ("enc", "mp"), axis=0, tiled=True)
+    all_cand = lax.all_gather(candidates, ("enc", "mp"), axis=0, tiled=True)
+    all_cand = all_cand.reshape(owners, slot_count)
+
     e_pre = lax.psum_scatter(
         jnp.dot(hidden, proj_w, preferred_element_type=jnp.float32),
         "mp",
@@ -59,39 +65,40 @@
     scale = lax.rsqrt(jnp.sum(e_pre * e_pre, -1, keepdims=True) + 1e-06)
     embedded = (e_pre * scale).astype(jnp.bfloat16)
     local_blocks = embedded.reshape(blk_dev, BLK, emb_width)
-    flat_cand = candidates.reshape(-1)
-    owner_of = flat_cand // blk_dev
+
     slot_ids = jnp.arange(slot_count, dtype=jnp.int32)
-    same_owner = owner_of[:, None] == owner_of[None, :]
-    earlier = slot_ids[None, :] < slot_ids[:, None]
-    rank_in = jnp.sum(jnp.where(same_owner & earlier, 1, 0), 1).astype(jnp.int32)
-    dest = owner_of * capacity + rank_in
-    wanted = jnp.zeros((owners * capacity,), jnp.int32).at[dest].set(flat_cand % blk_dev)
-    served = lax.all_to_all(
-        wanted.reshape(owners, capacity), ("enc", "mp"), split_axis=0, concat_axis=0, tiled=True
-    ).reshape(-1)
-    grad_emb = jnp.zeros((blk_dev, BLK, emb_width), jnp.float32)
-    tiles = local_blocks[served].reshape(owners, capacity, BLK, emb_width)
-    arrived = lax.all_to_all(tiles, ("enc", "mp"), split_axis=0, concat_axis=0, tiled=True).reshape(
-        owners * capacity, BLK, emb_width
+    mine = (all_cand // blk_dev) == me
+    rank = jnp.cumsum(mine.astype(jnp.int32), axis=1) - 1
+    ranks = jnp.arange(capacity, dtype=jnp.int32)
+    pick = mine[:, None, :] & (rank[:, None, :] == ranks[None, :, None])
+    valid = jnp.any(pick, axis=2)
+    slot_of = jnp.sum(jnp.where(pick, slot_ids[None, None, :], 0), axis=2).astype(jnp.int32)
+    block_of = jnp.take_along_axis(all_cand, slot_of, axis=1)
+    local_of = block_of % blk_dev
+    query_of = jnp.arange(owners, dtype=jnp.int32)[:, None] * qry_dev + slot_of // cand_count
+
+    tiles = local_blocks[local_of]
+    q_e = all_queries[query_of]
+    valid_mask = block_valid(block_of, lengths)
+    sim_tile = jnp.einsum("scie,scje->scij", q_e, tiles, preferred_element_type=jnp.float32)
+    scores, weights = soft_max_sim(sim_tile, valid_mask[:, :, None, :])
+
+    placed = jnp.sum(jnp.where(pick, scores[:, :, None], jnp.float32(0)), axis=1)
+    all_scores = lax.psum(placed, ("enc", "mp")).reshape(owners * qry_dev, cand_count)
+    all_losses, d_score = loss_terms(all_scores)
+    losses = lax.dynamic_slice_in_dim(all_losses, me * qry_dev, qry_dev)
+
+    d_e = jnp.take_along_axis(d_score.reshape(owners, slot_count), slot_of, axis=1)
+    d_e = jnp.where(valid, d_e, jnp.float32(0))
+    occ_grad = jnp.einsum("scij,scie->scje", weights, q_e, preferred_element_type=jnp.float32)
+    occ_grad = (occ_grad * (d_e / query_len)[:, :, None, None]).astype(jnp.bfloat16)
+    onehot = (local_of[:, :, None] == jnp.arange(blk_dev, dtype=jnp.int32)) & valid[:, :, None]
+    grad_emb = jnp.einsum(
+        "scb,scx->bx",
+        onehot.astype(jnp.bfloat16),
+        occ_grad.reshape(owners, capacity, BLK * emb_width),
+        preferred_element_type=jnp.float32,
     )
-    mine = arrived[dest].reshape(qry_dev, cand_count, BLK, emb_width)
-    valid_mask = block_valid(candidates, lengths)
-    sim_tile = jnp.einsum("qie,qcje->qcij", queries, mine, preferred_element_type=jnp.float32)
-    scores, weights = soft_max_sim(sim_tile, valid_mask[:, :, None, :])
-    losses, d_score = loss_terms(scores)
-    occ_grad = jnp.einsum("qcij,qie->qcje", weights, queries, preferred_element_type=jnp.float32)
-    occ_grad = (occ_grad * (d_score / query_len)[:, :, None, None]).astype(jnp.bfloat16)
-    outgoing = jnp.zeros((owners * capacity, BLK, emb_width), jnp.bfloat16)
-    outgoing = outgoing.at[dest].set(occ_grad.reshape(slot_count, BLK, emb_width))
-    returned = lax.all_to_all(
-        outgoing.reshape(owners, capacity, BLK, emb_width),
-        ("enc", "mp"),
-        split_axis=0,
-        concat_axis=0,
-        tiled=True,
-    )
-    grad_emb = grad_emb.at[served].add(returned.reshape(-1, BLK, emb_width).astype(jnp.float32))
     grad_flat = grad_emb.reshape(row_share, emb_width)
     dot_e = jnp.sum(e_pre * grad_flat, -1, keepdims=True)
     de_pre = (scale * grad_flat - e_pre * (scale * scale * scale) * dot_e).astype(jnp.bfloat16)

time: 448 us -> 256 us (0.57)
  waiting for transfers between devices: 202 us -> 109 us
  blocking collectives: 125 us -> 56.2 us
  other arithmetic: 42.4 us -> 13.4 us
  matrix products: 24 us -> 34.7 us
  local copies, waits for them, and re-layouts: 33.4 us -> 27 us
  starting transfers between devices: 4.9 us -> 0.17 us
    all_to_all x2 -> x0, blocking collectives: 125 us -> none  [the longest x1 112 us: local(): lax.all_to_all(outgoing.reshape(owners, capacity, BLK, emb_width), ('enc'...]
    all_to_all x1 -> x0, waiting for transfers between devices: 75.5 us -> none  [local(): lax.all_to_all(tiles, ('enc', 'mp'), split_axis=0, concat_axis=0, tiled=T...]
    psum x0 -> x1, blocking collectives: none -> 32.9 us  [local(): lax.psum(placed, ('enc', 'mp')).reshape(owners * qry_dev, cand_count)]
    scatter-add x1 -> x0, other arithmetic: 26.2 us -> none  [local(): grad_emb.at[served]]
    all_gather x0 -> x1, blocking collectives: none -> 23.4 us  [local(): all_cand = lax.all_gather(candidates, ('enc', 'mp'), axis=0, tiled=True)]
    reduce_scatter x1, waiting for transfers between devices: 57.6 us -> 38.4 us  [local(): lax.psum_scatter(jnp.dot(hidden, proj_w, preferred_element_type=jnp.float...]
    scatter x2 -> x0, local copies, waits for them, and re-layouts: 16.7 us -> none  [the longest x1 15.7 us: local(): outgoing.at[dest].set(occ_grad.reshape(slot_count, BLK, emb_width))]
    dot_general x2 -> x3, matrix products: 8.21 us -> 18.9 us  [the longest x1 8 us: local(): jnp.einsum('scij,scie->scje', weights, q_e, preferred_element_type=jnp.fl...]
  transfers between devices with their start and end apart: 4 -> 4, of which waited for: 4 -> 4; matrix products, arithmetic and copies ran while one was open for 1% -> 7% of each run, Pallas kernels for 0% -> 0%
where the time goes in v1:
time: 256 us
  waiting for transfers between devices  109 us (43%)
  blocking collectives  56.2 us (22%)
  matrix products  34.7 us (14%)
  local copies, waits for them, and re-layouts  27 us (11%)
  between operations  15.7 us (6%)
  other arithmetic  13.4 us (5%)
    reduce_scatter x1, waiting for transfers between devices, local(): lax.psum_scatter(jnp.dot(hidden, proj_w, preferred_element_type=jnp.float...  38.4 us
    psum x1, waiting for transfers between devices, local(): grad_w = lax.psum(partial_w, 'enc')  34 us
    psum x1, blocking collectives, local(): lax.psum(placed, ('enc', 'mp')).reshape(owners * qry_dev, cand_count)  32.9 us
    all_gather x1, waiting for transfers between devices, local(): lax.all_gather(de_pre, 'mp', axis=0, tiled=True)  31.6 us
    all_gather x1, blocking collectives, local(): all_cand = lax.all_gather(candidates, ('enc', 'mp'), axis=0, tiled=True)  23.4 us
    dot_general x1, matrix products, local(): jnp.dot(hidden, proj_w, preferred_element_type=jnp.float32)  8.94 us
    dot_general x1, matrix products, local(): jnp.einsum('scij,scie->scje', weights, q_e, preferred_element_type=jnp.fl...  8 us
    reshape x1, local copies, waits for them, and re-layouts, local(): occ_grad.reshape(owners, capacity, BLK * emb_width)  7.31 us
  transfers between devices with their start and end apart: 4, of which 4 were waited for; matrix products, arithmetic and copies ran while one was open for 7% of the time, Pallas kernels for 0%

profile of v1, /device:TPU:0, one launch (start us, length us, event | category | flops | bytes accessed | tf_op | source)
XLA Modules:
  0.0 255.7 jit_solution(6291594766435006573)
XLA Ops:
  8.1 0.7 all-gather.3.cloned.1.call-update
  8.8 8.9 %fusion.27 = f32[16384,128]{1,0:T(8,128)} fusion(bf16[16384,256]{1,0:T(8,128)(2,1)} %param.5, bf16[256,128]{1,0:T(8,128)(2,1)S(1)} %copy-done), kind=kOutput, calls=%fused_computation.94 | convolution fusion | flops 1073741824 | bytes 16842752 | tf_op jit(solution)/shard_map/dot_general | solution.py:60
  17.9 0.6 copy-done.5
  18.5 23.4 %all_gather.9 = s32[128,16]{1,0:T(8,128)S(1)} all-gather(s32[8,16]{1,0:T(8,128)S(1)} %copy-done.5), channel_id=1, replica_groups=mesh['groups'=2,'enc'=4,'mp'=4] {'enc','mp'}, dimensions={0}, use_global_device_ids=true | all-gather | bytes 8704 | tf_op jit(solution)/shard_map/all_gather | solution.py:56
  41.9 0.3 reduce_window_sum.11
  42.2 0.4 select_reduce_fusion.2
  42.7 1.9 gather_fusion.3
  44.7 0.4 fusion.7
  45.6 1.9 gather_fusion
  47.7 0.1 add_compare_fusion
  47.8 3.8 %all-gather.3.cloned.1.call-done = bf16[128,32,128]{2,1,0:T(8,128)(2,1)} async-done(((bf16[8,32,128]{2,1,0:T(8,128)(2,1)}), bf16[128,32,128]{2,1,0:T(8,128)(2,1)}) %all-gather.3.cloned.1.call-update) | async-done | bytes 1048592 | tf_op jit(solution)/shard_map/all_gather | solution.py:55
  51.6 2.2 gather_fusion.1
  53.9 38.4 %reduce-scatter.2.cloned.1.call-done = f32[4096,128]{1,0:T(8,128)} async-done(((f32[16384,128]{1,0:T(8,128)}), f32[4096,128]{1,0:T(8,128)}) %reduce-scatter.2.cloned.1.call-update) | async-done | bytes 2097168 | tf_op jit(solution)/shard_map/reduce_scatter | solution.py:59
  92.3 2.2 multiply_reduce_fusion.1
  94.5 1.9 multiply_convert_fusion.1
  96.4 3.0 %gather_fusion.2 = bf16[256,64,128]{2,1,0:T(8,128)(2,1)} fusion(bf16[64,64,128]{2,1,0:T(8,128)(2,1)S(1)} %bitcast.55, s32[1024]{0:T(1024)S(1)} %pad_clamp_fusion), kind=kCustom, calls=%fused_computation.2 | custom fusion | bytes 8389632 | tf_op jit(solution)/shard_map/gather | solution.py:80
  99.5 4.6 %select_reduce_fusion = (f32[16,16,32]{2,1,0:T(8,128)S(1)}, f32[16,16,32,64]{3,2,1,0:T(8,128)S(1)}) fusion(pred[16,16,64]{2,1,0:T(8,128)(4,1)S(1)} %add_compare_fusion, bf16[16,16,32,128]{3,2,1,0:T(8,128)(2,1)S(1)} %bitcast.57, bf16[16,16,64,128]{3,2,1,0:T(8,128)(2,1)} %bitcast.56), kind=kOutput, calls=%fused_computation.10 | convolution fusion | flops 135258112 | bytes 8437760 | tf_op jit(solution)/shard_map/scie,scje->scij/dot_general | solution.py:83
  104.1 2.0 copy-done.4
  106.0 2.4 fusion.1
  108.9 32.9 %psum.14 = f32[128,16]{0,1:T(8,128)S(1)} all-reduce(f32[128,16]{0,1:T(8,128)S(1)} %copy.32), channel_id=1, replica_groups=mesh['groups'=2,'enc'=4,'mp'=4] {'enc','mp'}, use_global_device_ids=true, to_apply=%region_8.9 | all-reduce | flops 2048 | bytes 16384 | tf_op jit(solution)/shard_map/psum | solution.py:87
  142.0 1.9 gather_fusion.4
  144.0 8.0 %multiply_convert_fusion = bf16[16,16,64,128]{3,2,1,0:T(8,128)(2,1)} fusion(f32[16,16]{1,0:T(8,128)S(1)} %select_multiply_fusion, bf16[16,16,32,128]{3,2,1,0:T(8,128)(2,1)S(1)} %bitcast.58, f32[16,16,32,64]{3,2,1,0:T(8,128)} %copy-done.4, f32[16,16,32]{2,1,0:T(8,128)S(1)} %fusion.1, f32[16,16,32]{2,1,0:T(8,128)S(1)} %get-tuple-element.26, ...), kind=kOutput, calls=%fused_computation.6 | convolution fusion | flops 140509184 | bytes 8471552 | tf_op jit(solution)/shard_map/scij,scie->scje/dot_general | solution.py:93
  152.0 7.3 %reshape.384 = bf16[16,16,8192]{2,1,0:T(8,128)(2,1)} reshape(bf16[16,16,64,128]{3,2,1,0:T(8,128)(2,1)} %multiply_convert_fusion) | data formatting | bytes 8388608 | tf_op jit(solution)/shard_map/reshape | solution.py:99
  159.3 6.3 %convolution_bitcast_fusion = f32[64,8192]{1,0:T(8,128)} fusion(bf16[16,16,8192]{2,1,0:T(8,128)(2,1)} %reshape.384, s32[16,16]{0,1:T(8,128)S(1)} %copy.33, pred[16,16]{0,1:T(8,128)(4,1)S(1)} %copy.34), kind=kOutput, calls=%fused_computation.5 | convolution fusion | flops 268468224 | bytes 6292736 | tf_op jit(solution)/shard_map/scb,scx->bx/dot_general | solution.py:96
  165.6 2.7 %reshape.385 = f32[4096,128]{1,0:T(8,128)} reshape(f32[64,8192]{1,0:T(8,128)} %convolution_bitcast_fusion) | data formatting | bytes 4194304 | tf_op jit(solution)/shard_map/reshape | solution.py:102
  168.3 2.4 multiply_reduce_fusion
  170.6 2.9 %subtract_convert_fusion = bf16[4096,128]{1,0:T(8,128)(2,1)} fusion(f32[4096,128]{1,0:T(8,128)S(1)} %copy-done.2, f32[4096,128]{1,0:T(8,128)S(1)} %copy-done.3, f32[4096]{0:T(1024)S(1)} %multiply_reduce_fusion, f32[4096]{0:T(1024)S(1)} %get-tuple-element.20, f32[4096]{0:T(1024)S(1)} %get-tuple-element.21), kind=kLoop, calls=%fused_computation.12 | loop fusion | flops 2621440 | bytes 5292032 | tf_op jit(solution)/shard_map/convert_element_type | solution.py:104
  173.6 31.6 %all-gather.5.cloned.1.call-done = bf16[16384,128]{1,0:T(8,128)(2,1)} async-done(((bf16[4096,128]{1,0:T(8,128)(2,1)}), bf16[16384,128]{1,0:T(8,128)(2,1)}) %all-gather.5.cloned.1.call-update) | async-done | bytes 4194320 | tf_op jit(solution)/shard_map/all_gather | solution.py:105
  205.2 6.8 %convolution_bitcast_fusion.1 = f32[256,128]{0,1:T(8,128)} fusion(bf16[16384,128]{1,0:T(8,128)(2,1)} %all-gather.5.cloned.1.call-done, bf16[16384,256]{1,0:T(8,128)(2,1)} %param.5), kind=kOutput, calls=%fused_computation.20 | convolution fusion | flops 1073741824 | bytes 12713984 | tf_op jit(solution)/shard_map/dot_general | solution.py:37
  212.1 0.6 dynamic_slice.3
  212.7 34.0 %all-reduce.2.cloned.1.call-done = f32[256,128]{0,1:T(8,128)} async-done(((f32[256,128]{0,1:T(8,128)}), f32[256,128]{0,1:T(8,128)}) %all-reduce.2.cloned.1.call-update) | async-done | bytes 131088 | tf_op jit(solution)/shard_map/psum | solution.py:106
  246.7 1.7 copy.37
  (52 shorter events, 1.9 us)
Async XLA Ops:
  8.0 0.8 copy-start
  8.0 43.6 %all-gather.3.cloned.1.call-start = ((), (), s32[]{:S(2)}) async-start(), calls=%async_computation.1 | async-start | bytes 1114112 | tf_op jit(solution)/shard_map/all_gather | solution.py:55
  8.7 83.5 %reduce-scatter.2.cloned.1.call-start = ((), (), s32[]{:S(2)}) async-start(), calls=%async_computation.2 | async-start | bytes 10485760 | tf_op jit(solution)/shard_map/reduce_scatter | solution.py:59
  17.8 0.7 copy-start.5
  17.8 187.4 %all-gather.5.cloned.1.call-start = ((), (), s32[]{:S(2)}) async-start(), calls=%async_computation.3 | async-start | bytes 5242880 | tf_op jit(solution)/shard_map/all_gather | solution.py:105
  42.7 2.9 %copy-start.1 = (s32[256]{0:T(256)S(1)}, s32[256]{0:T(256)}, u32[]{:S(2)}) copy-start(s32[256]{0:T(256)} %param.8) | copy-start | bytes 3076
  104.1 2.0 copy-start.4
  159.3 9.0 %copy-start.2 = (f32[4096,128]{1,0:T(8,128)S(1)}, f32[4096,128]{1,0:T(8,128)}, u32[]{:S(2)}) copy-start(f32[4096,128]{1,0:T(8,128)} %reduce-scatter.2.cloned.1.call-done) | copy-start | bytes 6291460
  168.3 2.4 copy-start.3
  173.5 73.1 %all-reduce.2.cloned.1.call-start = ((), (), s32[]{:S(2)}) async-start(), calls=%async_computation.4 | async-start | bytes 262144 | tf_op jit(solution)/shard_map/psum | solution.py:106
Sparse Core Ops, SparseCore 0:
  11.0 40.5 all-gather.2
  212.2 34.4 all-reduce.1
Sparse Core Ops, SparseCore 1:
  17.9 74.3 reduce-scatter.1
  173.6 31.5 all-gather.4

commit v2 on v1

--- a/solution.py
+++ b/solution.py
@@ -39,6 +39,60 @@
     )
 
 
+def xor_perm(value, axis, bit):
+    count = lax.axis_size(axis)
+    return lax.ppermute(value, axis, [(i, i ^ bit) for i in range(count)])
+
+
+def is_pow2(count):
+    return count & (count - 1) == 0
+
+
+def reduce_scatter_rows(value, axis):
+    count = lax.axis_size(axis)
+    if not is_pow2(count):
+        return lax.psum_scatter(value, axis, scatter_dimension=0, tiled=True)
+    me = lax.axis_index(axis)
+    acc = value.reshape((count, -1) + value.shape[1:])
+    bit = 1
+    while bit < count:
+        acc = acc.reshape((acc.shape[0] // 2, 2) + acc.shape[1:])
+        low = (me // bit) % 2 == 0
+        keep = jnp.where(low, acc[:, 0], acc[:, 1])
+        send = jnp.where(low, acc[:, 1], acc[:, 0])
+        acc = keep + xor_perm(send, axis, bit)
+        bit *= 2
+    return acc.reshape((-1,) + value.shape[1:])
+
+
+def all_gather_rows(value, axis):
+    count = lax.axis_size(axis)
+    if not is_pow2(count):
+        return lax.all_gather(value, axis, axis=0, tiled=True)
+    me = lax.axis_index(axis)
+    arr = value[None]
+    bit = count // 2
+    while bit >= 1:
+        low = (me // bit) % 2 == 0
+        other = xor_perm(arr, axis, bit)
+        first = jnp.where(low, arr, other)
+        second = jnp.where(low, other, arr)
+        arr = jnp.stack([first, second], axis=1).reshape((-1,) + value.shape)
+        bit //= 2
+    return arr.reshape((-1,) + value.shape[1:])
+
+
+def all_sum(value, axis):
+    count = lax.axis_size(axis)
+    if not is_pow2(count):
+        return lax.psum(value, axis)
+    bit = 1
+    while bit < count:
+        value = value + xor_perm(value, axis, bit)
+        bit *= 2
+    return value
+
+
 def local(hidden, proj_w, queries, lengths, candidates):
     mp_count = lax.axis_size("mp")
     owners = lax.axis_size("enc") * mp_count
@@ -56,11 +110,8 @@
     all_cand = lax.all_gather(candidates, ("enc", "mp"), axis=0, tiled=True)
     all_cand = all_cand.reshape(owners, slot_count)
 
-    e_pre = lax.psum_scatter(
-        jnp.dot(hidden, proj_w, preferred_element_type=jnp.float32),
-        "mp",
-        scatter_dimension=0,
-        tiled=True,
+    e_pre = reduce_scatter_rows(
+        jnp.dot(hidden, proj_w, preferred_element_type=jnp.float32), "mp"
     )
     scale = lax.rsqrt(jnp.sum(e_pre * e_pre, -1, keepdims=True) + 1e-06)
     embedded = (e_pre * scale).astype(jnp.bfloat16)
@@ -84,7 +135,7 @@
     scores, weights = soft_max_sim(sim_tile, valid_mask[:, :, None, :])
 
     placed = jnp.sum(jnp.where(pick, scores[:, :, None], jnp.float32(0)), axis=1)
-    all_scores = lax.psum(placed, ("enc", "mp")).reshape(owners * qry_dev, cand_count)
+    all_scores = all_sum(lax.psum(placed, "mp"), "enc").reshape(owners * qry_dev, cand_count)
     all_losses, d_score = loss_terms(all_scores)
     losses = lax.dynamic_slice_in_dim(all_losses, me * qry_dev, qry_dev)
 
@@ -102,8 +153,8 @@
     grad_flat = grad_emb.reshape(row_share, emb_width)
     dot_e = jnp.sum(e_pre * grad_flat, -1, keepdims=True)
     de_pre = (scale * grad_flat - e_pre * (scale * scale * scale) * dot_e).astype(jnp.bfloat16)
-    partial_w = left_product(hidden, lax.all_gather(de_pre, "mp", axis=0, tiled=True))
-    grad_w = lax.psum(partial_w, "enc")
+    partial_w = left_product(hidden, all_gather_rows(de_pre, "mp"))
+    grad_w = all_sum(partial_w, "enc")
     return (losses, grad_w)
 
 

time: 256 us -> 217 us (0.85)
  blocking collectives: 56.2 us -> 29 us
  waiting for transfers between devices: 109 us -> 84.4 us
  local copies, waits for them, and re-layouts: 27 us -> 37.1 us
  other arithmetic: 13.4 us -> 21.7 us
  matrix products: 34.7 us -> 26.8 us
  starting transfers between devices: 0.17 us -> 2.99 us
    ppermute x0 -> x8, waiting for transfers between devices: none -> 78.1 us  [xor_perm(): return lax.ppermute(value, axis, [(i, i ^ bit) for i in range(count)])]
    reduce_scatter x1 -> x0, waiting for transfers between devices: 38.4 us -> none  [local(): lax.psum_scatter(jnp.dot(hidden, proj_w, preferred_element_type=jnp.float...]
    psum x1 -> x0, waiting for transfers between devices: 34 us -> none  [local(): grad_w = lax.psum(partial_w, 'enc')]
    all_gather x1 -> x0, waiting for transfers between devices: 31.6 us -> none  [local(): lax.all_gather(de_pre, 'mp', axis=0, tiled=True)]
    psum x1, blocking collectives: 32.9 us -> 6.04 us  [local(): lax.psum(placed, 'mp')]
    unnamed x13 -> x22, local copies, waits for them, and re-layouts: 4.29 us -> 10.2 us
    reshape x0 -> x2, other arithmetic: none -> 5.53 us  [the longest x1 5.34 us: reduce_scatter_rows(): acc = acc.reshape((acc.shape[0] // 2, 2) + acc.shape[1:])]
    dot_general x1, matrix products: 6.84 us -> 1.53 us  [left_product(): lax.dot_general(left, right, (((0,), (0,)), ((), ())), preferred_element_...]
  transfers between devices with their start and end apart: 4 -> 9, of which waited for: 4 -> 8; matrix products, arithmetic and copies ran while one was open for 7% -> 7% of each run, Pallas kernels for 0% -> 0%
where the time goes in v2:
time: 217 us; the launch traced here: 216 us
  waiting for transfers between devices  84.4 us (39%)
  local copies, waits for them, and re-layouts  37.1 us (17%)
  blocking collectives  29 us (13%)
  matrix products  26.8 us (12%)
  other arithmetic  21.7 us (10%)
  between operations  14.4 us (7%)
  starting transfers between devices  2.99 us (1%)
    ppermute x8, waiting for transfers between devices, xor_perm(): return lax.ppermute(value, axis, [(i, i ^ bit) for i in range(count)])  78.1 us
    all_gather x1, blocking collectives, local(): all_cand = lax.all_gather(candidates, ('enc', 'mp'), axis=0, tiled=True)  22.9 us
    unnamed x22, local copies, waits for them, and re-layouts  10.2 us
    dot_general x1, matrix products, local(): jnp.einsum('scij,scie->scje', weights, q_e, preferred_element_type=jnp.fl...  8.23 us
    reshape x1, local copies, waits for them, and re-layouts, local(): occ_grad.reshape(owners, capacity, BLK * emb_width)  7.31 us
    all_gather x1, waiting for transfers between devices, local(): all_queries = lax.all_gather(queries, ('enc', 'mp'), axis=0, tiled=True)  6.35 us
    dot_general x1, matrix products, local(): jnp.einsum('scb,scx->bx', onehot.astype(jnp.bfloat16), occ_grad.reshape(o...  6.14 us
    psum x1, blocking collectives, local(): lax.psum(placed, 'mp')  6.04 us
  transfers between devices with their start and end apart: 9, of which 8 were waited for; matrix products, arithmetic and copies ran while one was open for 7% of the time, Pallas kernels for 0%

profile of v2, /device:TPU:0, one launch (start us, length us, event | category | flops | bytes accessed | tf_op | source)
XLA Modules:
  0.0 216.4 jit_solution(15538874289616361412)
XLA Ops:
  8.0 5.7 %fusion.30 = f32[16384,128]{1,0:T(8,128)S(1)} fusion(bf16[16384,256]{1,0:T(8,128)(2,1)} %param.5, bf16[256,128]{1,0:T(8,128)(2,1)S(1)} %copy-done), kind=kOutput, calls=%fused_computation.108 | convolution fusion | flops 1073741824 | bytes 16842752 | tf_op jit(solution)/shard_map/dot_general | solution.py:114
  13.7 2.6 %select_bitcast_fusion = f32[2,4096,128]{2,1,0:T(8,128)} fusion(f32[2,2,4096,128]{3,2,1,0:T(8,128)S(1)} %bitcast.103, pred[]{:T(512)S(6)} %eq.60), kind=kLoop, calls=%fused_computation.15 | loop fusion | flops 1048576 | bytes 12582913 | tf_op jit(solution)/shard_map/jit(_where)/select_n | solution.py:62
  16.4 1.8 copy-done.3
  18.7 22.9 %all_gather.6 = s32[128,16]{1,0:T(8,128)S(1)} all-gather(s32[8,16]{1,0:T(8,128)S(1)} %copy-done.7), channel_id=1, replica_groups=mesh['groups'=2,'enc'=4,'mp'=4] {'enc','mp'}, dimensions={0}, use_global_device_ids=true | all-gather | bytes 8704 | tf_op jit(solution)/shard_map/all_gather | solution.py:110
  41.7 5.3 %fusion = f32[1,2,4096,128]{3,2,1,0:T(8,128)S(1)} fusion(f32[2,4096,128]{2,1,0:T(8,128)} %collective-permute-done, f32[2,2,4096,128]{3,2,1,0:T(8,128)} %bitcast.104, pred[]{:T(512)S(6)} %eq.60), kind=kLoop, calls=%fused_computation.11 | loop fusion | flops 2097152 | bytes 16777216 | tf_op jit(solution)/shard_map/reshape | solution.py:59
  47.1 1.9 copy-done.4
  50.1 1.9 gather_fusion.3
  52.4 1.9 gather_fusion
  54.7 6.4 %all-gather.2.cloned.1.call-done = bf16[128,32,128]{2,1,0:T(8,128)(2,1)} async-done(((bf16[8,32,128]{2,1,0:T(8,128)(2,1)}), bf16[128,32,128]{2,1,0:T(8,128)(2,1)}) %all-gather.2.cloned.1.call-update) | async-done | bytes 1048592 | tf_op jit(solution)/shard_map/all_gather | solution.py:109
  61.1 3.5 %gather_fusion.1 = bf16[256,32,128]{2,1,0:T(8,128)(2,1)} fusion(bf16[128,32,128]{2,1,0:T(8,128)(2,1)} %all-gather.2.cloned.1.call-done, s32[1024]{0:T(1024)S(1)} %pad_clamp_fusion.1), kind=kCustom, calls=%fused_computation.1 | custom fusion | bytes 4195328 | tf_op jit(solution)/shard_map/gather | solution.py:132
  64.6 32.7 %collective-permute-done.1 = f32[1,4096,128]{2,1,0:T(8,128)} collective-permute-done((f32[1,4096,128]{2,1,0:T(8,128)S(1)}, f32[1,4096,128]{2,1,0:T(8,128)}, u32[]{:S(2)}, u32[]{:S(2)}) %collective-permute-start.1) | collective-permute-done | bytes 2097184 | tf_op jit(solution)/shard_map/ppermute | solution.py:44
  97.3 3.5 %fusion.3 = (f32[4096]{0:T(1024)S(1)}, f32[1,4096,128]{2,1,0:T(8,128)S(1)}) fusion(f32[1,4096,128]{2,1,0:T(8,128)} %collective-permute-done.1, f32[1,2,4096,128]{3,2,1,0:T(8,128)} %copy-done.4, pred[]{:T(512)S(6)} %eq.59), kind=kLoop, calls=%fused_computation.21 | loop fusion | flops 2093056 | bytes 8404993 | tf_op jit(solution)/shard_map/reduce_sum | solution.py:116
  101.6 3.0 %gather_fusion.2 = bf16[256,64,128]{2,1,0:T(8,128)(2,1)} fusion(bf16[64,64,128]{2,1,0:T(8,128)(2,1)S(1)} %multiply_convert_fusion.1, s32[1024]{0:T(1024)S(1)} %pad_clamp_fusion), kind=kCustom, calls=%fused_computation.2 | custom fusion | bytes 8389632 | tf_op jit(solution)/shard_map/gather | solution.py:131
  104.6 5.2 %select_reduce_fusion = (f32[16,16,32]{2,1,0:T(8,128)S(1)}, f32[16,16,32,64]{3,2,1,0:T(8,128)S(1)}) fusion(pred[16,16,64]{2,1,0:T(8,128)(4,1)S(1)} %add_compare_fusion, bf16[16,16,32,128]{3,2,1,0:T(8,128)(2,1)} %bitcast.110, bf16[16,16,64,128]{3,2,1,0:T(8,128)(2,1)} %bitcast.109), kind=kOutput, calls=%fused_computation.16 | convolution fusion | flops 135258112 | bytes 8437760 | tf_op jit(solution)/shard_map/scie,scje->scij/dot_general | solution.py:134
  109.8 2.0 copy-done.5
  111.8 2.4 %fusion.2 = f32[16,16,32]{2,1,0:T(8,128)S(1)} fusion(f32[16,16,32,64]{3,2,1,0:T(8,128)S(1)} %get-tuple-element.33, f32[16,16,32]{2,1,0:T(8,128)S(1)} %get-tuple-element.32, pred[16,16,64]{2,1,0:T(8,128)(4,1)S(1)} %add_compare_fusion), kind=kLoop, calls=%fused_computation.17 | loop fusion | flops 1564672 | bytes 2179072 | tf_op jit(solution)/shard_map/reduce_sum | solution.py:22
  114.4 6.0 %psum.7 = f32[16,128]{1,0:T(8,128)S(1)} all-reduce(f32[16,128]{1,0:T(8,128)S(1)} %select_reduce_fusion.1), channel_id=1, replica_groups=mesh['groups'=2,'enc'=4,'mp'=4] {'mp'}, use_global_device_ids=true, to_apply=%region_7.8 | all-reduce | flops 2048 | bytes 16384 | tf_op jit(solution)/shard_map/psum | solution.py:138
  120.6 3.6 %collective-permute-done.2 = f32[16,128]{1,0:T(8,128)S(1)} collective-permute-done((f32[16,128]{1,0:T(8,128)S(1)}, f32[16,128]{1,0:T(8,128)S(1)}, u32[]{:S(2)}, u32[]{:S(2)}) %collective-permute-start.2) | collective-permute-done | bytes 8224 | tf_op jit(solution)/shard_map/ppermute | solution.py:44
  125.2 3.6 %collective-permute-done.3 = f32[16,128]{1,0:T(8,128)S(1)} collective-permute-done((f32[16,128]{1,0:T(8,128)S(1)}, f32[16,128]{1,0:T(8,128)S(1)}, u32[]{:S(2)}, u32[]{:S(2)}) %collective-permute-start.3) | collective-permute-done | bytes 8224 | tf_op jit(solution)/shard_map/ppermute | solution.py:44
  129.4 1.9 gather_fusion.4
  131.4 8.2 %multiply_convert_fusion = bf16[16,16,64,128]{3,2,1,0:T(8,128)(2,1)} fusion(f32[16,16]{1,0:T(8,128)S(1)} %select_multiply_fusion, bf16[16,16,32,128]{3,2,1,0:T(8,128)(2,1)} %bitcast.111, f32[16,16,32,64]{3,2,1,0:T(8,128)} %copy-done.5, f32[16,16,32]{2,1,0:T(8,128)S(1)} %fusion.2, f32[16,16,32]{2,1,0:T(8,128)S(1)} %get-tuple-element.32, ...), kind=kOutput, calls=%fused_computation.6 | convolution fusion | flops 140509184 | bytes 8471552 | tf_op jit(solution)/shard_map/scij,scie->scje/dot_general | solution.py:144
  139.6 7.3 %reshape.496 = bf16[16,16,8192]{2,1,0:T(8,128)(2,1)} reshape(bf16[16,16,64,128]{3,2,1,0:T(8,128)(2,1)} %multiply_convert_fusion) | data formatting | bytes 8388608 | tf_op jit(solution)/shard_map/reshape | solution.py:150
  146.9 6.1 %convolution_bitcast_fusion = f32[64,8192]{1,0:T(8,128)} fusion(bf16[16,16,8192]{2,1,0:T(8,128)(2,1)} %reshape.496, s32[16,16]{0,1:T(8,128)S(1)} %copy.51, pred[16,16]{0,1:T(8,128)(4,1)S(1)} %copy.52), kind=kOutput, calls=%fused_computation.5 | convolution fusion | flops 268468224 | bytes 6292736 | tf_op jit(solution)/shard_map/scb,scx->bx/dot_general | solution.py:147
  153.1 2.7 %reshape.498 = f32[4096,128]{1,0:T(8,128)} reshape(f32[64,8192]{1,0:T(8,128)} %convolution_bitcast_fusion) | data formatting | bytes 4194304 | tf_op jit(solution)/shard_map/reshape | solution.py:153
  155.8 2.7 %reshape.497 = f32[1,4096,128]{2,1,0:T(8,128)} reshape(f32[64,8192]{1,0:T(8,128)} %convolution_bitcast_fusion) | data formatting | bytes 4194304 | tf_op jit(solution)/shard_map/reshape | solution.py:153
  158.5 2.4 %fusion.4 = f32[4096]{0:T(1024)S(1)} fusion(f32[4096,128]{1,0:T(8,128)} %reshape.498, f32[1,4096,128]{2,1,0:T(8,128)S(1)} %get-tuple-element.19), kind=kLoop, calls=%fused_computation.22 | loop fusion | flops 1044480 | bytes 4210688 | tf_op jit(solution)/shard_map/reduce_sum | solution.py:154
  160.8 1.9 subtract_convert_fusion
  163.9 21.4 %collective-permute-done.4 = bf16[1,4096,128]{2,1,0:T(8,128)(2,1)S(1)} collective-permute-done((bf16[1,4096,128]{2,1,0:T(8,128)(2,1)S(1)}, bf16[1,4096,128]{2,1,0:T(8,128)(2,1)S(1)}, u32[]{:S(2)}, u32[]{:S(2)}) %collective-permute-start.4) | collective-permute-done | bytes 1048608 | tf_op jit(solution)/shard_map/ppermute | solution.py:44
  185.8 4.1 %collective-permute-done.5 = bf16[2,4096,128]{2,1,0:T(8,128)(2,1)S(1)} collective-permute-done((bf16[2,4096,128]{2,1,0:T(8,128)(2,1)S(1)}, bf16[2,4096,128]{2,1,0:T(8,128)(2,1)S(1)}, u32[]{:S(2)}, u32[]{:S(2)}) %collective-permute-start.5) | collective-permute-done | bytes 2097184 | tf_op jit(solution)/shard_map/ppermute | solution.py:44
  193.5 1.5 convolution_bitcast_fusion.1
  195.3 5.3 %collective-permute-done.6 = f32[256,128]{0,1:T(8,128)S(1)} collective-permute-done((f32[256,128]{0,1:T(8,128)S(1)}, f32[256,128]{0,1:T(8,128)S(1)}, u32[]{:S(2)}, u32[]{:S(2)}) %collective-permute-start.6) | collective-permute-done | bytes 131104 | tf_op jit(solution)/shard_map/ppermute | solution.py:44
  201.6 7.3 %collective-permute-done.7 = f32[256,128]{0,1:T(8,128)S(1)} collective-permute-done((f32[256,128]{0,1:T(8,128)S(1)}, f32[256,128]{0,1:T(8,128)S(1)}, u32[]{:S(2)}, u32[]{:S(2)}) %collective-permute-start.7) | collective-permute-done | bytes 131104 | tf_op jit(solution)/shard_map/ppermute | solution.py:44
  (82 shorter events, 13.0 us)
Async XLA Ops:
  7.2 0.8 copy-start
  7.2 53.9 %all-gather.2.cloned.1.call-start = ((), (), s32[]{:S(2)}) async-start(), calls=%async_computation | async-start | bytes 1114112 | tf_op jit(solution)/shard_map/all_gather | solution.py:109
  13.7 4.5 %copy-start.3 = (f32[16384,128]{1,0:T(8,128)}, f32[16384,128]{1,0:T(8,128)S(1)}, u32[]{:S(2)}) copy-start(f32[16384,128]{1,0:T(8,128)S(1)} %fusion.30) | copy-start | bytes 25165828
  13.7 5.0 %copy-start.7 = (s32[8,16]{1,0:T(8,128)S(1)}, s32[8,16]{1,0:T(8,128)}, u32[]{:S(2)}) copy-start(s32[8,16]{1,0:T(8,128)} %param.9) | copy-start | bytes 1540
  18.2 23.5 %collective-permute-start = (f32[2,4096,128]{2,1,0:T(8,128)}, f32[2,4096,128]{2,1,0:T(8,128)}, u32[]{:S(2)}, u32[]{:S(2)}) collective-permute-start(f32[2,4096,128]{2,1,0:T(8,128)} %select_bitcast_fusion), channel_id=1, source_target_pairs={{0,1},{1,0},{2,3},{3,2},{4,5},{5,4},{6,7},{7,6},{8,9},{9,8},{10,11... | collective-permute-start | bytes 12582920 | tf_op jit(solution)/shard_map/ppermute | solution.py:44
  47.1 1.9 copy-start.4
  49.2 48.0 %collective-permute-start.1 = (f32[1,4096,128]{2,1,0:T(8,128)S(1)}, f32[1,4096,128]{2,1,0:T(8,128)}, u32[]{:S(2)}, u32[]{:S(2)}) collective-permute-start(f32[1,4096,128]{2,1,0:T(8,128)S(1)} %select_bitcast_fusion.3), channel_id=1, source_target_pairs={{0,2},{1,3},{2,0},{3,1},{4,6},{5,7},{6,4},{7,5},{8,10},{9,11},{10,... | collective-permute-start | bytes 6291464 | tf_op jit(solution)/shard_map/ppermute | solution.py:44
  50.1 2.3 %copy-start.2 = (s32[256]{0:T(256)S(1)}, s32[256]{0:T(256)}, u32[]{:S(2)}) copy-start(s32[256]{0:T(256)} %param.8) | copy-start | bytes 3076
  109.8 2.0 copy-start.5
  120.5 3.7 %collective-permute-start.2 = (f32[16,128]{1,0:T(8,128)S(1)}, f32[16,128]{1,0:T(8,128)S(1)}, u32[]{:S(2)}, u32[]{:S(2)}) collective-permute-start(f32[16,128]{1,0:T(8,128)S(1)} %psum.7), channel_id=1, source_target_pairs={{0,4},{4,0},{8,12},{12,8},{1,5},{5,1},{9,13},{13,9},{2,6},{6,2},{1... | collective-permute-start | bytes 24584 | tf_op jit(solution)/shard_map/ppermute | solution.py:44
  124.2 4.5 %collective-permute-start.3 = (f32[16,128]{1,0:T(8,128)S(1)}, f32[16,128]{1,0:T(8,128)S(1)}, u32[]{:S(2)}, u32[]{:S(2)}) collective-permute-start(f32[16,128]{1,0:T(8,128)S(1)} %add.254), channel_id=1, source_target_pairs={{0,8},{4,12},{8,0},{12,4},{1,9},{5,13},{9,1},{13,5},{2,10},{6,14},... | collective-permute-start | bytes 24584 | tf_op jit(solution)/shard_map/ppermute | solution.py:44
  158.5 2.4 %copy-start.6 = (f32[1,4096,128]{2,1,0:T(8,128)S(1)}, f32[1,4096,128]{2,1,0:T(8,128)}, u32[]{:S(2)}) copy-start(f32[1,4096,128]{2,1,0:T(8,128)} %reshape.497) | copy-start | bytes 6291460
  162.8 22.6 %collective-permute-start.4 = (bf16[1,4096,128]{2,1,0:T(8,128)(2,1)S(1)}, bf16[1,4096,128]{2,1,0:T(8,128)(2,1)S(1)}, u32[]{:S(2)}, u32[]{:S(2)}) collective-permute-start(bf16[1,4096,128]{2,1,0:T(8,128)(2,1)S(1)} %subtract_convert_fusion), channel_id=1, source_target_pairs={{0,2},{1,3},{2,0},{3,1},{4,6},{5,7},{6,4},{7,5},{8,10},{9,11},{10,... | collective-permute-start | bytes 3145736 | tf_op jit(solution)/shard_map/ppermute | solution.py:44
  185.7 4.2 %collective-permute-start.5 = (bf16[2,4096,128]{2,1,0:T(8,128)(2,1)S(1)}, bf16[2,4096,128]{2,1,0:T(8,128)(2,1)S(1)}, u32[]{:S(2)}, u32[]{:S(2)}) collective-permute-start(bf16[2,4096,128]{2,1,0:T(8,128)(2,1)S(1)} %maximum_bitcast_fusion), channel_id=1, source_target_pairs={{0,1},{1,0},{2,3},{3,2},{4,5},{5,4},{6,7},{7,6},{8,9},{9,8},{10,11... | collective-permute-start | bytes 6291464 | tf_op jit(solution)/shard_map/ppermute | solution.py:44
  189.9 2.2 %slice-start = ((s8[8388608]{0:T(1024)(128)(4,1)}), s8[4194304]{0:T(1024)(128)(4,1)S(1)}, s32[]{:S(2)}) async-start(s8[8388608]{0:T(1024)(128)(4,1)} %bitcast.105), calls=%async_computation.1 | async-start | bytes 8388608
  190.2 3.3 %slice-start.1 = ((s8[8388608]{0:T(1024)(128)(4,1)}), s8[4194304]{0:T(1024)(128)(4,1)S(1)}, s32[]{:S(2)}) async-start(s8[8388608]{0:T(1024)(128)(4,1)} %bitcast.105), calls=%async_computation.2 | async-start | bytes 8388608
  193.5 16.1 %copy-start.1 = (bf16[256,128]{1,0:T(8,128)(2,1)S(1)}, bf16[256,128]{1,0:T(8,128)(2,1)}, u32[]{:S(2)}) copy-start(bf16[256,128]{1,0:T(8,128)(2,1)} %param.6) | copy-start | bytes 196612
  195.0 5.6 %collective-permute-start.6 = (f32[256,128]{0,1:T(8,128)S(1)}, f32[256,128]{0,1:T(8,128)S(1)}, u32[]{:S(2)}, u32[]{:S(2)}) collective-permute-start(f32[256,128]{0,1:T(8,128)S(1)} %convolution_bitcast_fusion.1), channel_id=1, source_target_pairs={{0,4},{4,0},{8,12},{12,8},{1,5},{5,1},{9,13},{13,9},{2,6},{6,2},{1... | collective-permute-start | bytes 393224 | tf_op jit(solution)/shard_map/ppermute | solution.py:44
  200.6 8.2 %collective-permute-start.7 = (f32[256,128]{0,1:T(8,128)S(1)}, f32[256,128]{0,1:T(8,128)S(1)}, u32[]{:S(2)}, u32[]{:S(2)}) collective-permute-start(f32[256,128]{0,1:T(8,128)S(1)} %add.261), channel_id=1, source_target_pairs={{0,8},{4,12},{8,0},{12,4},{1,9},{5,13},{9,1},{13,5},{2,10},{6,14},... | collective-permute-start | bytes 393224 | tf_op jit(solution)/shard_map/ppermute | solution.py:44
Sparse Core Ops, SparseCore 0:
  18.8 42.2 all-gather.1

commit v3 on v2

--- a/solution.py
+++ b/solution.py
@@ -134,6 +134,8 @@
     sim_tile = jnp.einsum("scie,scje->scij", q_e, tiles, preferred_element_type=jnp.float32)
     scores, weights = soft_max_sim(sim_tile, valid_mask[:, :, None, :])
 
+    occ_raw = jnp.einsum("scij,scie->scje", weights, q_e, preferred_element_type=jnp.float32)
+
     placed = jnp.sum(jnp.where(pick, scores[:, :, None], jnp.float32(0)), axis=1)
     all_scores = all_sum(lax.psum(placed, "mp"), "enc").reshape(owners * qry_dev, cand_count)
     all_losses, d_score = loss_terms(all_scores)
@@ -141,13 +143,12 @@
 
     d_e = jnp.take_along_axis(d_score.reshape(owners, slot_count), slot_of, axis=1)
     d_e = jnp.where(valid, d_e, jnp.float32(0))
-    occ_grad = jnp.einsum("scij,scie->scje", weights, q_e, preferred_element_type=jnp.float32)
-    occ_grad = (occ_grad * (d_e / query_len)[:, :, None, None]).astype(jnp.bfloat16)
+    occ_grad = (occ_raw * (d_e / query_len)[:, :, None, None]).astype(jnp.bfloat16)
     onehot = (local_of[:, :, None] == jnp.arange(blk_dev, dtype=jnp.int32)) & valid[:, :, None]
     grad_emb = jnp.einsum(
-        "scb,scx->bx",
+        "scb,scje->bje",
         onehot.astype(jnp.bfloat16),
-        occ_grad.reshape(owners, capacity, BLK * emb_width),
+        occ_grad,
         preferred_element_type=jnp.float32,
     )
     grad_flat = grad_emb.reshape(row_share, emb_width)

time: 217 us -> 199 us (0.917)
  local copies, waits for them, and re-layouts: 37.1 us -> 25.8 us
  matrix products: 26.8 us -> 22 us
    reshape x3 -> x0, local copies, waits for them, and re-layouts: 12.7 us -> none  [the longest x1 7.31 us: local(): occ_grad.reshape(owners, capacity, BLK * emb_width)]
    dot_general x1, matrix products: 6.14 us -> 2.62 us  [local(): jnp.einsum('scb,scje->bje', onehot.astype(jnp.bfloat16), occ_grad, prefer...]
    unnamed x22 -> x20, local copies, waits for them, and re-layouts: 10.2 us -> 10.2 us
  transfers between devices with their start and end apart: 9 -> 9, of which waited for: 8 -> 8; matrix products, arithmetic and copies ran while one was open for 7% -> 8% of each run, Pallas kernels for 0% -> 0%
where the time goes in v3:
time: 199 us
  waiting for transfers between devices  84.5 us (42%)
  blocking collectives  29 us (15%)
  local copies, waits for them, and re-layouts  25.8 us (13%)
  matrix products  22 us (11%)
  other arithmetic  20 us (10%)
  between operations  14.5 us (7%)
  starting transfers between devices  2.99 us (2%)
    ppermute x8, waiting for transfers between devices, xor_perm(): return lax.ppermute(value, axis, [(i, i ^ bit) for i in range(count)])  78.1 us
    all_gather x1, blocking collectives, local(): all_cand = lax.all_gather(candidates, ('enc', 'mp'), axis=0, tiled=True)  22.9 us
    unnamed x20, local copies, waits for them, and re-layouts  10.2 us
    dot_general x1, matrix products, local(): jnp.einsum('scij,scie->scje', weights, q_e, preferred_element_type=jnp.fl...  6.94 us
    all_gather x1, waiting for transfers between devices, local(): all_queries = lax.all_gather(queries, ('enc', 'mp'), axis=0, tiled=True)  6.35 us
    psum x1, blocking collectives, local(): lax.psum(placed, 'mp')  6.04 us
    dot_general x1, matrix products, local(): jnp.dot(hidden, proj_w, preferred_element_type=jnp.float32)  5.7 us
    reshape x1, other arithmetic, reduce_scatter_rows(): acc = acc.reshape((acc.shape[0] // 2, 2) + acc.shape[1:])  5.34 us
  transfers between devices with their start and end apart: 9, of which 8 were waited for; matrix products, arithmetic and copies ran while one was open for 8% of the time, Pallas kernels for 0%

profile of v3, /device:TPU:0, one launch (start us, length us, event | category | flops | bytes accessed | tf_op | source)
XLA Modules:
  0.0 198.7 jit_solution(12886464144895850502)
XLA Ops:
  8.0 5.7 %fusion.37 = f32[16384,128]{1,0:T(8,128)S(1)} fusion(bf16[16384,256]{1,0:T(8,128)(2,1)} %param.5, bf16[256,128]{1,0:T(8,128)(2,1)S(1)} %copy-done), kind=kOutput, calls=%fused_computation.112 | convolution fusion | flops 1073741824 | bytes 16842752 | tf_op jit(solution)/shard_map/dot_general | solution.py:114
  13.7 2.6 %select_bitcast_fusion = f32[2,4096,128]{2,1,0:T(8,128)} fusion(f32[2,2,4096,128]{3,2,1,0:T(8,128)S(1)} %bitcast.112, pred[]{:T(512)S(6)} %eq.60), kind=kLoop, calls=%fused_computation.15 | loop fusion | flops 1048576 | bytes 12582913 | tf_op jit(solution)/shard_map/jit(_where)/select_n | solution.py:62
  16.4 1.8 copy-done.3
  18.7 22.9 %all_gather.6 = s32[128,16]{1,0:T(8,128)S(1)} all-gather(s32[8,16]{1,0:T(8,128)S(1)} %copy-done.6), channel_id=1, replica_groups=mesh['groups'=2,'enc'=4,'mp'=4] {'enc','mp'}, dimensions={0}, use_global_device_ids=true | all-gather | bytes 8704 | tf_op jit(solution)/shard_map/all_gather | solution.py:110
  41.7 5.3 %fusion = f32[1,2,4096,128]{3,2,1,0:T(8,128)S(1)} fusion(f32[2,4096,128]{2,1,0:T(8,128)} %collective-permute-done, f32[2,2,4096,128]{3,2,1,0:T(8,128)} %bitcast.113, pred[]{:T(512)S(6)} %eq.60), kind=kLoop, calls=%fused_computation.10 | loop fusion | flops 2097152 | bytes 16777216 | tf_op jit(solution)/shard_map/reshape | solution.py:59
  47.1 1.9 copy-done.4
  50.1 1.9 gather_fusion.3
  52.4 1.9 gather_fusion
  54.7 6.4 %all-gather.2.cloned.1.call-done = bf16[128,32,128]{2,1,0:T(8,128)(2,1)} async-done(((bf16[8,32,128]{2,1,0:T(8,128)(2,1)}), bf16[128,32,128]{2,1,0:T(8,128)(2,1)}) %all-gather.2.cloned.1.call-update) | async-done | bytes 1048592 | tf_op jit(solution)/shard_map/all_gather | solution.py:109
  61.1 3.4 %gather_fusion.1 = bf16[256,32,128]{2,1,0:T(8,128)(2,1)} fusion(bf16[128,32,128]{2,1,0:T(8,128)(2,1)} %all-gather.2.cloned.1.call-done, s32[1024]{0:T(1024)S(1)} %pad_clamp_fusion.1), kind=kCustom, calls=%fused_computation.1 | custom fusion | bytes 4195328 | tf_op jit(solution)/shard_map/gather | solution.py:132
  64.5 32.8 %collective-permute-done.1 = f32[1,4096,128]{2,1,0:T(8,128)} collective-permute-done((f32[1,4096,128]{2,1,0:T(8,128)S(1)}, f32[1,4096,128]{2,1,0:T(8,128)}, u32[]{:S(2)}, u32[]{:S(2)}) %collective-permute-start.1) | collective-permute-done | bytes 2097184 | tf_op jit(solution)/shard_map/ppermute | solution.py:44
  97.3 3.5 %fusion.7 = (f32[4096]{0:T(1024)S(1)}, f32[1,4096,128]{2,1,0:T(8,128)S(1)}) fusion(f32[1,4096,128]{2,1,0:T(8,128)} %collective-permute-done.1, f32[1,2,4096,128]{3,2,1,0:T(8,128)} %copy-done.4, pred[]{:T(512)S(6)} %eq.59), kind=kLoop, calls=%fused_computation.25 | loop fusion | flops 2093056 | bytes 8404993 | tf_op jit(solution)/shard_map/reduce_sum | solution.py:116
  101.6 3.0 %gather_fusion.2 = bf16[256,64,128]{2,1,0:T(8,128)(2,1)} fusion(bf16[64,64,128]{2,1,0:T(8,128)(2,1)S(1)} %multiply_convert_fusion.1, s32[1024]{0:T(1024)S(1)} %pad_clamp_fusion), kind=kCustom, calls=%fused_computation.2 | custom fusion | bytes 8389632 | tf_op jit(solution)/shard_map/gather | solution.py:131
  104.6 5.2 %select_reduce_fusion = (f32[16,16,32]{2,1,0:T(8,128)S(1)}, f32[16,16,32,64]{3,2,1,0:T(8,128)S(1)}) fusion(pred[16,16,64]{2,1,0:T(8,128)(4,1)S(1)} %add_compare_fusion, bf16[16,16,32,128]{3,2,1,0:T(8,128)(2,1)} %bitcast.120, bf16[16,16,64,128]{3,2,1,0:T(8,128)(2,1)} %bitcast.119), kind=kOutput, calls=%fused_computation.16 | convolution fusion | flops 135258112 | bytes 8437760 | tf_op jit(solution)/shard_map/scie,scje->scij/dot_general | solution.py:134
  109.8 1.9 copy-done.5
  111.7 2.4 %fusion.3 = f32[16,16,32]{2,1,0:T(8,128)S(1)} fusion(f32[16,16,32,64]{3,2,1,0:T(8,128)S(1)} %get-tuple-element.33, f32[16,16,32]{2,1,0:T(8,128)S(1)} %get-tuple-element.32, pred[16,16,64]{2,1,0:T(8,128)(4,1)S(1)} %add_compare_fusion), kind=kLoop, calls=%fused_computation.17 | loop fusion | flops 1564672 | bytes 2179072 | tf_op jit(solution)/shard_map/reduce_sum | solution.py:22
  114.4 6.0 %psum.7 = f32[16,128]{1,0:T(8,128)S(1)} all-reduce(f32[16,128]{1,0:T(8,128)S(1)} %select_reduce_fusion.1), channel_id=1, replica_groups=mesh['groups'=2,'enc'=4,'mp'=4] {'mp'}, use_global_device_ids=true, to_apply=%region_7.8 | all-reduce | flops 2048 | bytes 16384 | tf_op jit(solution)/shard_map/psum | solution.py:140
  120.5 3.6 %collective-permute-done.2 = f32[16,128]{1,0:T(8,128)S(1)} collective-permute-done((f32[16,128]{1,0:T(8,128)S(1)}, f32[16,128]{1,0:T(8,128)S(1)}, u32[]{:S(2)}, u32[]{:S(2)}) %collective-permute-start.2) | collective-permute-done | bytes 8224 | tf_op jit(solution)/shard_map/ppermute | solution.py:44
  125.1 3.6 %collective-permute-done.3 = f32[16,128]{1,0:T(8,128)S(1)} collective-permute-done((f32[16,128]{1,0:T(8,128)S(1)}, f32[16,128]{1,0:T(8,128)S(1)}, u32[]{:S(2)}, u32[]{:S(2)}) %collective-permute-start.3) | collective-permute-done | bytes 8224 | tf_op jit(solution)/shard_map/ppermute | solution.py:44
  129.3 1.9 gather_fusion.4
  131.3 6.9 %multiply_convert_fusion = bf16[16,16,64,128]{3,2,1,0:T(8,128)(2,1)S(1)} fusion(f32[16,16]{1,0:T(8,128)S(1)} %select_multiply_fusion, bf16[16,16,32,128]{3,2,1,0:T(8,128)(2,1)} %bitcast.121, f32[16,16,32,64]{3,2,1,0:T(8,128)} %copy-done.5, f32[16,16,32]{2,1,0:T(8,128)S(1)} %fusion.3, f32[16,16,32]{2,1,0:T(8,128)S(1)} %get-tuple-element.32, ...), kind=kOutput, calls=%fused_computation.5 | convolution fusion | flops 140509184 | bytes 8471552 | tf_op jit(solution)/shard_map/scij,scie->scje/dot_general | solution.py:137
  138.3 2.6 %fusion.12 = f32[64,64,128]{2,0,1:T(8,128)S(1)} fusion(bf16[16,16,64,128]{3,2,1,0:T(8,128)(2,1)S(1)} %multiply_convert_fusion, s32[16,16]{0,1:T(8,128)S(1)} %copy.58, pred[16,16]{0,1:T(8,128)(4,1)S(1)} %copy.59), kind=kOutput, calls=%fused_computation.35 | convolution fusion | flops 268468224 | bytes 6292736 | tf_op jit(solution)/shard_map/scb,scje->bje/dot_general | solution.py:148
  140.9 1.2 copy.62
  142.8 1.9 fusion.6
  144.7 1.1 collective-permute-start.4
  145.9 21.4 %collective-permute-done.4 = bf16[1,4096,128]{2,1,0:T(8,128)(2,1)S(1)} collective-permute-done((bf16[1,4096,128]{2,1,0:T(8,128)(2,1)S(1)}, bf16[1,4096,128]{2,1,0:T(8,128)(2,1)S(1)}, u32[]{:S(2)}, u32[]{:S(2)}) %collective-permute-start.4) | collective-permute-done | bytes 1048608 | tf_op jit(solution)/shard_map/ppermute | solution.py:44
  167.7 4.1 %collective-permute-done.5 = bf16[2,4096,128]{2,1,0:T(8,128)(2,1)S(1)} collective-permute-done((bf16[2,4096,128]{2,1,0:T(8,128)(2,1)S(1)}, bf16[2,4096,128]{2,1,0:T(8,128)(2,1)S(1)}, u32[]{:S(2)}, u32[]{:S(2)}) %collective-permute-start.5) | collective-permute-done | bytes 2097184 | tf_op jit(solution)/shard_map/ppermute | solution.py:44
  172.8 1.5 slice-done
  174.3 1.4 slice-done.1
  175.7 1.5 convolution_bitcast_fusion
  177.6 5.3 %collective-permute-done.6 = f32[256,128]{0,1:T(8,128)S(1)} collective-permute-done((f32[256,128]{0,1:T(8,128)S(1)}, f32[256,128]{0,1:T(8,128)S(1)}, u32[]{:S(2)}, u32[]{:S(2)}) %collective-permute-start.6) | collective-permute-done | bytes 131104 | tf_op jit(solution)/shard_map/ppermute | solution.py:44
  183.8 7.3 %collective-permute-done.7 = f32[256,128]{0,1:T(8,128)S(1)} collective-permute-done((f32[256,128]{0,1:T(8,128)S(1)}, f32[256,128]{0,1:T(8,128)S(1)}, u32[]{:S(2)}, u32[]{:S(2)}) %collective-permute-start.7) | collective-permute-done | bytes 131104 | tf_op jit(solution)/shard_map/ppermute | solution.py:44
  (79 shorter events, 9.9 us)
Async XLA Ops:
  7.2 0.8 copy-start
  7.2 53.9 %all-gather.2.cloned.1.call-start = ((), (), s32[]{:S(2)}) async-start(), calls=%async_computation | async-start | bytes 1114112 | tf_op jit(solution)/shard_map/all_gather | solution.py:109
  13.7 4.5 %copy-start.3 = (f32[16384,128]{1,0:T(8,128)}, f32[16384,128]{1,0:T(8,128)S(1)}, u32[]{:S(2)}) copy-start(f32[16384,128]{1,0:T(8,128)S(1)} %fusion.37) | copy-start | bytes 25165828
  13.7 5.0 %copy-start.6 = (s32[8,16]{1,0:T(8,128)S(1)}, s32[8,16]{1,0:T(8,128)}, u32[]{:S(2)}) copy-start(s32[8,16]{1,0:T(8,128)} %param.9) | copy-start | bytes 1540
  18.2 23.5 %collective-permute-start = (f32[2,4096,128]{2,1,0:T(8,128)}, f32[2,4096,128]{2,1,0:T(8,128)}, u32[]{:S(2)}, u32[]{:S(2)}) collective-permute-start(f32[2,4096,128]{2,1,0:T(8,128)} %select_bitcast_fusion), channel_id=1, source_target_pairs={{0,1},{1,0},{2,3},{3,2},{4,5},{5,4},{6,7},{7,6},{8,9},{9,8},{10,11... | collective-permute-start | bytes 12582920 | tf_op jit(solution)/shard_map/ppermute | solution.py:44
  47.1 1.9 copy-start.4
  49.2 48.0 %collective-permute-start.1 = (f32[1,4096,128]{2,1,0:T(8,128)S(1)}, f32[1,4096,128]{2,1,0:T(8,128)}, u32[]{:S(2)}, u32[]{:S(2)}) collective-permute-start(f32[1,4096,128]{2,1,0:T(8,128)S(1)} %select_bitcast_fusion.3), channel_id=1, source_target_pairs={{0,2},{1,3},{2,0},{3,1},{4,6},{5,7},{6,4},{7,5},{8,10},{9,11},{10,... | collective-permute-start | bytes 6291464 | tf_op jit(solution)/shard_map/ppermute | solution.py:44
  50.1 2.3 %copy-start.2 = (s32[256]{0:T(256)S(1)}, s32[256]{0:T(256)}, u32[]{:S(2)}) copy-start(s32[256]{0:T(256)} %param.8) | copy-start | bytes 3076
  109.8 1.9 copy-start.5
  120.4 3.7 %collective-permute-start.2 = (f32[16,128]{1,0:T(8,128)S(1)}, f32[16,128]{1,0:T(8,128)S(1)}, u32[]{:S(2)}, u32[]{:S(2)}) collective-permute-start(f32[16,128]{1,0:T(8,128)S(1)} %psum.7), channel_id=1, source_target_pairs={{0,4},{4,0},{8,12},{12,8},{1,5},{5,1},{9,13},{13,9},{2,6},{6,2},{1... | collective-permute-start | bytes 24584 | tf_op jit(solution)/shard_map/ppermute | solution.py:44
  124.2 4.5 %collective-permute-start.3 = (f32[16,128]{1,0:T(8,128)S(1)}, f32[16,128]{1,0:T(8,128)S(1)}, u32[]{:S(2)}, u32[]{:S(2)}) collective-permute-start(f32[16,128]{1,0:T(8,128)S(1)} %add.254), channel_id=1, source_target_pairs={{0,8},{4,12},{8,0},{12,4},{1,9},{5,13},{9,1},{13,5},{2,10},{6,14},... | collective-permute-start | bytes 24584 | tf_op jit(solution)/shard_map/ppermute | solution.py:44
  144.7 22.6 %collective-permute-start.4 = (bf16[1,4096,128]{2,1,0:T(8,128)(2,1)S(1)}, bf16[1,4096,128]{2,1,0:T(8,128)(2,1)S(1)}, u32[]{:S(2)}, u32[]{:S(2)}) collective-permute-start(bf16[1,4096,128]{2,1,0:T(8,128)(2,1)S(1)} %fusion.6), channel_id=1, source_target_pairs={{0,2},{1,3},{2,0},{3,1},{4,6},{5,7},{6,4},{7,5},{8,10},{9,11},{10,... | collective-permute-start | bytes 3145736 | tf_op jit(solution)/shard_map/ppermute | solution.py:44
  167.6 4.2 %collective-permute-start.5 = (bf16[2,4096,128]{2,1,0:T(8,128)(2,1)S(1)}, bf16[2,4096,128]{2,1,0:T(8,128)(2,1)S(1)}, u32[]{:S(2)}, u32[]{:S(2)}) collective-permute-start(bf16[2,4096,128]{2,1,0:T(8,128)(2,1)S(1)} %maximum_bitcast_fusion), channel_id=1, source_target_pairs={{0,1},{1,0},{2,3},{3,2},{4,5},{5,4},{6,7},{7,6},{8,9},{9,8},{10,11... | collective-permute-start | bytes 6291464 | tf_op jit(solution)/shard_map/ppermute | solution.py:44
  172.1 2.2 %slice-start = ((s8[8388608]{0:T(1024)(128)(4,1)}), s8[4194304]{0:T(1024)(128)(4,1)S(1)}, s32[]{:S(2)}) async-start(s8[8388608]{0:T(1024)(128)(4,1)} %bitcast.114), calls=%async_computation.1 | async-start | bytes 8388608
  172.5 3.2 %slice-start.1 = ((s8[8388608]{0:T(1024)(128)(4,1)}), s8[4194304]{0:T(1024)(128)(4,1)S(1)}, s32[]{:S(2)}) async-start(s8[8388608]{0:T(1024)(128)(4,1)} %bitcast.114), calls=%async_computation.2 | async-start | bytes 8388608
  175.7 16.1 %copy-start.1 = (bf16[256,128]{1,0:T(8,128)(2,1)S(1)}, bf16[256,128]{1,0:T(8,128)(2,1)}, u32[]{:S(2)}) copy-start(bf16[256,128]{1,0:T(8,128)(2,1)} %param.6) | copy-start | bytes 196612
  177.2 5.6 %collective-permute-start.6 = (f32[256,128]{0,1:T(8,128)S(1)}, f32[256,128]{0,1:T(8,128)S(1)}, u32[]{:S(2)}, u32[]{:S(2)}) collective-permute-start(f32[256,128]{0,1:T(8,128)S(1)} %convolution_bitcast_fusion), channel_id=1, source_target_pairs={{0,4},{4,0},{8,12},{12,8},{1,5},{5,1},{9,13},{13,9},{2,6},{6,2},{1... | collective-permute-start | bytes 393224 | tf_op jit(solution)/shard_map/ppermute | solution.py:44
  182.9 8.2 %collective-permute-start.7 = (f32[256,128]{0,1:T(8,128)S(1)}, f32[256,128]{0,1:T(8,128)S(1)}, u32[]{:S(2)}, u32[]{:S(2)}) collective-permute-start(f32[256,128]{0,1:T(8,128)S(1)} %add.261), channel_id=1, source_target_pairs={{0,8},{4,12},{8,0},{12,4},{1,9},{5,13},{9,1},{13,5},{2,10},{6,14},... | collective-permute-start | bytes 393224 | tf_op jit(solution)/shard_map/ppermute | solution.py:44
Sparse Core Ops, SparseCore 0:
  18.8 42.2 all-gather.1

commit v4 on v3

--- a/solution.py
+++ b/solution.py
@@ -106,13 +106,23 @@
     capacity = 2 * slot_count // owners
     me = lax.axis_index("enc") * mp_count + lax.axis_index("mp")
 
-    all_queries = lax.all_gather(queries, ("enc", "mp"), axis=0, tiled=True)
-    all_cand = lax.all_gather(candidates, ("enc", "mp"), axis=0, tiled=True)
+    all_queries = all_gather_rows(all_gather_rows(queries, "mp"), "enc")
+    all_cand = all_gather_rows(all_gather_rows(candidates, "mp"), "enc")
     all_cand = all_cand.reshape(owners, slot_count)
 
-    e_pre = reduce_scatter_rows(
-        jnp.dot(hidden, proj_w, preferred_element_type=jnp.float32), "mp"
-    )
+    chunks = 4 if row_share % (4 * BLK) == 0 else 1
+    split_rows = hidden.reshape(mp_count, chunks, row_share // chunks, hidden.shape[1])
+    e_pre = jnp.stack(
+        [
+            reduce_scatter_rows(
+                jnp.dot(split_rows[:, k], proj_w, preferred_element_type=jnp.float32).reshape(
+                    mp_count * (row_share // chunks), emb_width
+                ),
+                "mp",
+            )
+            for k in range(chunks)
+        ]
+    ).reshape(row_share, emb_width)
     scale = lax.rsqrt(jnp.sum(e_pre * e_pre, -1, keepdims=True) + 1e-06)
     embedded = (e_pre * scale).astype(jnp.bfloat16)
     local_blocks = embedded.reshape(blk_dev, BLK, emb_width)

time: 199 us -> 206 us (1.035)
  starting transfers between devices: 2.99 us -> 28.7 us
  blocking collectives: 29 us -> 5.77 us
  waiting for transfers between devices: 84.5 us -> 102 us
  between operations: 14.5 us -> 1.22 us
    ppermute x8 -> x22, starting transfers between devices: 2.95 us -> 28.7 us  [xor_perm(): return lax.ppermute(value, axis, [(i, i ^ bit) for i in range(count)])]
    ppermute x8 -> x22, waiting for transfers between devices: 78.1 us -> 102 us  [xor_perm(): return lax.ppermute(value, axis, [(i, i ^ bit) for i in range(count)])]
    all_gather x1 -> x0, blocking collectives: 22.9 us -> none  [local(): all_cand = lax.all_gather(candidates, ('enc', 'mp'), axis=0, tiled=True)]
    unnamed x20 -> x29, local copies, waits for them, and re-layouts: 10.2 us -> 3.76 us
    all_gather x1 -> x0, waiting for transfers between devices: 6.35 us -> none  [local(): all_queries = lax.all_gather(queries, ('enc', 'mp'), axis=0, tiled=True)]
    slice x0 -> x1, local copies, waits for them, and re-layouts: none -> 4.76 us  [local(): split_rows[:, k]]
    reduce_sum x1, other arithmetic: 3.47 us -> 0.62 us  [local(): scale = lax.rsqrt(jnp.sum(e_pre * e_pre, -1, keepdims=True) + 1e-06)]
    dot_general x1, matrix products: 2.62 us -> 4.95 us  [local(): jnp.einsum('scb,scje->bje', onehot.astype(jnp.bfloat16), occ_grad, prefer...]
  transfers between devices with their start and end apart: 9 -> 22, of which waited for: 8 -> 15; matrix products, arithmetic and copies ran while one was open for 8% -> 15% of each run, Pallas kernels for 0% -> 0%
where the time goes in v4:
time: 206 us
  waiting for transfers between devices  102 us (50%)
  starting transfers between devices  28.7 us (14%)
  local copies, waits for them, and re-layouts  24.8 us (12%)
  matrix products  23 us (11%)
  other arithmetic  20.5 us (10%)
  blocking collectives  5.77 us (3%)
    ppermute x22, waiting for transfers between devices, xor_perm(): return lax.ppermute(value, axis, [(i, i ^ bit) for i in range(count)])  102 us
    ppermute x22, starting transfers between devices, xor_perm(): return lax.ppermute(value, axis, [(i, i ^ bit) for i in range(count)])  28.7 us
    dot_general x1, matrix products, local(): jnp.einsum('scij,scie->scje', weights, q_e, preferred_element_type=jnp.fl...  6.94 us
    reshape x4, other arithmetic, reduce_scatter_rows(): acc = acc.reshape((acc.shape[0] // 2, 2) + acc.shape[1:])  6.5 us
    psum x1, blocking collectives, local(): lax.psum(placed, 'mp')  5.77 us
    dot_general x1, matrix products, local(): jnp.einsum('scie,scje->scij', q_e, tiles, preferred_element_type=jnp.floa...  5.2 us
    dot_general x1, matrix products, local(): jnp.einsum('scb,scje->bje', onehot.astype(jnp.bfloat16), occ_grad, prefer...  4.95 us
    select_n x8, other arithmetic, reduce_scatter_rows(): send = jnp.where(low, acc[:, 1], acc[:, 0])  4.82 us
  transfers between devices with their start and end apart: 22, of which 15 were waited for; matrix products, arithmetic and copies ran while one was open for 15% of the time, Pallas kernels for 0%

profile of v4, /device:TPU:0, one launch (start us, length us, event | category | flops | bytes accessed | tf_op | source)
XLA Modules:
  0.0 205.7 jit_solution(8952737700300384375)
XLA Ops:
  0.6 3.0 %collective-permute-start = (s32[1,8,16]{2,1,0:T(8,128)}, s32[1,8,16]{2,1,0:T(8,128)S(1)}, u32[]{:S(2)}, u32[]{:S(2)}) collective-permute-start(s32[1,8,16]{2,1,0:T(8,128)} %bitcast.292), channel_id=1, source_target_pairs={{0,2},{1,3},{2,0},{3,1},{4,6},{5,7},{6,4},{7,5},{8,10},{9,11},{10,... | collective-permute-start | bytes 1544 | tf_op jit(solution)/shard_map/ppermute | solution.py:44
  3.7 4.8 %fusion.55 = (bf16[4,1,1024,256]{3,2,1,0:T(8,128)(2,1)}, bf16[4,1,1024,256]{3,2,1,0:T(8,128)(2,1)S(1)}, bf16[4,1,1024,256]{3,2,1,0:T(8,128)(2,1)S(1)}, bf16[4,1,1024,256]{3,2,1,0:T(8,128)(2,1)S(1)}) fusion(bf16[4,4,1024,256]{3,2,1,0:T(8,128)(2,1)} %bitcast.270), kind=kLoop, calls=%fused_computation.167 | loop fusion | bytes 16777216 | tf_op jit(solution)/shard_map/slice | solution.py:118
  15.3 2.3 %fusion.3 = f32[2,2,1024,128]{3,2,1,0:T(8,128)S(1)} fusion(bf16[256,128]{1,0:T(8,128)(2,1)S(1)} %copy-done, bf16[2,2,1024,256]{3,2,1,0:T(8,128)(2,1)} %bitcast.282), kind=kOutput, calls=%fused_computation.15 | convolution fusion | flops 268435456 | bytes 4259840 | tf_op jit(solution)/shard_map/dot_general | solution.py:118
  17.6 3.1 %collective-permute-start.2 = (s32[1,32,16]{2,1,0:T(8,128)S(1)}, s32[1,32,16]{2,1,0:T(8,128)S(1)}, u32[]{:S(2)}, u32[]{:S(2)}) collective-permute-start(s32[1,32,16]{2,1,0:T(8,128)S(1)} %bitcast.289), channel_id=1, source_target_pairs={{0,8},{4,12},{8,0},{12,4},{1,9},{5,13},{9,1},{13,5},{2,10},{6,14},... | collective-permute-start | bytes 6152 | tf_op jit(solution)/shard_map/ppermute | solution.py:44
  22.4 2.0 collective-permute-start.3
  24.4 2.0 collective-permute-done.3
  27.3 1.9 gather_fusion.3
  31.0 3.0 %collective-permute-start.6 = (bf16[1,32,32,128]{3,2,1,0:T(8,128)(2,1)S(1)}, bf16[1,32,32,128]{3,2,1,0:T(8,128)(2,1)S(1)}, u32[]{:S(2)}, u32[]{:S(2)}) collective-permute-start(bf16[1,32,32,128]{3,2,1,0:T(8,128)(2,1)S(1)} %bitcast.286), channel_id=1, source_target_pairs={{0,8},{4,12},{8,0},{12,4},{1,9},{5,13},{9,1},{13,5},{2,10},{6,14},... | collective-permute-start | bytes 786440 | tf_op jit(solution)/shard_map/ppermute | solution.py:44
  34.1 1.9 gather_fusion
  36.2 10.2 %collective-permute-done.6 = bf16[1,32,32,128]{3,2,1,0:T(8,128)(2,1)S(1)} collective-permute-done((bf16[1,32,32,128]{3,2,1,0:T(8,128)(2,1)S(1)}, bf16[1,32,32,128]{3,2,1,0:T(8,128)(2,1)S(1)}, u32[]{:S(2)}, u32[]{:S(2)}) %collective-permute-start.6) | collective-permute-done | bytes 262176 | tf_op jit(solution)/shard_map/ppermute | solution.py:44
  47.5 12.7 %collective-permute-done.7 = bf16[2,32,32,128]{3,2,1,0:T(8,128)(2,1)S(1)} collective-permute-done((bf16[2,32,32,128]{3,2,1,0:T(8,128)(2,1)S(1)}, bf16[2,32,32,128]{3,2,1,0:T(8,128)(2,1)S(1)}, u32[]{:S(2)}, u32[]{:S(2)}) %collective-permute-start.7) | collective-permute-done | bytes 524320 | tf_op jit(solution)/shard_map/ppermute | solution.py:44
  60.5 2.2 %gather_fusion.1 = bf16[256,32,128]{2,1,0:T(8,128)(2,1)} fusion(bf16[128,32,128]{2,1,0:T(8,128)(2,1)S(1)} %bitcast.278, s32[1024]{0:T(1024)S(1)} %pad_clamp_fusion.1), kind=kCustom, calls=%fused_computation.1 | custom fusion | bytes 4195328 | tf_op jit(solution)/shard_map/gather | solution.py:142
  62.7 2.1 %fusion.25 = f32[1,2,1024,128]{3,2,1,0:T(8,128)S(1)} fusion(f32[2,1024,128]{2,1,0:T(8,128)} %collective-permute-done.14, f32[2,2,1024,128]{3,2,0,1:T(8,128)} %copy-done.5, pred[]{:T(512)S(6)} %eq.88), kind=kLoop, calls=%fused_computation.46 | loop fusion | flops 524288 | bytes 4194305 | tf_op jit(solution)/shard_map/reshape | solution.py:59
  73.8 6.0 %collective-permute-done.15 = f32[1,1024,128]{2,1,0:T(8,128)S(1)} collective-permute-done((f32[1,1024,128]{2,1,0:T(8,128)S(1)}, f32[1,1024,128]{2,1,0:T(8,128)S(1)}, u32[]{:S(2)}, u32[]{:S(2)}) %collective-permute-start.15) | collective-permute-done | bytes 524320 | tf_op jit(solution)/shard_map/ppermute | solution.py:44
  79.9 11.2 %collective-permute-done.13 = f32[1,1024,128]{2,1,0:T(8,128)S(1)} collective-permute-done((f32[1,1024,128]{2,1,0:T(8,128)S(1)}, f32[1,1024,128]{2,1,0:T(8,128)S(1)}, u32[]{:S(2)}, u32[]{:S(2)}) %collective-permute-start.13) | collective-permute-done | bytes 524320 | tf_op jit(solution)/shard_map/ppermute | solution.py:44
  91.1 11.2 %collective-permute-done.11 = f32[1,1024,128]{2,1,0:T(8,128)S(1)} collective-permute-done((f32[1,1024,128]{2,1,0:T(8,128)S(1)}, f32[1,1024,128]{2,1,0:T(8,128)S(1)}, u32[]{:S(2)}, u32[]{:S(2)}) %collective-permute-start.11) | collective-permute-done | bytes 524320 | tf_op jit(solution)/shard_map/ppermute | solution.py:44
  102.4 9.0 %collective-permute-done.9 = f32[1,1024,128]{2,1,0:T(8,128)S(1)} collective-permute-done((f32[1,1024,128]{2,1,0:T(8,128)S(1)}, f32[1,1024,128]{2,1,0:T(8,128)S(1)}, u32[]{:S(2)}, u32[]{:S(2)}) %collective-permute-start.9) | collective-permute-done | bytes 524320 | tf_op jit(solution)/shard_map/ppermute | solution.py:44
  112.9 3.1 %gather_fusion.2 = bf16[256,64,128]{2,1,0:T(8,128)(2,1)} fusion(bf16[64,64,128]{2,1,0:T(8,128)(2,1)S(1)} %multiply_convert_fusion.1, s32[1024]{0:T(1024)S(1)} %pad_clamp_fusion), kind=kCustom, calls=%fused_computation.2 | custom fusion | bytes 8389632 | tf_op jit(solution)/shard_map/gather | solution.py:141
  116.0 5.2 %select_reduce_fusion = (f32[16,16,32]{2,1,0:T(8,128)S(1)}, f32[16,16,32,64]{3,2,1,0:T(8,128)S(1)}) fusion(pred[16,16,64]{2,1,0:T(8,128)(4,1)S(1)} %add_compare_fusion, bf16[16,16,32,128]{3,2,1,0:T(8,128)(2,1)} %bitcast.280, bf16[16,16,64,128]{3,2,1,0:T(8,128)(2,1)} %bitcast.277), kind=kOutput, calls=%fused_computation.11 | convolution fusion | flops 135258112 | bytes 8437760 | tf_op jit(solution)/shard_map/scie,scje->scij/dot_general | solution.py:144
  121.2 2.6 %fusion.2 = f32[16,16,32]{2,1,0:T(8,128)S(1)} fusion(f32[16,16,32,64]{3,2,1,0:T(8,128)S(1)} %get-tuple-element.55, f32[16,16,32]{2,1,0:T(8,128)S(1)} %get-tuple-element.54, pred[16,16,64]{2,1,0:T(8,128)(4,1)S(1)} %add_compare_fusion), kind=kLoop, calls=%fused_computation.12 | loop fusion | flops 1564672 | bytes 2179072 | tf_op jit(solution)/shard_map/reduce_sum | solution.py:22
  124.0 5.8 %psum.7 = f32[16,128]{1,0:T(8,128)S(1)} all-reduce(f32[16,128]{1,0:T(8,128)S(1)} %select_reduce_fusion.1), channel_id=1, replica_groups=mesh['groups'=2,'enc'=4,'mp'=4] {'mp'}, use_global_device_ids=true, to_apply=%region_7.8 | all-reduce | flops 2048 | bytes 16384 | tf_op jit(solution)/shard_map/psum | solution.py:150
  133.5 3.3 %collective-permute-start.17 = (f32[16,128]{1,0:T(8,128)S(1)}, f32[16,128]{1,0:T(8,128)S(1)}, u32[]{:S(2)}, u32[]{:S(2)}) collective-permute-start(f32[16,128]{1,0:T(8,128)S(1)} %add.301), channel_id=1, source_target_pairs={{0,8},{4,12},{8,0},{12,4},{1,9},{5,13},{9,1},{13,5},{2,10},{6,14},... | collective-permute-start | bytes 24584 | tf_op jit(solution)/shard_map/ppermute | solution.py:44
  139.1 1.9 gather_fusion.4
  141.1 6.9 %multiply_convert_fusion = bf16[16,16,64,128]{3,2,1,0:T(8,128)(2,1)S(1)} fusion(f32[16,16]{1,0:T(8,128)S(1)} %select_multiply_fusion, bf16[16,16,32,128]{3,2,1,0:T(8,128)(2,1)} %bitcast.281, f32[16,16,32,64]{3,2,1,0:T(8,128)} %copy-done.8, f32[16,16,32]{2,1,0:T(8,128)S(1)} %fusion.2, f32[16,16,32]{2,1,0:T(8,128)S(1)} %get-tuple-element.54, ...), kind=kOutput, calls=%fused_computation.5 | convolution fusion | flops 140509184 | bytes 8471552 | tf_op jit(solution)/shard_map/scij,scie->scje/dot_general | solution.py:147
  148.0 5.0 %fusion.14 = (f32[64,64]{0,1:T(8,128)S(1)}, f32[64,64,128]{2,0,1:T(8,128)}) fusion(f32[64,64,128]{2,1,0:T(8,128)S(1)} %bitcast.274, bf16[16,16,64,128]{3,2,1,0:T(8,128)(2,1)S(1)} %multiply_convert_fusion, s32[16,16]{0,1:T(8,128)S(1)} %copy.179, pred[16,16]{0,1:T(8,128)(4,1)S(1)} %copy.180), kind=kOutput, calls=%fused_computation.29 | convolution fusion | flops 269512704 | bytes 8406272 | tf_op jit(solution)/shard_map/scb,scje->bje/dot_general | solution.py:158
  153.1 2.8 %copy.183 = f32[64,64,128]{2,1,0:T(8,128)S(1)} copy(f32[64,64,128]{2,0,1:T(8,128)} %get-tuple-element.57) | data formatting | bytes 4194304 | tf_op jit(solution)/shard_map/scb,scje->bje/dot_general | solution.py:158
  156.0 1.9 fusion.7
  159.7 21.1 %collective-permute-done.18 = bf16[1,4096,128]{2,1,0:T(8,128)(2,1)S(1)} collective-permute-done((bf16[1,4096,128]{2,1,0:T(8,128)(2,1)S(1)}, bf16[1,4096,128]{2,1,0:T(8,128)(2,1)S(1)}, u32[]{:S(2)}, u32[]{:S(2)}) %collective-permute-start.18) | collective-permute-done | bytes 1048608 | tf_op jit(solution)/shard_map/ppermute | solution.py:44
  181.3 4.1 %collective-permute-done.19 = bf16[2,4096,128]{2,1,0:T(8,128)(2,1)S(1)} collective-permute-done((bf16[2,4096,128]{2,1,0:T(8,128)(2,1)S(1)}, bf16[2,4096,128]{2,1,0:T(8,128)(2,1)S(1)}, u32[]{:S(2)}, u32[]{:S(2)}) %collective-permute-start.19) | collective-permute-done | bytes 2097184 | tf_op jit(solution)/shard_map/ppermute | solution.py:44
  192.3 4.1 %collective-permute-done.20 = f32[256,128]{0,1:T(8,128)S(1)} collective-permute-done((f32[256,128]{0,1:T(8,128)S(1)}, f32[256,128]{0,1:T(8,128)S(1)}, u32[]{:S(2)}, u32[]{:S(2)}) %collective-permute-start.20) | collective-permute-done | bytes 131104 | tf_op jit(solution)/shard_map/ppermute | solution.py:44
  196.4 2.8 %collective-permute-start.21 = (f32[256,128]{0,1:T(8,128)S(1)}, f32[256,128]{0,1:T(8,128)S(1)}, u32[]{:S(2)}, u32[]{:S(2)}) collective-permute-start(f32[256,128]{0,1:T(8,128)S(1)} %add.308), channel_id=1, source_target_pairs={{0,8},{4,12},{8,0},{12,4},{1,9},{5,13},{9,1},{13,5},{2,10},{6,14},... | collective-permute-start | bytes 393224 | tf_op jit(solution)/shard_map/ppermute | solution.py:44
  199.8 5.2 %collective-permute-done.21 = f32[256,128]{0,1:T(8,128)S(1)} collective-permute-done((f32[256,128]{0,1:T(8,128)S(1)}, f32[256,128]{0,1:T(8,128)S(1)}, u32[]{:S(2)}, u32[]{:S(2)}) %collective-permute-start.21) | collective-permute-done | bytes 131104 | tf_op jit(solution)/shard_map/ppermute | solution.py:44
  (150 shorter events, 40.1 us)
Async XLA Ops:
  0.6 7.9 %copy-start = (bf16[256,128]{1,0:T(8,128)(2,1)S(1)}, bf16[256,128]{1,0:T(8,128)(2,1)}, u32[]{:S(2)}) copy-start(bf16[256,128]{1,0:T(8,128)(2,1)} %param.6) | copy-start | bytes 196612
  0.6 14.0 %collective-permute-start = (s32[1,8,16]{2,1,0:T(8,128)}, s32[1,8,16]{2,1,0:T(8,128)S(1)}, u32[]{:S(2)}, u32[]{:S(2)}) collective-permute-start(s32[1,8,16]{2,1,0:T(8,128)} %bitcast.292), channel_id=1, source_target_pairs={{0,2},{1,3},{2,0},{3,1},{4,6},{5,7},{6,4},{7,5},{8,10},{9,11},{10,... | collective-permute-start | bytes 1544 | tf_op jit(solution)/shard_map/ppermute | solution.py:44
  3.6 25.7 %collective-permute-start.4 = (bf16[1,8,32,128]{3,2,1,0:T(8,128)(2,1)}, bf16[1,8,32,128]{3,2,1,0:T(8,128)(2,1)S(1)}, u32[]{:S(2)}, u32[]{:S(2)}) collective-permute-start(bf16[1,8,32,128]{3,2,1,0:T(8,128)(2,1)} %bitcast.291), channel_id=1, source_target_pairs={{0,2},{1,3},{2,0},{3,1},{4,6},{5,7},{6,4},{7,5},{8,10},{9,11},{10,... | collective-permute-start | bytes 196616 | tf_op jit(solution)/shard_map/ppermute | solution.py:44
  10.5 52.2 %collective-permute-start.14 = (f32[2,1024,128]{2,1,0:T(8,128)}, f32[2,1024,128]{2,1,0:T(8,128)}, u32[]{:S(2)}, u32[]{:S(2)}) collective-permute-start(f32[2,1024,128]{2,1,0:T(8,128)} %select_bitcast_fusion.4), channel_id=1, source_target_pairs={{0,1},{1,0},{2,3},{3,2},{4,5},{5,4},{6,7},{7,6},{8,9},{9,8},{10,11... | collective-permute-start | bytes 3145736 | tf_op jit(solution)/shard_map/ppermute | solution.py:44
  11.2 2.4 %copy-start.3 = (f32[2,2,1024,128]{3,2,0,1:T(8,128)}, f32[2,2,1024,128]{3,2,0,1:T(8,128)S(1)}, u32[]{:S(2)}) copy-start(f32[2,2,1024,128]{3,2,0,1:T(8,128)S(1)} %fusion.10) | copy-start | bytes 6291460
  12.3 54.1 %collective-permute-start.12 = (f32[2,1024,128]{2,1,0:T(8,128)}, f32[2,1024,128]{2,1,0:T(8,128)}, u32[]{:S(2)}, u32[]{:S(2)}) collective-permute-start(f32[2,1024,128]{2,1,0:T(8,128)} %select_bitcast_fusion.5), channel_id=1, source_target_pairs={{0,1},{1,0},{2,3},{3,2},{4,5},{5,4},{6,7},{7,6},{8,9},{9,8},{10,11... | collective-permute-start | bytes 3145736 | tf_op jit(solution)/shard_map/ppermute | solution.py:44
  14.7 53.9 %collective-permute-start.10 = (f32[2,1024,128]{2,1,0:T(8,128)}, f32[2,1024,128]{2,1,0:T(8,128)}, u32[]{:S(2)}, u32[]{:S(2)}) collective-permute-start(f32[2,1024,128]{2,1,0:T(8,128)} %select_bitcast_fusion.6), channel_id=1, source_target_pairs={{0,1},{1,0},{2,3},{3,2},{4,5},{5,4},{6,7},{7,6},{8,9},{9,8},{10,11... | collective-permute-start | bytes 3145736 | tf_op jit(solution)/shard_map/ppermute | solution.py:44
  14.7 2.9 %collective-permute-start.1 = (s32[2,8,16]{2,1,0:T(8,128)S(1)}, s32[2,8,16]{2,1,0:T(8,128)S(1)}, u32[]{:S(2)}, u32[]{:S(2)}) collective-permute-start(s32[2,8,16]{2,1,0:T(8,128)S(1)} %add_bitcast_fusion.1), channel_id=1, source_target_pairs={{0,1},{1,0},{2,3},{3,2},{4,5},{5,4},{6,7},{7,6},{8,9},{9,8},{10,11... | collective-permute-start | bytes 3080 | tf_op jit(solution)/shard_map/ppermute | solution.py:44
  17.6 3.2 %copy-start.6 = (f32[2,2,1024,128]{3,2,1,0:T(8,128)}, f32[2,2,1024,128]{3,2,1,0:T(8,128)S(1)}, u32[]{:S(2)}) copy-start(f32[2,2,1024,128]{3,2,1,0:T(8,128)S(1)} %fusion.3) | copy-start | bytes 6291460
  17.6 4.8 %collective-permute-start.2 = (s32[1,32,16]{2,1,0:T(8,128)S(1)}, s32[1,32,16]{2,1,0:T(8,128)S(1)}, u32[]{:S(2)}, u32[]{:S(2)}) collective-permute-start(s32[1,32,16]{2,1,0:T(8,128)S(1)} %bitcast.289), channel_id=1, source_target_pairs={{0,8},{4,12},{8,0},{12,4},{1,9},{5,13},{9,1},{13,5},{2,10},{6,14},... | collective-permute-start | bytes 6152 | tf_op jit(solution)/shard_map/ppermute | solution.py:44
  22.4 4.0 %collective-permute-start.3 = (s32[2,32,16]{2,1,0:T(8,128)S(1)}, s32[2,32,16]{2,1,0:T(8,128)S(1)}, u32[]{:S(2)}, u32[]{:S(2)}) collective-permute-start(s32[2,32,16]{2,1,0:T(8,128)S(1)} %add_bitcast_fusion), channel_id=1, source_target_pairs={{0,4},{4,0},{8,12},{12,8},{1,5},{5,1},{9,13},{13,9},{2,6},{6,2},{1... | collective-permute-start | bytes 12296 | tf_op jit(solution)/shard_map/ppermute | solution.py:44
  26.4 45.2 %collective-permute-start.8 = (f32[2,1024,128]{2,1,0:T(8,128)}, f32[2,1024,128]{2,1,0:T(8,128)}, u32[]{:S(2)}, u32[]{:S(2)}) collective-permute-start(f32[2,1024,128]{2,1,0:T(8,128)} %select_bitcast_fusion.7), channel_id=1, source_target_pairs={{0,1},{1,0},{2,3},{3,2},{4,5},{5,4},{6,7},{7,6},{8,9},{9,8},{10,11... | collective-permute-start | bytes 3145736 | tf_op jit(solution)/shard_map/ppermute | solution.py:44
  29.2 4.9 %copy-start.2 = (s32[256]{0:T(256)S(1)}, s32[256]{0:T(256)}, u32[]{:S(2)}) copy-start(s32[256]{0:T(256)} %param.8) | copy-start | bytes 3076
  29.4 1.6 collective-permute-start.5
  31.0 15.4 %collective-permute-start.6 = (bf16[1,32,32,128]{3,2,1,0:T(8,128)(2,1)S(1)}, bf16[1,32,32,128]{3,2,1,0:T(8,128)(2,1)S(1)}, u32[]{:S(2)}, u32[]{:S(2)}) collective-permute-start(bf16[1,32,32,128]{3,2,1,0:T(8,128)(2,1)S(1)} %bitcast.286), channel_id=1, source_target_pairs={{0,8},{4,12},{8,0},{12,4},{1,9},{5,13},{9,1},{13,5},{2,10},{6,14},... | collective-permute-start | bytes 786440 | tf_op jit(solution)/shard_map/ppermute | solution.py:44
  46.5 13.7 %collective-permute-start.7 = (bf16[2,32,32,128]{3,2,1,0:T(8,128)(2,1)S(1)}, bf16[2,32,32,128]{3,2,1,0:T(8,128)(2,1)S(1)}, u32[]{:S(2)}, u32[]{:S(2)}) collective-permute-start(bf16[2,32,32,128]{3,2,1,0:T(8,128)(2,1)S(1)} %maximum_bitcast_fusion.1), channel_id=1, source_target_pairs={{0,4},{4,0},{8,12},{12,8},{1,5},{5,1},{9,13},{13,9},{2,6},{6,2},{1... | collective-permute-start | bytes 1572872 | tf_op jit(solution)/shard_map/ppermute | solution.py:44
  62.7 3.8 %copy-start.4 = (f32[2,2,1024,128]{3,2,0,1:T(8,128)S(1)}, f32[2,2,1024,128]{3,2,0,1:T(8,128)}, u32[]{:S(2)}) copy-start(f32[2,2,1024,128]{3,2,0,1:T(8,128)} %copy-done.3) | copy-start | bytes 6291460
  64.9 14.9 %collective-permute-start.15 = (f32[1,1024,128]{2,1,0:T(8,128)S(1)}, f32[1,1024,128]{2,1,0:T(8,128)S(1)}, u32[]{:S(2)}, u32[]{:S(2)}) collective-permute-start(f32[1,1024,128]{2,1,0:T(8,128)S(1)} %select_bitcast_fusion.8), channel_id=1, source_target_pairs={{0,2},{1,3},{2,0},{3,1},{4,6},{5,7},{6,4},{7,5},{8,10},{9,11},{10,... | collective-permute-start | bytes 1572872 | tf_op jit(solution)/shard_map/ppermute | solution.py:44
  68.0 3.6 %copy-start.7 = (f32[2,2,1024,128]{3,2,1,0:T(8,128)S(1)}, f32[2,2,1024,128]{3,2,1,0:T(8,128)}, u32[]{:S(2)}) copy-start(f32[2,2,1024,128]{3,2,1,0:T(8,128)} %copy-done.6) | copy-start | bytes 6291460
  68.0 23.0 %collective-permute-start.13 = (f32[1,1024,128]{2,1,0:T(8,128)S(1)}, f32[1,1024,128]{2,1,0:T(8,128)S(1)}, u32[]{:S(2)}, u32[]{:S(2)}) collective-permute-start(f32[1,1024,128]{2,1,0:T(8,128)S(1)} %select_bitcast_fusion.9), channel_id=1, source_target_pairs={{0,2},{1,3},{2,0},{3,1},{4,6},{5,7},{6,4},{7,5},{8,10},{9,11},{10,... | collective-permute-start | bytes 1572872 | tf_op jit(solution)/shard_map/ppermute | solution.py:44
  70.1 32.2 %collective-permute-start.11 = (f32[1,1024,128]{2,1,0:T(8,128)S(1)}, f32[1,1024,128]{2,1,0:T(8,128)S(1)}, u32[]{:S(2)}, u32[]{:S(2)}) collective-permute-start(f32[1,1024,128]{2,1,0:T(8,128)S(1)} %select_bitcast_fusion.10), channel_id=1, source_target_pairs={{0,2},{1,3},{2,0},{3,1},{4,6},{5,7},{6,4},{7,5},{8,10},{9,11},{10,... | collective-permute-start | bytes 1572872 | tf_op jit(solution)/shard_map/ppermute | solution.py:44
  73.2 38.2 %collective-permute-start.9 = (f32[1,1024,128]{2,1,0:T(8,128)S(1)}, f32[1,1024,128]{2,1,0:T(8,128)S(1)}, u32[]{:S(2)}, u32[]{:S(2)}) collective-permute-start(f32[1,1024,128]{2,1,0:T(8,128)S(1)} %select_bitcast_fusion.11), channel_id=1, source_target_pairs={{0,2},{1,3},{2,0},{3,1},{4,6},{5,7},{6,4},{7,5},{8,10},{9,11},{10,... | collective-permute-start | bytes 1572872 | tf_op jit(solution)/shard_map/ppermute | solution.py:44
  121.2 2.6 %copy-start.8 = (f32[16,16,32,64]{3,2,1,0:T(8,128)}, f32[16,16,32,64]{3,2,1,0:T(8,128)S(1)}, u32[]{:S(2)}) copy-start(f32[16,16,32,64]{3,2,1,0:T(8,128)S(1)} %get-tuple-element.55) | copy-start | bytes 6291460
  129.8 3.7 %collective-permute-start.16 = (f32[16,128]{1,0:T(8,128)S(1)}, f32[16,128]{1,0:T(8,128)S(1)}, u32[]{:S(2)}, u32[]{:S(2)}) collective-permute-start(f32[16,128]{1,0:T(8,128)S(1)} %psum.7), channel_id=1, source_target_pairs={{0,4},{4,0},{8,12},{12,8},{1,5},{5,1},{9,13},{13,9},{2,6},{6,2},{1... | collective-permute-start | bytes 24584 | tf_op jit(solution)/shard_map/ppermute | solution.py:44
  133.5 4.9 %collective-permute-start.17 = (f32[16,128]{1,0:T(8,128)S(1)}, f32[16,128]{1,0:T(8,128)S(1)}, u32[]{:S(2)}, u32[]{:S(2)}) collective-permute-start(f32[16,128]{1,0:T(8,128)S(1)} %add.301), channel_id=1, source_target_pairs={{0,8},{4,12},{8,0},{12,4},{1,9},{5,13},{9,1},{13,5},{2,10},{6,14},... | collective-permute-start | bytes 24584 | tf_op jit(solution)/shard_map/ppermute | solution.py:44
  157.9 22.9 %collective-permute-start.18 = (bf16[1,4096,128]{2,1,0:T(8,128)(2,1)S(1)}, bf16[1,4096,128]{2,1,0:T(8,128)(2,1)S(1)}, u32[]{:S(2)}, u32[]{:S(2)}) collective-permute-start(bf16[1,4096,128]{2,1,0:T(8,128)(2,1)S(1)} %fusion.7), channel_id=1, source_target_pairs={{0,2},{1,3},{2,0},{3,1},{4,6},{5,7},{6,4},{7,5},{8,10},{9,11},{10,... | collective-permute-start | bytes 3145736 | tf_op jit(solution)/shard_map/ppermute | solution.py:44
  181.2 4.2 %collective-permute-start.19 = (bf16[2,4096,128]{2,1,0:T(8,128)(2,1)S(1)}, bf16[2,4096,128]{2,1,0:T(8,128)(2,1)S(1)}, u32[]{:S(2)}, u32[]{:S(2)}) collective-permute-start(bf16[2,4096,128]{2,1,0:T(8,128)(2,1)S(1)} %maximum_bitcast_fusion), channel_id=1, source_target_pairs={{0,1},{1,0},{2,3},{3,2},{4,5},{5,4},{6,7},{7,6},{8,9},{9,8},{10,11... | collective-permute-start | bytes 6291464 | tf_op jit(solution)/shard_map/ppermute | solution.py:44
  185.7 2.2 %slice-start = ((s8[8388608]{0:T(1024)(128)(4,1)}), s8[4194304]{0:T(1024)(128)(4,1)S(1)}, s32[]{:S(2)}) async-start(s8[8388608]{0:T(1024)(128)(4,1)} %bitcast.271), calls=%async_computation | async-start | bytes 8388608
  186.1 3.2 %slice-start.1 = ((s8[8388608]{0:T(1024)(128)(4,1)}), s8[4194304]{0:T(1024)(128)(4,1)S(1)}, s32[]{:S(2)}) async-start(s8[8388608]{0:T(1024)(128)(4,1)} %bitcast.271), calls=%async_computation.1 | async-start | bytes 8388608
  189.3 16.5 %copy-start.1 = (bf16[256,128]{1,0:T(8,128)(2,1)S(1)}, bf16[256,128]{1,0:T(8,128)(2,1)}, u32[]{:S(2)}) copy-start(bf16[256,128]{1,0:T(8,128)(2,1)} %param.6) | copy-start | bytes 196612
  190.8 5.6 %collective-permute-start.20 = (f32[256,128]{0,1:T(8,128)S(1)}, f32[256,128]{0,1:T(8,128)S(1)}, u32[]{:S(2)}, u32[]{:S(2)}) collective-permute-start(f32[256,128]{0,1:T(8,128)S(1)} %convolution_bitcast_fusion), channel_id=1, source_target_pairs={{0,4},{4,0},{8,12},{12,8},{1,5},{5,1},{9,13},{13,9},{2,6},{6,2},{1... | collective-permute-start | bytes 393224 | tf_op jit(solution)/shard_map/ppermute | solution.py:44
  196.4 8.5 %collective-permute-start.21 = (f32[256,128]{0,1:T(8,128)S(1)}, f32[256,128]{0,1:T(8,128)S(1)}, u32[]{:S(2)}, u32[]{:S(2)}) collective-permute-start(f32[256,128]{0,1:T(8,128)S(1)} %add.308), channel_id=1, source_target_pairs={{0,8},{4,12},{8,0},{12,4},{1,9},{5,13},{9,1},{13,5},{2,10},{6,14},... | collective-permute-start | bytes 393224 | tf_op jit(solution)/shard_map/ppermute | solution.py:44
  (3 other events, 5.1 us)

commit v5 on v3

--- a/solution.py
+++ b/solution.py
@@ -48,21 +48,22 @@
     return count & (count - 1) == 0
 
 
-def reduce_scatter_rows(value, axis):
-    count = lax.axis_size(axis)
-    if not is_pow2(count):
-        return lax.psum_scatter(value, axis, scatter_dimension=0, tiled=True)
+def halving_steps(values, axis):
+    count = lax.axis_size(axis)
     me = lax.axis_index(axis)
-    acc = value.reshape((count, -1) + value.shape[1:])
+    accs = [v.reshape((count, -1) + v.shape[1:]) for v in values]
     bit = 1
-    while bit < count:
-        acc = acc.reshape((acc.shape[0] // 2, 2) + acc.shape[1:])
-        low = (me // bit) % 2 == 0
-        keep = jnp.where(low, acc[:, 0], acc[:, 1])
-        send = jnp.where(low, acc[:, 1], acc[:, 0])
-        acc = keep + xor_perm(send, axis, bit)
+    while True:
+        keeps, sends = [], []
+        for acc in accs:
+            acc = acc.reshape((acc.shape[0] // 2, 2) + acc.shape[1:])
+            low = (me // bit) % 2 == 0
+            keeps.append(jnp.where(low, acc[:, 0], acc[:, 1]))
+            sends.append(jnp.where(low, acc[:, 1], acc[:, 0]))
+        if bit * 2 >= count:
+            return keeps, sends, bit
+        accs = [k + xor_perm(t, axis, bit) for k, t in zip(keeps, sends)]
         bit *= 2
-    return acc.reshape((-1,) + value.shape[1:])
 
 
 def all_gather_rows(value, axis):
@@ -106,13 +107,42 @@
     capacity = 2 * slot_count // owners
     me = lax.axis_index("enc") * mp_count + lax.axis_index("mp")
 
-    all_queries = lax.all_gather(queries, ("enc", "mp"), axis=0, tiled=True)
-    all_cand = lax.all_gather(candidates, ("enc", "mp"), axis=0, tiled=True)
+    chunks = 4 if row_share % (4 * BLK) == 0 else 1
+    split_rows = hidden.reshape(mp_count, chunks, row_share // chunks, hidden.shape[1])
+    partials = [
+        jnp.dot(split_rows[:, k], proj_w, preferred_element_type=jnp.float32).reshape(
+            mp_count * (row_share // chunks), emb_width
+        )
+        for k in range(chunks)
+    ]
+    if is_pow2(mp_count) and mp_count > 1:
+        keeps, sends, bit = halving_steps(partials, "mp")
+        last, queries, candidates = lax.optimization_barrier((sends[-1], queries, candidates))
+        sends = sends[:-1] + [last]
+        pieces = [k + xor_perm(t, "mp", bit) for k, t in zip(keeps, sends)]
+        pieces = [p.reshape(-1, emb_width) for p in pieces]
+    else:
+        pieces = [
+            lax.psum_scatter(p, "mp", scatter_dimension=0, tiled=True) for p in partials
+        ]
+    e_pre = jnp.stack(pieces).reshape(row_share, emb_width)
+
+    packed = jnp.concatenate(
+        [
+            queries.reshape(qry_dev, query_len * emb_width).astype(jnp.float32),
+            candidates.astype(jnp.float32),
+        ],
+        axis=1,
+    )
+    packed = lax.all_gather(packed, ("enc", "mp"), axis=0, tiled=True)
+    all_queries = (
+        packed[:, : query_len * emb_width]
+        .astype(jnp.bfloat16)
+        .reshape(owners * qry_dev, query_len, emb_width)
+    )
+    all_cand = packed[:, query_len * emb_width :].astype(jnp.int32)
     all_cand = all_cand.reshape(owners, slot_count)
 
-    e_pre = reduce_scatter_rows(
-        jnp.dot(hidden, proj_w, preferred_element_type=jnp.float32), "mp"
-    )
     scale = lax.rsqrt(jnp.sum(e_pre * e_pre, -1, keepdims=True) + 1e-06)
     embedded = (e_pre * scale).astype(jnp.bfloat16)
     local_blocks = embedded.reshape(blk_dev, BLK, emb_width)

time: 199 us -> 201 us (1.010)
  blocking collectives: 29 us -> 6.44 us
  starting transfers between devices: 2.99 us -> 16.9 us
  local copies, waits for them, and re-layouts: 25.8 us -> 33.5 us
  matrix products: 22 us -> 24.6 us
    all_gather x1 -> x0, blocking collectives: 22.9 us -> none  [local(): all_cand = lax.all_gather(candidates, ('enc', 'mp'), axis=0, tiled=True)]
    ppermute x8 -> x14, starting transfers between devices: 2.95 us -> 16.8 us  [xor_perm(): return lax.ppermute(value, axis, [(i, i ^ bit) for i in range(count)])]
    all_gather x1, waiting for transfers between devices: 6.35 us -> 0.02 us  [local(): packed = lax.all_gather(packed, ('enc', 'mp'), axis=0, tiled=True)]
    slice x0 -> x1, local copies, waits for them, and re-layouts: none -> 5.7 us  [local(): split_rows[:, k]]
    ppermute x8 -> x14, waiting for transfers between devices: 78.1 us -> 83.2 us  [xor_perm(): return lax.ppermute(value, axis, [(i, i ^ bit) for i in range(count)])]
    reduce_sum x1, other arithmetic: 3.47 us -> 0.62 us  [local(): scale = lax.rsqrt(jnp.sum(e_pre * e_pre, -1, keepdims=True) + 1e-06)]
    dot_general x1, matrix products: 2.62 us -> 4.94 us  [local(): jnp.einsum('scb,scje->bje', onehot.astype(jnp.bfloat16), occ_grad, prefer...]
    reshape x1 -> x4, other arithmetic: 5.34 us -> 7.02 us  [halving_steps(): acc = acc.reshape((acc.shape[0] // 2, 2) + acc.shape[1:])]
  transfers between devices with their start and end apart: 9 -> 15, of which waited for: 8 -> 10; matrix products, arithmetic and copies ran while one was open for 8% -> 9% of each run, Pallas kernels for 0% -> 0%
where the time goes in v5:
time: 201 us
  waiting for transfers between devices  83.3 us (41%)
  local copies, waits for them, and re-layouts  33.5 us (17%)
  matrix products  24.6 us (12%)
  other arithmetic  21.6 us (11%)
  starting transfers between devices  16.9 us (8%)
  between operations  14.5 us (7%)
  blocking collectives  6.44 us (3%)
    ppermute x14, waiting for transfers between devices, xor_perm(): return lax.ppermute(value, axis, [(i, i ^ bit) for i in range(count)])  83.2 us
    ppermute x14, starting transfers between devices, xor_perm(): return lax.ppermute(value, axis, [(i, i ^ bit) for i in range(count)])  16.8 us
    unnamed x32, local copies, waits for them, and re-layouts  10.4 us
    reshape x4, other arithmetic, halving_steps(): acc = acc.reshape((acc.shape[0] // 2, 2) + acc.shape[1:])  7.02 us
    dot_general x1, matrix products, local(): jnp.einsum('scij,scie->scje', weights, q_e, preferred_element_type=jnp.fl...  6.94 us
    psum x1, blocking collectives, local(): lax.psum(placed, 'mp')  6.44 us
    dot_general x4, matrix products, local(): jnp.dot(split_rows[:, k], proj_w, preferred_element_type=jnp.float32)  5.95 us
    slice x1, local copies, waits for them, and re-layouts, local(): split_rows[:, k]  5.7 us
  transfers between devices with their start and end apart: 15, of which 10 were waited for; matrix products, arithmetic and copies ran while one was open for 9% of the time, Pallas kernels for 0%

profile of v5, /device:TPU:0, one launch (start us, length us, event | category | flops | bytes accessed | tf_op | source)
XLA Modules:
  0.0 200.7 jit_solution(17665478317519932077)
XLA Ops:
  7.2 5.7 %fusion.56 = (bf16[4,1,1024,256]{3,2,1,0:T(8,128)(2,1)}, bf16[4,1,1024,256]{3,2,1,0:T(8,128)(2,1)}, bf16[4,1,1024,256]{3,2,1,0:T(8,128)(2,1)}, bf16[4,1,1024,256]{3,2,1,0:T(8,128)(2,1)S(1)}) fusion(bf16[4,4,1024,256]{3,2,1,0:T(8,128)(2,1)} %bitcast.209), kind=kLoop, calls=%fused_computation.149 | loop fusion | bytes 16777216 | tf_op jit(solution)/shard_map/slice | solution.py:113
  12.9 2.3 %fusion.3 = f32[2,2,1024,128]{3,2,1,0:T(8,128)S(1)} fusion(bf16[256,128]{1,0:T(8,128)(2,1)S(1)} %copy-done, bf16[2,2,1024,256]{3,2,1,0:T(8,128)(2,1)} %bitcast.224), kind=kOutput, calls=%fused_computation.16 | convolution fusion | flops 268435456 | bytes 4259840 | tf_op jit(solution)/shard_map/dot_general | solution.py:113
  22.3 2.0 %fusion.25 = f32[1,2,1024,128]{3,2,1,0:T(8,128)S(1)} fusion(f32[2,1024,128]{2,1,0:T(8,128)} %collective-permute-done, f32[2,2,1024,128]{3,2,1,0:T(8,128)} %copy-done.4, pred[]{:T(512)S(6)} %eq.67), kind=kLoop, calls=%fused_computation.45 | loop fusion | flops 524288 | bytes 4194305 | tf_op jit(solution)/shard_map/reshape | solution.py:59
  26.0 2.3 %fusion.12 = f32[2,2,1024,128]{3,2,0,1:T(8,128)S(1)} fusion(bf16[256,128]{1,0:T(8,128)(2,1)S(1)} %copy-done, bf16[2,2,1024,256]{3,2,1,0:T(8,128)(2,1)} %bitcast.221), kind=kOutput, calls=%fused_computation.27 | convolution fusion | flops 268435456 | bytes 4259840 | tf_op jit(solution)/shard_map/dot_general | solution.py:113
  30.8 2.9 %collective-permute-start.7 = (f32[1,1024,128]{2,1,0:T(8,128)}, f32[1,1024,128]{2,1,0:T(8,128)S(1)}, u32[]{:S(2)}, u32[]{:S(2)}) collective-permute-start(f32[1,1024,128]{2,1,0:T(8,128)} %select_bitcast_fusion.11), channel_id=1, source_target_pairs={{0,2},{1,3},{2,0},{3,1},{4,6},{5,7},{6,4},{7,5},{8,10},{9,11},{10,... | collective-permute-start | bytes 1572872 | tf_op jit(solution)/shard_map/ppermute | solution.py:44
  33.7 2.0 fusion.26
  37.5 1.9 collective-permute-start.4
  41.2 6.9 %collective-permute-done.7 = f32[1,1024,128]{2,1,0:T(8,128)S(1)} collective-permute-done((f32[1,1024,128]{2,1,0:T(8,128)}, f32[1,1024,128]{2,1,0:T(8,128)S(1)}, u32[]{:S(2)}, u32[]{:S(2)}) %collective-permute-start.7) | collective-permute-done | bytes 524320 | tf_op jit(solution)/shard_map/ppermute | solution.py:44
  48.2 14.8 %collective-permute-done.6 = f32[1,1024,128]{2,1,0:T(8,128)S(1)} collective-permute-done((f32[1,1024,128]{2,1,0:T(8,128)S(1)}, f32[1,1024,128]{2,1,0:T(8,128)S(1)}, u32[]{:S(2)}, u32[]{:S(2)}) %collective-permute-start.6) | collective-permute-done | bytes 524320 | tf_op jit(solution)/shard_map/ppermute | solution.py:44
  63.1 13.3 %collective-permute-done.4 = f32[1,1024,128]{2,1,0:T(8,128)S(1)} collective-permute-done((f32[1,1024,128]{2,1,0:T(8,128)S(1)}, f32[1,1024,128]{2,1,0:T(8,128)S(1)}, u32[]{:S(2)}, u32[]{:S(2)}) %collective-permute-start.4) | collective-permute-done | bytes 524320 | tf_op jit(solution)/shard_map/ppermute | solution.py:44
  76.5 10.5 %collective-permute-done.2 = f32[1,1024,128]{2,1,0:T(8,128)S(1)} collective-permute-done((f32[1,1024,128]{2,1,0:T(8,128)S(1)}, f32[1,1024,128]{2,1,0:T(8,128)S(1)}, u32[]{:S(2)}, u32[]{:S(2)}) %collective-permute-start.2) | collective-permute-done | bytes 524320 | tf_op jit(solution)/shard_map/ppermute | solution.py:44
  90.2 1.9 gather_fusion.3
  92.8 1.9 gather_fusion
  94.9 1.8 fusion.22
  98.2 3.4 %gather_fusion.1 = bf16[256,32,128]{2,1,0:T(8,128)(2,1)} fusion(bf16[128,32,128]{2,1,0:T(8,128)(2,1)} %bitcast.217, s32[1024]{0:T(1024)S(1)} %pad_clamp_fusion.1), kind=kCustom, calls=%fused_computation.1 | custom fusion | bytes 4195328 | tf_op jit(solution)/shard_map/gather | solution.py:162
  101.6 3.0 %gather_fusion.2 = bf16[256,64,128]{2,1,0:T(8,128)(2,1)} fusion(bf16[64,64,128]{2,1,0:T(8,128)(2,1)S(1)} %multiply_convert_fusion.1, s32[1024]{0:T(1024)S(1)} %pad_clamp_fusion), kind=kCustom, calls=%fused_computation.2 | custom fusion | bytes 8389632 | tf_op jit(solution)/shard_map/gather | solution.py:161
  104.6 5.2 %select_reduce_fusion = (f32[16,16,32]{2,1,0:T(8,128)S(1)}, f32[16,16,32,64]{3,2,1,0:T(8,128)S(1)}) fusion(pred[16,16,64]{2,1,0:T(8,128)(4,1)S(1)} %add_compare_fusion, bf16[16,16,32,128]{3,2,1,0:T(8,128)(2,1)} %bitcast.219, bf16[16,16,64,128]{3,2,1,0:T(8,128)(2,1)} %bitcast.216), kind=kOutput, calls=%fused_computation.11 | convolution fusion | flops 135258112 | bytes 8437760 | tf_op jit(solution)/shard_map/scie,scje->scij/dot_general | solution.py:164
  109.8 2.4 %fusion.2 = f32[16,16,32]{2,1,0:T(8,128)S(1)} fusion(f32[16,16,32,64]{3,2,1,0:T(8,128)S(1)} %get-tuple-element.45, f32[16,16,32]{2,1,0:T(8,128)S(1)} %get-tuple-element.44, pred[16,16,64]{2,1,0:T(8,128)(4,1)S(1)} %add_compare_fusion), kind=kLoop, calls=%fused_computation.12 | loop fusion | flops 1564672 | bytes 2179072 | tf_op jit(solution)/shard_map/reduce_sum | solution.py:22
  112.5 6.4 %psum.7 = f32[16,128]{1,0:T(8,128)S(1)} all-reduce(f32[16,128]{1,0:T(8,128)S(1)} %select_reduce_fusion.1), channel_id=1, replica_groups=mesh['groups'=2,'enc'=4,'mp'=4] {'mp'}, use_global_device_ids=true, to_apply=%region_7.8 | all-reduce | flops 2048 | bytes 16384 | tf_op jit(solution)/shard_map/psum | solution.py:170
  120.6 2.0 %collective-permute-done.8 = f32[16,128]{1,0:T(8,128)S(1)} collective-permute-done((f32[16,128]{1,0:T(8,128)S(1)}, f32[16,128]{1,0:T(8,128)S(1)}, u32[]{:S(2)}, u32[]{:S(2)}) %collective-permute-start.8) | collective-permute-done | bytes 8224 | tf_op jit(solution)/shard_map/ppermute | solution.py:44
  122.7 2.6 %collective-permute-start.9 = (f32[16,128]{1,0:T(8,128)S(1)}, f32[16,128]{1,0:T(8,128)S(1)}, u32[]{:S(2)}, u32[]{:S(2)}) collective-permute-start(f32[16,128]{1,0:T(8,128)S(1)} %add.285), channel_id=1, source_target_pairs={{0,8},{4,12},{8,0},{12,4},{1,9},{5,13},{9,1},{13,5},{2,10},{6,14},... | collective-permute-start | bytes 24584 | tf_op jit(solution)/shard_map/ppermute | solution.py:44
  127.9 1.9 gather_fusion.4
  129.9 6.9 %multiply_convert_fusion = bf16[16,16,64,128]{3,2,1,0:T(8,128)(2,1)S(1)} fusion(f32[16,16]{1,0:T(8,128)S(1)} %select_multiply_fusion, bf16[16,16,32,128]{3,2,1,0:T(8,128)(2,1)} %bitcast.220, f32[16,16,32,64]{3,2,1,0:T(8,128)} %copy-done.7, f32[16,16,32]{2,1,0:T(8,128)S(1)} %fusion.2, f32[16,16,32]{2,1,0:T(8,128)S(1)} %get-tuple-element.44, ...), kind=kOutput, calls=%fused_computation.5 | convolution fusion | flops 140509184 | bytes 8471552 | tf_op jit(solution)/shard_map/scij,scie->scje/dot_general | solution.py:167
  136.8 4.9 %fusion.14 = (f32[64,64]{0,1:T(8,128)S(1)}, f32[64,64,128]{2,0,1:T(8,128)}) fusion(f32[64,64,128]{2,1,0:T(8,128)S(1)} %bitcast.213, bf16[16,16,64,128]{3,2,1,0:T(8,128)(2,1)S(1)} %multiply_convert_fusion, s32[16,16]{0,1:T(8,128)S(1)} %copy.154, pred[16,16]{0,1:T(8,128)(4,1)S(1)} %copy.155), kind=kOutput, calls=%fused_computation.30 | convolution fusion | flops 269512704 | bytes 8406272 | tf_op jit(solution)/shard_map/scb,scje->bje/dot_general | solution.py:178
  141.9 2.8 %copy.158 = f32[64,64,128]{2,1,0:T(8,128)S(1)} copy(f32[64,64,128]{2,0,1:T(8,128)} %get-tuple-element.47) | data formatting | bytes 4194304 | tf_op jit(solution)/shard_map/scb,scje->bje/dot_general | solution.py:178
  144.7 1.9 fusion.7
  148.1 21.0 %collective-permute-done.10 = bf16[1,4096,128]{2,1,0:T(8,128)(2,1)S(1)} collective-permute-done((bf16[1,4096,128]{2,1,0:T(8,128)(2,1)S(1)}, bf16[1,4096,128]{2,1,0:T(8,128)(2,1)S(1)}, u32[]{:S(2)}, u32[]{:S(2)}) %collective-permute-start.10) | collective-permute-done | bytes 1048608 | tf_op jit(solution)/shard_map/ppermute | solution.py:44
  169.5 4.1 %collective-permute-done.11 = bf16[2,4096,128]{2,1,0:T(8,128)(2,1)S(1)} collective-permute-done((bf16[2,4096,128]{2,1,0:T(8,128)(2,1)S(1)}, bf16[2,4096,128]{2,1,0:T(8,128)(2,1)S(1)}, u32[]{:S(2)}, u32[]{:S(2)}) %collective-permute-start.11) | collective-permute-done | bytes 2097184 | tf_op jit(solution)/shard_map/ppermute | solution.py:44
  179.0 1.7 collective-permute-start.12
  180.7 3.9 %collective-permute-done.12 = f32[256,128]{0,1:T(8,128)S(1)} collective-permute-done((f32[256,128]{0,1:T(8,128)S(1)}, f32[256,128]{0,1:T(8,128)S(1)}, u32[]{:S(2)}, u32[]{:S(2)}) %collective-permute-start.12) | collective-permute-done | bytes 131104 | tf_op jit(solution)/shard_map/ppermute | solution.py:44
  184.6 2.7 %collective-permute-start.13 = (f32[256,128]{0,1:T(8,128)S(1)}, f32[256,128]{0,1:T(8,128)S(1)}, u32[]{:S(2)}, u32[]{:S(2)}) collective-permute-start(f32[256,128]{0,1:T(8,128)S(1)} %add.292), channel_id=1, source_target_pairs={{0,8},{4,12},{8,0},{12,4},{1,9},{5,13},{9,1},{13,5},{2,10},{6,14},... | collective-permute-start | bytes 393224 | tf_op jit(solution)/shard_map/ppermute | solution.py:44
  187.9 5.2 %collective-permute-done.13 = f32[256,128]{0,1:T(8,128)S(1)} collective-permute-done((f32[256,128]{0,1:T(8,128)S(1)}, f32[256,128]{0,1:T(8,128)S(1)}, u32[]{:S(2)}, u32[]{:S(2)}) %collective-permute-start.13) | collective-permute-done | bytes 131104 | tf_op jit(solution)/shard_map/ppermute | solution.py:44
  (125 shorter events, 33.6 us)
Async XLA Ops:
  7.2 5.8 %copy-start = (bf16[256,128]{1,0:T(8,128)(2,1)S(1)}, bf16[256,128]{1,0:T(8,128)(2,1)}, u32[]{:S(2)}) copy-start(bf16[256,128]{1,0:T(8,128)(2,1)} %param.6) | copy-start | bytes 196612
  7.2 81.3 %all-gather.2.cloned.1.call-start = ((), (), s32[]{:S(2)}) async-start(), calls=%async_computation | async-start | bytes 2297856 | tf_op jit(solution)/shard_map/all_gather | solution.py:137
  15.2 1.4 copy-start.4
  15.4 6.9 %collective-permute-start = (f32[2,1024,128]{2,1,0:T(8,128)S(1)}, f32[2,1024,128]{2,1,0:T(8,128)}, u32[]{:S(2)}, u32[]{:S(2)}) collective-permute-start(f32[2,1024,128]{2,1,0:T(8,128)S(1)} %select_bitcast_fusion.7), channel_id=1, source_target_pairs={{0,1},{1,0},{2,3},{3,2},{4,5},{5,4},{6,7},{7,6},{8,9},{9,8},{10,11... | collective-permute-start | bytes 3145736 | tf_op jit(solution)/shard_map/ppermute | solution.py:44
  17.3 3.4 %copy-start.3 = (f32[2,2,1024,128]{3,2,0,1:T(8,128)}, f32[2,2,1024,128]{3,2,0,1:T(8,128)S(1)}, u32[]{:S(2)}) copy-start(f32[2,2,1024,128]{3,2,0,1:T(8,128)S(1)} %fusion.8) | copy-start | bytes 6291460
  17.3 2.7 %copy-start.8 = (bf16[4,1,1024,256]{3,2,1,0:T(8,128)(2,1)S(1)}, bf16[4,1,1024,256]{3,2,1,0:T(8,128)(2,1)}, u32[]{:S(2)}) copy-start(bf16[4,1,1024,256]{3,2,1,0:T(8,128)(2,1)} %get-tuple-element.29) | copy-start | bytes 6291460
  18.4 15.4 %collective-permute-start.5 = (f32[2,1024,128]{2,1,0:T(8,128)}, f32[2,1024,128]{2,1,0:T(8,128)}, u32[]{:S(2)}, u32[]{:S(2)}) collective-permute-start(f32[2,1024,128]{2,1,0:T(8,128)} %select_bitcast_fusion.4), channel_id=1, source_target_pairs={{0,1},{1,0},{2,3},{3,2},{4,5},{5,4},{6,7},{7,6},{8,9},{9,8},{10,11... | collective-permute-start | bytes 3145736 | tf_op jit(solution)/shard_map/ppermute | solution.py:44
  21.8 14.1 %collective-permute-start.3 = (f32[2,1024,128]{2,1,0:T(8,128)}, f32[2,1024,128]{2,1,0:T(8,128)}, u32[]{:S(2)}, u32[]{:S(2)}) collective-permute-start(f32[2,1024,128]{2,1,0:T(8,128)} %select_bitcast_fusion.5), channel_id=1, source_target_pairs={{0,1},{1,0},{2,3},{3,2},{4,5},{5,4},{6,7},{7,6},{8,9},{9,8},{10,11... | collective-permute-start | bytes 3145736 | tf_op jit(solution)/shard_map/ppermute | solution.py:44
  22.3 2.9 %copy-start.10 = (s32[8,16]{1,0:T(8,128)S(1)}, s32[8,16]{1,0:T(8,128)}, u32[]{:S(2)}) copy-start(s32[8,16]{1,0:T(8,128)} %param.9) | copy-start | bytes 1540
  22.3 2.9 %copy-start.9 = (bf16[8,32,128]{2,1,0:T(8,128)(2,1)S(1)}, bf16[8,32,128]{2,1,0:T(8,128)(2,1)}, u32[]{:S(2)}) copy-start(bf16[8,32,128]{2,1,0:T(8,128)(2,1)} %param.7) | copy-start | bytes 196612
  28.3 1.3 copy-start.5
  30.7 8.7 %collective-permute-start.1 = (f32[2,1024,128]{2,1,0:T(8,128)}, f32[2,1024,128]{2,1,0:T(8,128)}, u32[]{:S(2)}, u32[]{:S(2)}) collective-permute-start(f32[2,1024,128]{2,1,0:T(8,128)} %select_bitcast_fusion.6), channel_id=1, source_target_pairs={{0,1},{1,0},{2,3},{3,2},{4,5},{5,4},{6,7},{7,6},{8,9},{9,8},{10,11... | collective-permute-start | bytes 3145736 | tf_op jit(solution)/shard_map/ppermute | solution.py:44
  30.8 17.3 %collective-permute-start.7 = (f32[1,1024,128]{2,1,0:T(8,128)}, f32[1,1024,128]{2,1,0:T(8,128)S(1)}, u32[]{:S(2)}, u32[]{:S(2)}) collective-permute-start(f32[1,1024,128]{2,1,0:T(8,128)} %select_bitcast_fusion.11), channel_id=1, source_target_pairs={{0,2},{1,3},{2,0},{3,1},{4,6},{5,7},{6,4},{7,5},{8,10},{9,11},{10,... | collective-permute-start | bytes 1572872 | tf_op jit(solution)/shard_map/ppermute | solution.py:44
  35.8 3.6 %copy-start.6 = (f32[2,2,1024,128]{3,2,0,1:T(8,128)S(1)}, f32[2,2,1024,128]{3,2,0,1:T(8,128)}, u32[]{:S(2)}) copy-start(f32[2,2,1024,128]{3,2,0,1:T(8,128)} %copy-done.5) | copy-start | bytes 6291460
  35.8 27.2 %collective-permute-start.6 = (f32[1,1024,128]{2,1,0:T(8,128)S(1)}, f32[1,1024,128]{2,1,0:T(8,128)S(1)}, u32[]{:S(2)}, u32[]{:S(2)}) collective-permute-start(f32[1,1024,128]{2,1,0:T(8,128)S(1)} %select_bitcast_fusion.8), channel_id=1, source_target_pairs={{0,2},{1,3},{2,0},{3,1},{4,6},{5,7},{6,4},{7,5},{8,10},{9,11},{10,... | collective-permute-start | bytes 1572872 | tf_op jit(solution)/shard_map/ppermute | solution.py:44
  37.5 38.9 %collective-permute-start.4 = (f32[1,1024,128]{2,1,0:T(8,128)S(1)}, f32[1,1024,128]{2,1,0:T(8,128)S(1)}, u32[]{:S(2)}, u32[]{:S(2)}) collective-permute-start(f32[1,1024,128]{2,1,0:T(8,128)S(1)} %select_bitcast_fusion.9), channel_id=1, source_target_pairs={{0,2},{1,3},{2,0},{3,1},{4,6},{5,7},{6,4},{7,5},{8,10},{9,11},{10,... | collective-permute-start | bytes 1572872 | tf_op jit(solution)/shard_map/ppermute | solution.py:44
  41.0 46.0 %collective-permute-start.2 = (f32[1,1024,128]{2,1,0:T(8,128)S(1)}, f32[1,1024,128]{2,1,0:T(8,128)S(1)}, u32[]{:S(2)}, u32[]{:S(2)}) collective-permute-start(f32[1,1024,128]{2,1,0:T(8,128)S(1)} %select_bitcast_fusion.10), channel_id=1, source_target_pairs={{0,2},{1,3},{2,0},{3,1},{4,6},{5,7},{6,4},{7,5},{8,10},{9,11},{10,... | collective-permute-start | bytes 1572872 | tf_op jit(solution)/shard_map/ppermute | solution.py:44
  92.1 0.7 copy-start.2
  109.8 2.4 %copy-start.7 = (f32[16,16,32,64]{3,2,1,0:T(8,128)}, f32[16,16,32,64]{3,2,1,0:T(8,128)S(1)}, u32[]{:S(2)}) copy-start(f32[16,16,32,64]{3,2,1,0:T(8,128)S(1)} %get-tuple-element.45) | copy-start | bytes 6291460
  119.0 3.7 %collective-permute-start.8 = (f32[16,128]{1,0:T(8,128)S(1)}, f32[16,128]{1,0:T(8,128)S(1)}, u32[]{:S(2)}, u32[]{:S(2)}) collective-permute-start(f32[16,128]{1,0:T(8,128)S(1)} %psum.7), channel_id=1, source_target_pairs={{0,4},{4,0},{8,12},{12,8},{1,5},{5,1},{9,13},{13,9},{2,6},{6,2},{1... | collective-permute-start | bytes 24584 | tf_op jit(solution)/shard_map/ppermute | solution.py:44
  122.7 4.5 %collective-permute-start.9 = (f32[16,128]{1,0:T(8,128)S(1)}, f32[16,128]{1,0:T(8,128)S(1)}, u32[]{:S(2)}, u32[]{:S(2)}) collective-permute-start(f32[16,128]{1,0:T(8,128)S(1)} %add.285), channel_id=1, source_target_pairs={{0,8},{4,12},{8,0},{12,4},{1,9},{5,13},{9,1},{13,5},{2,10},{6,14},... | collective-permute-start | bytes 24584 | tf_op jit(solution)/shard_map/ppermute | solution.py:44
  146.7 22.4 %collective-permute-start.10 = (bf16[1,4096,128]{2,1,0:T(8,128)(2,1)S(1)}, bf16[1,4096,128]{2,1,0:T(8,128)(2,1)S(1)}, u32[]{:S(2)}, u32[]{:S(2)}) collective-permute-start(bf16[1,4096,128]{2,1,0:T(8,128)(2,1)S(1)} %fusion.7), channel_id=1, source_target_pairs={{0,2},{1,3},{2,0},{3,1},{4,6},{5,7},{6,4},{7,5},{8,10},{9,11},{10,... | collective-permute-start | bytes 3145736 | tf_op jit(solution)/shard_map/ppermute | solution.py:44
  169.4 4.2 %collective-permute-start.11 = (bf16[2,4096,128]{2,1,0:T(8,128)(2,1)S(1)}, bf16[2,4096,128]{2,1,0:T(8,128)(2,1)S(1)}, u32[]{:S(2)}, u32[]{:S(2)}) collective-permute-start(bf16[2,4096,128]{2,1,0:T(8,128)(2,1)S(1)} %maximum_bitcast_fusion), channel_id=1, source_target_pairs={{0,1},{1,0},{2,3},{3,2},{4,5},{5,4},{6,7},{7,6},{8,9},{9,8},{10,11... | collective-permute-start | bytes 6291464 | tf_op jit(solution)/shard_map/ppermute | solution.py:44
  173.9 2.2 %slice-start = ((s8[8388608]{0:T(1024)(128)(4,1)}), s8[4194304]{0:T(1024)(128)(4,1)S(1)}, s32[]{:S(2)}) async-start(s8[8388608]{0:T(1024)(128)(4,1)} %bitcast.210), calls=%async_computation.1 | async-start | bytes 8388608
  174.3 3.2 %slice-start.1 = ((s8[8388608]{0:T(1024)(128)(4,1)}), s8[4194304]{0:T(1024)(128)(4,1)S(1)}, s32[]{:S(2)}) async-start(s8[8388608]{0:T(1024)(128)(4,1)} %bitcast.210), calls=%async_computation.2 | async-start | bytes 8388608
  177.5 16.4 %copy-start.1 = (bf16[256,128]{1,0:T(8,128)(2,1)S(1)}, bf16[256,128]{1,0:T(8,128)(2,1)}, u32[]{:S(2)}) copy-start(bf16[256,128]{1,0:T(8,128)(2,1)} %param.6) | copy-start | bytes 196612
  179.0 5.6 %collective-permute-start.12 = (f32[256,128]{0,1:T(8,128)S(1)}, f32[256,128]{0,1:T(8,128)S(1)}, u32[]{:S(2)}, u32[]{:S(2)}) collective-permute-start(f32[256,128]{0,1:T(8,128)S(1)} %convolution_bitcast_fusion), channel_id=1, source_target_pairs={{0,4},{4,0},{8,12},{12,8},{1,5},{5,1},{9,13},{13,9},{2,6},{6,2},{1... | collective-permute-start | bytes 393224 | tf_op jit(solution)/shard_map/ppermute | solution.py:44
  184.6 8.5 %collective-permute-start.13 = (f32[256,128]{0,1:T(8,128)S(1)}, f32[256,128]{0,1:T(8,128)S(1)}, u32[]{:S(2)}, u32[]{:S(2)}) collective-permute-start(f32[256,128]{0,1:T(8,128)S(1)} %add.292), channel_id=1, source_target_pairs={{0,8},{4,12},{8,0},{12,4},{1,9},{5,13},{9,1},{13,5},{2,10},{6,14},... | collective-permute-start | bytes 393224 | tf_op jit(solution)/shard_map/ppermute | solution.py:44
Sparse Core Ops, SparseCore 0:
  26.1 49.9 all-gather.1

commit v6 on v5

--- a/solution.py
+++ b/solution.py
@@ -85,13 +85,28 @@
 
 def all_sum(value, axis):
     count = lax.axis_size(axis)
-    if not is_pow2(count):
-        return lax.psum(value, axis)
-    bit = 1
-    while bit < count:
-        value = value + xor_perm(value, axis, bit)
-        bit *= 2
-    return value
+    if count > 4:
+        if not is_pow2(count):
+            return lax.psum(value, axis)
+        bit = 1
+        while bit < count:
+            value = value + xor_perm(value, axis, bit)
+            bit *= 2
+        return value
+    me = lax.axis_index(axis)
+    got = [value] + [
+        lax.ppermute(value, axis, [(i, (i + k) % count) for i in range(count)])
+        for k in range(1, count)
+    ]
+    stacked = jnp.stack(got)
+    by_source = [
+        lax.dynamic_index_in_dim(stacked, (me - src) % count, 0, keepdims=False)
+        for src in range(count)
+    ]
+    total = by_source[0]
+    for part in by_source[1:]:
+        total = total + part
+    return total
 
 
 def local(hidden, proj_w, queries, lengths, candidates):
@@ -106,6 +121,8 @@
     slot_count = qry_dev * cand_count
     capacity = 2 * slot_count // owners
     me = lax.axis_index("enc") * mp_count + lax.axis_index("mp")
+    all_cand = lax.all_gather(candidates, ("enc", "mp"), axis=0, tiled=True)
+    all_cand = all_cand.reshape(owners, slot_count)
 
     chunks = 4 if row_share % (4 * BLK) == 0 else 1
     split_rows = hidden.reshape(mp_count, chunks, row_share // chunks, hidden.shape[1])
@@ -117,7 +134,7 @@
     ]
     if is_pow2(mp_count) and mp_count > 1:
         keeps, sends, bit = halving_steps(partials, "mp")
-        last, queries, candidates = lax.optimization_barrier((sends[-1], queries, candidates))
+        last, queries = lax.optimization_barrier((sends[-1], queries))
         sends = sends[:-1] + [last]
         pieces = [k + xor_perm(t, "mp", bit) for k, t in zip(keeps, sends)]
         pieces = [p.reshape(-1, emb_width) for p in pieces]
@@ -140,8 +157,7 @@
         .astype(jnp.bfloat16)
         .reshape(owners * qry_dev, query_len, emb_width)
     )
-    all_cand = packed[:, query_len * emb_width :].astype(jnp.int32)
-    all_cand = all_cand.reshape(owners, slot_count)
+    late_cand = packed[:, query_len * emb_width :].astype(jnp.int32).reshape(owners, slot_count)
 
     scale = lax.rsqrt(jnp.sum(e_pre * e_pre, -1, keepdims=True) + 1e-06)
     embedded = (e_pre * scale).astype(jnp.bfloat16)
@@ -174,7 +190,8 @@
     d_e = jnp.take_along_axis(d_score.reshape(owners, slot_count), slot_of, axis=1)
     d_e = jnp.where(valid, d_e, jnp.float32(0))
     occ_grad = (occ_raw * (d_e / query_len)[:, :, None, None]).astype(jnp.bfloat16)
-    onehot = (local_of[:, :, None] == jnp.arange(blk_dev, dtype=jnp.int32)) & valid[:, :, None]
+    late_local = jnp.take_along_axis(late_cand, slot_of, axis=1) % blk_dev
+    onehot = (late_local[:, :, None] == jnp.arange(blk_dev, dtype=jnp.int32)) & valid[:, :, None]
     grad_emb = jnp.einsum(
         "scb,scje->bje",
         onehot.astype(jnp.bfloat16),

time: 201 us -> 227 us (1.13)
  blocking collectives: 6.44 us -> 28.9 us
  starting transfers between devices: 16.9 us -> 12 us
  waiting for transfers between devices: 83.3 us -> 87.2 us
  other arithmetic: 21.6 us -> 24.8 us
    all_gather x0 -> x1, blocking collectives: none -> 23 us  [local(): all_cand = lax.all_gather(candidates, ('enc', 'mp'), axis=0, tiled=True)]
    ppermute x0 -> x6, waiting for transfers between devices: none -> 14.6 us  [all_sum(): lax.ppermute(value, axis, [(i, (i + k) % count) for i in range(count)])]
    ppermute x14 -> x10, waiting for transfers between devices: 83.2 us -> 72.6 us  [xor_perm(): return lax.ppermute(value, axis, [(i, i ^ bit) for i in range(count)])]
    ppermute x14 -> x10, starting transfers between devices: 16.8 us -> 7.19 us  [xor_perm(): return lax.ppermute(value, axis, [(i, i ^ bit) for i in range(count)])]
    ppermute x0 -> x6, starting transfers between devices: none -> 4.78 us  [all_sum(): lax.ppermute(value, axis, [(i, (i + k) % count) for i in range(count)])]
    unnamed x32 -> x34, local copies, waits for them, and re-layouts: 10.4 us -> 10.2 us
  transfers between devices with their start and end apart: 15 -> 17, of which waited for: 10 -> 11; matrix products, arithmetic and copies ran while one was open for 9% -> 9% of each run, Pallas kernels for 0% -> 0%
where the time goes in v6:
time: 227 us; the launch traced here: 226 us
  waiting for transfers between devices  87.2 us (38%)
  local copies, waits for them, and re-layouts  35.4 us (16%)
  blocking collectives  28.9 us (13%)
  other arithmetic  24.8 us (11%)
  matrix products  23 us (10%)
  between operations  14.6 us (6%)
  starting transfers between devices  12 us (5%)
    ppermute x10, waiting for transfers between devices, xor_perm(): return lax.ppermute(value, axis, [(i, i ^ bit) for i in range(count)])  72.6 us
    all_gather x1, blocking collectives, local(): all_cand = lax.all_gather(candidates, ('enc', 'mp'), axis=0, tiled=True)  23 us
    ppermute x6, waiting for transfers between devices, all_sum(): lax.ppermute(value, axis, [(i, (i + k) % count) for i in range(count)])  14.6 us
    unnamed x34, local copies, waits for them, and re-layouts  10.2 us
    ppermute x10, starting transfers between devices, xor_perm(): return lax.ppermute(value, axis, [(i, i ^ bit) for i in range(count)])  7.19 us
    reshape x4, other arithmetic, halving_steps(): acc = acc.reshape((acc.shape[0] // 2, 2) + acc.shape[1:])  7.04 us
    dot_general x1, matrix products, local(): jnp.einsum('scij,scie->scje', weights, q_e, preferred_element_type=jnp.fl...  6.95 us
    psum x1, blocking collectives, local(): lax.psum(placed, 'mp')  5.86 us
  transfers between devices with their start and end apart: 17, of which 11 were waited for; matrix products, arithmetic and copies ran while one was open for 9% of the time, Pallas kernels for 0%

profile of v6, /device:TPU:0, one launch (start us, length us, event | category | flops | bytes accessed | tf_op | source)
XLA Modules:
  0.0 226.0 jit_solution(129747521362593953)
XLA Ops:
  7.2 5.7 %fusion.60 = (bf16[4,1,1024,256]{3,2,1,0:T(8,128)(2,1)}, bf16[4,1,1024,256]{3,2,1,0:T(8,128)(2,1)S(1)}, bf16[4,1,1024,256]{3,2,1,0:T(8,128)(2,1)}, bf16[4,1,1024,256]{3,2,1,0:T(8,128)(2,1)}) fusion(bf16[4,4,1024,256]{3,2,1,0:T(8,128)(2,1)} %bitcast.212), kind=kLoop, calls=%fused_computation.155 | loop fusion | bytes 16777216 | tf_op jit(solution)/shard_map/slice | solution.py:130
  12.9 2.3 %fusion.3 = f32[2,2,1024,128]{3,2,1,0:T(8,128)S(1)} fusion(bf16[256,128]{1,0:T(8,128)(2,1)S(1)} %copy-done, bf16[2,2,1024,256]{3,2,1,0:T(8,128)(2,1)} %bitcast.227), kind=kOutput, calls=%fused_computation.17 | convolution fusion | flops 268435456 | bytes 4259840 | tf_op jit(solution)/shard_map/dot_general | solution.py:130
  25.8 23.0 %all_gather.6 = s32[128,16]{1,0:T(8,128)S(1)} all-gather(s32[8,16]{1,0:T(8,128)S(1)} %copy-done.11), channel_id=1, replica_groups=mesh['groups'=2,'enc'=4,'mp'=4] {'enc','mp'}, dimensions={0}, use_global_device_ids=true | all-gather | bytes 8704 | tf_op jit(solution)/shard_map/all_gather | solution.py:124
  49.5 2.0 fusion.25
  53.5 1.9 gather_fusion.4
  56.2 2.2 fusion.26
  58.4 1.9 collective-permute-start.6
  63.6 1.9 collective-permute-start.2
  65.5 7.1 %collective-permute-done.7 = f32[1,1024,128]{2,1,0:T(8,128)S(1)} collective-permute-done((f32[1,1024,128]{2,1,0:T(8,128)}, f32[1,1024,128]{2,1,0:T(8,128)S(1)}, u32[]{:S(2)}, u32[]{:S(2)}) %collective-permute-start.7) | collective-permute-done | bytes 524320 | tf_op jit(solution)/shard_map/ppermute | solution.py:44
  72.6 15.8 %collective-permute-done.6 = f32[1,1024,128]{2,1,0:T(8,128)S(1)} collective-permute-done((f32[1,1024,128]{2,1,0:T(8,128)S(1)}, f32[1,1024,128]{2,1,0:T(8,128)S(1)}, u32[]{:S(2)}, u32[]{:S(2)}) %collective-permute-start.6) | collective-permute-done | bytes 524320 | tf_op jit(solution)/shard_map/ppermute | solution.py:44
  88.5 12.3 %collective-permute-done.4 = f32[1,1024,128]{2,1,0:T(8,128)S(1)} collective-permute-done((f32[1,1024,128]{2,1,0:T(8,128)S(1)}, f32[1,1024,128]{2,1,0:T(8,128)S(1)}, u32[]{:S(2)}, u32[]{:S(2)}) %collective-permute-start.4) | collective-permute-done | bytes 524320 | tf_op jit(solution)/shard_map/ppermute | solution.py:44
  100.9 10.6 %collective-permute-done.2 = f32[1,1024,128]{2,1,0:T(8,128)S(1)} collective-permute-done((f32[1,1024,128]{2,1,0:T(8,128)S(1)}, f32[1,1024,128]{2,1,0:T(8,128)S(1)}, u32[]{:S(2)}, u32[]{:S(2)}) %collective-permute-start.2) | collective-permute-done | bytes 524320 | tf_op jit(solution)/shard_map/ppermute | solution.py:44
  114.0 1.9 gather_fusion.5
  116.6 1.9 gather_fusion
  118.6 1.8 fusion.22
  121.8 3.4 %gather_fusion.1 = bf16[256,32,128]{2,1,0:T(8,128)(2,1)} fusion(bf16[128,32,128]{2,1,0:T(8,128)(2,1)} %bitcast.220, s32[1024]{0:T(1024)S(1)} %pad_clamp_fusion.1), kind=kCustom, calls=%fused_computation.3 | custom fusion | bytes 4195328 | tf_op jit(solution)/shard_map/gather | solution.py:178
  125.3 3.1 %gather_fusion.2 = bf16[256,64,128]{2,1,0:T(8,128)(2,1)} fusion(bf16[64,64,128]{2,1,0:T(8,128)(2,1)S(1)} %multiply_convert_fusion.1, s32[1024]{0:T(1024)S(1)} %pad_clamp_fusion), kind=kCustom, calls=%fused_computation.4 | custom fusion | bytes 8389632 | tf_op jit(solution)/shard_map/gather | solution.py:177
  128.4 5.2 %select_reduce_fusion = (f32[16,16,32]{2,1,0:T(8,128)S(1)}, f32[16,16,32,64]{3,2,1,0:T(8,128)S(1)}) fusion(pred[16,16,64]{2,1,0:T(8,128)(4,1)S(1)} %add_compare_fusion, bf16[16,16,32,128]{3,2,1,0:T(8,128)(2,1)} %bitcast.222, bf16[16,16,64,128]{3,2,1,0:T(8,128)(2,1)} %bitcast.219), kind=kOutput, calls=%fused_computation.12 | convolution fusion | flops 135258112 | bytes 8437760 | tf_op jit(solution)/shard_map/scie,scje->scij/dot_general | solution.py:180
  133.6 2.4 %fusion.2 = f32[16,16,32]{2,1,0:T(8,128)S(1)} fusion(f32[16,16,32,64]{3,2,1,0:T(8,128)S(1)} %get-tuple-element.47, f32[16,16,32]{2,1,0:T(8,128)S(1)} %get-tuple-element.46, pred[16,16,64]{2,1,0:T(8,128)(4,1)S(1)} %add_compare_fusion), kind=kLoop, calls=%fused_computation.13 | loop fusion | flops 1564672 | bytes 2179072 | tf_op jit(solution)/shard_map/reduce_sum | solution.py:22
  136.3 5.9 %psum.7 = f32[16,128]{1,0:T(8,128)S(1)} all-reduce(f32[16,128]{1,0:T(8,128)S(1)} %select_reduce_fusion.1), channel_id=1, replica_groups=mesh['groups'=2,'enc'=4,'mp'=4] {'mp'}, use_global_device_ids=true, to_apply=%region_7.9 | all-reduce | flops 2048 | bytes 16384 | tf_op jit(solution)/shard_map/psum | solution.py:186
  142.5 1.8 collective-permute-start.8
  149.0 1.9 gather_fusion.3
  151.0 6.9 %multiply_convert_fusion = bf16[16,16,64,128]{3,2,1,0:T(8,128)(2,1)S(1)} fusion(f32[16,16]{1,0:T(8,128)S(1)} %select_multiply_fusion, bf16[16,16,32,128]{3,2,1,0:T(8,128)(2,1)} %bitcast.223, f32[16,16,32,64]{3,2,1,0:T(8,128)} %copy-done.7, f32[16,16,32]{2,1,0:T(8,128)S(1)} %fusion.2, f32[16,16,32]{2,1,0:T(8,128)S(1)} %get-tuple-element.46, ...), kind=kOutput, calls=%fused_computation.6 | convolution fusion | flops 140509184 | bytes 8471552 | tf_op jit(solution)/shard_map/scij,scie->scje/dot_general | solution.py:183
  157.9 5.0 %fusion.14 = (f32[64,64]{0,1:T(8,128)S(1)}, f32[64,64,128]{2,0,1:T(8,128)}) fusion(f32[64,64,128]{2,1,0:T(8,128)S(1)} %bitcast.216, bf16[16,16,64,128]{3,2,1,0:T(8,128)(2,1)S(1)} %multiply_convert_fusion, s32[16,16]{0,1:T(8,128)S(1)} %copy.154, pred[16,16]{0,1:T(8,128)(4,1)S(1)} %copy.155), kind=kOutput, calls=%fused_computation.31 | convolution fusion | flops 269512704 | bytes 8406272 | tf_op jit(solution)/shard_map/scb,scje->bje/dot_general | solution.py:195
  163.0 2.8 %copy.158 = f32[64,64,128]{2,1,0:T(8,128)S(1)} copy(f32[64,64,128]{2,0,1:T(8,128)} %get-tuple-element.49) | data formatting | bytes 4194304 | tf_op jit(solution)/shard_map/scb,scje->bje/dot_general | solution.py:195
  165.8 1.9 fusion.7
  168.9 22.3 %collective-permute-done.11 = bf16[1,4096,128]{2,1,0:T(8,128)(2,1)S(1)} collective-permute-done((bf16[1,4096,128]{2,1,0:T(8,128)(2,1)S(1)}, bf16[1,4096,128]{2,1,0:T(8,128)(2,1)S(1)}, u32[]{:S(2)}, u32[]{:S(2)}) %collective-permute-start.11) | collective-permute-done | bytes 1048608 | tf_op jit(solution)/shard_map/ppermute | solution.py:44
  192.9 4.5 %collective-permute-done.12 = bf16[2,4096,128]{2,1,0:T(8,128)(2,1)} collective-permute-done((bf16[2,4096,128]{2,1,0:T(8,128)(2,1)}, bf16[2,4096,128]{2,1,0:T(8,128)(2,1)}, u32[]{:S(2)}, u32[]{:S(2)}) %collective-permute-start.12) | collective-permute-done | bytes 2097184 | tf_op jit(solution)/shard_map/ppermute | solution.py:44
  197.4 1.9 select_bitcast_fusion.1
  204.4 1.8 collective-permute-start.15
  207.7 2.5 %collective-permute-done.15 = f32[256,128]{0,1:T(8,128)S(1)} collective-permute-done((f32[256,128]{0,1:T(8,128)S(1)}, f32[256,128]{0,1:T(8,128)S(1)}, u32[]{:S(2)}, u32[]{:S(2)}) %collective-permute-start.15) | collective-permute-done | bytes 131104 | tf_op jit(solution)/shard_map/ppermute | solution.py:98
  210.2 8.1 %collective-permute-done.14 = f32[256,128]{0,1:T(8,128)S(1)} collective-permute-done((f32[256,128]{0,1:T(8,128)S(1)}, f32[256,128]{0,1:T(8,128)S(1)}, u32[]{:S(2)}, u32[]{:S(2)}) %collective-permute-start.14) | collective-permute-done | bytes 131104 | tf_op jit(solution)/shard_map/ppermute | solution.py:98
  (134 shorter events, 37.5 us)
Async XLA Ops:
  7.2 5.8 %copy-start = (bf16[256,128]{1,0:T(8,128)(2,1)S(1)}, bf16[256,128]{1,0:T(8,128)(2,1)}, u32[]{:S(2)}) copy-start(bf16[256,128]{1,0:T(8,128)(2,1)} %param.8) | copy-start | bytes 196612
  7.2 105.9 %all-gather.2.cloned.1.call-start = ((), (), s32[]{:S(2)}) async-start(), calls=%async_computation | async-start | bytes 2297856 | tf_op jit(solution)/shard_map/all_gather | solution.py:154
  15.2 1.3 copy-start.6
  15.2 2.3 %copy-start.9 = (bf16[4,1,1024,256]{3,2,1,0:T(8,128)(2,1)S(1)}, bf16[4,1,1024,256]{3,2,1,0:T(8,128)(2,1)}, u32[]{:S(2)}) copy-start(bf16[4,1,1024,256]{3,2,1,0:T(8,128)(2,1)} %get-tuple-element.30) | copy-start | bytes 6291460
  15.4 34.2 %collective-permute-start = (f32[2,1024,128]{2,1,0:T(8,128)S(1)}, f32[2,1024,128]{2,1,0:T(8,128)}, u32[]{:S(2)}, u32[]{:S(2)}) collective-permute-start(f32[2,1024,128]{2,1,0:T(8,128)S(1)} %select_bitcast_fusion.7), channel_id=1, source_target_pairs={{0,1},{1,0},{2,3},{3,2},{4,5},{5,4},{6,7},{7,6},{8,9},{9,8},{10,11... | collective-permute-start | bytes 3145736 | tf_op jit(solution)/shard_map/ppermute | solution.py:44
  18.3 1.7 copy-start.5
  19.5 36.6 %collective-permute-start.5 = (f32[2,1024,128]{2,1,0:T(8,128)}, f32[2,1024,128]{2,1,0:T(8,128)}, u32[]{:S(2)}, u32[]{:S(2)}) collective-permute-start(f32[2,1024,128]{2,1,0:T(8,128)} %select_bitcast_fusion.4), channel_id=1, source_target_pairs={{0,1},{1,0},{2,3},{3,2},{4,5},{5,4},{6,7},{7,6},{8,9},{9,8},{10,11... | collective-permute-start | bytes 3145736 | tf_op jit(solution)/shard_map/ppermute | solution.py:44
  20.7 3.4 %copy-start.3 = (f32[2,2,1024,128]{3,2,0,1:T(8,128)}, f32[2,2,1024,128]{3,2,0,1:T(8,128)S(1)}, u32[]{:S(2)}) copy-start(f32[2,2,1024,128]{3,2,0,1:T(8,128)S(1)} %fusion.10) | copy-start | bytes 6291460
  20.7 2.7 %copy-start.8 = (bf16[4,1,1024,256]{3,2,1,0:T(8,128)(2,1)S(1)}, bf16[4,1,1024,256]{3,2,1,0:T(8,128)(2,1)}, u32[]{:S(2)}) copy-start(bf16[4,1,1024,256]{3,2,1,0:T(8,128)(2,1)} %get-tuple-element.27) | copy-start | bytes 6291460
  21.8 38.5 %collective-permute-start.3 = (f32[2,1024,128]{2,1,0:T(8,128)}, f32[2,1024,128]{2,1,0:T(8,128)}, u32[]{:S(2)}, u32[]{:S(2)}) collective-permute-start(f32[2,1024,128]{2,1,0:T(8,128)} %select_bitcast_fusion.5), channel_id=1, source_target_pairs={{0,1},{1,0},{2,3},{3,2},{4,5},{5,4},{6,7},{7,6},{8,9},{9,8},{10,11... | collective-permute-start | bytes 3145736 | tf_op jit(solution)/shard_map/ppermute | solution.py:44
  24.1 1.6 copy-start.11
  25.3 36.8 %collective-permute-start.1 = (f32[2,1024,128]{2,1,0:T(8,128)}, f32[2,1024,128]{2,1,0:T(8,128)}, u32[]{:S(2)}, u32[]{:S(2)}) collective-permute-start(f32[2,1024,128]{2,1,0:T(8,128)} %select_bitcast_fusion.6), channel_id=1, source_target_pairs={{0,1},{1,0},{2,3},{3,2},{4,5},{5,4},{6,7},{7,6},{8,9},{9,8},{10,11... | collective-permute-start | bytes 3145736 | tf_op jit(solution)/shard_map/ppermute | solution.py:44
  49.5 2.9 %copy-start.10 = (bf16[8,32,128]{2,1,0:T(8,128)(2,1)S(1)}, bf16[8,32,128]{2,1,0:T(8,128)(2,1)}, u32[]{:S(2)}) copy-start(bf16[8,32,128]{2,1,0:T(8,128)(2,1)} %param.9) | copy-start | bytes 196612
  56.1 4.3 %copy-start.4 = (f32[2,2,1024,128]{3,2,0,1:T(8,128)S(1)}, f32[2,2,1024,128]{3,2,0,1:T(8,128)}, u32[]{:S(2)}) copy-start(f32[2,2,1024,128]{3,2,0,1:T(8,128)} %copy-done.3) | copy-start | bytes 6291460
  56.1 16.5 %collective-permute-start.7 = (f32[1,1024,128]{2,1,0:T(8,128)}, f32[1,1024,128]{2,1,0:T(8,128)S(1)}, u32[]{:S(2)}, u32[]{:S(2)}) collective-permute-start(f32[1,1024,128]{2,1,0:T(8,128)} %select_bitcast_fusion.11), channel_id=1, source_target_pairs={{0,2},{1,3},{2,0},{3,1},{4,6},{5,7},{6,4},{7,5},{8,10},{9,11},{10,... | collective-permute-start | bytes 1572872 | tf_op jit(solution)/shard_map/ppermute | solution.py:44
  58.4 30.0 %collective-permute-start.6 = (f32[1,1024,128]{2,1,0:T(8,128)S(1)}, f32[1,1024,128]{2,1,0:T(8,128)S(1)}, u32[]{:S(2)}, u32[]{:S(2)}) collective-permute-start(f32[1,1024,128]{2,1,0:T(8,128)S(1)} %select_bitcast_fusion.8), channel_id=1, source_target_pairs={{0,2},{1,3},{2,0},{3,1},{4,6},{5,7},{6,4},{7,5},{8,10},{9,11},{10,... | collective-permute-start | bytes 1572872 | tf_op jit(solution)/shard_map/ppermute | solution.py:44
  61.9 38.9 %collective-permute-start.4 = (f32[1,1024,128]{2,1,0:T(8,128)S(1)}, f32[1,1024,128]{2,1,0:T(8,128)S(1)}, u32[]{:S(2)}, u32[]{:S(2)}) collective-permute-start(f32[1,1024,128]{2,1,0:T(8,128)S(1)} %select_bitcast_fusion.9), channel_id=1, source_target_pairs={{0,2},{1,3},{2,0},{3,1},{4,6},{5,7},{6,4},{7,5},{8,10},{9,11},{10,... | collective-permute-start | bytes 1572872 | tf_op jit(solution)/shard_map/ppermute | solution.py:44
  63.6 47.9 %collective-permute-start.2 = (f32[1,1024,128]{2,1,0:T(8,128)S(1)}, f32[1,1024,128]{2,1,0:T(8,128)S(1)}, u32[]{:S(2)}, u32[]{:S(2)}) collective-permute-start(f32[1,1024,128]{2,1,0:T(8,128)S(1)} %select_bitcast_fusion.10), channel_id=1, source_target_pairs={{0,2},{1,3},{2,0},{3,1},{4,6},{5,7},{6,4},{7,5},{8,10},{9,11},{10,... | collective-permute-start | bytes 1572872 | tf_op jit(solution)/shard_map/ppermute | solution.py:44
  115.9 0.7 copy-start.2
  133.6 2.4 %copy-start.7 = (f32[16,16,32,64]{3,2,1,0:T(8,128)}, f32[16,16,32,64]{3,2,1,0:T(8,128)S(1)}, u32[]{:S(2)}) copy-start(f32[16,16,32,64]{3,2,1,0:T(8,128)S(1)} %get-tuple-element.47) | copy-start | bytes 6291460
  142.2 3.7 %collective-permute-start.10 = (f32[16,128]{1,0:T(8,128)S(1)}, f32[16,128]{1,0:T(8,128)S(1)}, u32[]{:S(2)}, u32[]{:S(2)}) collective-permute-start(f32[16,128]{1,0:T(8,128)S(1)} %psum.7), channel_id=1, source_target_pairs={{0,12},{4,0},{8,4},{12,8},{1,13},{5,1},{9,5},{13,9},{2,14},{6,2},{... | collective-permute-start | bytes 24584 | tf_op jit(solution)/shard_map/ppermute | solution.py:98
  142.2 4.7 %collective-permute-start.9 = (f32[16,128]{1,0:T(8,128)S(1)}, f32[16,128]{1,0:T(8,128)S(1)}, u32[]{:S(2)}, u32[]{:S(2)}) collective-permute-start(f32[16,128]{1,0:T(8,128)S(1)} %psum.7), channel_id=1, source_target_pairs={{0,8},{4,12},{8,0},{12,4},{1,9},{5,13},{9,1},{13,5},{2,10},{6,14},... | collective-permute-start | bytes 24584 | tf_op jit(solution)/shard_map/ppermute | solution.py:98
  142.5 5.9 %collective-permute-start.8 = (f32[16,128]{1,0:T(8,128)S(1)}, f32[16,128]{1,0:T(8,128)S(1)}, u32[]{:S(2)}, u32[]{:S(2)}) collective-permute-start(f32[16,128]{1,0:T(8,128)S(1)} %psum.7), channel_id=1, source_target_pairs={{0,4},{4,8},{8,12},{12,0},{1,5},{5,9},{9,13},{13,1},{2,6},{6,10},{... | collective-permute-start | bytes 24584 | tf_op jit(solution)/shard_map/ppermute | solution.py:98
  167.8 23.4 %collective-permute-start.11 = (bf16[1,4096,128]{2,1,0:T(8,128)(2,1)S(1)}, bf16[1,4096,128]{2,1,0:T(8,128)(2,1)S(1)}, u32[]{:S(2)}, u32[]{:S(2)}) collective-permute-start(bf16[1,4096,128]{2,1,0:T(8,128)(2,1)S(1)} %fusion.7), channel_id=1, source_target_pairs={{0,2},{1,3},{2,0},{3,1},{4,6},{5,7},{6,4},{7,5},{8,10},{9,11},{10,... | collective-permute-start | bytes 3145736 | tf_op jit(solution)/shard_map/ppermute | solution.py:44
  192.9 4.5 %collective-permute-start.12 = (bf16[2,4096,128]{2,1,0:T(8,128)(2,1)}, bf16[2,4096,128]{2,1,0:T(8,128)(2,1)}, u32[]{:S(2)}, u32[]{:S(2)}) collective-permute-start(bf16[2,4096,128]{2,1,0:T(8,128)(2,1)} %maximum_bitcast_fusion), channel_id=1, source_target_pairs={{0,1},{1,0},{2,3},{3,2},{4,5},{5,4},{6,7},{7,6},{8,9},{9,8},{10,11... | collective-permute-start | bytes 6291464 | tf_op jit(solution)/shard_map/ppermute | solution.py:44
  199.2 2.2 slice-start
  199.7 3.2 %slice-start.1 = ((s8[8388608]{0:T(1024)(128)(4,1)}), s8[4194304]{0:T(1024)(128)(4,1)S(1)}, s32[]{:S(2)}) async-start(s8[8388608]{0:T(1024)(128)(4,1)} %bitcast.213), calls=%async_computation.2 | async-start | bytes 8388608
  202.8 16.3 %copy-start.1 = (bf16[256,128]{1,0:T(8,128)(2,1)S(1)}, bf16[256,128]{1,0:T(8,128)(2,1)}, u32[]{:S(2)}) copy-start(bf16[256,128]{1,0:T(8,128)(2,1)} %param.8) | copy-start | bytes 196612
  204.4 5.8 %collective-permute-start.15 = (f32[256,128]{0,1:T(8,128)S(1)}, f32[256,128]{0,1:T(8,128)S(1)}, u32[]{:S(2)}, u32[]{:S(2)}) collective-permute-start(f32[256,128]{0,1:T(8,128)S(1)} %bitcast.228), channel_id=1, source_target_pairs={{0,12},{4,0},{8,4},{12,8},{1,13},{5,1},{9,5},{13,9},{2,14},{6,2},{... | collective-permute-start | bytes 393224 | tf_op jit(solution)/shard_map/ppermute | solution.py:98
  206.2 12.1 %collective-permute-start.14 = (f32[256,128]{0,1:T(8,128)S(1)}, f32[256,128]{0,1:T(8,128)S(1)}, u32[]{:S(2)}, u32[]{:S(2)}) collective-permute-start(f32[256,128]{0,1:T(8,128)S(1)} %bitcast.229), channel_id=1, source_target_pairs={{0,8},{4,12},{8,0},{12,4},{1,9},{5,13},{9,1},{13,5},{2,10},{6,14},... | collective-permute-start | bytes 393224 | tf_op jit(solution)/shard_map/ppermute | solution.py:98
  206.4 11.9 %collective-permute-start.13 = (f32[256,128]{0,1:T(8,128)S(1)}, f32[256,128]{0,1:T(8,128)S(1)}, u32[]{:S(2)}, u32[]{:S(2)}) collective-permute-start(f32[256,128]{0,1:T(8,128)S(1)} %bitcast.230), channel_id=1, source_target_pairs={{0,4},{4,8},{8,12},{12,0},{1,5},{5,9},{9,13},{13,1},{2,6},{6,10},{... | collective-permute-start | bytes 393224 | tf_op jit(solution)/shard_map/ppermute | solution.py:98
Sparse Core Ops, SparseCore 0:
  53.4 44.8 all-gather.1

commit v7 on v6

--- a/solution.py
+++ b/solution.py
@@ -121,8 +121,15 @@
     slot_count = qry_dev * cand_count
     capacity = 2 * slot_count // owners
     me = lax.axis_index("enc") * mp_count + lax.axis_index("mp")
-    all_cand = lax.all_gather(candidates, ("enc", "mp"), axis=0, tiled=True)
-    all_cand = all_cand.reshape(owners, slot_count)
+
+    packed = jnp.concatenate(
+        [
+            queries.reshape(qry_dev, query_len * emb_width).astype(jnp.float32),
+            candidates.astype(jnp.float32),
+        ],
+        axis=1,
+    )
+    packed = all_gather_rows(packed, "mp")
 
     chunks = 4 if row_share % (4 * BLK) == 0 else 1
     split_rows = hidden.reshape(mp_count, chunks, row_share // chunks, hidden.shape[1])
@@ -134,7 +141,7 @@
     ]
     if is_pow2(mp_count) and mp_count > 1:
         keeps, sends, bit = halving_steps(partials, "mp")
-        last, queries = lax.optimization_barrier((sends[-1], queries))
+        last, packed = lax.optimization_barrier((sends[-1], packed))
         sends = sends[:-1] + [last]
         pieces = [k + xor_perm(t, "mp", bit) for k, t in zip(keeps, sends)]
         pieces = [p.reshape(-1, emb_width) for p in pieces]
@@ -144,24 +151,13 @@
         ]
     e_pre = jnp.stack(pieces).reshape(row_share, emb_width)
 
-    packed = jnp.concatenate(
-        [
-            queries.reshape(qry_dev, query_len * emb_width).astype(jnp.float32),
-            candidates.astype(jnp.float32),
-        ],
-        axis=1,
-    )
-    packed = lax.all_gather(packed, ("enc", "mp"), axis=0, tiled=True)
+    packed = all_gather_rows(packed, "enc")
     all_queries = (
         packed[:, : query_len * emb_width]
         .astype(jnp.bfloat16)
         .reshape(owners * qry_dev, query_len, emb_width)
     )
-    late_cand = packed[:, query_len * emb_width :].astype(jnp.int32).reshape(owners, slot_count)
-
-    scale = lax.rsqrt(jnp.sum(e_pre * e_pre, -1, keepdims=True) + 1e-06)
-    embedded = (e_pre * scale).astype(jnp.bfloat16)
-    local_blocks = embedded.reshape(blk_dev, BLK, emb_width)
+    all_cand = packed[:, query_len * emb_width :].astype(jnp.int32).reshape(owners, slot_count)
 
     slot_ids = jnp.arange(slot_count, dtype=jnp.int32)
     mine = (all_cand // blk_dev) == me
@@ -174,8 +170,14 @@
     local_of = block_of % blk_dev
     query_of = jnp.arange(owners, dtype=jnp.int32)[:, None] * qry_dev + slot_of // cand_count
 
+    q_e = all_queries[query_of]
+
+
+    scale = lax.rsqrt(jnp.sum(e_pre * e_pre, -1, keepdims=True) + 1e-06)
+    embedded = (e_pre * scale).astype(jnp.bfloat16)
+    local_blocks = embedded.reshape(blk_dev, BLK, emb_width)
+
     tiles = local_blocks[local_of]
-    q_e = all_queries[query_of]
     valid_mask = block_valid(block_of, lengths)
     sim_tile = jnp.einsum("scie,scje->scij", q_e, tiles, preferred_element_type=jnp.float32)
     scores, weights = soft_max_sim(sim_tile, valid_mask[:, :, None, :])
@@ -183,15 +185,14 @@
     occ_raw = jnp.einsum("scij,scie->scje", weights, q_e, preferred_element_type=jnp.float32)
 
     placed = jnp.sum(jnp.where(pick, scores[:, :, None], jnp.float32(0)), axis=1)
-    all_scores = all_sum(lax.psum(placed, "mp"), "enc").reshape(owners * qry_dev, cand_count)
+    all_scores = all_sum(all_sum(placed, "mp"), "enc").reshape(owners * qry_dev, cand_count)
     all_losses, d_score = loss_terms(all_scores)
     losses = lax.dynamic_slice_in_dim(all_losses, me * qry_dev, qry_dev)
 
     d_e = jnp.take_along_axis(d_score.reshape(owners, slot_count), slot_of, axis=1)
     d_e = jnp.where(valid, d_e, jnp.float32(0))
     occ_grad = (occ_raw * (d_e / query_len)[:, :, None, None]).astype(jnp.bfloat16)
-    late_local = jnp.take_along_axis(late_cand, slot_of, axis=1) % blk_dev
-    onehot = (late_local[:, :, None] == jnp.arange(blk_dev, dtype=jnp.int32)) & valid[:, :, None]
+    onehot = (local_of[:, :, None] == jnp.arange(blk_dev, dtype=jnp.int32)) & valid[:, :, None]
     grad_emb = jnp.einsum(
         "scb,scje->bje",
         onehot.astype(jnp.bfloat16),

time: 227 us -> 201 us (0.89)
  blocking collectives: 28.9 us -> 0 us
  between operations: 14.6 us -> 1.28 us
  starting transfers between devices: 12 us -> 20.2 us
  waiting for transfers between devices: 87.2 us -> 94.1 us
    all_gather x1 -> x0, blocking collectives: 23 us -> none  [local(): all_cand = lax.all_gather(candidates, ('enc', 'mp'), axis=0, tiled=True)]
    ppermute x10 -> x14, starting transfers between devices: 7.19 us -> 13.2 us  [xor_perm(): return lax.ppermute(value, axis, [(i, i ^ bit) for i in range(count)])]
    psum x1 -> x0, blocking collectives: 5.86 us -> none  [local(): lax.psum(placed, 'mp')]
    ppermute x10 -> x14, waiting for transfers between devices: 72.6 us -> 76.7 us  [xor_perm(): return lax.ppermute(value, axis, [(i, i ^ bit) for i in range(count)])]
    another operation x3 -> x9, other arithmetic: 2.39 us -> 5.5 us  [all_gather_rows(): arr = jnp.stack([first, second], axis=1).reshape((-1,) + value.shape)]
    ppermute x6 -> x9, waiting for transfers between devices: 14.6 us -> 17.4 us  [all_sum(): lax.ppermute(value, axis, [(i, (i + k) % count) for i in range(count)])]
    reshape x4, other arithmetic: 7.04 us -> 4.74 us  [halving_steps(): acc = acc.reshape((acc.shape[0] // 2, 2) + acc.shape[1:])]
    ppermute x6 -> x9, starting transfers between devices: 4.78 us -> 7.04 us  [all_sum(): lax.ppermute(value, axis, [(i, (i + k) % count) for i in range(count)])]
  transfers between devices with their start and end apart: 17 -> 23, of which waited for: 11 -> 15; matrix products, arithmetic and copies ran while one was open for 9% -> 8% of each run, Pallas kernels for 0% -> 0%
where the time goes in v7:
time: 201 us; the launch traced here: 200 us
  waiting for transfers between devices  94.1 us (47%)
  local copies, waits for them, and re-layouts  35.2 us (18%)
  other arithmetic  26.3 us (13%)
  matrix products  23 us (11%)
  starting transfers between devices  20.2 us (10%)
    ppermute x14, waiting for transfers between devices, xor_perm(): return lax.ppermute(value, axis, [(i, i ^ bit) for i in range(count)])  76.7 us
    ppermute x9, waiting for transfers between devices, all_sum(): lax.ppermute(value, axis, [(i, (i + k) % count) for i in range(count)])  17.4 us
    ppermute x14, starting transfers between devices, xor_perm(): return lax.ppermute(value, axis, [(i, i ^ bit) for i in range(count)])  13.2 us
    unnamed x44, local copies, waits for them, and re-layouts  11.9 us
    ppermute x9, starting transfers between devices, all_sum(): lax.ppermute(value, axis, [(i, (i + k) % count) for i in range(count)])  7.04 us
    dot_general x1, matrix products, local(): jnp.einsum('scij,scie->scje', weights, q_e, preferred_element_type=jnp.fl...  6.94 us
    slice x1, local copies, waits for them, and re-layouts, local(): split_rows[:, k]  5.76 us
    another operation x9, other arithmetic, all_gather_rows(): arr = jnp.stack([first, second], axis=1).reshape((-1,) + value.shape)  5.5 us
  transfers between devices with their start and end apart: 23, of which 15 were waited for; matrix products, arithmetic and copies ran while one was open for 8% of the time, Pallas kernels for 0%

profile of v7, /device:TPU:0, one launch (start us, length us, event | category | flops | bytes accessed | tf_op | source)
XLA Modules:
  0.0 200.0 jit_solution(137648130964680305)
XLA Ops:
  0.7 5.8 %fusion.56 = (bf16[4,1,1024,256]{3,2,1,0:T(8,128)(2,1)}, bf16[4,1,1024,256]{3,2,1,0:T(8,128)(2,1)S(1)}, bf16[4,1,1024,256]{3,2,1,0:T(8,128)(2,1)}, bf16[4,1,1024,256]{3,2,1,0:T(8,128)(2,1)}) fusion(bf16[4,4,1024,256]{3,2,1,0:T(8,128)(2,1)} %bitcast.265), kind=kLoop, calls=%fused_computation.166 | loop fusion | bytes 16777216 | tf_op jit(solution)/shard_map/slice | solution.py:137
  6.4 2.3 %fusion.3 = f32[2,2,1024,128]{3,2,1,0:T(8,128)S(1)} fusion(bf16[256,128]{1,0:T(8,128)(2,1)S(1)} %copy-done, bf16[2,2,1024,256]{3,2,1,0:T(8,128)(2,1)} %bitcast.280), kind=kOutput, calls=%fused_computation.17 | convolution fusion | flops 268435456 | bytes 4259840 | tf_op jit(solution)/shard_map/dot_general | solution.py:137
  10.4 2.6 %collective-permute-start.1 = (f32[1,8,4112]{2,1,0:T(8,128)S(1)}, f32[1,8,4112]{2,1,0:T(8,128)S(1)}, u32[]{:S(2)}, u32[]{:S(2)}) collective-permute-start(f32[1,8,4112]{2,1,0:T(8,128)S(1)} %maximum_bitcast_fusion.3), channel_id=1, source_target_pairs={{0,2},{1,3},{2,0},{3,1},{4,6},{5,7},{6,4},{7,5},{8,10},{9,11},{10,... | collective-permute-start | bytes 394760 | tf_op jit(solution)/shard_map/ppermute | solution.py:44
  25.1 2.7 %collective-permute-start.3 = (f32[1,32,4112]{2,1,0:T(8,128)S(1)}, f32[1,32,4112]{2,1,0:T(8,128)S(1)}, u32[]{:S(2)}, u32[]{:S(2)}) collective-permute-start(f32[1,32,4112]{2,1,0:T(8,128)S(1)} %bitcast.283), channel_id=1, source_target_pairs={{0,8},{4,12},{8,0},{12,4},{1,9},{5,13},{9,1},{13,5},{2,10},{6,14},... | collective-permute-start | bytes 1579016 | tf_op jit(solution)/shard_map/ppermute | solution.py:44
  35.3 7.2 %collective-permute-done.11 = f32[1,1024,128]{2,1,0:T(8,128)S(1)} collective-permute-done((f32[1,1024,128]{2,1,0:T(8,128)S(1)}, f32[1,1024,128]{2,1,0:T(8,128)S(1)}, u32[]{:S(2)}, u32[]{:S(2)}) %collective-permute-start.11) | collective-permute-done | bytes 524320 | tf_op jit(solution)/shard_map/ppermute | solution.py:44
  42.6 11.2 %collective-permute-done.10 = f32[1,1024,128]{2,1,0:T(8,128)S(1)} collective-permute-done((f32[1,1024,128]{2,1,0:T(8,128)S(1)}, f32[1,1024,128]{2,1,0:T(8,128)S(1)}, u32[]{:S(2)}, u32[]{:S(2)}) %collective-permute-start.10) | collective-permute-done | bytes 524320 | tf_op jit(solution)/shard_map/ppermute | solution.py:44
  53.8 11.2 %collective-permute-done.8 = f32[1,1024,128]{2,1,0:T(8,128)S(1)} collective-permute-done((f32[1,1024,128]{2,1,0:T(8,128)S(1)}, f32[1,1024,128]{2,1,0:T(8,128)S(1)}, u32[]{:S(2)}, u32[]{:S(2)}) %collective-permute-start.8) | collective-permute-done | bytes 524320 | tf_op jit(solution)/shard_map/ppermute | solution.py:44
  67.9 7.4 %collective-permute-done.6 = f32[1,1024,128]{2,1,0:T(8,128)S(1)} collective-permute-done((f32[1,1024,128]{2,1,0:T(8,128)S(1)}, f32[1,1024,128]{2,1,0:T(8,128)S(1)}, u32[]{:S(2)}, u32[]{:S(2)}) %collective-permute-start.6) | collective-permute-done | bytes 524320 | tf_op jit(solution)/shard_map/ppermute | solution.py:44
  76.8 13.8 %collective-permute-done.4 = f32[2,32,4112]{2,1,0:T(8,128)} collective-permute-done((f32[2,32,4112]{2,1,0:T(8,128)}, f32[2,32,4112]{2,1,0:T(8,128)}, u32[]{:S(2)}, u32[]{:S(2)}) %collective-permute-start.4) | collective-permute-done | bytes 1052704 | tf_op jit(solution)/shard_map/ppermute | solution.py:44
  90.6 1.7 select_bitcast_fusion.3
  94.8 1.9 gather_fusion.3
  96.9 2.8 %fusion.22 = bf16[16,8,32,128]{3,1,2,0:T(8,128)(2,1)} fusion(f32[128,4112]{1,0:T(8,128)} %bitcast.282), kind=kLoop, calls=%fused_computation.44 | loop fusion | bytes 2097152
  99.9 1.9 gather_fusion
  101.9 2.5 %copy.190 = bf16[16,8,32,128]{3,2,1,0:T(8,128)(2,1)} copy(bf16[16,8,32,128]{3,1,2,0:T(8,128)(2,1)} %fusion.22) | data formatting | bytes 2097152
  104.7 3.4 %gather_fusion.1 = bf16[256,32,128]{2,1,0:T(8,128)(2,1)} fusion(bf16[128,32,128]{2,1,0:T(8,128)(2,1)} %bitcast.273, s32[1024]{0:T(1024)S(1)} %pad_clamp_fusion.1), kind=kCustom, calls=%fused_computation.1 | custom fusion | bytes 4195328 | tf_op jit(solution)/shard_map/gather | solution.py:173
  108.1 3.0 %gather_fusion.2 = bf16[256,64,128]{2,1,0:T(8,128)(2,1)} fusion(bf16[64,64,128]{2,1,0:T(8,128)(2,1)S(1)} %multiply_convert_fusion.1, s32[1024]{0:T(1024)S(1)} %pad_clamp_fusion), kind=kCustom, calls=%fused_computation.2 | custom fusion | bytes 8389632 | tf_op jit(solution)/shard_map/gather | solution.py:180
  111.1 5.2 %select_reduce_fusion = (f32[16,16,32]{2,1,0:T(8,128)S(1)}, f32[16,16,32,64]{3,2,1,0:T(8,128)S(1)}) fusion(pred[16,16,64]{2,1,0:T(8,128)(4,1)S(1)} %add_compare_fusion, bf16[16,16,32,128]{3,2,1,0:T(8,128)(2,1)} %bitcast.275, bf16[16,16,64,128]{3,2,1,0:T(8,128)(2,1)} %bitcast.272), kind=kOutput, calls=%fused_computation.11 | convolution fusion | flops 135258112 | bytes 8437760 | tf_op jit(solution)/shard_map/scie,scje->scij/dot_general | solution.py:182
  116.4 2.6 %fusion.2 = f32[16,16,32]{2,1,0:T(8,128)S(1)} fusion(f32[16,16,32,64]{3,2,1,0:T(8,128)S(1)} %get-tuple-element.51, f32[16,16,32]{2,1,0:T(8,128)S(1)} %get-tuple-element.50, pred[16,16,64]{2,1,0:T(8,128)(4,1)S(1)} %add_compare_fusion), kind=kLoop, calls=%fused_computation.12 | loop fusion | flops 1564672 | bytes 2179072 | tf_op jit(solution)/shard_map/reduce_sum | solution.py:22
  119.3 1.6 collective-permute-start.13
  127.7 2.3 %collective-permute-done.16 = f32[16,128]{1,0:T(8,128)S(1)} collective-permute-done((f32[16,128]{1,0:T(8,128)S(1)}, f32[16,128]{1,0:T(8,128)S(1)}, u32[]{:S(2)}, u32[]{:S(2)}) %collective-permute-start.16) | collective-permute-done | bytes 8224 | tf_op jit(solution)/shard_map/ppermute | solution.py:98
  130.0 2.5 %collective-permute-done.15 = f32[16,128]{1,0:T(8,128)S(1)} collective-permute-done((f32[16,128]{1,0:T(8,128)S(1)}, f32[16,128]{1,0:T(8,128)S(1)}, u32[]{:S(2)}, u32[]{:S(2)}) %collective-permute-start.15) | collective-permute-done | bytes 8224 | tf_op jit(solution)/shard_map/ppermute | solution.py:98
  133.2 1.9 gather_fusion.4
  135.2 6.9 %multiply_convert_fusion = bf16[16,16,64,128]{3,2,1,0:T(8,128)(2,1)S(1)} fusion(f32[16,16]{1,0:T(8,128)S(1)} %select_multiply_fusion, bf16[16,16,32,128]{3,2,1,0:T(8,128)(2,1)} %bitcast.276, f32[16,16,32,64]{3,2,1,0:T(8,128)} %copy-done.9, f32[16,16,32]{2,1,0:T(8,128)S(1)} %fusion.2, f32[16,16,32]{2,1,0:T(8,128)S(1)} %get-tuple-element.50, ...), kind=kOutput, calls=%fused_computation.5 | convolution fusion | flops 140509184 | bytes 8471552 | tf_op jit(solution)/shard_map/scij,scie->scje/dot_general | solution.py:185
  142.2 4.9 %fusion.14 = (f32[64,64]{0,1:T(8,128)S(1)}, f32[64,64,128]{2,0,1:T(8,128)}) fusion(f32[64,64,128]{2,1,0:T(8,128)S(1)} %bitcast.269, bf16[16,16,64,128]{3,2,1,0:T(8,128)(2,1)S(1)} %multiply_convert_fusion, s32[16,16]{0,1:T(8,128)S(1)} %copy.166, pred[16,16]{0,1:T(8,128)(4,1)S(1)} %copy.167), kind=kOutput, calls=%fused_computation.31 | convolution fusion | flops 269512704 | bytes 8406272 | tf_op jit(solution)/shard_map/scb,scje->bje/dot_general | solution.py:196
  147.3 2.8 %copy.170 = f32[64,64,128]{2,1,0:T(8,128)S(1)} copy(f32[64,64,128]{2,0,1:T(8,128)} %get-tuple-element.53) | data formatting | bytes 4194304 | tf_op jit(solution)/shard_map/scb,scje->bje/dot_general | solution.py:196
  150.1 1.9 fusion.7
  152.7 21.2 %collective-permute-done.18 = bf16[1,4096,128]{2,1,0:T(8,128)(2,1)S(1)} collective-permute-done((bf16[1,4096,128]{2,1,0:T(8,128)(2,1)S(1)}, bf16[1,4096,128]{2,1,0:T(8,128)(2,1)S(1)}, u32[]{:S(2)}, u32[]{:S(2)}) %collective-permute-start.18) | collective-permute-done | bytes 1048608 | tf_op jit(solution)/shard_map/ppermute | solution.py:44
  175.5 4.5 %collective-permute-done.19 = bf16[2,4096,128]{2,1,0:T(8,128)(2,1)} collective-permute-done((bf16[2,4096,128]{2,1,0:T(8,128)(2,1)}, bf16[2,4096,128]{2,1,0:T(8,128)(2,1)}, u32[]{:S(2)}, u32[]{:S(2)}) %collective-permute-start.19) | collective-permute-done | bytes 2097184 | tf_op jit(solution)/shard_map/ppermute | solution.py:44
  180.0 1.9 select_bitcast_fusion.1
  187.1 1.9 collective-permute-start.20
  189.6 4.1 %collective-permute-done.22 = f32[256,128]{0,1:T(8,128)S(1)} collective-permute-done((f32[256,128]{0,1:T(8,128)S(1)}, f32[256,128]{0,1:T(8,128)S(1)}, u32[]{:S(2)}, u32[]{:S(2)}) %collective-permute-start.22) | collective-permute-done | bytes 131104 | tf_op jit(solution)/shard_map/ppermute | solution.py:98
  193.7 5.4 %collective-permute-done.21 = f32[256,128]{0,1:T(8,128)S(1)} collective-permute-done((f32[256,128]{0,1:T(8,128)S(1)}, f32[256,128]{0,1:T(8,128)S(1)}, u32[]{:S(2)}, u32[]{:S(2)}) %collective-permute-start.21) | collective-permute-done | bytes 131104 | tf_op jit(solution)/shard_map/ppermute | solution.py:98
  (163 shorter events, 45.8 us)
Async XLA Ops:
  0.6 5.8 %copy-start = (bf16[256,128]{1,0:T(8,128)(2,1)S(1)}, bf16[256,128]{1,0:T(8,128)(2,1)}, u32[]{:S(2)}) copy-start(bf16[256,128]{1,0:T(8,128)(2,1)} %param.6) | copy-start | bytes 196612
  8.7 5.0 %copy-start.5 = (f32[2,2,1024,128]{3,2,1,0:T(8,128)}, f32[2,2,1024,128]{3,2,1,0:T(8,128)S(1)}, u32[]{:S(2)}) copy-start(f32[2,2,1024,128]{3,2,1,0:T(8,128)S(1)} %fusion.3) | copy-start | bytes 6291460
  8.7 4.3 %copy-start.11 = (bf16[4,1,1024,256]{3,2,1,0:T(8,128)(2,1)S(1)}, bf16[4,1,1024,256]{3,2,1,0:T(8,128)(2,1)}, u32[]{:S(2)}) copy-start(bf16[4,1,1024,256]{3,2,1,0:T(8,128)(2,1)} %get-tuple-element.29) | copy-start | bytes 6291460
  9.9 13.4 %collective-permute-start = (f32[2,1024,128]{2,1,0:T(8,128)}, f32[2,1024,128]{2,1,0:T(8,128)}, u32[]{:S(2)}, u32[]{:S(2)}) collective-permute-start(f32[2,1024,128]{2,1,0:T(8,128)} %select_bitcast_fusion.9), channel_id=1, source_target_pairs={{0,1},{1,0},{2,3},{3,2},{4,5},{5,4},{6,7},{7,6},{8,9},{9,8},{10,11... | collective-permute-start | bytes 3145736 | tf_op jit(solution)/shard_map/ppermute | solution.py:44
  10.4 8.9 %collective-permute-start.1 = (f32[1,8,4112]{2,1,0:T(8,128)S(1)}, f32[1,8,4112]{2,1,0:T(8,128)S(1)}, u32[]{:S(2)}, u32[]{:S(2)}) collective-permute-start(f32[1,8,4112]{2,1,0:T(8,128)S(1)} %maximum_bitcast_fusion.3), channel_id=1, source_target_pairs={{0,2},{1,3},{2,0},{3,1},{4,6},{5,7},{6,4},{7,5},{8,10},{9,11},{10,... | collective-permute-start | bytes 394760 | tf_op jit(solution)/shard_map/ppermute | solution.py:44
  15.0 14.0 %collective-permute-start.9 = (f32[2,1024,128]{2,1,0:T(8,128)}, f32[2,1024,128]{2,1,0:T(8,128)}, u32[]{:S(2)}, u32[]{:S(2)}) collective-permute-start(f32[2,1024,128]{2,1,0:T(8,128)} %select_bitcast_fusion.6), channel_id=1, source_target_pairs={{0,1},{1,0},{2,3},{3,2},{4,5},{5,4},{6,7},{7,6},{8,9},{9,8},{10,11... | collective-permute-start | bytes 3145736 | tf_op jit(solution)/shard_map/ppermute | solution.py:44
  17.0 14.3 %collective-permute-start.7 = (f32[2,1024,128]{2,1,0:T(8,128)}, f32[2,1024,128]{2,1,0:T(8,128)}, u32[]{:S(2)}, u32[]{:S(2)}) collective-permute-start(f32[2,1024,128]{2,1,0:T(8,128)} %select_bitcast_fusion.7), channel_id=1, source_target_pairs={{0,1},{1,0},{2,3},{3,2},{4,5},{5,4},{6,7},{7,6},{8,9},{9,8},{10,11... | collective-permute-start | bytes 3145736 | tf_op jit(solution)/shard_map/ppermute | solution.py:44
  20.2 1.9 collective-permute-start.2
  21.5 12.7 %collective-permute-start.5 = (f32[2,1024,128]{2,1,0:T(8,128)}, f32[2,1024,128]{2,1,0:T(8,128)S(1)}, u32[]{:S(2)}, u32[]{:S(2)}) collective-permute-start(f32[2,1024,128]{2,1,0:T(8,128)} %select_bitcast_fusion.8), channel_id=1, source_target_pairs={{0,1},{1,0},{2,3},{3,2},{4,5},{5,4},{6,7},{7,6},{8,9},{9,8},{10,11... | collective-permute-start | bytes 3145736 | tf_op jit(solution)/shard_map/ppermute | solution.py:44
  23.2 5.8 %copy-start.8 = (f32[2,2,1024,128]{3,2,0,1:T(8,128)S(1)}, f32[2,2,1024,128]{3,2,0,1:T(8,128)}, u32[]{:S(2)}) copy-start(f32[2,2,1024,128]{3,2,0,1:T(8,128)} %copy-done.7) | copy-start | bytes 6291460
  25.1 6.3 %copy-start.4 = (f32[2,2,1024,128]{3,2,0,1:T(8,128)S(1)}, f32[2,2,1024,128]{3,2,0,1:T(8,128)}, u32[]{:S(2)}) copy-start(f32[2,2,1024,128]{3,2,0,1:T(8,128)} %copy-done.3) | copy-start | bytes 6291460
  25.1 40.0 %collective-permute-start.3 = (f32[1,32,4112]{2,1,0:T(8,128)S(1)}, f32[1,32,4112]{2,1,0:T(8,128)S(1)}, u32[]{:S(2)}, u32[]{:S(2)}) collective-permute-start(f32[1,32,4112]{2,1,0:T(8,128)S(1)} %bitcast.283), channel_id=1, source_target_pairs={{0,8},{4,12},{8,0},{12,4},{1,9},{5,13},{9,1},{13,5},{2,10},{6,14},... | collective-permute-start | bytes 1579016 | tf_op jit(solution)/shard_map/ppermute | solution.py:44
  27.7 14.8 %collective-permute-start.11 = (f32[1,1024,128]{2,1,0:T(8,128)S(1)}, f32[1,1024,128]{2,1,0:T(8,128)S(1)}, u32[]{:S(2)}, u32[]{:S(2)}) collective-permute-start(f32[1,1024,128]{2,1,0:T(8,128)S(1)} %select_bitcast_fusion.15), channel_id=1, source_target_pairs={{0,2},{1,3},{2,0},{3,1},{4,6},{5,7},{6,4},{7,5},{8,10},{9,11},{10,... | collective-permute-start | bytes 1572872 | tf_op jit(solution)/shard_map/ppermute | solution.py:44
  30.6 23.2 %collective-permute-start.10 = (f32[1,1024,128]{2,1,0:T(8,128)S(1)}, f32[1,1024,128]{2,1,0:T(8,128)S(1)}, u32[]{:S(2)}, u32[]{:S(2)}) collective-permute-start(f32[1,1024,128]{2,1,0:T(8,128)S(1)} %select_bitcast_fusion.12), channel_id=1, source_target_pairs={{0,2},{1,3},{2,0},{3,1},{4,6},{5,7},{6,4},{7,5},{8,10},{9,11},{10,... | collective-permute-start | bytes 1572872 | tf_op jit(solution)/shard_map/ppermute | solution.py:44
  32.9 32.1 %collective-permute-start.8 = (f32[1,1024,128]{2,1,0:T(8,128)S(1)}, f32[1,1024,128]{2,1,0:T(8,128)S(1)}, u32[]{:S(2)}, u32[]{:S(2)}) collective-permute-start(f32[1,1024,128]{2,1,0:T(8,128)S(1)} %select_bitcast_fusion.13), channel_id=1, source_target_pairs={{0,2},{1,3},{2,0},{3,1},{4,6},{5,7},{6,4},{7,5},{8,10},{9,11},{10,... | collective-permute-start | bytes 1572872 | tf_op jit(solution)/shard_map/ppermute | solution.py:44
  34.5 40.8 %collective-permute-start.6 = (f32[1,1024,128]{2,1,0:T(8,128)S(1)}, f32[1,1024,128]{2,1,0:T(8,128)S(1)}, u32[]{:S(2)}, u32[]{:S(2)}) collective-permute-start(f32[1,1024,128]{2,1,0:T(8,128)S(1)} %select_bitcast_fusion.14), channel_id=1, source_target_pairs={{0,2},{1,3},{2,0},{3,1},{4,6},{5,7},{6,4},{7,5},{8,10},{9,11},{10,... | collective-permute-start | bytes 1572872 | tf_op jit(solution)/shard_map/ppermute | solution.py:44
  65.2 10.1 %copy-start.13 = (f32[1,1,32,4112]{3,2,1,0:T(8,128)}, f32[1,1,32,4112]{3,2,1,0:T(8,128)S(1)}, u32[]{:S(2)}) copy-start(f32[1,1,32,4112]{3,2,1,0:T(8,128)S(1)} %get-tuple-element.38) | copy-start | bytes 1579012
  65.2 10.1 %copy-start.14 = (f32[1,1,32,4112]{3,2,1,0:T(8,128)}, f32[1,1,32,4112]{3,2,1,0:T(8,128)S(1)}, u32[]{:S(2)}) copy-start(f32[1,1,32,4112]{3,2,1,0:T(8,128)S(1)} %get-tuple-element.39) | copy-start | bytes 1579012
  66.3 24.3 %collective-permute-start.4 = (f32[2,32,4112]{2,1,0:T(8,128)}, f32[2,32,4112]{2,1,0:T(8,128)}, u32[]{:S(2)}, u32[]{:S(2)}) collective-permute-start(f32[2,32,4112]{2,1,0:T(8,128)} %maximum_bitcast_fusion.1), channel_id=1, source_target_pairs={{0,4},{4,0},{8,12},{12,8},{1,5},{5,1},{9,13},{13,9},{2,6},{6,2},{1... | collective-permute-start | bytes 3158024 | tf_op jit(solution)/shard_map/ppermute | solution.py:44
  119.2 2.4 %collective-permute-start.14 = (f32[16,128]{1,0:T(8,128)S(1)}, f32[16,128]{1,0:T(8,128)S(1)}, u32[]{:S(2)}, u32[]{:S(2)}) collective-permute-start(f32[16,128]{1,0:T(8,128)S(1)} %select_reduce_fusion.1), channel_id=1, source_target_pairs={{0,3},{1,0},{2,1},{3,2},{4,7},{5,4},{6,5},{7,6},{8,11},{9,8},{10,9... | collective-permute-start | bytes 24584 | tf_op jit(solution)/shard_map/ppermute | solution.py:98
  119.3 3.7 %collective-permute-start.13 = (f32[16,128]{1,0:T(8,128)S(1)}, f32[16,128]{1,0:T(8,128)S(1)}, u32[]{:S(2)}, u32[]{:S(2)}) collective-permute-start(f32[16,128]{1,0:T(8,128)S(1)} %select_reduce_fusion.1), channel_id=1, source_target_pairs={{0,2},{1,3},{2,0},{3,1},{4,6},{5,7},{6,4},{7,5},{8,10},{9,11},{10,... | collective-permute-start | bytes 24584 | tf_op jit(solution)/shard_map/ppermute | solution.py:98
  121.0 3.1 %collective-permute-start.12 = (f32[16,128]{1,0:T(8,128)S(1)}, f32[16,128]{1,0:T(8,128)S(1)}, u32[]{:S(2)}, u32[]{:S(2)}) collective-permute-start(f32[16,128]{1,0:T(8,128)S(1)} %select_reduce_fusion.1), channel_id=1, source_target_pairs={{0,1},{1,2},{2,3},{3,0},{4,5},{5,6},{6,7},{7,4},{8,9},{9,10},{10,1... | collective-permute-start | bytes 24584 | tf_op jit(solution)/shard_map/ppermute | solution.py:98
  124.0 3.7 %collective-permute-start.17 = (f32[16,128]{1,0:T(8,128)S(1)}, f32[16,128]{1,0:T(8,128)S(1)}, u32[]{:S(2)}, u32[]{:S(2)}) collective-permute-start(f32[16,128]{1,0:T(8,128)S(1)} %fusion.63), channel_id=1, source_target_pairs={{0,12},{4,0},{8,4},{12,8},{1,13},{5,1},{9,5},{13,9},{2,14},{6,2},{... | collective-permute-start | bytes 24584 | tf_op jit(solution)/shard_map/ppermute | solution.py:98
  125.5 4.6 %collective-permute-start.16 = (f32[16,128]{1,0:T(8,128)S(1)}, f32[16,128]{1,0:T(8,128)S(1)}, u32[]{:S(2)}, u32[]{:S(2)}) collective-permute-start(f32[16,128]{1,0:T(8,128)S(1)} %fusion.63), channel_id=1, source_target_pairs={{0,8},{4,12},{8,0},{12,4},{1,9},{5,13},{9,1},{13,5},{2,10},{6,14},... | collective-permute-start | bytes 24584 | tf_op jit(solution)/shard_map/ppermute | solution.py:98
  127.1 5.4 %collective-permute-start.15 = (f32[16,128]{1,0:T(8,128)S(1)}, f32[16,128]{1,0:T(8,128)S(1)}, u32[]{:S(2)}, u32[]{:S(2)}) collective-permute-start(f32[16,128]{1,0:T(8,128)S(1)} %fusion.63), channel_id=1, source_target_pairs={{0,4},{4,8},{8,12},{12,0},{1,5},{5,9},{9,13},{13,1},{2,6},{6,10},{... | collective-permute-start | bytes 24584 | tf_op jit(solution)/shard_map/ppermute | solution.py:98
  152.0 21.8 %collective-permute-start.18 = (bf16[1,4096,128]{2,1,0:T(8,128)(2,1)S(1)}, bf16[1,4096,128]{2,1,0:T(8,128)(2,1)S(1)}, u32[]{:S(2)}, u32[]{:S(2)}) collective-permute-start(bf16[1,4096,128]{2,1,0:T(8,128)(2,1)S(1)} %fusion.7), channel_id=1, source_target_pairs={{0,2},{1,3},{2,0},{3,1},{4,6},{5,7},{6,4},{7,5},{8,10},{9,11},{10,... | collective-permute-start | bytes 3145736 | tf_op jit(solution)/shard_map/ppermute | solution.py:44
  175.5 4.5 %collective-permute-start.19 = (bf16[2,4096,128]{2,1,0:T(8,128)(2,1)}, bf16[2,4096,128]{2,1,0:T(8,128)(2,1)}, u32[]{:S(2)}, u32[]{:S(2)}) collective-permute-start(bf16[2,4096,128]{2,1,0:T(8,128)(2,1)} %maximum_bitcast_fusion), channel_id=1, source_target_pairs={{0,1},{1,0},{2,3},{3,2},{4,5},{5,4},{6,7},{7,6},{8,9},{9,8},{10,11... | collective-permute-start | bytes 6291464 | tf_op jit(solution)/shard_map/ppermute | solution.py:44
  182.2 3.2 %slice-start.1 = ((s8[8388608]{0:T(1024)(128)(4,1)}), s8[4194304]{0:T(1024)(128)(4,1)S(1)}, s32[]{:S(2)}) async-start(s8[8388608]{0:T(1024)(128)(4,1)} %bitcast.266), calls=%async_computation.1 | async-start | bytes 8388608
  185.4 14.6 %copy-start.1 = (bf16[256,128]{1,0:T(8,128)(2,1)S(1)}, bf16[256,128]{1,0:T(8,128)(2,1)}, u32[]{:S(2)}) copy-start(bf16[256,128]{1,0:T(8,128)(2,1)} %param.6) | copy-start | bytes 196612
  186.9 6.8 %collective-permute-start.22 = (f32[256,128]{0,1:T(8,128)S(1)}, f32[256,128]{0,1:T(8,128)S(1)}, u32[]{:S(2)}, u32[]{:S(2)}) collective-permute-start(f32[256,128]{0,1:T(8,128)S(1)} %bitcast.287), channel_id=1, source_target_pairs={{0,12},{4,0},{8,4},{12,8},{1,13},{5,1},{9,5},{13,9},{2,14},{6,2},{... | collective-permute-start | bytes 393224 | tf_op jit(solution)/shard_map/ppermute | solution.py:98
  187.0 12.1 %collective-permute-start.21 = (f32[256,128]{0,1:T(8,128)S(1)}, f32[256,128]{0,1:T(8,128)S(1)}, u32[]{:S(2)}, u32[]{:S(2)}) collective-permute-start(f32[256,128]{0,1:T(8,128)S(1)} %bitcast.288), channel_id=1, source_target_pairs={{0,8},{4,12},{8,0},{12,4},{1,9},{5,13},{9,1},{13,5},{2,10},{6,14},... | collective-permute-start | bytes 393224 | tf_op jit(solution)/shard_map/ppermute | solution.py:98
  187.1 12.1 %collective-permute-start.20 = (f32[256,128]{0,1:T(8,128)S(1)}, f32[256,128]{0,1:T(8,128)S(1)}, u32[]{:S(2)}, u32[]{:S(2)}) collective-permute-start(f32[256,128]{0,1:T(8,128)S(1)} %bitcast.289), channel_id=1, source_target_pairs={{0,4},{4,8},{8,12},{12,0},{1,5},{5,9},{9,13},{13,1},{2,6},{6,10},{... | collective-permute-start | bytes 393224 | tf_op jit(solution)/shard_map/ppermute | solution.py:98
  (10 other events, 20.7 us)

commit v8 on v7

--- a/solution.py
+++ b/solution.py
@@ -141,8 +141,8 @@
     ]
     if is_pow2(mp_count) and mp_count > 1:
         keeps, sends, bit = halving_steps(partials, "mp")
-        last, packed = lax.optimization_barrier((sends[-1], packed))
-        sends = sends[:-1] + [last]
+        first, packed = lax.optimization_barrier((sends[0], packed))
+        sends = [first] + sends[1:]
         pieces = [k + xor_perm(t, "mp", bit) for k, t in zip(keeps, sends)]
         pieces = [p.reshape(-1, emb_width) for p in pieces]
     else:

time: 201 us -> 202 us (level)
  no operation moved by 1% of the time
where the time goes in v8:
time: 202 us
  waiting for transfers between devices  95.7 us (47%)
  local copies, waits for them, and re-layouts  35.2 us (17%)
  other arithmetic  26.3 us (13%)
  matrix products  23 us (11%)
  starting transfers between devices  20.2 us (10%)
    ppermute x14, waiting for transfers between devices, xor_perm(): return lax.ppermute(value, axis, [(i, i ^ bit) for i in range(count)])  78.3 us
    ppermute x9, waiting for transfers between devices, all_sum(): lax.ppermute(value, axis, [(i, (i + k) % count) for i in range(count)])  17.4 us
    ppermute x14, starting transfers between devices, xor_perm(): return lax.ppermute(value, axis, [(i, i ^ bit) for i in range(count)])  13.1 us
    unnamed x44, local copies, waits for them, and re-layouts  11.9 us
    ppermute x9, starting transfers between devices, all_sum(): lax.ppermute(value, axis, [(i, (i + k) % count) for i in range(count)])  7.05 us
    dot_general x1, matrix products, local(): jnp.einsum('scij,scie->scje', weights, q_e, preferred_element_type=jnp.fl...  6.94 us
    slice x1, local copies, waits for them, and re-layouts, local(): split_rows[:, k]  5.76 us
    another operation x9, other arithmetic, all_gather_rows(): arr = jnp.stack([first, second], axis=1).reshape((-1,) + value.shape)  5.5 us
  transfers between devices with their start and end apart: 23, of which 15 were waited for; matrix products, arithmetic and copies ran while one was open for 8% of the time, Pallas kernels for 0%

profile of v8, /device:TPU:0, one launch (start us, length us, event | category | flops | bytes accessed | tf_op | source)
XLA Modules:
  0.0 201.6 jit_solution(10151005671894095614)
XLA Ops:
  0.7 5.8 %fusion.56 = (bf16[4,1,1024,256]{3,2,1,0:T(8,128)(2,1)}, bf16[4,1,1024,256]{3,2,1,0:T(8,128)(2,1)S(1)}, bf16[4,1,1024,256]{3,2,1,0:T(8,128)(2,1)}, bf16[4,1,1024,256]{3,2,1,0:T(8,128)(2,1)}) fusion(bf16[4,4,1024,256]{3,2,1,0:T(8,128)(2,1)} %bitcast.265), kind=kLoop, calls=%fused_computation.166 | loop fusion | bytes 16777216 | tf_op jit(solution)/shard_map/slice | solution.py:137
  6.4 2.3 %fusion.3 = f32[2,2,1024,128]{3,2,1,0:T(8,128)S(1)} fusion(bf16[256,128]{1,0:T(8,128)(2,1)S(1)} %copy-done, bf16[2,2,1024,256]{3,2,1,0:T(8,128)(2,1)} %bitcast.280), kind=kOutput, calls=%fused_computation.17 | convolution fusion | flops 268435456 | bytes 4259840 | tf_op jit(solution)/shard_map/dot_general | solution.py:137
  10.4 2.6 %collective-permute-start.1 = (f32[1,8,4112]{2,1,0:T(8,128)S(1)}, f32[1,8,4112]{2,1,0:T(8,128)S(1)}, u32[]{:S(2)}, u32[]{:S(2)}) collective-permute-start(f32[1,8,4112]{2,1,0:T(8,128)S(1)} %maximum_bitcast_fusion.3), channel_id=1, source_target_pairs={{0,2},{1,3},{2,0},{3,1},{4,6},{5,7},{6,4},{7,5},{8,10},{9,11},{10,... | collective-permute-start | bytes 394760 | tf_op jit(solution)/shard_map/ppermute | solution.py:44
  25.1 2.6 %collective-permute-start.3 = (f32[1,32,4112]{2,1,0:T(8,128)S(1)}, f32[1,32,4112]{2,1,0:T(8,128)S(1)}, u32[]{:S(2)}, u32[]{:S(2)}) collective-permute-start(f32[1,32,4112]{2,1,0:T(8,128)S(1)} %bitcast.283), channel_id=1, source_target_pairs={{0,8},{4,12},{8,0},{12,4},{1,9},{5,13},{9,1},{13,5},{2,10},{6,14},... | collective-permute-start | bytes 1579016 | tf_op jit(solution)/shard_map/ppermute | solution.py:44
  35.3 8.8 %collective-permute-done.11 = f32[1,1024,128]{2,1,0:T(8,128)S(1)} collective-permute-done((f32[1,1024,128]{2,1,0:T(8,128)S(1)}, f32[1,1024,128]{2,1,0:T(8,128)S(1)}, u32[]{:S(2)}, u32[]{:S(2)}) %collective-permute-start.11) | collective-permute-done | bytes 524320 | tf_op jit(solution)/shard_map/ppermute | solution.py:44
  44.2 11.2 %collective-permute-done.9 = f32[1,1024,128]{2,1,0:T(8,128)S(1)} collective-permute-done((f32[1,1024,128]{2,1,0:T(8,128)S(1)}, f32[1,1024,128]{2,1,0:T(8,128)S(1)}, u32[]{:S(2)}, u32[]{:S(2)}) %collective-permute-start.9) | collective-permute-done | bytes 524320 | tf_op jit(solution)/shard_map/ppermute | solution.py:44
  55.4 11.2 %collective-permute-done.7 = f32[1,1024,128]{2,1,0:T(8,128)S(1)} collective-permute-done((f32[1,1024,128]{2,1,0:T(8,128)S(1)}, f32[1,1024,128]{2,1,0:T(8,128)S(1)}, u32[]{:S(2)}, u32[]{:S(2)}) %collective-permute-start.7) | collective-permute-done | bytes 524320 | tf_op jit(solution)/shard_map/ppermute | solution.py:44
  69.5 7.4 %collective-permute-done.5 = f32[1,1024,128]{2,1,0:T(8,128)S(1)} collective-permute-done((f32[1,1024,128]{2,1,0:T(8,128)S(1)}, f32[1,1024,128]{2,1,0:T(8,128)S(1)}, u32[]{:S(2)}, u32[]{:S(2)}) %collective-permute-start.5) | collective-permute-done | bytes 524320 | tf_op jit(solution)/shard_map/ppermute | solution.py:44
  78.4 13.8 %collective-permute-done.4 = f32[2,32,4112]{2,1,0:T(8,128)} collective-permute-done((f32[2,32,4112]{2,1,0:T(8,128)}, f32[2,32,4112]{2,1,0:T(8,128)}, u32[]{:S(2)}, u32[]{:S(2)}) %collective-permute-start.4) | collective-permute-done | bytes 1052704 | tf_op jit(solution)/shard_map/ppermute | solution.py:44
  92.2 1.7 select_bitcast_fusion.3
  96.4 1.9 gather_fusion.3
  98.5 2.8 %fusion.22 = bf16[16,8,32,128]{3,1,2,0:T(8,128)(2,1)} fusion(f32[128,4112]{1,0:T(8,128)} %bitcast.282), kind=kLoop, calls=%fused_computation.44 | loop fusion | bytes 2097152
  101.4 1.9 gather_fusion
  103.5 2.5 %copy.190 = bf16[16,8,32,128]{3,2,1,0:T(8,128)(2,1)} copy(bf16[16,8,32,128]{3,1,2,0:T(8,128)(2,1)} %fusion.22) | data formatting | bytes 2097152
  106.3 3.4 %gather_fusion.1 = bf16[256,32,128]{2,1,0:T(8,128)(2,1)} fusion(bf16[128,32,128]{2,1,0:T(8,128)(2,1)} %bitcast.273, s32[1024]{0:T(1024)S(1)} %pad_clamp_fusion.1), kind=kCustom, calls=%fused_computation.1 | custom fusion | bytes 4195328 | tf_op jit(solution)/shard_map/gather | solution.py:173
  109.7 3.0 %gather_fusion.2 = bf16[256,64,128]{2,1,0:T(8,128)(2,1)} fusion(bf16[64,64,128]{2,1,0:T(8,128)(2,1)S(1)} %multiply_convert_fusion.1, s32[1024]{0:T(1024)S(1)} %pad_clamp_fusion), kind=kCustom, calls=%fused_computation.2 | custom fusion | bytes 8389632 | tf_op jit(solution)/shard_map/gather | solution.py:180
  112.7 5.2 %select_reduce_fusion = (f32[16,16,32]{2,1,0:T(8,128)S(1)}, f32[16,16,32,64]{3,2,1,0:T(8,128)S(1)}) fusion(pred[16,16,64]{2,1,0:T(8,128)(4,1)S(1)} %add_compare_fusion, bf16[16,16,32,128]{3,2,1,0:T(8,128)(2,1)} %bitcast.275, bf16[16,16,64,128]{3,2,1,0:T(8,128)(2,1)} %bitcast.272), kind=kOutput, calls=%fused_computation.11 | convolution fusion | flops 135258112 | bytes 8437760 | tf_op jit(solution)/shard_map/scie,scje->scij/dot_general | solution.py:182
  118.0 2.6 %fusion.2 = f32[16,16,32]{2,1,0:T(8,128)S(1)} fusion(f32[16,16,32,64]{3,2,1,0:T(8,128)S(1)} %get-tuple-element.51, f32[16,16,32]{2,1,0:T(8,128)S(1)} %get-tuple-element.50, pred[16,16,64]{2,1,0:T(8,128)(4,1)S(1)} %add_compare_fusion), kind=kLoop, calls=%fused_computation.12 | loop fusion | flops 1564672 | bytes 2179072 | tf_op jit(solution)/shard_map/reduce_sum | solution.py:22
  120.9 1.7 collective-permute-start.13
  129.4 2.3 %collective-permute-done.16 = f32[16,128]{1,0:T(8,128)S(1)} collective-permute-done((f32[16,128]{1,0:T(8,128)S(1)}, f32[16,128]{1,0:T(8,128)S(1)}, u32[]{:S(2)}, u32[]{:S(2)}) %collective-permute-start.16) | collective-permute-done | bytes 8224 | tf_op jit(solution)/shard_map/ppermute | solution.py:98
  131.6 2.5 %collective-permute-done.15 = f32[16,128]{1,0:T(8,128)S(1)} collective-permute-done((f32[16,128]{1,0:T(8,128)S(1)}, f32[16,128]{1,0:T(8,128)S(1)}, u32[]{:S(2)}, u32[]{:S(2)}) %collective-permute-start.15) | collective-permute-done | bytes 8224 | tf_op jit(solution)/shard_map/ppermute | solution.py:98
  134.8 1.9 gather_fusion.4
  136.8 6.9 %multiply_convert_fusion = bf16[16,16,64,128]{3,2,1,0:T(8,128)(2,1)S(1)} fusion(f32[16,16]{1,0:T(8,128)S(1)} %select_multiply_fusion, bf16[16,16,32,128]{3,2,1,0:T(8,128)(2,1)} %bitcast.276, f32[16,16,32,64]{3,2,1,0:T(8,128)} %copy-done.9, f32[16,16,32]{2,1,0:T(8,128)S(1)} %fusion.2, f32[16,16,32]{2,1,0:T(8,128)S(1)} %get-tuple-element.50, ...), kind=kOutput, calls=%fused_computation.5 | convolution fusion | flops 140509184 | bytes 8471552 | tf_op jit(solution)/shard_map/scij,scie->scje/dot_general | solution.py:185
  143.8 4.9 %fusion.14 = (f32[64,64]{0,1:T(8,128)S(1)}, f32[64,64,128]{2,0,1:T(8,128)}) fusion(f32[64,64,128]{2,1,0:T(8,128)S(1)} %bitcast.269, bf16[16,16,64,128]{3,2,1,0:T(8,128)(2,1)S(1)} %multiply_convert_fusion, s32[16,16]{0,1:T(8,128)S(1)} %copy.166, pred[16,16]{0,1:T(8,128)(4,1)S(1)} %copy.167), kind=kOutput, calls=%fused_computation.31 | convolution fusion | flops 269512704 | bytes 8406272 | tf_op jit(solution)/shard_map/scb,scje->bje/dot_general | solution.py:196
  148.9 2.8 %copy.170 = f32[64,64,128]{2,1,0:T(8,128)S(1)} copy(f32[64,64,128]{2,0,1:T(8,128)} %get-tuple-element.53) | data formatting | bytes 4194304 | tf_op jit(solution)/shard_map/scb,scje->bje/dot_general | solution.py:196
  151.7 1.9 fusion.7
  154.3 21.2 %collective-permute-done.18 = bf16[1,4096,128]{2,1,0:T(8,128)(2,1)S(1)} collective-permute-done((bf16[1,4096,128]{2,1,0:T(8,128)(2,1)S(1)}, bf16[1,4096,128]{2,1,0:T(8,128)(2,1)S(1)}, u32[]{:S(2)}, u32[]{:S(2)}) %collective-permute-start.18) | collective-permute-done | bytes 1048608 | tf_op jit(solution)/shard_map/ppermute | solution.py:44
  177.1 4.5 %collective-permute-done.19 = bf16[2,4096,128]{2,1,0:T(8,128)(2,1)} collective-permute-done((bf16[2,4096,128]{2,1,0:T(8,128)(2,1)}, bf16[2,4096,128]{2,1,0:T(8,128)(2,1)}, u32[]{:S(2)}, u32[]{:S(2)}) %collective-permute-start.19) | collective-permute-done | bytes 2097184 | tf_op jit(solution)/shard_map/ppermute | solution.py:44
  181.6 1.9 select_bitcast_fusion.1
  188.7 1.9 collective-permute-start.20
  191.2 4.1 %collective-permute-done.22 = f32[256,128]{0,1:T(8,128)S(1)} collective-permute-done((f32[256,128]{0,1:T(8,128)S(1)}, f32[256,128]{0,1:T(8,128)S(1)}, u32[]{:S(2)}, u32[]{:S(2)}) %collective-permute-start.22) | collective-permute-done | bytes 131104 | tf_op jit(solution)/shard_map/ppermute | solution.py:98
  195.4 5.4 %collective-permute-done.21 = f32[256,128]{0,1:T(8,128)S(1)} collective-permute-done((f32[256,128]{0,1:T(8,128)S(1)}, f32[256,128]{0,1:T(8,128)S(1)}, u32[]{:S(2)}, u32[]{:S(2)}) %collective-permute-start.21) | collective-permute-done | bytes 131104 | tf_op jit(solution)/shard_map/ppermute | solution.py:98
  (163 shorter events, 45.7 us)
Async XLA Ops:
  0.6 5.8 %copy-start = (bf16[256,128]{1,0:T(8,128)(2,1)S(1)}, bf16[256,128]{1,0:T(8,128)(2,1)}, u32[]{:S(2)}) copy-start(bf16[256,128]{1,0:T(8,128)(2,1)} %param.6) | copy-start | bytes 196612
  8.7 5.0 %copy-start.5 = (f32[2,2,1024,128]{3,2,1,0:T(8,128)}, f32[2,2,1024,128]{3,2,1,0:T(8,128)S(1)}, u32[]{:S(2)}) copy-start(f32[2,2,1024,128]{3,2,1,0:T(8,128)S(1)} %fusion.3) | copy-start | bytes 6291460
  8.7 4.3 %copy-start.11 = (bf16[4,1,1024,256]{3,2,1,0:T(8,128)(2,1)S(1)}, bf16[4,1,1024,256]{3,2,1,0:T(8,128)(2,1)}, u32[]{:S(2)}) copy-start(bf16[4,1,1024,256]{3,2,1,0:T(8,128)(2,1)} %get-tuple-element.29) | copy-start | bytes 6291460
  9.9 13.4 %collective-permute-start = (f32[2,1024,128]{2,1,0:T(8,128)}, f32[2,1024,128]{2,1,0:T(8,128)}, u32[]{:S(2)}, u32[]{:S(2)}) collective-permute-start(f32[2,1024,128]{2,1,0:T(8,128)} %select_bitcast_fusion.9), channel_id=1, source_target_pairs={{0,1},{1,0},{2,3},{3,2},{4,5},{5,4},{6,7},{7,6},{8,9},{9,8},{10,11... | collective-permute-start | bytes 3145736 | tf_op jit(solution)/shard_map/ppermute | solution.py:44
  10.4 9.0 %collective-permute-start.1 = (f32[1,8,4112]{2,1,0:T(8,128)S(1)}, f32[1,8,4112]{2,1,0:T(8,128)S(1)}, u32[]{:S(2)}, u32[]{:S(2)}) collective-permute-start(f32[1,8,4112]{2,1,0:T(8,128)S(1)} %maximum_bitcast_fusion.3), channel_id=1, source_target_pairs={{0,2},{1,3},{2,0},{3,1},{4,6},{5,7},{6,4},{7,5},{8,10},{9,11},{10,... | collective-permute-start | bytes 394760 | tf_op jit(solution)/shard_map/ppermute | solution.py:44
  15.0 12.7 %collective-permute-start.10 = (f32[2,1024,128]{2,1,0:T(8,128)}, f32[2,1024,128]{2,1,0:T(8,128)}, u32[]{:S(2)}, u32[]{:S(2)}) collective-permute-start(f32[2,1024,128]{2,1,0:T(8,128)} %select_bitcast_fusion.6), channel_id=1, source_target_pairs={{0,1},{1,0},{2,3},{3,2},{4,5},{5,4},{6,7},{7,6},{8,9},{9,8},{10,11... | collective-permute-start | bytes 3145736 | tf_op jit(solution)/shard_map/ppermute | solution.py:44
  17.0 13.6 %collective-permute-start.8 = (f32[2,1024,128]{2,1,0:T(8,128)}, f32[2,1024,128]{2,1,0:T(8,128)}, u32[]{:S(2)}, u32[]{:S(2)}) collective-permute-start(f32[2,1024,128]{2,1,0:T(8,128)} %select_bitcast_fusion.7), channel_id=1, source_target_pairs={{0,1},{1,0},{2,3},{3,2},{4,5},{5,4},{6,7},{7,6},{8,9},{9,8},{10,11... | collective-permute-start | bytes 3145736 | tf_op jit(solution)/shard_map/ppermute | solution.py:44
  20.2 1.9 collective-permute-start.2
  21.5 11.4 %collective-permute-start.6 = (f32[2,1024,128]{2,1,0:T(8,128)}, f32[2,1024,128]{2,1,0:T(8,128)S(1)}, u32[]{:S(2)}, u32[]{:S(2)}) collective-permute-start(f32[2,1024,128]{2,1,0:T(8,128)} %select_bitcast_fusion.8), channel_id=1, source_target_pairs={{0,1},{1,0},{2,3},{3,2},{4,5},{5,4},{6,7},{7,6},{8,9},{9,8},{10,11... | collective-permute-start | bytes 3145736 | tf_op jit(solution)/shard_map/ppermute | solution.py:44
  23.3 4.5 %copy-start.8 = (f32[2,2,1024,128]{3,2,0,1:T(8,128)S(1)}, f32[2,2,1024,128]{3,2,0,1:T(8,128)}, u32[]{:S(2)}) copy-start(f32[2,2,1024,128]{3,2,0,1:T(8,128)} %copy-done.7) | copy-start | bytes 6291460
  25.1 5.6 %copy-start.4 = (f32[2,2,1024,128]{3,2,0,1:T(8,128)S(1)}, f32[2,2,1024,128]{3,2,0,1:T(8,128)}, u32[]{:S(2)}) copy-start(f32[2,2,1024,128]{3,2,0,1:T(8,128)} %copy-done.3) | copy-start | bytes 6291460
  25.1 41.6 %collective-permute-start.3 = (f32[1,32,4112]{2,1,0:T(8,128)S(1)}, f32[1,32,4112]{2,1,0:T(8,128)S(1)}, u32[]{:S(2)}, u32[]{:S(2)}) collective-permute-start(f32[1,32,4112]{2,1,0:T(8,128)S(1)} %bitcast.283), channel_id=1, source_target_pairs={{0,8},{4,12},{8,0},{12,4},{1,9},{5,13},{9,1},{13,5},{2,10},{6,14},... | collective-permute-start | bytes 1579016 | tf_op jit(solution)/shard_map/ppermute | solution.py:44
  29.3 14.9 %collective-permute-start.11 = (f32[1,1024,128]{2,1,0:T(8,128)S(1)}, f32[1,1024,128]{2,1,0:T(8,128)S(1)}, u32[]{:S(2)}, u32[]{:S(2)}) collective-permute-start(f32[1,1024,128]{2,1,0:T(8,128)S(1)} %select_bitcast_fusion.12), channel_id=1, source_target_pairs={{0,2},{1,3},{2,0},{3,1},{4,6},{5,7},{6,4},{7,5},{8,10},{9,11},{10,... | collective-permute-start | bytes 1572872 | tf_op jit(solution)/shard_map/ppermute | solution.py:44
  32.2 23.2 %collective-permute-start.9 = (f32[1,1024,128]{2,1,0:T(8,128)S(1)}, f32[1,1024,128]{2,1,0:T(8,128)S(1)}, u32[]{:S(2)}, u32[]{:S(2)}) collective-permute-start(f32[1,1024,128]{2,1,0:T(8,128)S(1)} %select_bitcast_fusion.13), channel_id=1, source_target_pairs={{0,2},{1,3},{2,0},{3,1},{4,6},{5,7},{6,4},{7,5},{8,10},{9,11},{10,... | collective-permute-start | bytes 1572872 | tf_op jit(solution)/shard_map/ppermute | solution.py:44
  33.2 33.4 %collective-permute-start.7 = (f32[1,1024,128]{2,1,0:T(8,128)S(1)}, f32[1,1024,128]{2,1,0:T(8,128)S(1)}, u32[]{:S(2)}, u32[]{:S(2)}) collective-permute-start(f32[1,1024,128]{2,1,0:T(8,128)S(1)} %select_bitcast_fusion.14), channel_id=1, source_target_pairs={{0,2},{1,3},{2,0},{3,1},{4,6},{5,7},{6,4},{7,5},{8,10},{9,11},{10,... | collective-permute-start | bytes 1572872 | tf_op jit(solution)/shard_map/ppermute | solution.py:44
  34.6 42.3 %collective-permute-start.5 = (f32[1,1024,128]{2,1,0:T(8,128)S(1)}, f32[1,1024,128]{2,1,0:T(8,128)S(1)}, u32[]{:S(2)}, u32[]{:S(2)}) collective-permute-start(f32[1,1024,128]{2,1,0:T(8,128)S(1)} %select_bitcast_fusion.15), channel_id=1, source_target_pairs={{0,2},{1,3},{2,0},{3,1},{4,6},{5,7},{6,4},{7,5},{8,10},{9,11},{10,... | collective-permute-start | bytes 1572872 | tf_op jit(solution)/shard_map/ppermute | solution.py:44
  66.8 10.1 %copy-start.13 = (f32[1,1,32,4112]{3,2,1,0:T(8,128)}, f32[1,1,32,4112]{3,2,1,0:T(8,128)S(1)}, u32[]{:S(2)}) copy-start(f32[1,1,32,4112]{3,2,1,0:T(8,128)S(1)} %get-tuple-element.38) | copy-start | bytes 1579012
  66.8 10.1 %copy-start.14 = (f32[1,1,32,4112]{3,2,1,0:T(8,128)}, f32[1,1,32,4112]{3,2,1,0:T(8,128)S(1)}, u32[]{:S(2)}) copy-start(f32[1,1,32,4112]{3,2,1,0:T(8,128)S(1)} %get-tuple-element.39) | copy-start | bytes 1579012
  67.9 24.3 %collective-permute-start.4 = (f32[2,32,4112]{2,1,0:T(8,128)}, f32[2,32,4112]{2,1,0:T(8,128)}, u32[]{:S(2)}, u32[]{:S(2)}) collective-permute-start(f32[2,32,4112]{2,1,0:T(8,128)} %maximum_bitcast_fusion.1), channel_id=1, source_target_pairs={{0,4},{4,0},{8,12},{12,8},{1,5},{5,1},{9,13},{13,9},{2,6},{6,2},{1... | collective-permute-start | bytes 3158024 | tf_op jit(solution)/shard_map/ppermute | solution.py:44
  120.8 2.4 %collective-permute-start.14 = (f32[16,128]{1,0:T(8,128)S(1)}, f32[16,128]{1,0:T(8,128)S(1)}, u32[]{:S(2)}, u32[]{:S(2)}) collective-permute-start(f32[16,128]{1,0:T(8,128)S(1)} %select_reduce_fusion.1), channel_id=1, source_target_pairs={{0,3},{1,0},{2,1},{3,2},{4,7},{5,4},{6,5},{7,6},{8,11},{9,8},{10,9... | collective-permute-start | bytes 24584 | tf_op jit(solution)/shard_map/ppermute | solution.py:98
  120.9 3.7 %collective-permute-start.13 = (f32[16,128]{1,0:T(8,128)S(1)}, f32[16,128]{1,0:T(8,128)S(1)}, u32[]{:S(2)}, u32[]{:S(2)}) collective-permute-start(f32[16,128]{1,0:T(8,128)S(1)} %select_reduce_fusion.1), channel_id=1, source_target_pairs={{0,2},{1,3},{2,0},{3,1},{4,6},{5,7},{6,4},{7,5},{8,10},{9,11},{10,... | collective-permute-start | bytes 24584 | tf_op jit(solution)/shard_map/ppermute | solution.py:98
  122.6 3.1 %collective-permute-start.12 = (f32[16,128]{1,0:T(8,128)S(1)}, f32[16,128]{1,0:T(8,128)S(1)}, u32[]{:S(2)}, u32[]{:S(2)}) collective-permute-start(f32[16,128]{1,0:T(8,128)S(1)} %select_reduce_fusion.1), channel_id=1, source_target_pairs={{0,1},{1,2},{2,3},{3,0},{4,5},{5,6},{6,7},{7,4},{8,9},{9,10},{10,1... | collective-permute-start | bytes 24584 | tf_op jit(solution)/shard_map/ppermute | solution.py:98
  125.7 3.7 %collective-permute-start.17 = (f32[16,128]{1,0:T(8,128)S(1)}, f32[16,128]{1,0:T(8,128)S(1)}, u32[]{:S(2)}, u32[]{:S(2)}) collective-permute-start(f32[16,128]{1,0:T(8,128)S(1)} %fusion.63), channel_id=1, source_target_pairs={{0,12},{4,0},{8,4},{12,8},{1,13},{5,1},{9,5},{13,9},{2,14},{6,2},{... | collective-permute-start | bytes 24584 | tf_op jit(solution)/shard_map/ppermute | solution.py:98
  127.1 4.6 %collective-permute-start.16 = (f32[16,128]{1,0:T(8,128)S(1)}, f32[16,128]{1,0:T(8,128)S(1)}, u32[]{:S(2)}, u32[]{:S(2)}) collective-permute-start(f32[16,128]{1,0:T(8,128)S(1)} %fusion.63), channel_id=1, source_target_pairs={{0,8},{4,12},{8,0},{12,4},{1,9},{5,13},{9,1},{13,5},{2,10},{6,14},... | collective-permute-start | bytes 24584 | tf_op jit(solution)/shard_map/ppermute | solution.py:98
  128.7 5.4 %collective-permute-start.15 = (f32[16,128]{1,0:T(8,128)S(1)}, f32[16,128]{1,0:T(8,128)S(1)}, u32[]{:S(2)}, u32[]{:S(2)}) collective-permute-start(f32[16,128]{1,0:T(8,128)S(1)} %fusion.63), channel_id=1, source_target_pairs={{0,4},{4,8},{8,12},{12,0},{1,5},{5,9},{9,13},{13,1},{2,6},{6,10},{... | collective-permute-start | bytes 24584 | tf_op jit(solution)/shard_map/ppermute | solution.py:98
  153.6 21.8 %collective-permute-start.18 = (bf16[1,4096,128]{2,1,0:T(8,128)(2,1)S(1)}, bf16[1,4096,128]{2,1,0:T(8,128)(2,1)S(1)}, u32[]{:S(2)}, u32[]{:S(2)}) collective-permute-start(bf16[1,4096,128]{2,1,0:T(8,128)(2,1)S(1)} %fusion.7), channel_id=1, source_target_pairs={{0,2},{1,3},{2,0},{3,1},{4,6},{5,7},{6,4},{7,5},{8,10},{9,11},{10,... | collective-permute-start | bytes 3145736 | tf_op jit(solution)/shard_map/ppermute | solution.py:44
  177.1 4.5 %collective-permute-start.19 = (bf16[2,4096,128]{2,1,0:T(8,128)(2,1)}, bf16[2,4096,128]{2,1,0:T(8,128)(2,1)}, u32[]{:S(2)}, u32[]{:S(2)}) collective-permute-start(bf16[2,4096,128]{2,1,0:T(8,128)(2,1)} %maximum_bitcast_fusion), channel_id=1, source_target_pairs={{0,1},{1,0},{2,3},{3,2},{4,5},{5,4},{6,7},{7,6},{8,9},{9,8},{10,11... | collective-permute-start | bytes 6291464 | tf_op jit(solution)/shard_map/ppermute | solution.py:44
  183.8 3.2 %slice-start.1 = ((s8[8388608]{0:T(1024)(128)(4,1)}), s8[4194304]{0:T(1024)(128)(4,1)S(1)}, s32[]{:S(2)}) async-start(s8[8388608]{0:T(1024)(128)(4,1)} %bitcast.266), calls=%async_computation.1 | async-start | bytes 8388608
  187.0 14.6 %copy-start.1 = (bf16[256,128]{1,0:T(8,128)(2,1)S(1)}, bf16[256,128]{1,0:T(8,128)(2,1)}, u32[]{:S(2)}) copy-start(bf16[256,128]{1,0:T(8,128)(2,1)} %param.6) | copy-start | bytes 196612
  188.6 6.8 %collective-permute-start.22 = (f32[256,128]{0,1:T(8,128)S(1)}, f32[256,128]{0,1:T(8,128)S(1)}, u32[]{:S(2)}, u32[]{:S(2)}) collective-permute-start(f32[256,128]{0,1:T(8,128)S(1)} %bitcast.287), channel_id=1, source_target_pairs={{0,12},{4,0},{8,4},{12,8},{1,13},{5,1},{9,5},{13,9},{2,14},{6,2},{... | collective-permute-start | bytes 393224 | tf_op jit(solution)/shard_map/ppermute | solution.py:98
  188.6 12.1 %collective-permute-start.21 = (f32[256,128]{0,1:T(8,128)S(1)}, f32[256,128]{0,1:T(8,128)S(1)}, u32[]{:S(2)}, u32[]{:S(2)}) collective-permute-start(f32[256,128]{0,1:T(8,128)S(1)} %bitcast.288), channel_id=1, source_target_pairs={{0,8},{4,12},{8,0},{12,4},{1,9},{5,13},{9,1},{13,5},{2,10},{6,14},... | collective-permute-start | bytes 393224 | tf_op jit(solution)/shard_map/ppermute | solution.py:98
  188.7 12.1 %collective-permute-start.20 = (f32[256,128]{0,1:T(8,128)S(1)}, f32[256,128]{0,1:T(8,128)S(1)}, u32[]{:S(2)}, u32[]{:S(2)}) collective-permute-start(f32[256,128]{0,1:T(8,128)S(1)} %bitcast.289), channel_id=1, source_target_pairs={{0,4},{4,8},{8,12},{12,0},{1,5},{5,9},{9,13},{13,1},{2,6},{6,10},{... | collective-permute-start | bytes 393224 | tf_op jit(solution)/shard_map/ppermute | solution.py:98
  (10 other events, 20.7 us)

commit v9 on v8

--- a/solution.py
+++ b/solution.py
@@ -83,6 +83,26 @@
     return arr.reshape((-1,) + value.shape[1:])
 
 
+def all_gather_many(values, axis):
+    count = lax.axis_size(axis)
+    if not is_pow2(count):
+        return [lax.all_gather(v, axis, axis=0, tiled=True) for v in values]
+    me = lax.axis_index(axis)
+    arrs = [v[None] for v in values]
+    bit = count // 2
+    while bit >= 1:
+        low = (me // bit) % 2 == 0
+        others = lax.ppermute(arrs, axis, [(i, i ^ bit) for i in range(count)])
+        arrs = [
+            jnp.stack([jnp.where(low, a, o), jnp.where(low, o, a)], axis=1).reshape(
+                (-1,) + v.shape
+            )
+            for a, o, v in zip(arrs, others, values)
+        ]
+        bit //= 2
+    return [a.reshape((-1,) + v.shape[1:]) for a, v in zip(arrs, values)]
+
+
 def all_sum(value, axis):
     count = lax.axis_size(axis)
     if count > 4:
@@ -122,14 +142,8 @@
     capacity = 2 * slot_count // owners
     me = lax.axis_index("enc") * mp_count + lax.axis_index("mp")
 
-    packed = jnp.concatenate(
-        [
-            queries.reshape(qry_dev, query_len * emb_width).astype(jnp.float32),
-            candidates.astype(jnp.float32),
-        ],
-        axis=1,
-    )
-    packed = all_gather_rows(packed, "mp")
+    all_queries, all_cand = all_gather_many(all_gather_many([queries, candidates], "mp"), "enc")
+    all_cand = all_cand.reshape(owners, slot_count)
 
     chunks = 4 if row_share % (4 * BLK) == 0 else 1
     split_rows = hidden.reshape(mp_count, chunks, row_share // chunks, hidden.shape[1])
@@ -141,8 +155,7 @@
     ]
     if is_pow2(mp_count) and mp_count > 1:
         keeps, sends, bit = halving_steps(partials, "mp")
-        first, packed = lax.optimization_barrier((sends[0], packed))
-        sends = [first] + sends[1:]
+        sends, all_queries, all_cand = lax.optimization_barrier((sends, all_queries, all_cand))
         pieces = [k + xor_perm(t, "mp", bit) for k, t in zip(keeps, sends)]
         pieces = [p.reshape(-1, emb_width) for p in pieces]
     else:
@@ -150,14 +163,6 @@
             lax.psum_scatter(p, "mp", scatter_dimension=0, tiled=True) for p in partials
         ]
     e_pre = jnp.stack(pieces).reshape(row_share, emb_width)
-
-    packed = all_gather_rows(packed, "enc")
-    all_queries = (
-        packed[:, : query_len * emb_width]
-        .astype(jnp.bfloat16)
-        .reshape(owners * qry_dev, query_len, emb_width)
-    )
-    all_cand = packed[:, query_len * emb_width :].astype(jnp.int32).reshape(owners, slot_count)
 
     slot_ids = jnp.arange(slot_count, dtype=jnp.int32)
     mine = (all_cand // blk_dev) == me

time: 202 us -> 219 us (1.084)
  waiting for transfers between devices: 95.7 us -> 105 us
  other arithmetic: 26.3 us -> 31.6 us
  starting transfers between devices: 20.2 us -> 24.8 us
  local copies, waits for them, and re-layouts: 35.2 us -> 31.9 us
    ppermute x0 -> x8, waiting for transfers between devices: none -> 25.5 us  [all_gather_many(): others = lax.ppermute(arrs, axis, [(i, i ^ bit) for i in range(count)])]
    ppermute x14 -> x10, waiting for transfers between devices: 78.3 us -> 61.9 us  [xor_perm(): return lax.ppermute(value, axis, [(i, i ^ bit) for i in range(count)])]
    ppermute x0 -> x8, starting transfers between devices: none -> 8.54 us  [all_gather_many(): others = lax.ppermute(arrs, axis, [(i, i ^ bit) for i in range(count)])]
    ppermute x14 -> x10, starting transfers between devices: 13.1 us -> 6.81 us  [xor_perm(): return lax.ppermute(value, axis, [(i, i ^ bit) for i in range(count)])]
    add x4, other arithmetic: 0.31 us -> 4.79 us  [local(): pieces = [k + xor_perm(t, 'mp', bit) for k, t in zip(keeps, sends)]]
    select_n x8, other arithmetic: 4.75 us -> 8.15 us  [halving_steps(): sends.append(jnp.where(low, acc[:, 1], acc[:, 0]))]
    unnamed x44 -> x47, local copies, waits for them, and re-layouts: 11.9 us -> 8.55 us
    another operation x9 -> x3, other arithmetic: 5.5 us -> 2.39 us  [all_gather_rows(): arr = jnp.stack([first, second], axis=1).reshape((-1,) + value.shape)]
  transfers between devices with their start and end apart: 23 -> 27, of which waited for: 15 -> 17; matrix products, arithmetic and copies ran while one was open for 8% -> 12% of each run, Pallas kernels for 0% -> 0%
where the time goes in v9:
time: 219 us
  waiting for transfers between devices  105 us (48%)
  local copies, waits for them, and re-layouts  31.9 us (15%)
  other arithmetic  31.6 us (14%)
  starting transfers between devices  24.8 us (11%)
  matrix products  24.6 us (11%)
    ppermute x10, waiting for transfers between devices, xor_perm(): return lax.ppermute(value, axis, [(i, i ^ bit) for i in range(count)])  61.9 us
    ppermute x8, waiting for transfers between devices, all_gather_many(): others = lax.ppermute(arrs, axis, [(i, i ^ bit) for i in range(count)])  25.5 us
    ppermute x9, waiting for transfers between devices, all_sum(): lax.ppermute(value, axis, [(i, (i + k) % count) for i in range(count)])  17.2 us
    ppermute x9, starting transfers between devices, all_sum(): lax.ppermute(value, axis, [(i, (i + k) % count) for i in range(count)])  9.45 us
    unnamed x47, local copies, waits for them, and re-layouts  8.55 us
    ppermute x8, starting transfers between devices, all_gather_many(): others = lax.ppermute(arrs, axis, [(i, i ^ bit) for i in range(count)])  8.54 us
    select_n x8, other arithmetic, halving_steps(): sends.append(jnp.where(low, acc[:, 1], acc[:, 0]))  8.15 us
    dot_general x1, matrix products, local(): jnp.einsum('scij,scie->scje', weights, q_e, preferred_element_type=jnp.fl...  6.94 us
  transfers between devices with their start and end apart: 27, of which 17 were waited for; matrix products, arithmetic and copies ran while one was open for 12% of the time, Pallas kernels for 0%

profile of v9, /device:TPU:0, one launch (start us, length us, event | category | flops | bytes accessed | tf_op | source)
XLA Modules:
  0.0 218.7 jit_solution(13508221091836080973)
XLA Ops:
  0.7 6.0 %fusion.55 = (bf16[4,1,1024,256]{3,2,1,0:T(8,128)(2,1)}, bf16[4,1,1024,256]{3,2,1,0:T(8,128)(2,1)}, bf16[4,1,1024,256]{3,2,1,0:T(8,128)(2,1)}, bf16[4,1,1024,256]{3,2,1,0:T(8,128)(2,1)}) fusion(bf16[4,4,1024,256]{3,2,1,0:T(8,128)(2,1)} %bitcast.285), kind=kLoop, calls=%fused_computation.172 | loop fusion | bytes 16777216 | tf_op jit(solution)/shard_map/slice | solution.py:151
  6.7 2.3 %fusion.3 = f32[2,2,1024,128]{3,2,1,0:T(8,128)S(1)} fusion(bf16[256,128]{1,0:T(8,128)(2,1)S(1)} %copy-done, bf16[2,2,1024,256]{3,2,1,0:T(8,128)(2,1)} %bitcast.300), kind=kOutput, calls=%fused_computation.15 | convolution fusion | flops 268435456 | bytes 4259840 | tf_op jit(solution)/shard_map/dot_general | solution.py:151
  17.5 2.5 %collective-permute-start.4 = (bf16[1,8,32,128]{3,2,1,0:T(8,128)(2,1)S(1)}, bf16[1,8,32,128]{3,2,1,0:T(8,128)(2,1)S(1)}, u32[]{:S(2)}, u32[]{:S(2)}) collective-permute-start(bf16[1,8,32,128]{3,2,1,0:T(8,128)(2,1)S(1)} %bitcast.313), channel_id=1, source_target_pairs={{0,2},{1,3},{2,0},{3,1},{4,6},{5,7},{6,4},{7,5},{8,10},{9,11},{10,... | collective-permute-start | bytes 196616 | tf_op jit(solution)/shard_map/ppermute | solution.py:95
  20.0 2.3 %fusion.8 = f32[2,2,1024,128]{3,2,0,1:T(8,128)S(1)} fusion(bf16[256,128]{1,0:T(8,128)(2,1)S(1)} %copy-done, bf16[2,2,1024,256]{3,2,1,0:T(8,128)(2,1)} %bitcast.297), kind=kOutput, calls=%fused_computation.22 | convolution fusion | flops 268435456 | bytes 4259840 | tf_op jit(solution)/shard_map/dot_general | solution.py:151
  26.4 3.1 %collective-permute-start.6 = (bf16[1,32,32,128]{3,2,1,0:T(8,128)(2,1)S(1)}, bf16[1,32,32,128]{3,2,1,0:T(8,128)(2,1)S(1)}, u32[]{:S(2)}, u32[]{:S(2)}) collective-permute-start(bf16[1,32,32,128]{3,2,1,0:T(8,128)(2,1)S(1)} %bitcast.301), channel_id=1, source_target_pairs={{0,8},{4,12},{8,0},{12,4},{1,9},{5,13},{9,1},{13,5},{2,10},{6,14},... | collective-permute-start | bytes 786440 | tf_op jit(solution)/shard_map/ppermute | solution.py:95
  29.6 12.6 %collective-permute-done.6 = bf16[1,32,32,128]{3,2,1,0:T(8,128)(2,1)S(1)} collective-permute-done((bf16[1,32,32,128]{3,2,1,0:T(8,128)(2,1)S(1)}, bf16[1,32,32,128]{3,2,1,0:T(8,128)(2,1)S(1)}, u32[]{:S(2)}, u32[]{:S(2)}) %collective-permute-start.6) | collective-permute-done | bytes 262176 | tf_op jit(solution)/shard_map/ppermute | solution.py:95
  45.3 12.1 %collective-permute-done.11 = s32[2,32,16]{2,1,0:T(8,128)S(1)} collective-permute-done((s32[2,32,16]{2,1,0:T(8,128)S(1)}, s32[2,32,16]{2,1,0:T(8,128)S(1)}, u32[]{:S(2)}, u32[]{:S(2)}) %collective-permute-start.11) | collective-permute-done | bytes 4128 | tf_op jit(solution)/shard_map/ppermute | solution.py:95
  70.2 1.9 gather_fusion.3
  77.2 1.9 gather_fusion
  79.4 2.2 %gather_fusion.1 = bf16[256,32,128]{2,1,0:T(8,128)(2,1)} fusion(bf16[128,32,128]{2,1,0:T(8,128)(2,1)S(1)} %bitcast.293, s32[1024]{0:T(1024)S(1)} %pad_clamp_fusion.1), kind=kCustom, calls=%fused_computation.1 | custom fusion | bytes 4195328 | tf_op jit(solution)/shard_map/gather | solution.py:178
  81.8 6.3 %collective-permute-done.15 = f32[1,1024,128]{2,1,0:T(8,128)} collective-permute-done((f32[1,1024,128]{2,1,0:T(8,128)}, f32[1,1024,128]{2,1,0:T(8,128)}, u32[]{:S(2)}, u32[]{:S(2)}) %collective-permute-start.15) | collective-permute-done | bytes 524320 | tf_op jit(solution)/shard_map/ppermute | solution.py:44
  89.5 9.8 %collective-permute-done.14 = f32[1,1024,128]{2,1,0:T(8,128)} collective-permute-done((f32[1,1024,128]{2,1,0:T(8,128)}, f32[1,1024,128]{2,1,0:T(8,128)}, u32[]{:S(2)}, u32[]{:S(2)}) %collective-permute-start.14) | collective-permute-done | bytes 524320 | tf_op jit(solution)/shard_map/ppermute | solution.py:44
  100.4 10.1 %collective-permute-done.13 = f32[1,1024,128]{2,1,0:T(8,128)} collective-permute-done((f32[1,1024,128]{2,1,0:T(8,128)}, f32[1,1024,128]{2,1,0:T(8,128)}, u32[]{:S(2)}, u32[]{:S(2)}) %collective-permute-start.13) | collective-permute-done | bytes 524320 | tf_op jit(solution)/shard_map/ppermute | solution.py:44
  111.6 9.7 %collective-permute-done.12 = f32[1,1024,128]{2,1,0:T(8,128)} collective-permute-done((f32[1,1024,128]{2,1,0:T(8,128)}, f32[1,1024,128]{2,1,0:T(8,128)}, u32[]{:S(2)}, u32[]{:S(2)}) %collective-permute-start.12) | collective-permute-done | bytes 524320 | tf_op jit(solution)/shard_map/ppermute | solution.py:44
  123.9 3.1 %gather_fusion.2 = bf16[256,64,128]{2,1,0:T(8,128)(2,1)} fusion(bf16[64,64,128]{2,1,0:T(8,128)(2,1)S(1)} %multiply_convert_fusion.1, s32[1024]{0:T(1024)S(1)} %pad_clamp_fusion), kind=kCustom, calls=%fused_computation.2 | custom fusion | bytes 8389632 | tf_op jit(solution)/shard_map/gather | solution.py:185
  127.0 5.2 %select_reduce_fusion = (f32[16,16,32]{2,1,0:T(8,128)S(1)}, f32[16,16,32,64]{3,2,1,0:T(8,128)S(1)}) fusion(pred[16,16,64]{2,1,0:T(8,128)(4,1)S(1)} %add_compare_fusion, bf16[16,16,32,128]{3,2,1,0:T(8,128)(2,1)} %bitcast.295, bf16[16,16,64,128]{3,2,1,0:T(8,128)(2,1)} %bitcast.292), kind=kOutput, calls=%fused_computation.11 | convolution fusion | flops 135258112 | bytes 8437760 | tf_op jit(solution)/shard_map/scie,scje->scij/dot_general | solution.py:187
  132.2 2.6 %fusion.2 = f32[16,16,32]{2,1,0:T(8,128)S(1)} fusion(f32[16,16,32,64]{3,2,1,0:T(8,128)S(1)} %get-tuple-element.67, f32[16,16,32]{2,1,0:T(8,128)S(1)} %get-tuple-element.66, pred[16,16,64]{2,1,0:T(8,128)(4,1)S(1)} %add_compare_fusion), kind=kLoop, calls=%fused_computation.12 | loop fusion | flops 1564672 | bytes 2179072 | tf_op jit(solution)/shard_map/reduce_sum | solution.py:22
  137.0 2.3 %collective-permute-done.17 = f32[16,128]{1,0:T(8,128)S(1)} collective-permute-done((f32[16,128]{1,0:T(8,128)S(1)}, f32[16,128]{1,0:T(8,128)S(1)}, u32[]{:S(2)}, u32[]{:S(2)}) %collective-permute-start.17) | collective-permute-done | bytes 8224 | tf_op jit(solution)/shard_map/ppermute | solution.py:118
  139.6 4.2 %collective-permute-start.21 = (f32[16,128]{1,0:T(8,128)S(1)}, f32[16,128]{1,0:T(8,128)S(1)}, u32[]{:S(2)}, u32[]{:S(2)}) collective-permute-start(f32[16,128]{1,0:T(8,128)S(1)} %fusion.62), channel_id=1, source_target_pairs={{0,12},{4,0},{8,4},{12,8},{1,13},{5,1},{9,5},{13,9},{2,14},{6,2},{... | collective-permute-start | bytes 24584 | tf_op jit(solution)/shard_map/ppermute | solution.py:118
  145.2 3.2 %collective-permute-done.20 = f32[16,128]{1,0:T(8,128)S(1)} collective-permute-done((f32[16,128]{1,0:T(8,128)S(1)}, f32[16,128]{1,0:T(8,128)S(1)}, u32[]{:S(2)}, u32[]{:S(2)}) %collective-permute-start.20) | collective-permute-done | bytes 8224 | tf_op jit(solution)/shard_map/ppermute | solution.py:118
  149.9 1.9 gather_fusion.4
  151.9 6.9 %multiply_convert_fusion = bf16[16,16,64,128]{3,2,1,0:T(8,128)(2,1)S(1)} fusion(f32[16,16]{1,0:T(8,128)S(1)} %select_multiply_fusion, bf16[16,16,32,128]{3,2,1,0:T(8,128)(2,1)} %bitcast.296, f32[16,16,32,64]{3,2,1,0:T(8,128)} %copy-done.9, f32[16,16,32]{2,1,0:T(8,128)S(1)} %fusion.2, f32[16,16,32]{2,1,0:T(8,128)S(1)} %get-tuple-element.66, ...), kind=kOutput, calls=%fused_computation.5 | convolution fusion | flops 140509184 | bytes 8471552 | tf_op jit(solution)/shard_map/scij,scie->scje/dot_general | solution.py:190
  158.8 5.0 %fusion.14 = (f32[64,64]{0,1:T(8,128)S(1)}, f32[64,64,128]{2,0,1:T(8,128)}) fusion(f32[64,64,128]{2,1,0:T(8,128)S(1)} %bitcast.289, bf16[16,16,64,128]{3,2,1,0:T(8,128)(2,1)S(1)} %multiply_convert_fusion, s32[16,16]{0,1:T(8,128)S(1)} %copy.179, pred[16,16]{0,1:T(8,128)(4,1)S(1)} %copy.180), kind=kOutput, calls=%fused_computation.29 | convolution fusion | flops 269512704 | bytes 8406272 | tf_op jit(solution)/shard_map/scb,scje->bje/dot_general | solution.py:201
  163.9 2.8 %copy.183 = f32[64,64,128]{2,1,0:T(8,128)S(1)} copy(f32[64,64,128]{2,0,1:T(8,128)} %get-tuple-element.69) | data formatting | bytes 4194304 | tf_op jit(solution)/shard_map/scb,scje->bje/dot_general | solution.py:201
  166.8 1.9 fusion.7
  170.1 21.5 %collective-permute-done.22 = bf16[1,4096,128]{2,1,0:T(8,128)(2,1)S(1)} collective-permute-done((bf16[1,4096,128]{2,1,0:T(8,128)(2,1)S(1)}, bf16[1,4096,128]{2,1,0:T(8,128)(2,1)S(1)}, u32[]{:S(2)}, u32[]{:S(2)}) %collective-permute-start.22) | collective-permute-done | bytes 1048608 | tf_op jit(solution)/shard_map/ppermute | solution.py:44
  191.7 1.5 maximum_bitcast_fusion
  193.2 4.5 %collective-permute-done.23 = bf16[2,4096,128]{2,1,0:T(8,128)(2,1)} collective-permute-done((bf16[2,4096,128]{2,1,0:T(8,128)(2,1)}, bf16[2,4096,128]{2,1,0:T(8,128)(2,1)}, u32[]{:S(2)}, u32[]{:S(2)}) %collective-permute-start.23) | collective-permute-done | bytes 2097184 | tf_op jit(solution)/shard_map/ppermute | solution.py:44
  197.7 1.9 select_bitcast_fusion.1
  205.7 1.9 collective-permute-start.24
  208.2 3.3 %collective-permute-done.26 = f32[256,128]{0,1:T(8,128)S(1)} collective-permute-done((f32[256,128]{0,1:T(8,128)S(1)}, f32[256,128]{0,1:T(8,128)S(1)}, u32[]{:S(2)}, u32[]{:S(2)}) %collective-permute-start.26) | collective-permute-done | bytes 131104 | tf_op jit(solution)/shard_map/ppermute | solution.py:118
  211.5 6.3 %collective-permute-done.25 = f32[256,128]{0,1:T(8,128)S(1)} collective-permute-done((f32[256,128]{0,1:T(8,128)S(1)}, f32[256,128]{0,1:T(8,128)S(1)}, u32[]{:S(2)}, u32[]{:S(2)}) %collective-permute-start.25) | collective-permute-done | bytes 131104 | tf_op jit(solution)/shard_map/ppermute | solution.py:118
  (180 shorter events, 54.5 us)
Async XLA Ops:
  0.6 6.0 %copy-start = (bf16[256,128]{1,0:T(8,128)(2,1)S(1)}, bf16[256,128]{1,0:T(8,128)(2,1)}, u32[]{:S(2)}) copy-start(bf16[256,128]{1,0:T(8,128)(2,1)} %param.6) | copy-start | bytes 196612
  10.1 48.6 %collective-permute-start = (f32[2,1024,128]{2,1,0:T(8,128)}, f32[2,1024,128]{2,1,0:T(8,128)}, u32[]{:S(2)}, u32[]{:S(2)}) collective-permute-start(f32[2,1024,128]{2,1,0:T(8,128)} %select_bitcast_fusion.7), channel_id=1, source_target_pairs={{0,1},{1,0},{2,3},{3,2},{4,5},{5,4},{6,7},{7,6},{8,9},{9,8},{10,11... | collective-permute-start | bytes 3145736 | tf_op jit(solution)/shard_map/ppermute | solution.py:44
  13.5 47.5 %collective-permute-start.1 = (f32[2,1024,128]{2,1,0:T(8,128)}, f32[2,1024,128]{2,1,0:T(8,128)}, u32[]{:S(2)}, u32[]{:S(2)}) collective-permute-start(f32[2,1024,128]{2,1,0:T(8,128)} %select_bitcast_fusion.6), channel_id=1, source_target_pairs={{0,1},{1,0},{2,3},{3,2},{4,5},{5,4},{6,7},{7,6},{8,9},{9,8},{10,11... | collective-permute-start | bytes 3145736 | tf_op jit(solution)/shard_map/ppermute | solution.py:44
  17.0 47.6 %collective-permute-start.2 = (f32[2,1024,128]{2,1,0:T(8,128)}, f32[2,1024,128]{2,1,0:T(8,128)}, u32[]{:S(2)}, u32[]{:S(2)}) collective-permute-start(f32[2,1024,128]{2,1,0:T(8,128)} %select_bitcast_fusion.5), channel_id=1, source_target_pairs={{0,1},{1,0},{2,3},{3,2},{4,5},{5,4},{6,7},{7,6},{8,9},{9,8},{10,11... | collective-permute-start | bytes 3145736 | tf_op jit(solution)/shard_map/ppermute | solution.py:44
  17.5 7.4 %collective-permute-start.4 = (bf16[1,8,32,128]{3,2,1,0:T(8,128)(2,1)S(1)}, bf16[1,8,32,128]{3,2,1,0:T(8,128)(2,1)S(1)}, u32[]{:S(2)}, u32[]{:S(2)}) collective-permute-start(bf16[1,8,32,128]{3,2,1,0:T(8,128)(2,1)S(1)} %bitcast.313), channel_id=1, source_target_pairs={{0,2},{1,3},{2,0},{3,1},{4,6},{5,7},{6,4},{7,5},{8,10},{9,11},{10,... | collective-permute-start | bytes 196616 | tf_op jit(solution)/shard_map/ppermute | solution.py:95
  20.0 5.2 %collective-permute-start.8 = (s32[1,8,16]{2,1,0:T(8,128)S(1)}, s32[1,8,16]{2,1,0:T(8,128)S(1)}, u32[]{:S(2)}, u32[]{:S(2)}) collective-permute-start(s32[1,8,16]{2,1,0:T(8,128)S(1)} %bitcast.321), channel_id=1, source_target_pairs={{0,2},{1,3},{2,0},{3,1},{4,6},{5,7},{6,4},{7,5},{8,10},{9,11},{10,... | collective-permute-start | bytes 1544 | tf_op jit(solution)/shard_map/ppermute | solution.py:95
  24.9 1.4 collective-permute-start.5
  25.2 4.3 %collective-permute-start.9 = (s32[2,8,16]{2,1,0:T(8,128)S(1)}, s32[2,8,16]{2,1,0:T(8,128)S(1)}, u32[]{:S(2)}, u32[]{:S(2)}) collective-permute-start(s32[2,8,16]{2,1,0:T(8,128)S(1)} %add_bitcast_fusion.2), channel_id=1, source_target_pairs={{0,1},{1,0},{2,3},{3,2},{4,5},{5,4},{6,7},{7,6},{8,9},{9,8},{10,11... | collective-permute-start | bytes 3080 | tf_op jit(solution)/shard_map/ppermute | solution.py:95
  26.4 15.9 %collective-permute-start.6 = (bf16[1,32,32,128]{3,2,1,0:T(8,128)(2,1)S(1)}, bf16[1,32,32,128]{3,2,1,0:T(8,128)(2,1)S(1)}, u32[]{:S(2)}, u32[]{:S(2)}) collective-permute-start(bf16[1,32,32,128]{3,2,1,0:T(8,128)(2,1)S(1)} %bitcast.301), channel_id=1, source_target_pairs={{0,8},{4,12},{8,0},{12,4},{1,9},{5,13},{9,1},{13,5},{2,10},{6,14},... | collective-permute-start | bytes 786440 | tf_op jit(solution)/shard_map/ppermute | solution.py:95
  29.6 14.2 %collective-permute-start.10 = (s32[1,32,16]{2,1,0:T(8,128)S(1)}, s32[1,32,16]{2,1,0:T(8,128)S(1)}, u32[]{:S(2)}, u32[]{:S(2)}) collective-permute-start(s32[1,32,16]{2,1,0:T(8,128)S(1)} %bitcast.311), channel_id=1, source_target_pairs={{0,8},{4,12},{8,0},{12,4},{1,9},{5,13},{9,1},{13,5},{2,10},{6,14},... | collective-permute-start | bytes 6152 | tf_op jit(solution)/shard_map/ppermute | solution.py:95
  43.2 14.3 %collective-permute-start.7 = (bf16[2,32,32,128]{3,2,1,0:T(8,128)(2,1)}, bf16[2,32,32,128]{3,2,1,0:T(8,128)(2,1)S(1)}, u32[]{:S(2)}, u32[]{:S(2)}) collective-permute-start(bf16[2,32,32,128]{3,2,1,0:T(8,128)(2,1)} %maximum_bitcast_fusion.1), channel_id=1, source_target_pairs={{0,4},{4,0},{8,12},{12,8},{1,5},{5,1},{9,13},{13,9},{2,6},{6,2},{1... | collective-permute-start | bytes 1572872 | tf_op jit(solution)/shard_map/ppermute | solution.py:95
  43.8 13.6 %collective-permute-start.11 = (s32[2,32,16]{2,1,0:T(8,128)S(1)}, s32[2,32,16]{2,1,0:T(8,128)S(1)}, u32[]{:S(2)}, u32[]{:S(2)}) collective-permute-start(s32[2,32,16]{2,1,0:T(8,128)S(1)} %add_bitcast_fusion.1), channel_id=1, source_target_pairs={{0,4},{4,0},{8,12},{12,8},{1,5},{5,1},{9,13},{13,9},{2,6},{6,2},{1... | collective-permute-start | bytes 12296 | tf_op jit(solution)/shard_map/ppermute | solution.py:95
  57.4 9.7 %collective-permute-start.3 = (f32[2,1024,128]{2,1,0:T(8,128)}, f32[2,1024,128]{2,1,0:T(8,128)}, u32[]{:S(2)}, u32[]{:S(2)}) collective-permute-start(f32[2,1024,128]{2,1,0:T(8,128)} %select_bitcast_fusion.4), channel_id=1, source_target_pairs={{0,1},{1,0},{2,3},{3,2},{4,5},{5,4},{6,7},{7,6},{8,9},{9,8},{10,11... | collective-permute-start | bytes 3145736 | tf_op jit(solution)/shard_map/ppermute | solution.py:44
  72.1 5.0 %copy-start.2 = (s32[256]{0:T(256)S(1)}, s32[256]{0:T(256)}, u32[]{:S(2)}) copy-start(s32[256]{0:T(256)} %param.8) | copy-start | bytes 3076
  73.0 15.1 %collective-permute-start.15 = (f32[1,1024,128]{2,1,0:T(8,128)}, f32[1,1024,128]{2,1,0:T(8,128)}, u32[]{:S(2)}, u32[]{:S(2)}) collective-permute-start(f32[1,1024,128]{2,1,0:T(8,128)} %select_bitcast_fusion.10), channel_id=1, source_target_pairs={{0,2},{1,3},{2,0},{3,1},{4,6},{5,7},{6,4},{7,5},{8,10},{9,11},{10,... | collective-permute-start | bytes 1572872 | tf_op jit(solution)/shard_map/ppermute | solution.py:44
  74.2 25.1 %collective-permute-start.14 = (f32[1,1024,128]{2,1,0:T(8,128)}, f32[1,1024,128]{2,1,0:T(8,128)}, u32[]{:S(2)}, u32[]{:S(2)}) collective-permute-start(f32[1,1024,128]{2,1,0:T(8,128)} %select_bitcast_fusion.11), channel_id=1, source_target_pairs={{0,2},{1,3},{2,0},{3,1},{4,6},{5,7},{6,4},{7,5},{8,10},{9,11},{10,... | collective-permute-start | bytes 1572872 | tf_op jit(solution)/shard_map/ppermute | solution.py:44
  75.0 35.5 %collective-permute-start.13 = (f32[1,1024,128]{2,1,0:T(8,128)}, f32[1,1024,128]{2,1,0:T(8,128)}, u32[]{:S(2)}, u32[]{:S(2)}) collective-permute-start(f32[1,1024,128]{2,1,0:T(8,128)} %select_bitcast_fusion.12), channel_id=1, source_target_pairs={{0,2},{1,3},{2,0},{3,1},{4,6},{5,7},{6,4},{7,5},{8,10},{9,11},{10,... | collective-permute-start | bytes 1572872 | tf_op jit(solution)/shard_map/ppermute | solution.py:44
  76.3 45.1 %collective-permute-start.12 = (f32[1,1024,128]{2,1,0:T(8,128)}, f32[1,1024,128]{2,1,0:T(8,128)}, u32[]{:S(2)}, u32[]{:S(2)}) collective-permute-start(f32[1,1024,128]{2,1,0:T(8,128)} %select_bitcast_fusion.13), channel_id=1, source_target_pairs={{0,2},{1,3},{2,0},{3,1},{4,6},{5,7},{6,4},{7,5},{8,10},{9,11},{10,... | collective-permute-start | bytes 1572872 | tf_op jit(solution)/shard_map/ppermute | solution.py:44
  81.6 17.7 %copy-start.13 = (f32[1,2,1024,128]{3,2,1,0:T(8,128)S(1)}, f32[1,2,1024,128]{3,2,1,0:T(8,128)}, u32[]{:S(2)}) copy-start(f32[1,2,1024,128]{3,2,1,0:T(8,128)} %copy-done.12) | copy-start | bytes 3145732
  81.8 28.8 %copy-start.11 = (f32[1,2,1024,128]{3,2,1,0:T(8,128)S(1)}, f32[1,2,1024,128]{3,2,1,0:T(8,128)}, u32[]{:S(2)}) copy-start(f32[1,2,1024,128]{3,2,1,0:T(8,128)} %copy-done.10) | copy-start | bytes 3145732
  135.1 2.0 collective-permute-start.18
  135.7 3.7 %collective-permute-start.17 = (f32[16,128]{1,0:T(8,128)S(1)}, f32[16,128]{1,0:T(8,128)S(1)}, u32[]{:S(2)}, u32[]{:S(2)}) collective-permute-start(f32[16,128]{1,0:T(8,128)S(1)} %select_reduce_fusion.1), channel_id=1, source_target_pairs={{0,2},{1,3},{2,0},{3,1},{4,6},{5,7},{6,4},{7,5},{8,10},{9,11},{10,... | collective-permute-start | bytes 24584 | tf_op jit(solution)/shard_map/ppermute | solution.py:118
  136.5 3.1 %collective-permute-start.16 = (f32[16,128]{1,0:T(8,128)S(1)}, f32[16,128]{1,0:T(8,128)S(1)}, u32[]{:S(2)}, u32[]{:S(2)}) collective-permute-start(f32[16,128]{1,0:T(8,128)S(1)} %select_reduce_fusion.1), channel_id=1, source_target_pairs={{0,1},{1,2},{2,3},{3,0},{4,5},{5,6},{6,7},{7,4},{8,9},{9,10},{10,1... | collective-permute-start | bytes 24584 | tf_op jit(solution)/shard_map/ppermute | solution.py:118
  139.6 5.6 %collective-permute-start.21 = (f32[16,128]{1,0:T(8,128)S(1)}, f32[16,128]{1,0:T(8,128)S(1)}, u32[]{:S(2)}, u32[]{:S(2)}) collective-permute-start(f32[16,128]{1,0:T(8,128)S(1)} %fusion.62), channel_id=1, source_target_pairs={{0,12},{4,0},{8,4},{12,8},{1,13},{5,1},{9,5},{13,9},{2,14},{6,2},{... | collective-permute-start | bytes 24584 | tf_op jit(solution)/shard_map/ppermute | solution.py:118
  143.8 4.5 %collective-permute-start.20 = (f32[16,128]{1,0:T(8,128)S(1)}, f32[16,128]{1,0:T(8,128)S(1)}, u32[]{:S(2)}, u32[]{:S(2)}) collective-permute-start(f32[16,128]{1,0:T(8,128)S(1)} %fusion.62), channel_id=1, source_target_pairs={{0,8},{4,12},{8,0},{12,4},{1,9},{5,13},{9,1},{13,5},{2,10},{6,14},... | collective-permute-start | bytes 24584 | tf_op jit(solution)/shard_map/ppermute | solution.py:118
  143.8 5.4 %collective-permute-start.19 = (f32[16,128]{1,0:T(8,128)S(1)}, f32[16,128]{1,0:T(8,128)S(1)}, u32[]{:S(2)}, u32[]{:S(2)}) collective-permute-start(f32[16,128]{1,0:T(8,128)S(1)} %fusion.62), channel_id=1, source_target_pairs={{0,4},{4,8},{8,12},{12,0},{1,5},{5,9},{9,13},{13,1},{2,6},{6,10},{... | collective-permute-start | bytes 24584 | tf_op jit(solution)/shard_map/ppermute | solution.py:118
  168.7 22.8 %collective-permute-start.22 = (bf16[1,4096,128]{2,1,0:T(8,128)(2,1)S(1)}, bf16[1,4096,128]{2,1,0:T(8,128)(2,1)S(1)}, u32[]{:S(2)}, u32[]{:S(2)}) collective-permute-start(bf16[1,4096,128]{2,1,0:T(8,128)(2,1)S(1)} %fusion.7), channel_id=1, source_target_pairs={{0,2},{1,3},{2,0},{3,1},{4,6},{5,7},{6,4},{7,5},{8,10},{9,11},{10,... | collective-permute-start | bytes 3145736 | tf_op jit(solution)/shard_map/ppermute | solution.py:44
  193.2 4.5 %collective-permute-start.23 = (bf16[2,4096,128]{2,1,0:T(8,128)(2,1)}, bf16[2,4096,128]{2,1,0:T(8,128)(2,1)}, u32[]{:S(2)}, u32[]{:S(2)}) collective-permute-start(bf16[2,4096,128]{2,1,0:T(8,128)(2,1)} %maximum_bitcast_fusion), channel_id=1, source_target_pairs={{0,1},{1,0},{2,3},{3,2},{4,5},{5,4},{6,7},{7,6},{8,9},{9,8},{10,11... | collective-permute-start | bytes 6291464 | tf_op jit(solution)/shard_map/ppermute | solution.py:44
  203.1 15.5 %copy-start.1 = (bf16[256,128]{1,0:T(8,128)(2,1)S(1)}, bf16[256,128]{1,0:T(8,128)(2,1)}, u32[]{:S(2)}) copy-start(bf16[256,128]{1,0:T(8,128)(2,1)} %param.6) | copy-start | bytes 196612
  204.7 6.8 %collective-permute-start.26 = (f32[256,128]{0,1:T(8,128)S(1)}, f32[256,128]{0,1:T(8,128)S(1)}, u32[]{:S(2)}, u32[]{:S(2)}) collective-permute-start(f32[256,128]{0,1:T(8,128)S(1)} %bitcast.303), channel_id=1, source_target_pairs={{0,12},{4,0},{8,4},{12,8},{1,13},{5,1},{9,5},{13,9},{2,14},{6,2},{... | collective-permute-start | bytes 393224 | tf_op jit(solution)/shard_map/ppermute | solution.py:118
  205.3 12.5 %collective-permute-start.25 = (f32[256,128]{0,1:T(8,128)S(1)}, f32[256,128]{0,1:T(8,128)S(1)}, u32[]{:S(2)}, u32[]{:S(2)}) collective-permute-start(f32[256,128]{0,1:T(8,128)S(1)} %bitcast.304), channel_id=1, source_target_pairs={{0,8},{4,12},{8,0},{12,4},{1,9},{5,13},{9,1},{13,5},{2,10},{6,14},... | collective-permute-start | bytes 393224 | tf_op jit(solution)/shard_map/ppermute | solution.py:118
  205.7 12.1 %collective-permute-start.24 = (f32[256,128]{0,1:T(8,128)S(1)}, f32[256,128]{0,1:T(8,128)S(1)}, u32[]{:S(2)}, u32[]{:S(2)}) collective-permute-start(f32[256,128]{0,1:T(8,128)S(1)} %bitcast.305), channel_id=1, source_target_pairs={{0,4},{4,8},{8,12},{12,0},{1,5},{5,9},{9,13},{13,1},{2,6},{6,10},{... | collective-permute-start | bytes 393224 | tf_op jit(solution)/shard_map/ppermute | solution.py:118
  (17 other events, 43.5 us)

commit v10 on v3

--- a/solution.py
+++ b/solution.py
@@ -84,13 +84,28 @@
 
 def all_sum(value, axis):
     count = lax.axis_size(axis)
-    if not is_pow2(count):
-        return lax.psum(value, axis)
-    bit = 1
-    while bit < count:
-        value = value + xor_perm(value, axis, bit)
-        bit *= 2
-    return value
+    if count > 4:
+        if not is_pow2(count):
+            return lax.psum(value, axis)
+        bit = 1
+        while bit < count:
+            value = value + xor_perm(value, axis, bit)
+            bit *= 2
+        return value
+    me = lax.axis_index(axis)
+    got = [value] + [
+        lax.ppermute(value, axis, [(i, (i + k) % count) for i in range(count)])
+        for k in range(1, count)
+    ]
+    stacked = jnp.stack(got)
+    by_source = [
+        lax.dynamic_index_in_dim(stacked, (me - src) % count, 0, keepdims=False)
+        for src in range(count)
+    ]
+    total = by_source[0]
+    for part in by_source[1:]:
+        total = total + part
+    return total
 
 
 def local(hidden, proj_w, queries, lengths, candidates):
@@ -106,8 +121,19 @@
     capacity = 2 * slot_count // owners
     me = lax.axis_index("enc") * mp_count + lax.axis_index("mp")
 
-    all_queries = lax.all_gather(queries, ("enc", "mp"), axis=0, tiled=True)
-    all_cand = lax.all_gather(candidates, ("enc", "mp"), axis=0, tiled=True)
+    coded = jnp.concatenate(
+        [
+            (candidates // BLK).astype(jnp.bfloat16),
+            (candidates % BLK).astype(jnp.bfloat16),
+            jnp.zeros((qry_dev, emb_width - 2 * cand_count), jnp.bfloat16),
+        ],
+        axis=1,
+    )
+    packed = jnp.concatenate([queries, coded[:, None, :]], axis=1)
+    packed = lax.all_gather(packed, ("enc", "mp"), axis=0, tiled=True)
+    all_queries = packed[:, :query_len]
+    coded = packed[:, query_len, : 2 * cand_count].astype(jnp.int32)
+    all_cand = coded[:, :cand_count] * BLK + coded[:, cand_count:]
     all_cand = all_cand.reshape(owners, slot_count)
 
     e_pre = reduce_scatter_rows(

time: 199 us -> 218 us (1.095)
  waiting for transfers between devices: 84.5 us -> 113 us
  blocking collectives: 29 us -> 6.16 us
  starting transfers between devices: 2.99 us -> 12.8 us
  other arithmetic: 20 us -> 26 us
  local copies, waits for them, and re-layouts: 25.8 us -> 23.5 us
    all_gather x1, waiting for transfers between devices: 6.35 us -> 39.4 us  [local(): packed = lax.all_gather(packed, ('enc', 'mp'), axis=0, tiled=True)]
    all_gather x1 -> x0, blocking collectives: 22.9 us -> none  [local(): all_cand = lax.all_gather(candidates, ('enc', 'mp'), axis=0, tiled=True)]
    ppermute x8 -> x4, waiting for transfers between devices: 78.1 us -> 64.5 us  [xor_perm(): return lax.ppermute(value, axis, [(i, i ^ bit) for i in range(count)])]
    ppermute x0 -> x6, starting transfers between devices: none -> 9.5 us  [all_sum(): lax.ppermute(value, axis, [(i, (i + k) % count) for i in range(count)])]
    ppermute x0 -> x6, waiting for transfers between devices: none -> 8.82 us  [all_sum(): lax.ppermute(value, axis, [(i, (i + k) % count) for i in range(count)])]
    unnamed x20 -> x24, local copies, waits for them, and re-layouts: 10.2 us -> 8.96 us
  transfers between devices with their start and end apart: 9 -> 11, of which waited for: 8 -> 9; matrix products, arithmetic and copies ran while one was open for 8% -> 5% of each run, Pallas kernels for 0% -> 0%
where the time goes in v10:
time: 218 us
  waiting for transfers between devices  113 us (52%)
  other arithmetic  26 us (12%)
  local copies, waits for them, and re-layouts  23.5 us (11%)
  matrix products  22 us (10%)
  between operations  14.5 us (7%)
  starting transfers between devices  12.8 us (6%)
  blocking collectives  6.16 us (3%)
    ppermute x4, waiting for transfers between devices, xor_perm(): return lax.ppermute(value, axis, [(i, i ^ bit) for i in range(count)])  64.5 us
    all_gather x1, waiting for transfers between devices, local(): packed = lax.all_gather(packed, ('enc', 'mp'), axis=0, tiled=True)  39.4 us
    ppermute x6, starting transfers between devices, all_sum(): lax.ppermute(value, axis, [(i, (i + k) % count) for i in range(count)])  9.5 us
    unnamed x24, local copies, waits for them, and re-layouts  8.96 us
    ppermute x6, waiting for transfers between devices, all_sum(): lax.ppermute(value, axis, [(i, (i + k) % count) for i in range(count)])  8.82 us
    dot_general x1, matrix products, local(): jnp.einsum('scij,scie->scje', weights, q_e, preferred_element_type=jnp.fl...  6.94 us
    psum x1, blocking collectives, local(): lax.psum(placed, 'mp')  6.16 us
    dot_general x1, matrix products, local(): jnp.dot(hidden, proj_w, preferred_element_type=jnp.float32)  5.7 us
  transfers between devices with their start and end apart: 11, of which 9 were waited for; matrix products, arithmetic and copies ran while one was open for 5% of the time, Pallas kernels for 0%

profile of v10, /device:TPU:0, one launch (start us, length us, event | category | flops | bytes accessed | tf_op | source)
XLA Modules:
  0.0 217.6 jit_solution(7470360255420063320)
XLA Ops:
  8.0 5.7 %fusion.42 = f32[16384,128]{1,0:T(8,128)S(1)} fusion(bf16[16384,256]{1,0:T(8,128)(2,1)} %param.5, bf16[256,128]{1,0:T(8,128)(2,1)S(1)} %copy-done), kind=kOutput, calls=%fused_computation.131 | convolution fusion | flops 1073741824 | bytes 16842752 | tf_op jit(solution)/shard_map/dot_general | solution.py:140
  13.8 2.6 %select_bitcast_fusion = f32[2,4096,128]{2,1,0:T(8,128)} fusion(f32[2,2,4096,128]{3,2,1,0:T(8,128)S(1)} %bitcast.129, pred[]{:T(512)S(6)} %eq.70), kind=kLoop, calls=%fused_computation.15 | loop fusion | flops 1048576 | bytes 12582913 | tf_op jit(solution)/shard_map/jit(_where)/select_n | solution.py:62
  16.4 1.8 copy-done.3
  19.7 39.4 %all-gather.2.cloned.1.call-done = bf16[128,33,128]{2,0,1:T(8,128)(2,1)} async-done(((bf16[8,33,128]{2,0,1:T(8,128)(2,1)}), bf16[128,33,128]{2,0,1:T(8,128)(2,1)}) %all-gather.2.cloned.1.call-update) | async-done | bytes 1081360 | tf_op jit(solution)/shard_map/all_gather | solution.py:133
  59.8 5.2 %fusion = f32[1,2,4096,128]{3,2,1,0:T(8,128)S(1)} fusion(f32[2,4096,128]{2,1,0:T(8,128)} %collective-permute-done, f32[2,2,4096,128]{3,2,1,0:T(8,128)} %bitcast.130, pred[]{:T(512)S(6)} %eq.70), kind=kLoop, calls=%fused_computation.10 | loop fusion | flops 2097152 | bytes 16777216 | tf_op jit(solution)/shard_map/reshape | solution.py:59
  65.1 1.8 select_bitcast_fusion.3
  69.1 1.9 gather_fusion.3
  71.4 1.9 gather_fusion
  74.3 2.2 %gather_fusion.1 = bf16[256,32,128]{2,1,0:T(8,128)(2,1)} fusion(bf16[128,32,128]{2,1,0:T(8,128)(2,1)S(1)} %copy.89, s32[1024]{0:T(1024)S(1)} %pad_clamp_fusion.1), kind=kCustom, calls=%fused_computation.1 | custom fusion | bytes 4195328 | tf_op jit(solution)/shard_map/gather | solution.py:158
  76.6 38.3 %collective-permute-done.1 = f32[1,4096,128]{2,1,0:T(8,128)} collective-permute-done((f32[1,4096,128]{2,1,0:T(8,128)}, f32[1,4096,128]{2,1,0:T(8,128)}, u32[]{:S(2)}, u32[]{:S(2)}) %collective-permute-start.1) | collective-permute-done | bytes 2097184 | tf_op jit(solution)/shard_map/ppermute | solution.py:44
  114.9 3.5 %fusion.7 = (f32[4096]{0:T(1024)S(1)}, f32[1,4096,128]{2,1,0:T(8,128)S(1)}) fusion(f32[1,4096,128]{2,1,0:T(8,128)} %collective-permute-done.1, f32[1,2,4096,128]{3,2,1,0:T(8,128)} %copy-done.4, pred[]{:T(512)S(6)} %eq.69), kind=kLoop, calls=%fused_computation.25 | loop fusion | flops 2093056 | bytes 8404993 | tf_op jit(solution)/shard_map/reduce_sum | solution.py:142
  119.2 3.0 %gather_fusion.2 = bf16[256,64,128]{2,1,0:T(8,128)(2,1)} fusion(bf16[64,64,128]{2,1,0:T(8,128)(2,1)S(1)} %multiply_convert_fusion.1, s32[1024]{0:T(1024)S(1)} %pad_clamp_fusion), kind=kCustom, calls=%fused_computation.2 | custom fusion | bytes 8389632 | tf_op jit(solution)/shard_map/gather | solution.py:157
  122.2 5.2 %select_reduce_fusion = (f32[16,16,32]{2,1,0:T(8,128)S(1)}, f32[16,16,32,64]{3,2,1,0:T(8,128)S(1)}) fusion(pred[16,16,64]{2,1,0:T(8,128)(4,1)S(1)} %add_compare_fusion, bf16[16,16,32,128]{3,2,1,0:T(8,128)(2,1)} %bitcast.137, bf16[16,16,64,128]{3,2,1,0:T(8,128)(2,1)} %bitcast.136), kind=kOutput, calls=%fused_computation.16 | convolution fusion | flops 135258112 | bytes 8437760 | tf_op jit(solution)/shard_map/scie,scje->scij/dot_general | solution.py:160
  127.4 1.9 copy-done.5
  129.4 2.4 %fusion.3 = f32[16,16,32]{2,1,0:T(8,128)S(1)} fusion(f32[16,16,32,64]{3,2,1,0:T(8,128)S(1)} %get-tuple-element.37, f32[16,16,32]{2,1,0:T(8,128)S(1)} %get-tuple-element.36, pred[16,16,64]{2,1,0:T(8,128)(4,1)S(1)} %add_compare_fusion), kind=kLoop, calls=%fused_computation.17 | loop fusion | flops 1564672 | bytes 2179072 | tf_op jit(solution)/shard_map/reduce_sum | solution.py:22
  132.0 6.2 %psum.7 = f32[16,128]{1,0:T(8,128)S(1)} all-reduce(f32[16,128]{1,0:T(8,128)S(1)} %select_reduce_fusion.1), channel_id=1, replica_groups=mesh['groups'=2,'enc'=4,'mp'=4] {'mp'}, use_global_device_ids=true, to_apply=%region_7.8 | all-reduce | flops 2048 | bytes 16384 | tf_op jit(solution)/shard_map/psum | solution.py:166
  138.2 1.6 collective-permute-start.2
  140.8 2.1 collective-permute-start.4
  145.1 1.9 gather_fusion.4
  147.1 6.9 %multiply_convert_fusion = bf16[16,16,64,128]{3,2,1,0:T(8,128)(2,1)S(1)} fusion(f32[16,16]{1,0:T(8,128)S(1)} %select_multiply_fusion, bf16[16,16,32,128]{3,2,1,0:T(8,128)(2,1)} %bitcast.138, f32[16,16,32,64]{3,2,1,0:T(8,128)} %copy-done.5, f32[16,16,32]{2,1,0:T(8,128)S(1)} %fusion.3, f32[16,16,32]{2,1,0:T(8,128)S(1)} %get-tuple-element.36, ...), kind=kOutput, calls=%fused_computation.5 | convolution fusion | flops 140509184 | bytes 8471552 | tf_op jit(solution)/shard_map/scij,scie->scje/dot_general | solution.py:163
  154.1 2.6 %fusion.12 = f32[64,64,128]{2,0,1:T(8,128)S(1)} fusion(bf16[16,16,64,128]{3,2,1,0:T(8,128)(2,1)S(1)} %multiply_convert_fusion, s32[16,16]{0,1:T(8,128)S(1)} %copy.80, pred[16,16]{0,1:T(8,128)(4,1)S(1)} %copy.81), kind=kOutput, calls=%fused_computation.35 | convolution fusion | flops 268468224 | bytes 6292736 | tf_op jit(solution)/shard_map/scb,scje->bje/dot_general | solution.py:174
  158.5 1.9 fusion.6
  161.9 21.7 %collective-permute-done.5 = bf16[1,4096,128]{2,1,0:T(8,128)(2,1)S(1)} collective-permute-done((bf16[1,4096,128]{2,1,0:T(8,128)(2,1)S(1)}, bf16[1,4096,128]{2,1,0:T(8,128)(2,1)S(1)}, u32[]{:S(2)}, u32[]{:S(2)}) %collective-permute-start.5) | collective-permute-done | bytes 1048608 | tf_op jit(solution)/shard_map/ppermute | solution.py:44
  183.7 1.5 maximum_bitcast_fusion
  185.2 4.5 %collective-permute-done.6 = bf16[2,4096,128]{2,1,0:T(8,128)(2,1)} collective-permute-done((bf16[2,4096,128]{2,1,0:T(8,128)(2,1)}, bf16[2,4096,128]{2,1,0:T(8,128)(2,1)}, u32[]{:S(2)}, u32[]{:S(2)}) %collective-permute-start.6) | collective-permute-done | bytes 2097184 | tf_op jit(solution)/shard_map/ppermute | solution.py:44
  189.7 1.9 select_bitcast_fusion.2
  192.3 1.5 slice-done
  195.2 1.5 fusion.43
  196.7 1.7 collective-permute-start.7
  198.4 2.5 %collective-permute-start.8 = (f32[256,128]{0,1:T(8,128)S(1)}, f32[256,128]{0,1:T(8,128)S(1)}, u32[]{:S(2)}, u32[]{:S(2)}) collective-permute-start(f32[256,128]{0,1:T(8,128)S(1)} %bitcast.140), channel_id=1, source_target_pairs={{0,8},{4,12},{8,0},{12,4},{1,9},{5,13},{9,1},{13,5},{2,10},{6,14},... | collective-permute-start | bytes 393224 | tf_op jit(solution)/shard_map/ppermute | solution.py:97
  202.1 2.9 %collective-permute-done.7 = f32[256,128]{0,1:T(8,128)S(1)} collective-permute-done((f32[256,128]{0,1:T(8,128)S(1)}, f32[256,128]{0,1:T(8,128)S(1)}, u32[]{:S(2)}, u32[]{:S(2)}) %collective-permute-start.7) | collective-permute-done | bytes 131104 | tf_op jit(solution)/shard_map/ppermute | solution.py:97
  205.0 4.9 %collective-permute-done.8 = f32[256,128]{0,1:T(8,128)S(1)} collective-permute-done((f32[256,128]{0,1:T(8,128)S(1)}, f32[256,128]{0,1:T(8,128)S(1)}, u32[]{:S(2)}, u32[]{:S(2)}) %collective-permute-start.8) | collective-permute-done | bytes 131104 | tf_op jit(solution)/shard_map/ppermute | solution.py:97
  (95 shorter events, 18.2 us)
Async XLA Ops:
  7.2 0.8 copy-start
  7.2 51.9 %all-gather.2.cloned.1.call-start = ((), (), s32[]{:S(2)}) async-start(), calls=%async_computation | async-start | bytes 1148928 | tf_op jit(solution)/shard_map/all_gather | solution.py:133
  13.7 4.5 %copy-start.3 = (f32[16384,128]{1,0:T(8,128)}, f32[16384,128]{1,0:T(8,128)S(1)}, u32[]{:S(2)}) copy-start(f32[16384,128]{1,0:T(8,128)S(1)} %fusion.42) | copy-start | bytes 25165828
  13.7 4.9 %copy-start.6 = (bf16[8,32,128]{2,1,0:T(8,128)(2,1)S(1)}, bf16[8,32,128]{2,1,0:T(8,128)(2,1)}, u32[]{:S(2)}) copy-start(bf16[8,32,128]{2,1,0:T(8,128)(2,1)} %param.7) | copy-start | bytes 196612
  13.7 5.1 %copy-start.7 = (s32[8,16]{1,0:T(8,128)S(1)}, s32[8,16]{1,0:T(8,128)}, u32[]{:S(2)}) copy-start(s32[8,16]{1,0:T(8,128)} %param.9) | copy-start | bytes 1540
  18.2 41.6 %collective-permute-start = (f32[2,4096,128]{2,1,0:T(8,128)}, f32[2,4096,128]{2,1,0:T(8,128)}, u32[]{:S(2)}, u32[]{:S(2)}) collective-permute-start(f32[2,4096,128]{2,1,0:T(8,128)} %select_bitcast_fusion), channel_id=1, source_target_pairs={{0,1},{1,0},{2,3},{3,2},{4,5},{5,4},{6,7},{7,6},{8,9},{9,8},{10,11... | collective-permute-start | bytes 12582920 | tf_op jit(solution)/shard_map/ppermute | solution.py:44
  65.0 3.1 %copy-start.4 = (f32[1,2,4096,128]{3,2,1,0:T(8,128)}, f32[1,2,4096,128]{3,2,1,0:T(8,128)S(1)}, u32[]{:S(2)}) copy-start(f32[1,2,4096,128]{3,2,1,0:T(8,128)S(1)} %fusion) | copy-start | bytes 12582916
  66.8 48.1 %collective-permute-start.1 = (f32[1,4096,128]{2,1,0:T(8,128)}, f32[1,4096,128]{2,1,0:T(8,128)}, u32[]{:S(2)}, u32[]{:S(2)}) collective-permute-start(f32[1,4096,128]{2,1,0:T(8,128)} %select_bitcast_fusion.3), channel_id=1, source_target_pairs={{0,2},{1,3},{2,0},{3,1},{4,6},{5,7},{6,4},{7,5},{8,10},{9,11},{10,... | collective-permute-start | bytes 6291464 | tf_op jit(solution)/shard_map/ppermute | solution.py:44
  69.1 2.3 %copy-start.2 = (s32[256]{0:T(256)S(1)}, s32[256]{0:T(256)}, u32[]{:S(2)}) copy-start(s32[256]{0:T(256)} %param.8) | copy-start | bytes 3076
  71.4 2.1 slice-start.2
  127.4 1.9 copy-start.5
  138.2 5.5 %collective-permute-start.2 = (f32[16,128]{1,0:T(8,128)S(1)}, f32[16,128]{1,0:T(8,128)S(1)}, u32[]{:S(2)}, u32[]{:S(2)}) collective-permute-start(f32[16,128]{1,0:T(8,128)S(1)} %psum.7), channel_id=1, source_target_pairs={{0,4},{4,8},{8,12},{12,0},{1,5},{5,9},{9,13},{13,1},{2,6},{6,10},{... | collective-permute-start | bytes 24584 | tf_op jit(solution)/shard_map/ppermute | solution.py:97
  139.8 4.5 %collective-permute-start.3 = (f32[16,128]{1,0:T(8,128)S(1)}, f32[16,128]{1,0:T(8,128)S(1)}, u32[]{:S(2)}, u32[]{:S(2)}) collective-permute-start(f32[16,128]{1,0:T(8,128)S(1)} %psum.7), channel_id=1, source_target_pairs={{0,8},{4,12},{8,0},{12,4},{1,9},{5,13},{9,1},{13,5},{2,10},{6,14},... | collective-permute-start | bytes 24584 | tf_op jit(solution)/shard_map/ppermute | solution.py:97
  140.8 3.7 %collective-permute-start.4 = (f32[16,128]{1,0:T(8,128)S(1)}, f32[16,128]{1,0:T(8,128)S(1)}, u32[]{:S(2)}, u32[]{:S(2)}) collective-permute-start(f32[16,128]{1,0:T(8,128)S(1)} %psum.7), channel_id=1, source_target_pairs={{0,12},{4,0},{8,4},{12,8},{1,13},{5,1},{9,5},{13,9},{2,14},{6,2},{... | collective-permute-start | bytes 24584 | tf_op jit(solution)/shard_map/ppermute | solution.py:97
  160.5 23.1 %collective-permute-start.5 = (bf16[1,4096,128]{2,1,0:T(8,128)(2,1)S(1)}, bf16[1,4096,128]{2,1,0:T(8,128)(2,1)S(1)}, u32[]{:S(2)}, u32[]{:S(2)}) collective-permute-start(bf16[1,4096,128]{2,1,0:T(8,128)(2,1)S(1)} %fusion.6), channel_id=1, source_target_pairs={{0,2},{1,3},{2,0},{3,1},{4,6},{5,7},{6,4},{7,5},{8,10},{9,11},{10,... | collective-permute-start | bytes 3145736 | tf_op jit(solution)/shard_map/ppermute | solution.py:44
  185.2 4.5 %collective-permute-start.6 = (bf16[2,4096,128]{2,1,0:T(8,128)(2,1)}, bf16[2,4096,128]{2,1,0:T(8,128)(2,1)}, u32[]{:S(2)}, u32[]{:S(2)}) collective-permute-start(bf16[2,4096,128]{2,1,0:T(8,128)(2,1)} %maximum_bitcast_fusion), channel_id=1, source_target_pairs={{0,1},{1,0},{2,3},{3,2},{4,5},{5,4},{6,7},{7,6},{8,9},{9,8},{10,11... | collective-permute-start | bytes 6291464 | tf_op jit(solution)/shard_map/ppermute | solution.py:44
  191.6 2.2 %slice-start = ((s8[8388608]{0:T(1024)(128)(4,1)}), s8[4194304]{0:T(1024)(128)(4,1)S(1)}, s32[]{:S(2)}) async-start(s8[8388608]{0:T(1024)(128)(4,1)} %bitcast.131), calls=%async_computation.1 | async-start | bytes 8388608
  192.0 3.2 %slice-start.1 = ((s8[8388608]{0:T(1024)(128)(4,1)}), s8[4194304]{0:T(1024)(128)(4,1)S(1)}, s32[]{:S(2)}) async-start(s8[8388608]{0:T(1024)(128)(4,1)} %bitcast.131), calls=%async_computation.2 | async-start | bytes 8388608
  195.2 15.5 %copy-start.1 = (bf16[256,128]{1,0:T(8,128)(2,1)S(1)}, bf16[256,128]{1,0:T(8,128)(2,1)}, u32[]{:S(2)}) copy-start(bf16[256,128]{1,0:T(8,128)(2,1)} %param.6) | copy-start | bytes 196612
  196.7 8.3 %collective-permute-start.7 = (f32[256,128]{0,1:T(8,128)S(1)}, f32[256,128]{0,1:T(8,128)S(1)}, u32[]{:S(2)}, u32[]{:S(2)}) collective-permute-start(f32[256,128]{0,1:T(8,128)S(1)} %bitcast.139), channel_id=1, source_target_pairs={{0,4},{4,8},{8,12},{12,0},{1,5},{5,9},{9,13},{13,1},{2,6},{6,10},{... | collective-permute-start | bytes 393224 | tf_op jit(solution)/shard_map/ppermute | solution.py:97
  198.4 11.4 %collective-permute-start.8 = (f32[256,128]{0,1:T(8,128)S(1)}, f32[256,128]{0,1:T(8,128)S(1)}, u32[]{:S(2)}, u32[]{:S(2)}) collective-permute-start(f32[256,128]{0,1:T(8,128)S(1)} %bitcast.140), channel_id=1, source_target_pairs={{0,8},{4,12},{8,0},{12,4},{1,9},{5,13},{9,1},{13,5},{2,10},{6,14},... | collective-permute-start | bytes 393224 | tf_op jit(solution)/shard_map/ppermute | solution.py:97
  200.9 8.9 %collective-permute-start.9 = (f32[256,128]{0,1:T(8,128)S(1)}, f32[256,128]{0,1:T(8,128)S(1)}, u32[]{:S(2)}, u32[]{:S(2)}) collective-permute-start(f32[256,128]{0,1:T(8,128)S(1)} %bitcast.141), channel_id=1, source_target_pairs={{0,12},{4,0},{8,4},{12,8},{1,13},{5,1},{9,5},{13,9},{2,14},{6,2},{... | collective-permute-start | bytes 393224 | tf_op jit(solution)/shard_map/ppermute | solution.py:97
Sparse Core Ops, SparseCore 0:
  19.7 39.3 all-gather.1

commit v11 on v6

--- a/solution.py
+++ b/solution.py
@@ -121,6 +121,8 @@
     slot_count = qry_dev * cand_count
     capacity = 2 * slot_count // owners
     me = lax.axis_index("enc") * mp_count + lax.axis_index("mp")
+
+    all_queries = lax.all_gather(queries, ("enc", "mp"), axis=0, tiled=True)
     all_cand = lax.all_gather(candidates, ("enc", "mp"), axis=0, tiled=True)
     all_cand = all_cand.reshape(owners, slot_count)
 
@@ -134,8 +136,6 @@
     ]
     if is_pow2(mp_count) and mp_count > 1:
         keeps, sends, bit = halving_steps(partials, "mp")
-        last, queries = lax.optimization_barrier((sends[-1], queries))
-        sends = sends[:-1] + [last]
         pieces = [k + xor_perm(t, "mp", bit) for k, t in zip(keeps, sends)]
         pieces = [p.reshape(-1, emb_width) for p in pieces]
     else:
@@ -143,21 +143,6 @@
             lax.psum_scatter(p, "mp", scatter_dimension=0, tiled=True) for p in partials
         ]
     e_pre = jnp.stack(pieces).reshape(row_share, emb_width)
-
-    packed = jnp.concatenate(
-        [
-            queries.reshape(qry_dev, query_len * emb_width).astype(jnp.float32),
-            candidates.astype(jnp.float32),
-        ],
-        axis=1,
-    )
-    packed = lax.all_gather(packed, ("enc", "mp"), axis=0, tiled=True)
-    all_queries = (
-        packed[:, : query_len * emb_width]
-        .astype(jnp.bfloat16)
-        .reshape(owners * qry_dev, query_len, emb_width)
-    )
-    late_cand = packed[:, query_len * emb_width :].astype(jnp.int32).reshape(owners, slot_count)
 
     scale = lax.rsqrt(jnp.sum(e_pre * e_pre, -1, keepdims=True) + 1e-06)
     embedded = (e_pre * scale).astype(jnp.bfloat16)
@@ -190,8 +175,7 @@
     d_e = jnp.take_along_axis(d_score.reshape(owners, slot_count), slot_of, axis=1)
     d_e = jnp.where(valid, d_e, jnp.float32(0))
     occ_grad = (occ_raw * (d_e / query_len)[:, :, None, None]).astype(jnp.bfloat16)
-    late_local = jnp.take_along_axis(late_cand, slot_of, axis=1) % blk_dev
-    onehot = (late_local[:, :, None] == jnp.arange(blk_dev, dtype=jnp.int32)) & valid[:, :, None]
+    onehot = (local_of[:, :, None] == jnp.arange(blk_dev, dtype=jnp.int32)) & valid[:, :, None]
     grad_emb = jnp.einsum(
         "scb,scje->bje",
         onehot.astype(jnp.bfloat16),

time: 227 us -> 212 us (0.934)
  local copies, waits for them, and re-layouts: 35.4 us -> 29.4 us
  waiting for transfers between devices: 87.2 us -> 82.3 us
  other arithmetic: 24.8 us -> 21.7 us
    ppermute x10, waiting for transfers between devices: 72.6 us -> 66.9 us  [xor_perm(): return lax.ppermute(value, axis, [(i, i ^ bit) for i in range(count)])]
    unnamed x34 -> x31, local copies, waits for them, and re-layouts: 10.2 us -> 6.32 us
  transfers between devices with their start and end apart: 17 -> 17, of which waited for: 11 -> 11; matrix products, arithmetic and copies ran while one was open for 9% -> 15% of each run, Pallas kernels for 0% -> 0%
where the time goes in v11:
time: 212 us
  waiting for transfers between devices  82.3 us (39%)
  local copies, waits for them, and re-layouts  29.4 us (14%)
  blocking collectives  29 us (14%)
  matrix products  23 us (11%)
  other arithmetic  21.7 us (10%)
  between operations  14.6 us (7%)
  starting transfers between devices  11.7 us (6%)
    ppermute x10, waiting for transfers between devices, xor_perm(): return lax.ppermute(value, axis, [(i, i ^ bit) for i in range(count)])  66.9 us
    all_gather x1, blocking collectives, local(): all_cand = lax.all_gather(candidates, ('enc', 'mp'), axis=0, tiled=True)  23.1 us
    ppermute x6, waiting for transfers between devices, all_sum(): lax.ppermute(value, axis, [(i, (i + k) % count) for i in range(count)])  14.7 us
    dot_general x1, matrix products, local(): jnp.einsum('scij,scie->scje', weights, q_e, preferred_element_type=jnp.fl...  6.95 us
    ppermute x10, starting transfers between devices, xor_perm(): return lax.ppermute(value, axis, [(i, i ^ bit) for i in range(count)])  6.9 us
    unnamed x31, local copies, waits for them, and re-layouts  6.32 us
    psum x1, blocking collectives, local(): lax.psum(placed, 'mp')  5.86 us
    slice x1, local copies, waits for them, and re-layouts, local(): split_rows[:, k]  5.7 us
  transfers between devices with their start and end apart: 17, of which 11 were waited for; matrix products, arithmetic and copies ran while one was open for 15% of the time, Pallas kernels for 0%

profile of v11, /device:TPU:0, one launch (start us, length us, event | category | flops | bytes accessed | tf_op | source)
XLA Modules:
  0.0 211.7 jit_solution(10200625527502860151)
XLA Ops:
  7.9 5.7 %fusion.55 = (bf16[4,1,1024,256]{3,2,1,0:T(8,128)(2,1)}, bf16[4,1,1024,256]{3,2,1,0:T(8,128)(2,1)}, bf16[4,1,1024,256]{3,2,1,0:T(8,128)(2,1)S(1)}, bf16[4,1,1024,256]{3,2,1,0:T(8,128)(2,1)}) fusion(bf16[4,4,1024,256]{3,2,1,0:T(8,128)(2,1)} %bitcast.211), kind=kLoop, calls=%fused_computation.146 | loop fusion | bytes 16777216 | tf_op jit(solution)/shard_map/slice | solution.py:132
  13.6 2.3 %fusion.8 = f32[2,2,1024,128]{3,2,0,1:T(8,128)S(1)} fusion(bf16[256,128]{1,0:T(8,128)(2,1)S(1)} %copy-done, bf16[2,2,1024,256]{3,2,1,0:T(8,128)(2,1)} %bitcast.225), kind=kOutput, calls=%fused_computation.22 | convolution fusion | flops 268435456 | bytes 4259840 | tf_op jit(solution)/shard_map/dot_general | solution.py:132
  26.7 23.1 %all_gather.6 = s32[128,16]{1,0:T(8,128)S(1)} all-gather(s32[8,16]{1,0:T(8,128)S(1)} %copy-done.11), channel_id=1, replica_groups=mesh['groups'=2,'enc'=4,'mp'=4] {'enc','mp'}, dimensions={0}, use_global_device_ids=true | all-gather | bytes 8704 | tf_op jit(solution)/shard_map/all_gather | solution.py:126
  50.7 1.9 gather_fusion.3
  53.6 1.9 gather_fusion
  56.0 2.1 %fusion.25 = f32[1,2,1024,128]{3,2,1,0:T(8,128)S(1)} fusion(f32[2,1024,128]{2,1,0:T(8,128)} %collective-permute-done.6, f32[2,2,1024,128]{3,2,0,1:T(8,128)} %copy-done.7, pred[]{:T(512)S(6)} %eq.80), kind=kLoop, calls=%fused_computation.44 | loop fusion | flops 524288 | bytes 4194305 | tf_op jit(solution)/shard_map/reshape | solution.py:59
  58.5 1.6 fusion.26
  60.2 1.7 collective-permute-start.5
  64.1 1.7 collective-permute-start.1
  65.8 7.2 %collective-permute-done.7 = f32[1,1024,128]{2,1,0:T(8,128)S(1)} collective-permute-done((f32[1,1024,128]{2,1,0:T(8,128)S(1)}, f32[1,1024,128]{2,1,0:T(8,128)S(1)}, u32[]{:S(2)}, u32[]{:S(2)}) %collective-permute-start.7) | collective-permute-done | bytes 524320 | tf_op jit(solution)/shard_map/ppermute | solution.py:44
  73.1 11.2 %collective-permute-done.5 = f32[1,1024,128]{2,1,0:T(8,128)S(1)} collective-permute-done((f32[1,1024,128]{2,1,0:T(8,128)S(1)}, f32[1,1024,128]{2,1,0:T(8,128)S(1)}, u32[]{:S(2)}, u32[]{:S(2)}) %collective-permute-start.5) | collective-permute-done | bytes 524320 | tf_op jit(solution)/shard_map/ppermute | solution.py:44
  84.3 11.2 %collective-permute-done.3 = f32[1,1024,128]{2,1,0:T(8,128)S(1)} collective-permute-done((f32[1,1024,128]{2,1,0:T(8,128)S(1)}, f32[1,1024,128]{2,1,0:T(8,128)S(1)}, u32[]{:S(2)}, u32[]{:S(2)}) %collective-permute-start.3) | collective-permute-done | bytes 524320 | tf_op jit(solution)/shard_map/ppermute | solution.py:44
  95.6 10.6 %collective-permute-done.1 = f32[1,1024,128]{2,1,0:T(8,128)S(1)} collective-permute-done((f32[1,1024,128]{2,1,0:T(8,128)S(1)}, f32[1,1024,128]{2,1,0:T(8,128)S(1)}, u32[]{:S(2)}, u32[]{:S(2)}) %collective-permute-start.1) | collective-permute-done | bytes 524320 | tf_op jit(solution)/shard_map/ppermute | solution.py:44
  107.7 3.0 %gather_fusion.2 = bf16[256,64,128]{2,1,0:T(8,128)(2,1)} fusion(bf16[64,64,128]{2,1,0:T(8,128)(2,1)S(1)} %multiply_convert_fusion.1, s32[1024]{0:T(1024)S(1)} %pad_clamp_fusion), kind=kCustom, calls=%fused_computation.2 | custom fusion | bytes 8389632 | tf_op jit(solution)/shard_map/gather | solution.py:162
  110.7 3.4 %gather_fusion.1 = bf16[256,32,128]{2,1,0:T(8,128)(2,1)} fusion(bf16[128,32,128]{2,1,0:T(8,128)(2,1)} %all-gather.2.cloned.1.call-done, s32[1024]{0:T(1024)S(1)} %pad_clamp_fusion.1), kind=kCustom, calls=%fused_computation.1 | custom fusion | bytes 4195328 | tf_op jit(solution)/shard_map/gather | solution.py:163
  114.1 5.2 %select_reduce_fusion = (f32[16,16,32]{2,1,0:T(8,128)S(1)}, f32[16,16,32,64]{3,2,1,0:T(8,128)S(1)}) fusion(pred[16,16,64]{2,1,0:T(8,128)(4,1)S(1)} %add_compare_fusion, bf16[16,16,32,128]{3,2,1,0:T(8,128)(2,1)} %bitcast.220, bf16[16,16,64,128]{3,2,1,0:T(8,128)(2,1)} %bitcast.218), kind=kOutput, calls=%fused_computation.11 | convolution fusion | flops 135258112 | bytes 8437760 | tf_op jit(solution)/shard_map/scie,scje->scij/dot_general | solution.py:165
  119.3 2.4 %fusion.2 = f32[16,16,32]{2,1,0:T(8,128)S(1)} fusion(f32[16,16,32,64]{3,2,1,0:T(8,128)S(1)} %get-tuple-element.39, f32[16,16,32]{2,1,0:T(8,128)S(1)} %get-tuple-element.38, pred[16,16,64]{2,1,0:T(8,128)(4,1)S(1)} %add_compare_fusion), kind=kLoop, calls=%fused_computation.12 | loop fusion | flops 1564672 | bytes 2179072 | tf_op jit(solution)/shard_map/reduce_sum | solution.py:22
  122.0 5.9 %psum.7 = f32[16,128]{1,0:T(8,128)S(1)} all-reduce(f32[16,128]{1,0:T(8,128)S(1)} %select_reduce_fusion.1), channel_id=1, replica_groups=mesh['groups'=2,'enc'=4,'mp'=4] {'mp'}, use_global_device_ids=true, to_apply=%region_7.8 | all-reduce | flops 2048 | bytes 16384 | tf_op jit(solution)/shard_map/psum | solution.py:171
  128.1 1.8 collective-permute-start.8
  130.0 1.6 collective-permute-done.10
  134.7 1.9 gather_fusion.4
  136.7 6.9 %multiply_convert_fusion = bf16[16,16,64,128]{3,2,1,0:T(8,128)(2,1)S(1)} fusion(f32[16,16]{1,0:T(8,128)S(1)} %select_multiply_fusion, bf16[16,16,32,128]{3,2,1,0:T(8,128)(2,1)} %bitcast.221, f32[16,16,32,64]{3,2,1,0:T(8,128)} %copy-done.8, f32[16,16,32]{2,1,0:T(8,128)S(1)} %fusion.2, f32[16,16,32]{2,1,0:T(8,128)S(1)} %get-tuple-element.38, ...), kind=kOutput, calls=%fused_computation.5 | convolution fusion | flops 140509184 | bytes 8471552 | tf_op jit(solution)/shard_map/scij,scie->scje/dot_general | solution.py:168
  143.6 5.0 %fusion.14 = (f32[64,64]{0,1:T(8,128)S(1)}, f32[64,64,128]{2,0,1:T(8,128)}) fusion(f32[64,64,128]{2,1,0:T(8,128)S(1)} %bitcast.215, bf16[16,16,64,128]{3,2,1,0:T(8,128)(2,1)S(1)} %multiply_convert_fusion, s32[16,16]{0,1:T(8,128)S(1)} %copy.154, pred[16,16]{0,1:T(8,128)(4,1)S(1)} %copy.155), kind=kOutput, calls=%fused_computation.29 | convolution fusion | flops 269512704 | bytes 8406272 | tf_op jit(solution)/shard_map/scb,scje->bje/dot_general | solution.py:179
  148.7 2.8 %copy.158 = f32[64,64,128]{2,1,0:T(8,128)S(1)} copy(f32[64,64,128]{2,0,1:T(8,128)} %get-tuple-element.41) | data formatting | bytes 4194304 | tf_op jit(solution)/shard_map/scb,scje->bje/dot_general | solution.py:179
  151.6 1.9 fusion.7
  154.6 22.3 %collective-permute-done.11 = bf16[1,4096,128]{2,1,0:T(8,128)(2,1)S(1)} collective-permute-done((bf16[1,4096,128]{2,1,0:T(8,128)(2,1)S(1)}, bf16[1,4096,128]{2,1,0:T(8,128)(2,1)S(1)}, u32[]{:S(2)}, u32[]{:S(2)}) %collective-permute-start.11) | collective-permute-done | bytes 1048608 | tf_op jit(solution)/shard_map/ppermute | solution.py:44
  177.1 1.5 maximum_bitcast_fusion
  178.6 4.5 %collective-permute-done.12 = bf16[2,4096,128]{2,1,0:T(8,128)(2,1)} collective-permute-done((bf16[2,4096,128]{2,1,0:T(8,128)(2,1)}, bf16[2,4096,128]{2,1,0:T(8,128)(2,1)}, u32[]{:S(2)}, u32[]{:S(2)}) %collective-permute-start.12) | collective-permute-done | bytes 2097184 | tf_op jit(solution)/shard_map/ppermute | solution.py:44
  183.1 1.9 select_bitcast_fusion.1
  190.1 1.9 collective-permute-start.15
  193.4 2.5 %collective-permute-done.15 = f32[256,128]{0,1:T(8,128)S(1)} collective-permute-done((f32[256,128]{0,1:T(8,128)S(1)}, f32[256,128]{0,1:T(8,128)S(1)}, u32[]{:S(2)}, u32[]{:S(2)}) %collective-permute-start.15) | collective-permute-done | bytes 131104 | tf_op jit(solution)/shard_map/ppermute | solution.py:98
  195.9 8.1 %collective-permute-done.14 = f32[256,128]{0,1:T(8,128)S(1)} collective-permute-done((f32[256,128]{0,1:T(8,128)S(1)}, f32[256,128]{0,1:T(8,128)S(1)}, u32[]{:S(2)}, u32[]{:S(2)}) %collective-permute-start.14) | collective-permute-done | bytes 131104 | tf_op jit(solution)/shard_map/ppermute | solution.py:98
  (125 shorter events, 30.2 us)
Async XLA Ops:
  7.2 6.5 %copy-start = (bf16[256,128]{1,0:T(8,128)(2,1)S(1)}, bf16[256,128]{1,0:T(8,128)(2,1)}, u32[]{:S(2)}) copy-start(bf16[256,128]{1,0:T(8,128)(2,1)} %param.6) | copy-start | bytes 196612
  7.2 103.5 %all-gather.2.cloned.1.call-start = ((), (), s32[]{:S(2)}) async-start(), calls=%async_computation | async-start | bytes 1114112 | tf_op jit(solution)/shard_map/all_gather | solution.py:125
  15.9 1.7 copy-start.7
  15.9 2.7 %copy-start.10 = (bf16[4,1,1024,256]{3,2,1,0:T(8,128)(2,1)S(1)}, bf16[4,1,1024,256]{3,2,1,0:T(8,128)(2,1)}, u32[]{:S(2)}) copy-start(bf16[4,1,1024,256]{3,2,1,0:T(8,128)(2,1)} %get-tuple-element.23) | copy-start | bytes 6291460
  17.0 39.0 %collective-permute-start.6 = (f32[2,1024,128]{2,1,0:T(8,128)}, f32[2,1024,128]{2,1,0:T(8,128)}, u32[]{:S(2)}, u32[]{:S(2)}) collective-permute-start(f32[2,1024,128]{2,1,0:T(8,128)} %select_bitcast_fusion.4), channel_id=1, source_target_pairs={{0,1},{1,0},{2,3},{3,2},{4,5},{5,4},{6,7},{7,6},{8,9},{9,8},{10,11... | collective-permute-start | bytes 3145736 | tf_op jit(solution)/shard_map/ppermute | solution.py:44
  19.4 1.7 copy-start.5
  20.6 37.7 %collective-permute-start.4 = (f32[2,1024,128]{2,1,0:T(8,128)}, f32[2,1024,128]{2,1,0:T(8,128)}, u32[]{:S(2)}, u32[]{:S(2)}) collective-permute-start(f32[2,1024,128]{2,1,0:T(8,128)} %select_bitcast_fusion.5), channel_id=1, source_target_pairs={{0,1},{1,0},{2,3},{3,2},{4,5},{5,4},{6,7},{7,6},{8,9},{9,8},{10,11... | collective-permute-start | bytes 3145736 | tf_op jit(solution)/shard_map/ppermute | solution.py:44
  21.7 1.7 copy-start.3
  21.7 2.7 %copy-start.9 = (bf16[4,1,1024,256]{3,2,1,0:T(8,128)(2,1)S(1)}, bf16[4,1,1024,256]{3,2,1,0:T(8,128)(2,1)}, u32[]{:S(2)}) copy-start(bf16[4,1,1024,256]{3,2,1,0:T(8,128)(2,1)} %get-tuple-element.22) | copy-start | bytes 6291460
  22.9 39.1 %collective-permute-start.2 = (f32[2,1024,128]{2,1,0:T(8,128)}, f32[2,1024,128]{2,1,0:T(8,128)}, u32[]{:S(2)}, u32[]{:S(2)}) collective-permute-start(f32[2,1024,128]{2,1,0:T(8,128)} %select_bitcast_fusion.6), channel_id=1, source_target_pairs={{0,1},{1,0},{2,3},{3,2},{4,5},{5,4},{6,7},{7,6},{8,9},{9,8},{10,11... | collective-permute-start | bytes 3145736 | tf_op jit(solution)/shard_map/ppermute | solution.py:44
  25.2 1.6 copy-start.11
  26.3 37.6 %collective-permute-start = (f32[2,1024,128]{2,1,0:T(8,128)}, f32[2,1024,128]{2,1,0:T(8,128)S(1)}, u32[]{:S(2)}, u32[]{:S(2)}) collective-permute-start(f32[2,1024,128]{2,1,0:T(8,128)} %select_bitcast_fusion.7), channel_id=1, source_target_pairs={{0,1},{1,0},{2,3},{3,2},{4,5},{5,4},{6,7},{7,6},{8,9},{9,8},{10,11... | collective-permute-start | bytes 3145736 | tf_op jit(solution)/shard_map/ppermute | solution.py:44
  52.6 1.0 copy-start.2
  56.0 2.5 %copy-start.6 = (f32[2,2,1024,128]{3,2,0,1:T(8,128)S(1)}, f32[2,2,1024,128]{3,2,0,1:T(8,128)}, u32[]{:S(2)}) copy-start(f32[2,2,1024,128]{3,2,0,1:T(8,128)} %copy-done.5) | copy-start | bytes 6291460
  58.2 3.7 %copy-start.4 = (f32[2,2,1024,128]{3,2,0,1:T(8,128)S(1)}, f32[2,2,1024,128]{3,2,0,1:T(8,128)}, u32[]{:S(2)}) copy-start(f32[2,2,1024,128]{3,2,0,1:T(8,128)} %copy-done.3) | copy-start | bytes 6291460
  58.2 14.8 %collective-permute-start.7 = (f32[1,1024,128]{2,1,0:T(8,128)S(1)}, f32[1,1024,128]{2,1,0:T(8,128)S(1)}, u32[]{:S(2)}, u32[]{:S(2)}) collective-permute-start(f32[1,1024,128]{2,1,0:T(8,128)S(1)} %select_bitcast_fusion.8), channel_id=1, source_target_pairs={{0,2},{1,3},{2,0},{3,1},{4,6},{5,7},{6,4},{7,5},{8,10},{9,11},{10,... | collective-permute-start | bytes 1572872 | tf_op jit(solution)/shard_map/ppermute | solution.py:44
  60.2 24.1 %collective-permute-start.5 = (f32[1,1024,128]{2,1,0:T(8,128)S(1)}, f32[1,1024,128]{2,1,0:T(8,128)S(1)}, u32[]{:S(2)}, u32[]{:S(2)}) collective-permute-start(f32[1,1024,128]{2,1,0:T(8,128)S(1)} %select_bitcast_fusion.9), channel_id=1, source_target_pairs={{0,2},{1,3},{2,0},{3,1},{4,6},{5,7},{6,4},{7,5},{8,10},{9,11},{10,... | collective-permute-start | bytes 1572872 | tf_op jit(solution)/shard_map/ppermute | solution.py:44
  63.5 32.0 %collective-permute-start.3 = (f32[1,1024,128]{2,1,0:T(8,128)S(1)}, f32[1,1024,128]{2,1,0:T(8,128)S(1)}, u32[]{:S(2)}, u32[]{:S(2)}) collective-permute-start(f32[1,1024,128]{2,1,0:T(8,128)S(1)} %select_bitcast_fusion.10), channel_id=1, source_target_pairs={{0,2},{1,3},{2,0},{3,1},{4,6},{5,7},{6,4},{7,5},{8,10},{9,11},{10,... | collective-permute-start | bytes 1572872 | tf_op jit(solution)/shard_map/ppermute | solution.py:44
  64.1 42.0 %collective-permute-start.1 = (f32[1,1024,128]{2,1,0:T(8,128)S(1)}, f32[1,1024,128]{2,1,0:T(8,128)S(1)}, u32[]{:S(2)}, u32[]{:S(2)}) collective-permute-start(f32[1,1024,128]{2,1,0:T(8,128)S(1)} %select_bitcast_fusion.11), channel_id=1, source_target_pairs={{0,2},{1,3},{2,0},{3,1},{4,6},{5,7},{6,4},{7,5},{8,10},{9,11},{10,... | collective-permute-start | bytes 1572872 | tf_op jit(solution)/shard_map/ppermute | solution.py:44
  119.3 2.4 %copy-start.8 = (f32[16,16,32,64]{3,2,1,0:T(8,128)}, f32[16,16,32,64]{3,2,1,0:T(8,128)S(1)}, u32[]{:S(2)}) copy-start(f32[16,16,32,64]{3,2,1,0:T(8,128)S(1)} %get-tuple-element.39) | copy-start | bytes 6291460
  127.9 3.7 %collective-permute-start.10 = (f32[16,128]{1,0:T(8,128)S(1)}, f32[16,128]{1,0:T(8,128)S(1)}, u32[]{:S(2)}, u32[]{:S(2)}) collective-permute-start(f32[16,128]{1,0:T(8,128)S(1)} %psum.7), channel_id=1, source_target_pairs={{0,12},{4,0},{8,4},{12,8},{1,13},{5,1},{9,5},{13,9},{2,14},{6,2},{... | collective-permute-start | bytes 24584 | tf_op jit(solution)/shard_map/ppermute | solution.py:98
  128.0 4.7 %collective-permute-start.9 = (f32[16,128]{1,0:T(8,128)S(1)}, f32[16,128]{1,0:T(8,128)S(1)}, u32[]{:S(2)}, u32[]{:S(2)}) collective-permute-start(f32[16,128]{1,0:T(8,128)S(1)} %psum.7), channel_id=1, source_target_pairs={{0,8},{4,12},{8,0},{12,4},{1,9},{5,13},{9,1},{13,5},{2,10},{6,14},... | collective-permute-start | bytes 24584 | tf_op jit(solution)/shard_map/ppermute | solution.py:98
  128.1 5.9 %collective-permute-start.8 = (f32[16,128]{1,0:T(8,128)S(1)}, f32[16,128]{1,0:T(8,128)S(1)}, u32[]{:S(2)}, u32[]{:S(2)}) collective-permute-start(f32[16,128]{1,0:T(8,128)S(1)} %psum.7), channel_id=1, source_target_pairs={{0,4},{4,8},{8,12},{12,0},{1,5},{5,9},{9,13},{13,1},{2,6},{6,10},{... | collective-permute-start | bytes 24584 | tf_op jit(solution)/shard_map/ppermute | solution.py:98
  153.5 23.4 %collective-permute-start.11 = (bf16[1,4096,128]{2,1,0:T(8,128)(2,1)S(1)}, bf16[1,4096,128]{2,1,0:T(8,128)(2,1)S(1)}, u32[]{:S(2)}, u32[]{:S(2)}) collective-permute-start(bf16[1,4096,128]{2,1,0:T(8,128)(2,1)S(1)} %fusion.7), channel_id=1, source_target_pairs={{0,2},{1,3},{2,0},{3,1},{4,6},{5,7},{6,4},{7,5},{8,10},{9,11},{10,... | collective-permute-start | bytes 3145736 | tf_op jit(solution)/shard_map/ppermute | solution.py:44
  178.6 4.5 %collective-permute-start.12 = (bf16[2,4096,128]{2,1,0:T(8,128)(2,1)}, bf16[2,4096,128]{2,1,0:T(8,128)(2,1)}, u32[]{:S(2)}, u32[]{:S(2)}) collective-permute-start(bf16[2,4096,128]{2,1,0:T(8,128)(2,1)} %maximum_bitcast_fusion), channel_id=1, source_target_pairs={{0,1},{1,0},{2,3},{3,2},{4,5},{5,4},{6,7},{7,6},{8,9},{9,8},{10,11... | collective-permute-start | bytes 6291464 | tf_op jit(solution)/shard_map/ppermute | solution.py:44
  185.0 2.2 %slice-start = ((s8[8388608]{0:T(1024)(128)(4,1)}), s8[4194304]{0:T(1024)(128)(4,1)S(1)}, s32[]{:S(2)}) async-start(s8[8388608]{0:T(1024)(128)(4,1)} %bitcast.212), calls=%async_computation.1 | async-start | bytes 8388608
  185.4 3.2 %slice-start.1 = ((s8[8388608]{0:T(1024)(128)(4,1)}), s8[4194304]{0:T(1024)(128)(4,1)S(1)}, s32[]{:S(2)}) async-start(s8[8388608]{0:T(1024)(128)(4,1)} %bitcast.212), calls=%async_computation.2 | async-start | bytes 8388608
  188.6 16.3 %copy-start.1 = (bf16[256,128]{1,0:T(8,128)(2,1)S(1)}, bf16[256,128]{1,0:T(8,128)(2,1)}, u32[]{:S(2)}) copy-start(bf16[256,128]{1,0:T(8,128)(2,1)} %param.6) | copy-start | bytes 196612
  190.1 5.8 %collective-permute-start.15 = (f32[256,128]{0,1:T(8,128)S(1)}, f32[256,128]{0,1:T(8,128)S(1)}, u32[]{:S(2)}, u32[]{:S(2)}) collective-permute-start(f32[256,128]{0,1:T(8,128)S(1)} %bitcast.226), channel_id=1, source_target_pairs={{0,12},{4,0},{8,4},{12,8},{1,13},{5,1},{9,5},{13,9},{2,14},{6,2},{... | collective-permute-start | bytes 393224 | tf_op jit(solution)/shard_map/ppermute | solution.py:98
  191.9 12.1 %collective-permute-start.14 = (f32[256,128]{0,1:T(8,128)S(1)}, f32[256,128]{0,1:T(8,128)S(1)}, u32[]{:S(2)}, u32[]{:S(2)}) collective-permute-start(f32[256,128]{0,1:T(8,128)S(1)} %bitcast.227), channel_id=1, source_target_pairs={{0,8},{4,12},{8,0},{12,4},{1,9},{5,13},{9,1},{13,5},{2,10},{6,14},... | collective-permute-start | bytes 393224 | tf_op jit(solution)/shard_map/ppermute | solution.py:98
  192.1 11.9 %collective-permute-start.13 = (f32[256,128]{0,1:T(8,128)S(1)}, f32[256,128]{0,1:T(8,128)S(1)}, u32[]{:S(2)}, u32[]{:S(2)}) collective-permute-start(f32[256,128]{0,1:T(8,128)S(1)} %bitcast.228), channel_id=1, source_target_pairs={{0,4},{4,8},{8,12},{12,0},{1,5},{5,9},{9,13},{13,1},{2,6},{6,10},{... | collective-permute-start | bytes 393224 | tf_op jit(solution)/shard_map/ppermute | solution.py:98
Sparse Core Ops, SparseCore 0:
  10.2 40.6 all-gather.1

commit v12 on v9

--- a/solution.py
+++ b/solution.py
@@ -142,8 +142,7 @@
     capacity = 2 * slot_count // owners
     me = lax.axis_index("enc") * mp_count + lax.axis_index("mp")
 
-    all_queries, all_cand = all_gather_many(all_gather_many([queries, candidates], "mp"), "enc")
-    all_cand = all_cand.reshape(owners, slot_count)
+    gathered = all_gather_many([queries, candidates], "mp")
 
     chunks = 4 if row_share % (4 * BLK) == 0 else 1
     split_rows = hidden.reshape(mp_count, chunks, row_share // chunks, hidden.shape[1])
@@ -155,7 +154,8 @@
     ]
     if is_pow2(mp_count) and mp_count > 1:
         keeps, sends, bit = halving_steps(partials, "mp")
-        sends, all_queries, all_cand = lax.optimization_barrier((sends, all_queries, all_cand))
+        last, gathered = lax.optimization_barrier((sends[-1], gathered))
+        sends = sends[:-1] + [last]
         pieces = [k + xor_perm(t, "mp", bit) for k, t in zip(keeps, sends)]
         pieces = [p.reshape(-1, emb_width) for p in pieces]
     else:
@@ -163,6 +163,9 @@
             lax.psum_scatter(p, "mp", scatter_dimension=0, tiled=True) for p in partials
         ]
     e_pre = jnp.stack(pieces).reshape(row_share, emb_width)
+
+    all_queries, all_cand = all_gather_many(gathered, "enc")
+    all_cand = all_cand.reshape(owners, slot_count)
 
     slot_ids = jnp.arange(slot_count, dtype=jnp.int32)
     mine = (all_cand // blk_dev) == me

time: 219 us -> 181 us (0.83)
  waiting for transfers between devices: 105 us -> 68.7 us
    ppermute x8, waiting for transfers between devices: 25.5 us -> 7.16 us  [all_gather_many(): others = lax.ppermute(arrs, axis, [(i, i ^ bit) for i in range(count)])]
    ppermute x10, waiting for transfers between devices: 61.9 us -> 44.6 us  [xor_perm(): return lax.ppermute(value, axis, [(i, i ^ bit) for i in range(count)])]
    another operation x12, other arithmetic: 0.32 us -> 2.54 us  [all_gather_many(): jnp.stack([jnp.where(low, a, o), jnp.where(low, o, a)], axis=1)]
    unnamed x47 -> x43, local copies, waits for them, and re-layouts: 8.55 us -> 8.05 us
  transfers between devices with their start and end apart: 27 -> 27, of which waited for: 17 -> 14; matrix products, arithmetic and copies ran while one was open for 12% -> 19% of each run, Pallas kernels for 0% -> 0%
where the time goes in v12:
time: 181 us
  waiting for transfers between devices  68.7 us (38%)
  other arithmetic  32 us (18%)
  local copies, waits for them, and re-layouts  30.1 us (17%)
  matrix products  24.6 us (14%)
  starting transfers between devices  23.9 us (13%)
    ppermute x10, waiting for transfers between devices, xor_perm(): return lax.ppermute(value, axis, [(i, i ^ bit) for i in range(count)])  44.6 us
    ppermute x9, waiting for transfers between devices, all_sum(): lax.ppermute(value, axis, [(i, (i + k) % count) for i in range(count)])  16.9 us
    ppermute x9, starting transfers between devices, all_sum(): lax.ppermute(value, axis, [(i, (i + k) % count) for i in range(count)])  9.4 us
    unnamed x43, local copies, waits for them, and re-layouts  8.05 us
    ppermute x8, starting transfers between devices, all_gather_many(): others = lax.ppermute(arrs, axis, [(i, i ^ bit) for i in range(count)])  7.94 us
    ppermute x8, waiting for transfers between devices, all_gather_many(): others = lax.ppermute(arrs, axis, [(i, i ^ bit) for i in range(count)])  7.16 us
    select_n x8, other arithmetic, halving_steps(): sends.append(jnp.where(low, acc[:, 1], acc[:, 0]))  7.16 us
    dot_general x1, matrix products, local(): jnp.einsum('scij,scie->scje', weights, q_e, preferred_element_type=jnp.fl...  6.95 us
  transfers between devices with their start and end apart: 27, of which 14 were waited for; matrix products, arithmetic and copies ran while one was open for 19% of the time, Pallas kernels for 0%

profile of v12, /device:TPU:0, one launch (start us, length us, event | category | flops | bytes accessed | tf_op | source)
XLA Modules:
  0.0 180.6 jit_solution(6397685852089279379)
XLA Ops:
  0.7 5.7 %fusion.55 = (bf16[4,1,1024,256]{3,2,1,0:T(8,128)(2,1)}, bf16[4,1,1024,256]{3,2,1,0:T(8,128)(2,1)}, bf16[4,1,1024,256]{3,2,1,0:T(8,128)(2,1)}, bf16[4,1,1024,256]{3,2,1,0:T(8,128)(2,1)S(1)}) fusion(bf16[4,4,1024,256]{3,2,1,0:T(8,128)(2,1)} %bitcast.291), kind=kLoop, calls=%fused_computation.172 | loop fusion | bytes 16777216 | tf_op jit(solution)/shard_map/slice | solution.py:150
  6.4 2.3 %fusion.3 = f32[2,2,1024,128]{3,2,1,0:T(8,128)S(1)} fusion(bf16[256,128]{1,0:T(8,128)(2,1)S(1)} %copy-done, bf16[2,2,1024,256]{3,2,1,0:T(8,128)(2,1)} %bitcast.306), kind=kOutput, calls=%fused_computation.15 | convolution fusion | flops 268435456 | bytes 4259840 | tf_op jit(solution)/shard_map/dot_general | solution.py:150
  9.6 2.9 %collective-permute-start.1 = (bf16[1,8,32,128]{3,2,1,0:T(8,128)(2,1)S(1)}, bf16[1,8,32,128]{3,2,1,0:T(8,128)(2,1)S(1)}, u32[]{:S(2)}, u32[]{:S(2)}) collective-permute-start(bf16[1,8,32,128]{3,2,1,0:T(8,128)(2,1)S(1)} %bitcast.319), channel_id=1, source_target_pairs={{0,2},{1,3},{2,0},{3,1},{4,6},{5,7},{6,4},{7,5},{8,10},{9,11},{10,... | collective-permute-start | bytes 196616 | tf_op jit(solution)/shard_map/ppermute | solution.py:95
  17.9 2.3 %fusion.12 = f32[2,2,1024,128]{3,2,0,1:T(8,128)S(1)} fusion(bf16[256,128]{1,0:T(8,128)(2,1)S(1)} %copy-done, bf16[2,2,1024,256]{3,2,1,0:T(8,128)(2,1)} %bitcast.303), kind=kOutput, calls=%fused_computation.26 | convolution fusion | flops 268435456 | bytes 4259840 | tf_op jit(solution)/shard_map/dot_general | solution.py:150
  23.3 2.0 %collective-permute-done.4 = s32[2,8,16]{2,1,0:T(8,128)S(1)} collective-permute-done((s32[2,8,16]{2,1,0:T(8,128)S(1)}, s32[2,8,16]{2,1,0:T(8,128)S(1)}, u32[]{:S(2)}, u32[]{:S(2)}) %collective-permute-start.4) | collective-permute-done | bytes 1056 | tf_op jit(solution)/shard_map/ppermute | solution.py:95
  26.8 2.1 %fusion.24 = f32[1,2,1024,128]{3,2,1,0:T(8,128)S(1)} fusion(f32[2,1024,128]{2,1,0:T(8,128)} %collective-permute-done, f32[2,2,1024,128]{3,2,1,0:T(8,128)} %copy-done.5, pred[]{:T(512)S(6)} %eq.93), kind=kLoop, calls=%fused_computation.43 | loop fusion | flops 524288 | bytes 4194305 | tf_op jit(solution)/shard_map/reshape | solution.py:59
  29.8 3.1 %collective-permute-start.5 = (s32[1,32,16]{2,1,0:T(8,128)S(1)}, s32[1,32,16]{2,1,0:T(8,128)S(1)}, u32[]{:S(2)}, u32[]{:S(2)}) collective-permute-start(s32[1,32,16]{2,1,0:T(8,128)S(1)} %bitcast.317), channel_id=1, source_target_pairs={{0,8},{4,12},{8,0},{12,4},{1,9},{5,13},{9,1},{13,5},{2,10},{6,14},... | collective-permute-start | bytes 6152 | tf_op jit(solution)/shard_map/ppermute | solution.py:95
  33.0 1.8 %collective-permute-start.15 = (f32[1,1024,128]{2,1,0:T(8,128)}, f32[1,1024,128]{2,1,0:T(8,128)}, u32[]{:S(2)}, u32[]{:S(2)}) collective-permute-start(f32[1,1024,128]{2,1,0:T(8,128)} %select_bitcast_fusion.13), channel_id=1, source_target_pairs={{0,2},{1,3},{2,0},{3,1},{4,6},{5,7},{6,4},{7,5},{8,10},{9,11},{10,... | collective-permute-start | bytes 1572872 | tf_op jit(solution)/shard_map/ppermute | solution.py:44
  40.0 1.6 collective-permute-start.12
  44.3 3.9 %collective-permute-done.6 = s32[2,32,16]{2,1,0:T(8,128)S(1)} collective-permute-done((s32[2,32,16]{2,1,0:T(8,128)S(1)}, s32[2,32,16]{2,1,0:T(8,128)S(1)}, u32[]{:S(2)}, u32[]{:S(2)}) %collective-permute-start.6) | collective-permute-done | bytes 4128 | tf_op jit(solution)/shard_map/ppermute | solution.py:95
  50.2 1.9 %gather_fusion.3 = s32[256]{0:T(256)S(1)} fusion(s32[16,128]{1,0:T(8,128)S(1)} %reshape_reshape_reshape.2, s32[256]{0:T(256)S(1)} %reshape.776), kind=kCustom, calls=%fused_computation.3 | custom fusion | bytes 4096 | tf_op jit(solution)/shard_map/jit(take_along_axis)/gather | solution.py:177
  52.8 1.9 %gather_fusion = s32[256]{0:T(256)S(1)} fusion(s32[256]{0:T(256)S(1)} %copy-done.2, s32[1024]{0:T(1024)S(1)} %pad_clamp_fusion.2), kind=kCustom, calls=%fused_computation | custom fusion | bytes 3072 | tf_op jit(solution)/shard_map/gather | solution.py:15
  60.9 9.7 %collective-permute-done.12 = f32[1,1024,128]{2,1,0:T(8,128)} collective-permute-done((f32[1,1024,128]{2,1,0:T(8,128)}, f32[1,1024,128]{2,1,0:T(8,128)}, u32[]{:S(2)}, u32[]{:S(2)}) %collective-permute-start.12) | collective-permute-done | bytes 524320 | tf_op jit(solution)/shard_map/ppermute | solution.py:44
  71.7 9.0 %collective-permute-done.10 = f32[1,1024,128]{2,1,0:T(8,128)} collective-permute-done((f32[1,1024,128]{2,1,0:T(8,128)}, f32[1,1024,128]{2,1,0:T(8,128)}, u32[]{:S(2)}, u32[]{:S(2)}) %collective-permute-start.10) | collective-permute-done | bytes 524320 | tf_op jit(solution)/shard_map/ppermute | solution.py:44
  83.3 3.1 %gather_fusion.2 = bf16[256,64,128]{2,1,0:T(8,128)(2,1)} fusion(bf16[64,64,128]{2,1,0:T(8,128)(2,1)S(1)} %multiply_convert_fusion.1, s32[1024]{0:T(1024)S(1)} %pad_clamp_fusion), kind=kCustom, calls=%fused_computation.2 | custom fusion | bytes 8389632 | tf_op jit(solution)/shard_map/gather | solution.py:188
  87.7 2.2 %gather_fusion.1 = bf16[256,32,128]{2,1,0:T(8,128)(2,1)} fusion(bf16[128,32,128]{2,1,0:T(8,128)(2,1)S(1)} %bitcast.299, s32[1024]{0:T(1024)S(1)} %pad_clamp_fusion.1), kind=kCustom, calls=%fused_computation.1 | custom fusion | bytes 4195328 | tf_op jit(solution)/shard_map/gather | solution.py:181
  89.9 5.2 %select_reduce_fusion = (f32[16,16,32]{2,1,0:T(8,128)S(1)}, f32[16,16,32,64]{3,2,1,0:T(8,128)S(1)}) fusion(pred[16,16,64]{2,1,0:T(8,128)(4,1)S(1)} %add_compare_fusion, bf16[16,16,32,128]{3,2,1,0:T(8,128)(2,1)} %bitcast.301, bf16[16,16,64,128]{3,2,1,0:T(8,128)(2,1)} %bitcast.298), kind=kOutput, calls=%fused_computation.11 | convolution fusion | flops 135258112 | bytes 8437760 | tf_op jit(solution)/shard_map/scie,scje->scij/dot_general | solution.py:190
  95.2 2.6 %fusion.2 = f32[16,16,32]{2,1,0:T(8,128)S(1)} fusion(f32[16,16,32,64]{3,2,1,0:T(8,128)S(1)} %get-tuple-element.61, f32[16,16,32]{2,1,0:T(8,128)S(1)} %get-tuple-element.60, pred[16,16,64]{2,1,0:T(8,128)(4,1)S(1)} %add_compare_fusion), kind=kLoop, calls=%fused_computation.12 | loop fusion | flops 1564672 | bytes 2179072 | tf_op jit(solution)/shard_map/reduce_sum | solution.py:22
  99.8 2.0 %collective-permute-done.17 = f32[16,128]{1,0:T(8,128)S(1)} collective-permute-done((f32[16,128]{1,0:T(8,128)S(1)}, f32[16,128]{1,0:T(8,128)S(1)}, u32[]{:S(2)}, u32[]{:S(2)}) %collective-permute-start.17) | collective-permute-done | bytes 8224 | tf_op jit(solution)/shard_map/ppermute | solution.py:118
  102.7 3.6 %collective-permute-start.21 = (f32[16,128]{1,0:T(8,128)S(1)}, f32[16,128]{1,0:T(8,128)S(1)}, u32[]{:S(2)}, u32[]{:S(2)}) collective-permute-start(f32[16,128]{1,0:T(8,128)S(1)} %fusion.62), channel_id=1, source_target_pairs={{0,12},{4,0},{8,4},{12,8},{1,13},{5,1},{9,5},{13,9},{2,14},{6,2},{... | collective-permute-start | bytes 24584 | tf_op jit(solution)/shard_map/ppermute | solution.py:118
  107.7 3.2 %collective-permute-done.20 = f32[16,128]{1,0:T(8,128)S(1)} collective-permute-done((f32[16,128]{1,0:T(8,128)S(1)}, f32[16,128]{1,0:T(8,128)S(1)}, u32[]{:S(2)}, u32[]{:S(2)}) %collective-permute-start.20) | collective-permute-done | bytes 8224 | tf_op jit(solution)/shard_map/ppermute | solution.py:118
  112.5 1.9 %gather_fusion.4 = f32[256]{0:T(256)S(1)} fusion(f32[16,128]{1,0:T(8,128)S(1)} %reshape.748, s32[256]{0:T(256)S(1)} %reshape.776), kind=kCustom, calls=%fused_computation.4 | custom fusion | bytes 4096 | tf_op jit(solution)/shard_map/jit(take_along_axis)/gather | solution.py:200
  114.5 6.9 %multiply_convert_fusion = bf16[16,16,64,128]{3,2,1,0:T(8,128)(2,1)S(1)} fusion(f32[16,16]{1,0:T(8,128)S(1)} %select_multiply_fusion, bf16[16,16,32,128]{3,2,1,0:T(8,128)(2,1)} %bitcast.302, f32[16,16,32,64]{3,2,1,0:T(8,128)} %copy-done.8, f32[16,16,32]{2,1,0:T(8,128)S(1)} %fusion.2, f32[16,16,32]{2,1,0:T(8,128)S(1)} %get-tuple-element.60, ...), kind=kOutput, calls=%fused_computation.5 | convolution fusion | flops 140509184 | bytes 8471552 | tf_op jit(solution)/shard_map/scij,scie->scje/dot_general | solution.py:193
  121.4 5.0 %fusion.14 = (f32[64,64]{0,1:T(8,128)S(1)}, f32[64,64,128]{2,0,1:T(8,128)}) fusion(f32[64,64,128]{2,1,0:T(8,128)S(1)} %bitcast.295, bf16[16,16,64,128]{3,2,1,0:T(8,128)(2,1)S(1)} %multiply_convert_fusion, s32[16,16]{0,1:T(8,128)S(1)} %copy.179, pred[16,16]{0,1:T(8,128)(4,1)S(1)} %copy.180), kind=kOutput, calls=%fused_computation.29 | convolution fusion | flops 269512704 | bytes 8406272 | tf_op jit(solution)/shard_map/scb,scje->bje/dot_general | solution.py:204
  126.5 2.8 %copy.183 = f32[64,64,128]{2,1,0:T(8,128)S(1)} copy(f32[64,64,128]{2,0,1:T(8,128)} %get-tuple-element.63) | data formatting | bytes 4194304 | tf_op jit(solution)/shard_map/scb,scje->bje/dot_general | solution.py:204
  129.4 1.9 %fusion.7 = bf16[1,4096,128]{2,1,0:T(8,128)(2,1)S(1)} fusion(f32[4096]{0:T(1024)S(1)} %mul.134, f32[4096]{0:T(1024)S(1)} %multiply_multiply_fusion, f32[4096]{0:T(1024)S(1)} %bitcast.316, f32[1,4096,128]{2,1,0:T(8,128)S(1)} %bitcast.296, f32[1,4096,128]{2,1,0:T(8,128)S(1)} %bitcast.300), kind=kLoop, calls=%fused_computation.20 | loop fusion | flops 2621440 | bytes 5292032 | tf_op jit(solution)/shard_map/convert_element_type | solution.py:212
  132.0 21.4 %collective-permute-done.22 = bf16[1,4096,128]{2,1,0:T(8,128)(2,1)S(1)} collective-permute-done((bf16[1,4096,128]{2,1,0:T(8,128)(2,1)S(1)}, bf16[1,4096,128]{2,1,0:T(8,128)(2,1)S(1)}, u32[]{:S(2)}, u32[]{:S(2)}) %collective-permute-start.22) | collective-permute-done | bytes 1048608 | tf_op jit(solution)/shard_map/ppermute | solution.py:44
  155.1 4.5 %collective-permute-done.23 = bf16[2,4096,128]{2,1,0:T(8,128)(2,1)} collective-permute-done((bf16[2,4096,128]{2,1,0:T(8,128)(2,1)}, bf16[2,4096,128]{2,1,0:T(8,128)(2,1)}, u32[]{:S(2)}, u32[]{:S(2)}) %collective-permute-start.23) | collective-permute-done | bytes 2097184 | tf_op jit(solution)/shard_map/ppermute | solution.py:44
  159.6 1.9 %select_bitcast_fusion.1 = (bf16[2,1,4096,128]{3,2,0,1:T(8,128)(2,1)S(1)}, bf16[2,1,4096,128]{3,2,0,1:T(8,128)(2,1)S(1)}) fusion(bf16[2,4096,128]{2,1,0:T(8,128)(2,1)} %collective-permute-done.23, pred[]{:T(512)S(6)} %eq.93, bf16[1,1,4096,128]{3,2,1,0:T(8,128)(2,1)S(1)} %get-tuple-element.35, bf16[1,1,4096,128]{3,2,1,0:T(8,128)(2,1)S(1)} %get-tuple-element.34), kind=kLoop, calls=%fused_computation.31 | loop fusion | flops 3145728 | bytes 8388609 | tf_op jit(solution)/shard_map/stack | solution.py:81
  167.6 1.9 %collective-permute-start.24 = (f32[256,128]{0,1:T(8,128)S(1)}, f32[256,128]{0,1:T(8,128)S(1)}, u32[]{:S(2)}, u32[]{:S(2)}) collective-permute-start(f32[256,128]{0,1:T(8,128)S(1)} %bitcast.311), channel_id=1, source_target_pairs={{0,4},{4,8},{8,12},{12,0},{1,5},{5,9},{9,13},{13,1},{2,6},{6,10},{... | collective-permute-start | bytes 393224 | tf_op jit(solution)/shard_map/ppermute | solution.py:118
  170.1 3.2 %collective-permute-done.26 = f32[256,128]{0,1:T(8,128)S(1)} collective-permute-done((f32[256,128]{0,1:T(8,128)S(1)}, f32[256,128]{0,1:T(8,128)S(1)}, u32[]{:S(2)}, u32[]{:S(2)}) %collective-permute-start.26) | collective-permute-done | bytes 131104 | tf_op jit(solution)/shard_map/ppermute | solution.py:118
  173.3 6.4 %collective-permute-done.25 = f32[256,128]{0,1:T(8,128)S(1)} collective-permute-done((f32[256,128]{0,1:T(8,128)S(1)}, f32[256,128]{0,1:T(8,128)S(1)}, u32[]{:S(2)}, u32[]{:S(2)}) %collective-permute-start.25) | collective-permute-done | bytes 131104 | tf_op jit(solution)/shard_map/ppermute | solution.py:118
  (176 shorter events, 49.1 us)
Async XLA Ops:
  0.6 5.8 %copy-start = (bf16[256,128]{1,0:T(8,128)(2,1)S(1)}, bf16[256,128]{1,0:T(8,128)(2,1)}, u32[]{:S(2)}) copy-start(bf16[256,128]{1,0:T(8,128)(2,1)} %param.6) | copy-start | bytes 196612
  8.8 18.0 %collective-permute-start = (f32[2,1024,128]{2,1,0:T(8,128)S(1)}, f32[2,1024,128]{2,1,0:T(8,128)}, u32[]{:S(2)}, u32[]{:S(2)}) collective-permute-start(f32[2,1024,128]{2,1,0:T(8,128)S(1)} %select_bitcast_fusion.7), channel_id=1, source_target_pairs={{0,1},{1,0},{2,3},{3,2},{4,5},{5,4},{6,7},{7,6},{8,9},{9,8},{10,11... | collective-permute-start | bytes 3145736 | tf_op jit(solution)/shard_map/ppermute | solution.py:44
  9.6 13.6 %collective-permute-start.1 = (bf16[1,8,32,128]{3,2,1,0:T(8,128)(2,1)S(1)}, bf16[1,8,32,128]{3,2,1,0:T(8,128)(2,1)S(1)}, u32[]{:S(2)}, u32[]{:S(2)}) collective-permute-start(bf16[1,8,32,128]{3,2,1,0:T(8,128)(2,1)S(1)} %bitcast.319), channel_id=1, source_target_pairs={{0,2},{1,3},{2,0},{3,1},{4,6},{5,7},{6,4},{7,5},{8,10},{9,11},{10,... | collective-permute-start | bytes 196616 | tf_op jit(solution)/shard_map/ppermute | solution.py:95
  12.5 10.2 %collective-permute-start.3 = (s32[1,8,16]{2,1,0:T(8,128)S(1)}, s32[1,8,16]{2,1,0:T(8,128)S(1)}, u32[]{:S(2)}, u32[]{:S(2)}) collective-permute-start(s32[1,8,16]{2,1,0:T(8,128)S(1)} %bitcast.327), channel_id=1, source_target_pairs={{0,2},{1,3},{2,0},{3,1},{4,6},{5,7},{6,4},{7,5},{8,10},{9,11},{10,... | collective-permute-start | bytes 1544 | tf_op jit(solution)/shard_map/ppermute | solution.py:95
  14.4 18.6 %collective-permute-start.13 = (f32[2,1024,128]{2,1,0:T(8,128)}, f32[2,1024,128]{2,1,0:T(8,128)}, u32[]{:S(2)}, u32[]{:S(2)}) collective-permute-start(f32[2,1024,128]{2,1,0:T(8,128)} %select_bitcast_fusion.4), channel_id=1, source_target_pairs={{0,1},{1,0},{2,3},{3,2},{4,5},{5,4},{6,7},{7,6},{8,9},{9,8},{10,11... | collective-permute-start | bytes 3145736 | tf_op jit(solution)/shard_map/ppermute | solution.py:44
  17.8 19.3 %collective-permute-start.11 = (f32[2,1024,128]{2,1,0:T(8,128)}, f32[2,1024,128]{2,1,0:T(8,128)}, u32[]{:S(2)}, u32[]{:S(2)}) collective-permute-start(f32[2,1024,128]{2,1,0:T(8,128)} %select_bitcast_fusion.5), channel_id=1, source_target_pairs={{0,1},{1,0},{2,3},{3,2},{4,5},{5,4},{6,7},{7,6},{8,9},{9,8},{10,11... | collective-permute-start | bytes 3145736 | tf_op jit(solution)/shard_map/ppermute | solution.py:44
  22.7 17.3 %collective-permute-start.9 = (f32[2,1024,128]{2,1,0:T(8,128)}, f32[2,1024,128]{2,1,0:T(8,128)S(1)}, u32[]{:S(2)}, u32[]{:S(2)}) collective-permute-start(f32[2,1024,128]{2,1,0:T(8,128)} %select_bitcast_fusion.6), channel_id=1, source_target_pairs={{0,1},{1,0},{2,3},{3,2},{4,5},{5,4},{6,7},{7,6},{8,9},{9,8},{10,11... | collective-permute-start | bytes 3145736 | tf_op jit(solution)/shard_map/ppermute | solution.py:44
  23.2 2.2 %collective-permute-start.4 = (s32[2,8,16]{2,1,0:T(8,128)S(1)}, s32[2,8,16]{2,1,0:T(8,128)S(1)}, u32[]{:S(2)}, u32[]{:S(2)}) collective-permute-start(s32[2,8,16]{2,1,0:T(8,128)S(1)} %add_bitcast_fusion.2), channel_id=1, source_target_pairs={{0,1},{1,0},{2,3},{3,2},{4,5},{5,4},{6,7},{7,6},{8,9},{9,8},{10,11... | collective-permute-start | bytes 3080 | tf_op jit(solution)/shard_map/ppermute | solution.py:95
  25.4 1.3 collective-permute-start.2
  26.8 6.1 %copy-start.15 = (bf16[2,2,8,32,128]{4,3,2,1,0:T(8,128)(2,1)}, bf16[2,2,8,32,128]{4,3,2,1,0:T(8,128)(2,1)S(1)}, u32[]{:S(2)}) copy-start(bf16[2,2,8,32,128]{4,3,2,1,0:T(8,128)(2,1)S(1)} %pad_maximum_fusion.4) | copy-start | bytes 786436
  26.8 8.0 %copy-start.4 = (f32[2,2,1024,128]{3,2,0,1:T(8,128)S(1)}, f32[2,2,1024,128]{3,2,0,1:T(8,128)}, u32[]{:S(2)}) copy-start(f32[2,2,1024,128]{3,2,0,1:T(8,128)} %copy-done.3) | copy-start | bytes 6291460
  29.8 11.9 %collective-permute-start.5 = (s32[1,32,16]{2,1,0:T(8,128)S(1)}, s32[1,32,16]{2,1,0:T(8,128)S(1)}, u32[]{:S(2)}, u32[]{:S(2)}) collective-permute-start(s32[1,32,16]{2,1,0:T(8,128)S(1)} %bitcast.317), channel_id=1, source_target_pairs={{0,8},{4,12},{8,0},{12,4},{1,9},{5,13},{9,1},{13,5},{2,10},{6,14},... | collective-permute-start | bytes 6152 | tf_op jit(solution)/shard_map/ppermute | solution.py:95
  32.9 22.8 %collective-permute-start.7 = (bf16[1,32,32,128]{3,2,1,0:T(8,128)(2,1)S(1)}, bf16[1,32,32,128]{3,2,1,0:T(8,128)(2,1)}, u32[]{:S(2)}, u32[]{:S(2)}) collective-permute-start(bf16[1,32,32,128]{3,2,1,0:T(8,128)(2,1)S(1)} %bitcast.307), channel_id=1, source_target_pairs={{0,8},{4,12},{8,0},{12,4},{1,9},{5,13},{9,1},{13,5},{2,10},{6,14},... | collective-permute-start | bytes 786440 | tf_op jit(solution)/shard_map/ppermute | solution.py:95
  33.0 25.6 %collective-permute-start.15 = (f32[1,1024,128]{2,1,0:T(8,128)}, f32[1,1024,128]{2,1,0:T(8,128)}, u32[]{:S(2)}, u32[]{:S(2)}) collective-permute-start(f32[1,1024,128]{2,1,0:T(8,128)} %select_bitcast_fusion.13), channel_id=1, source_target_pairs={{0,2},{1,3},{2,0},{3,1},{4,6},{5,7},{6,4},{7,5},{8,10},{9,11},{10,... | collective-permute-start | bytes 1572872 | tf_op jit(solution)/shard_map/ppermute | solution.py:44
  37.2 22.6 %collective-permute-start.14 = (f32[1,1024,128]{2,1,0:T(8,128)}, f32[1,1024,128]{2,1,0:T(8,128)}, u32[]{:S(2)}, u32[]{:S(2)}) collective-permute-start(f32[1,1024,128]{2,1,0:T(8,128)} %select_bitcast_fusion.8), channel_id=1, source_target_pairs={{0,2},{1,3},{2,0},{3,1},{4,6},{5,7},{6,4},{7,5},{8,10},{9,11},{10,... | collective-permute-start | bytes 1572872 | tf_op jit(solution)/shard_map/ppermute | solution.py:44
  40.0 30.6 %collective-permute-start.12 = (f32[1,1024,128]{2,1,0:T(8,128)}, f32[1,1024,128]{2,1,0:T(8,128)}, u32[]{:S(2)}, u32[]{:S(2)}) collective-permute-start(f32[1,1024,128]{2,1,0:T(8,128)} %select_bitcast_fusion.9), channel_id=1, source_target_pairs={{0,2},{1,3},{2,0},{3,1},{4,6},{5,7},{6,4},{7,5},{8,10},{9,11},{10,... | collective-permute-start | bytes 1572872 | tf_op jit(solution)/shard_map/ppermute | solution.py:44
  41.8 6.4 %collective-permute-start.6 = (s32[2,32,16]{2,1,0:T(8,128)S(1)}, s32[2,32,16]{2,1,0:T(8,128)S(1)}, u32[]{:S(2)}, u32[]{:S(2)}) collective-permute-start(s32[2,32,16]{2,1,0:T(8,128)S(1)} %add_bitcast_fusion.1), channel_id=1, source_target_pairs={{0,4},{4,0},{8,12},{12,8},{1,5},{5,1},{9,13},{13,9},{2,6},{6,2},{1... | collective-permute-start | bytes 12296 | tf_op jit(solution)/shard_map/ppermute | solution.py:95
  48.2 32.5 %collective-permute-start.10 = (f32[1,1024,128]{2,1,0:T(8,128)}, f32[1,1024,128]{2,1,0:T(8,128)}, u32[]{:S(2)}, u32[]{:S(2)}) collective-permute-start(f32[1,1024,128]{2,1,0:T(8,128)} %select_bitcast_fusion.10), channel_id=1, source_target_pairs={{0,2},{1,3},{2,0},{3,1},{4,6},{5,7},{6,4},{7,5},{8,10},{9,11},{10,... | collective-permute-start | bytes 1572872 | tf_op jit(solution)/shard_map/ppermute | solution.py:44
  58.5 12.0 %copy-start.12 = (f32[1,2,1024,128]{3,2,1,0:T(8,128)S(1)}, f32[1,2,1024,128]{3,2,1,0:T(8,128)}, u32[]{:S(2)}) copy-start(f32[1,2,1024,128]{3,2,1,0:T(8,128)} %copy-done.11) | copy-start | bytes 3145732
  58.5 27.8 %collective-permute-start.8 = (bf16[2,32,32,128]{3,2,1,0:T(8,128)(2,1)}, bf16[2,32,32,128]{3,2,1,0:T(8,128)(2,1)}, u32[]{:S(2)}, u32[]{:S(2)}) collective-permute-start(bf16[2,32,32,128]{3,2,1,0:T(8,128)(2,1)} %maximum_bitcast_fusion.1), channel_id=1, source_target_pairs={{0,4},{4,0},{8,12},{12,8},{1,5},{5,1},{9,13},{13,9},{2,6},{6,2},{1... | collective-permute-start | bytes 1572872 | tf_op jit(solution)/shard_map/ppermute | solution.py:95
  98.0 1.8 %collective-permute-start.18 = (f32[16,128]{1,0:T(8,128)S(1)}, f32[16,128]{1,0:T(8,128)S(1)}, u32[]{:S(2)}, u32[]{:S(2)}) collective-permute-start(f32[16,128]{1,0:T(8,128)S(1)} %select_reduce_fusion.1), channel_id=1, source_target_pairs={{0,3},{1,0},{2,1},{3,2},{4,7},{5,4},{6,5},{7,6},{8,11},{9,8},{10,9... | collective-permute-start | bytes 24584 | tf_op jit(solution)/shard_map/ppermute | solution.py:118
  98.1 3.7 %collective-permute-start.17 = (f32[16,128]{1,0:T(8,128)S(1)}, f32[16,128]{1,0:T(8,128)S(1)}, u32[]{:S(2)}, u32[]{:S(2)}) collective-permute-start(f32[16,128]{1,0:T(8,128)S(1)} %select_reduce_fusion.1), channel_id=1, source_target_pairs={{0,2},{1,3},{2,0},{3,1},{4,6},{5,7},{6,4},{7,5},{8,10},{9,11},{10,... | collective-permute-start | bytes 24584 | tf_op jit(solution)/shard_map/ppermute | solution.py:118
  99.7 3.1 %collective-permute-start.16 = (f32[16,128]{1,0:T(8,128)S(1)}, f32[16,128]{1,0:T(8,128)S(1)}, u32[]{:S(2)}, u32[]{:S(2)}) collective-permute-start(f32[16,128]{1,0:T(8,128)S(1)} %select_reduce_fusion.1), channel_id=1, source_target_pairs={{0,1},{1,2},{2,3},{3,0},{4,5},{5,6},{6,7},{7,4},{8,9},{9,10},{10,1... | collective-permute-start | bytes 24584 | tf_op jit(solution)/shard_map/ppermute | solution.py:118
  102.7 5.0 %collective-permute-start.21 = (f32[16,128]{1,0:T(8,128)S(1)}, f32[16,128]{1,0:T(8,128)S(1)}, u32[]{:S(2)}, u32[]{:S(2)}) collective-permute-start(f32[16,128]{1,0:T(8,128)S(1)} %fusion.62), channel_id=1, source_target_pairs={{0,12},{4,0},{8,4},{12,8},{1,13},{5,1},{9,5},{13,9},{2,14},{6,2},{... | collective-permute-start | bytes 24584 | tf_op jit(solution)/shard_map/ppermute | solution.py:118
  106.4 4.5 %collective-permute-start.20 = (f32[16,128]{1,0:T(8,128)S(1)}, f32[16,128]{1,0:T(8,128)S(1)}, u32[]{:S(2)}, u32[]{:S(2)}) collective-permute-start(f32[16,128]{1,0:T(8,128)S(1)} %fusion.62), channel_id=1, source_target_pairs={{0,8},{4,12},{8,0},{12,4},{1,9},{5,13},{9,1},{13,5},{2,10},{6,14},... | collective-permute-start | bytes 24584 | tf_op jit(solution)/shard_map/ppermute | solution.py:118
  106.4 5.4 %collective-permute-start.19 = (f32[16,128]{1,0:T(8,128)S(1)}, f32[16,128]{1,0:T(8,128)S(1)}, u32[]{:S(2)}, u32[]{:S(2)}) collective-permute-start(f32[16,128]{1,0:T(8,128)S(1)} %fusion.62), channel_id=1, source_target_pairs={{0,4},{4,8},{8,12},{12,0},{1,5},{5,9},{9,13},{13,1},{2,6},{6,10},{... | collective-permute-start | bytes 24584 | tf_op jit(solution)/shard_map/ppermute | solution.py:118
  131.3 22.1 %collective-permute-start.22 = (bf16[1,4096,128]{2,1,0:T(8,128)(2,1)S(1)}, bf16[1,4096,128]{2,1,0:T(8,128)(2,1)S(1)}, u32[]{:S(2)}, u32[]{:S(2)}) collective-permute-start(bf16[1,4096,128]{2,1,0:T(8,128)(2,1)S(1)} %fusion.7), channel_id=1, source_target_pairs={{0,2},{1,3},{2,0},{3,1},{4,6},{5,7},{6,4},{7,5},{8,10},{9,11},{10,... | collective-permute-start | bytes 3145736 | tf_op jit(solution)/shard_map/ppermute | solution.py:44
  155.1 4.5 %collective-permute-start.23 = (bf16[2,4096,128]{2,1,0:T(8,128)(2,1)}, bf16[2,4096,128]{2,1,0:T(8,128)(2,1)}, u32[]{:S(2)}, u32[]{:S(2)}) collective-permute-start(bf16[2,4096,128]{2,1,0:T(8,128)(2,1)} %maximum_bitcast_fusion), channel_id=1, source_target_pairs={{0,1},{1,0},{2,3},{3,2},{4,5},{5,4},{6,7},{7,6},{8,9},{9,8},{10,11... | collective-permute-start | bytes 6291464 | tf_op jit(solution)/shard_map/ppermute | solution.py:44
  165.0 15.6 %copy-start.1 = (bf16[256,128]{1,0:T(8,128)(2,1)S(1)}, bf16[256,128]{1,0:T(8,128)(2,1)}, u32[]{:S(2)}) copy-start(bf16[256,128]{1,0:T(8,128)(2,1)} %param.6) | copy-start | bytes 196612
  166.6 6.8 %collective-permute-start.26 = (f32[256,128]{0,1:T(8,128)S(1)}, f32[256,128]{0,1:T(8,128)S(1)}, u32[]{:S(2)}, u32[]{:S(2)}) collective-permute-start(f32[256,128]{0,1:T(8,128)S(1)} %bitcast.309), channel_id=1, source_target_pairs={{0,12},{4,0},{8,4},{12,8},{1,13},{5,1},{9,5},{13,9},{2,14},{6,2},{... | collective-permute-start | bytes 393224 | tf_op jit(solution)/shard_map/ppermute | solution.py:118
  167.2 12.5 %collective-permute-start.25 = (f32[256,128]{0,1:T(8,128)S(1)}, f32[256,128]{0,1:T(8,128)S(1)}, u32[]{:S(2)}, u32[]{:S(2)}) collective-permute-start(f32[256,128]{0,1:T(8,128)S(1)} %bitcast.310), channel_id=1, source_target_pairs={{0,8},{4,12},{8,0},{12,4},{1,9},{5,13},{9,1},{13,5},{2,10},{6,14},... | collective-permute-start | bytes 393224 | tf_op jit(solution)/shard_map/ppermute | solution.py:118
  167.6 12.1 %collective-permute-start.24 = (f32[256,128]{0,1:T(8,128)S(1)}, f32[256,128]{0,1:T(8,128)S(1)}, u32[]{:S(2)}, u32[]{:S(2)}) collective-permute-start(f32[256,128]{0,1:T(8,128)S(1)} %bitcast.311), channel_id=1, source_target_pairs={{0,4},{4,8},{8,12},{12,0},{1,5},{5,9},{9,13},{13,1},{2,6},{6,10},{... | collective-permute-start | bytes 393224 | tf_op jit(solution)/shard_map/ppermute | solution.py:118
  (15 other events, 39.4 us)

commit v13 on v12

--- a/solution.py
+++ b/solution.py
@@ -201,16 +201,29 @@
     d_e = jnp.where(valid, d_e, jnp.float32(0))
     occ_grad = (occ_raw * (d_e / query_len)[:, :, None, None]).astype(jnp.bfloat16)
     onehot = (local_of[:, :, None] == jnp.arange(blk_dev, dtype=jnp.int32)) & valid[:, :, None]
-    grad_emb = jnp.einsum(
-        "scb,scje->bje",
-        onehot.astype(jnp.bfloat16),
-        occ_grad,
-        preferred_element_type=jnp.float32,
-    )
-    grad_flat = grad_emb.reshape(row_share, emb_width)
-    dot_e = jnp.sum(e_pre * grad_flat, -1, keepdims=True)
-    de_pre = (scale * grad_flat - e_pre * (scale * scale * scale) * dot_e).astype(jnp.bfloat16)
-    partial_w = left_product(hidden, all_gather_rows(de_pre, "mp"))
+    onehot = onehot.astype(jnp.bfloat16)
+    halves = 2 if blk_dev % 2 == 0 else 1
+    half_blk = blk_dev // halves
+    half_rows = half_blk * BLK
+    split_hidden = hidden.reshape(mp_count, halves, half_rows, hidden.shape[1])
+    cubed = e_pre * (scale * scale * scale)
+    partial_w = None
+    for h in range(halves):
+        grad_emb = jnp.einsum(
+            "scb,scje->bje",
+            onehot[:, :, h * half_blk : (h + 1) * half_blk],
+            occ_grad,
+            preferred_element_type=jnp.float32,
+        )
+        grad_flat = grad_emb.reshape(half_rows, emb_width)
+        rows = slice(h * half_rows, (h + 1) * half_rows)
+        dot_e = jnp.sum(e_pre[rows] * grad_flat, -1, keepdims=True)
+        de_pre = (scale[rows] * grad_flat - cubed[rows] * dot_e).astype(jnp.bfloat16)
+        term = left_product(
+            split_hidden[:, h].reshape(mp_count * half_rows, hidden.shape[1]),
+            all_gather_rows(de_pre, "mp"),
+        )
+        partial_w = term if partial_w is None else partial_w + term
     grad_w = all_sum(partial_w, "enc")
     return (losses, grad_w)
 

time: 181 us -> 186 us (1.028)
  waiting for transfers between devices: 68.7 us -> 63.3 us
  matrix products: 24.6 us -> 28.2 us
  other arithmetic: 32 us -> 35.3 us
    ppermute x10 -> x12, waiting for transfers between devices: 44.6 us -> 38.8 us  [xor_perm(): return lax.ppermute(value, axis, [(i, i ^ bit) for i in range(count)])]
    dot_general x1 -> x2, matrix products: 4.97 us -> 9.04 us  [local(): jnp.einsum('scb,scje->bje', onehot[:, :, h * half_blk:(h + 1) * half_blk]...]
    slice x0 -> x1, local copies, waits for them, and re-layouts: none -> 4.03 us  [local(): split_hidden[:, h].reshape(mp_count * half_rows, hidden.shape[1])]
    mul x1 -> x2, other arithmetic: 0.01 us -> 1.98 us  [local(): cubed = e_pre * (scale * scale * scale)]
    unnamed x43 -> x87, local copies, waits for them, and re-layouts: 8.05 us -> 6.25 us
    ppermute x10 -> x12, starting transfers between devices: 6.59 us -> 7.94 us  [xor_perm(): return lax.ppermute(value, axis, [(i, i ^ bit) for i in range(count)])]
  transfers between devices with their start and end apart: 27 -> 29, of which waited for: 14 -> 15; matrix products, arithmetic and copies ran while one was open for 19% -> 23% of each run, Pallas kernels for 0% -> 0%
where the time goes in v13:
time: 186 us
  waiting for transfers between devices  63.3 us (34%)
  other arithmetic  35.3 us (19%)
  local copies, waits for them, and re-layouts  31.9 us (17%)
  matrix products  28.2 us (15%)
  starting transfers between devices  25.3 us (14%)
    ppermute x12, waiting for transfers between devices, xor_perm(): return lax.ppermute(value, axis, [(i, i ^ bit) for i in range(count)])  38.8 us
    ppermute x9, waiting for transfers between devices, all_sum(): lax.ppermute(value, axis, [(i, (i + k) % count) for i in range(count)])  17.2 us
    ppermute x9, starting transfers between devices, all_sum(): lax.ppermute(value, axis, [(i, (i + k) % count) for i in range(count)])  9.41 us
    dot_general x2, matrix products, local(): jnp.einsum('scb,scje->bje', onehot[:, :, h * half_blk:(h + 1) * half_blk]...  9.04 us
    ppermute x8, starting transfers between devices, all_gather_many(): others = lax.ppermute(arrs, axis, [(i, i ^ bit) for i in range(count)])  7.97 us
    ppermute x12, starting transfers between devices, xor_perm(): return lax.ppermute(value, axis, [(i, i ^ bit) for i in range(count)])  7.94 us
    ppermute x8, waiting for transfers between devices, all_gather_many(): others = lax.ppermute(arrs, axis, [(i, i ^ bit) for i in range(count)])  7.25 us
    select_n x8, other arithmetic, halving_steps(): sends.append(jnp.where(low, acc[:, 1], acc[:, 0]))  6.91 us
  transfers between devices with their start and end apart: 29, of which 15 were waited for; matrix products, arithmetic and copies ran while one was open for 23% of the time, Pallas kernels for 0%

profile of v13, /device:TPU:0, one launch (start us, length us, event | category | flops | bytes accessed | tf_op | source)
XLA Modules:
  0.0 185.7 jit_solution(12905837361922373087)
XLA Ops:
  0.7 5.8 %fusion.59 = (bf16[4,1,1024,256]{3,2,1,0:T(8,128)(2,1)}, bf16[4,1,1024,256]{3,2,1,0:T(8,128)(2,1)}, bf16[4,1,1024,256]{3,2,1,0:T(8,128)(2,1)}, bf16[4,1,1024,256]{3,2,1,0:T(8,128)(2,1)S(1)}) fusion(bf16[4,4,1024,256]{3,2,1,0:T(8,128)(2,1)} %bitcast.330), kind=kLoop, calls=%fused_computation.193 | loop fusion | bytes 16777216 | tf_op jit(solution)/shard_map/slice | solution.py:150
  6.4 2.3 %fusion.5 = f32[2,2,1024,128]{3,2,1,0:T(8,128)S(1)} fusion(bf16[256,128]{1,0:T(8,128)(2,1)S(1)} %copy-done, bf16[2,2,1024,256]{3,2,1,0:T(8,128)(2,1)} %bitcast.344), kind=kOutput, calls=%fused_computation.17 | convolution fusion | flops 268435456 | bytes 4259840 | tf_op jit(solution)/shard_map/dot_general | solution.py:150
  9.6 2.9 %collective-permute-start.1 = (bf16[1,8,32,128]{3,2,1,0:T(8,128)(2,1)S(1)}, bf16[1,8,32,128]{3,2,1,0:T(8,128)(2,1)S(1)}, u32[]{:S(2)}, u32[]{:S(2)}) collective-permute-start(bf16[1,8,32,128]{3,2,1,0:T(8,128)(2,1)S(1)} %bitcast.360), channel_id=1, source_target_pairs={{0,2},{1,3},{2,0},{3,1},{4,6},{5,7},{6,4},{7,5},{8,10},{9,11},{10,... | collective-permute-start | bytes 196616 | tf_op jit(solution)/shard_map/ppermute | solution.py:95
  17.8 2.3 %fusion.11 = f32[2,2,1024,128]{3,2,0,1:T(8,128)S(1)} fusion(bf16[256,128]{1,0:T(8,128)(2,1)S(1)} %copy-done, bf16[2,2,1024,256]{3,2,1,0:T(8,128)(2,1)} %bitcast.341), kind=kOutput, calls=%fused_computation.24 | convolution fusion | flops 268435456 | bytes 4259840 | tf_op jit(solution)/shard_map/dot_general | solution.py:150
  23.2 2.0 %collective-permute-done.4 = s32[2,8,16]{2,1,0:T(8,128)S(1)} collective-permute-done((s32[2,8,16]{2,1,0:T(8,128)S(1)}, s32[2,8,16]{2,1,0:T(8,128)S(1)}, u32[]{:S(2)}, u32[]{:S(2)}) %collective-permute-start.4) | collective-permute-done | bytes 1056 | tf_op jit(solution)/shard_map/ppermute | solution.py:95
  26.7 2.1 %fusion.29 = f32[1,2,1024,128]{3,2,1,0:T(8,128)S(1)} fusion(f32[2,1024,128]{2,1,0:T(8,128)} %collective-permute-done, f32[2,2,1024,128]{3,2,1,0:T(8,128)} %copy-done.5, pred[]{:T(512)S(6)} %eq.97), kind=kLoop, calls=%fused_computation.49 | loop fusion | flops 524288 | bytes 4194305 | tf_op jit(solution)/shard_map/reshape | solution.py:59
  29.7 3.1 %collective-permute-start.5 = (s32[1,32,16]{2,1,0:T(8,128)S(1)}, s32[1,32,16]{2,1,0:T(8,128)S(1)}, u32[]{:S(2)}, u32[]{:S(2)}) collective-permute-start(s32[1,32,16]{2,1,0:T(8,128)S(1)} %bitcast.358), channel_id=1, source_target_pairs={{0,8},{4,12},{8,0},{12,4},{1,9},{5,13},{9,1},{13,5},{2,10},{6,14},... | collective-permute-start | bytes 6152 | tf_op jit(solution)/shard_map/ppermute | solution.py:95
  32.8 1.8 collective-permute-start.15
  41.6 1.7 collective-permute-start.6
  44.1 4.0 %collective-permute-done.6 = s32[2,32,16]{2,1,0:T(8,128)S(1)} collective-permute-done((s32[2,32,16]{2,1,0:T(8,128)S(1)}, s32[2,32,16]{2,1,0:T(8,128)S(1)}, u32[]{:S(2)}, u32[]{:S(2)}) %collective-permute-start.6) | collective-permute-done | bytes 4128 | tf_op jit(solution)/shard_map/ppermute | solution.py:95
  50.1 1.9 %gather_fusion.3 = s32[256]{0:T(256)S(1)} fusion(s32[16,128]{1,0:T(8,128)S(1)} %reshape_reshape_reshape.2, s32[256]{0:T(256)S(1)} %reshape.716), kind=kCustom, calls=%fused_computation.3 | custom fusion | bytes 4096 | tf_op jit(solution)/shard_map/jit(take_along_axis)/gather | solution.py:177
  52.8 1.9 %gather_fusion = s32[256]{0:T(256)S(1)} fusion(s32[256]{0:T(256)S(1)} %copy-done.2, s32[1024]{0:T(1024)S(1)} %pad_clamp_fusion.2), kind=kCustom, calls=%fused_computation | custom fusion | bytes 3072 | tf_op jit(solution)/shard_map/gather | solution.py:15
  60.5 9.9 %collective-permute-done.12 = f32[1,1024,128]{2,1,0:T(8,128)S(1)} collective-permute-done((f32[1,1024,128]{2,1,0:T(8,128)}, f32[1,1024,128]{2,1,0:T(8,128)S(1)}, u32[]{:S(2)}, u32[]{:S(2)}) %collective-permute-start.12) | collective-permute-done | bytes 524320 | tf_op jit(solution)/shard_map/ppermute | solution.py:44
  70.5 10.1 %collective-permute-done.10 = f32[1,1024,128]{2,1,0:T(8,128)} collective-permute-done((f32[1,1024,128]{2,1,0:T(8,128)}, f32[1,1024,128]{2,1,0:T(8,128)}, u32[]{:S(2)}, u32[]{:S(2)}) %collective-permute-start.10) | collective-permute-done | bytes 524320 | tf_op jit(solution)/shard_map/ppermute | solution.py:44
  82.7 2.0 %bitcast_multiply_fusion = f32[4096,128]{1,0:T(8,128)} fusion(f32[4,1024,128]{2,1,0:T(8,128)S(1)} %get-tuple-element.41, f32[4096]{0:T(1024)S(1)} %multiply_multiply_fusion), kind=kLoop, calls=%fused_computation.19 | loop fusion | flops 524288 | bytes 4210688 | tf_op jit(solution)/shard_map/mul | solution.py:209
  85.6 3.1 %gather_fusion.2 = bf16[256,64,128]{2,1,0:T(8,128)(2,1)} fusion(bf16[64,64,128]{2,1,0:T(8,128)(2,1)S(1)} %multiply_convert_fusion.1, s32[1024]{0:T(1024)S(1)} %pad_clamp_fusion), kind=kCustom, calls=%fused_computation.2 | custom fusion | bytes 8389632 | tf_op jit(solution)/shard_map/gather | solution.py:188
  92.6 4.6 %select_reduce_fusion = (f32[16,16,32]{2,1,0:T(8,128)S(1)}, f32[16,16,32,64]{3,2,1,0:T(8,128)S(1)}) fusion(pred[16,16,64]{2,1,0:T(8,128)(4,1)S(1)} %add_compare_fusion, bf16[16,16,32,128]{3,2,1,0:T(8,128)(2,1)S(1)} %bitcast.339, bf16[16,16,64,128]{3,2,1,0:T(8,128)(2,1)} %bitcast.333), kind=kOutput, calls=%fused_computation.8 | convolution fusion | flops 135258112 | bytes 8437760 | tf_op jit(solution)/shard_map/scie,scje->scij/dot_general | solution.py:190
  97.2 3.3 %fusion.4 = f32[16,16,32]{2,1,0:T(8,128)S(1)} fusion(f32[16,16,32,64]{3,2,1,0:T(8,128)S(1)} %get-tuple-element.71, f32[16,16,32]{2,1,0:T(8,128)S(1)} %get-tuple-element.70, pred[16,16,64]{2,1,0:T(8,128)(4,1)} %copy-done.29), kind=kLoop, calls=%fused_computation.13 | loop fusion | flops 1564672 | bytes 2179072 | tf_op jit(solution)/shard_map/reduce_sum | solution.py:22
  102.8 1.9 %collective-permute-done.17 = f32[16,128]{1,0:T(8,128)S(1)} collective-permute-done((f32[16,128]{1,0:T(8,128)S(1)}, f32[16,128]{1,0:T(8,128)S(1)}, u32[]{:S(2)}, u32[]{:S(2)}) %collective-permute-start.17) | collective-permute-done | bytes 8224 | tf_op jit(solution)/shard_map/ppermute | solution.py:118
  105.6 3.6 %collective-permute-start.21 = (f32[16,128]{1,0:T(8,128)S(1)}, f32[16,128]{1,0:T(8,128)S(1)}, u32[]{:S(2)}, u32[]{:S(2)}) collective-permute-start(f32[16,128]{1,0:T(8,128)S(1)} %fusion.68), channel_id=1, source_target_pairs={{0,12},{4,0},{8,4},{12,8},{1,13},{5,1},{9,5},{13,9},{2,14},{6,2},{... | collective-permute-start | bytes 24584 | tf_op jit(solution)/shard_map/ppermute | solution.py:118
  110.6 3.2 %collective-permute-done.20 = f32[16,128]{1,0:T(8,128)S(1)} collective-permute-done((f32[16,128]{1,0:T(8,128)S(1)}, f32[16,128]{1,0:T(8,128)S(1)}, u32[]{:S(2)}, u32[]{:S(2)}) %collective-permute-start.20) | collective-permute-done | bytes 8224 | tf_op jit(solution)/shard_map/ppermute | solution.py:118
  117.3 2.1 %gather_fusion.4 = f32[256]{0:T(256)S(1)} fusion(f32[16,128]{1,0:T(8,128)S(1)} %reshape.685, s32[256]{0:T(256)S(1)} %reshape.716), kind=kCustom, calls=%fused_computation.4 | custom fusion | bytes 4096 | tf_op jit(solution)/shard_map/jit(take_along_axis)/gather | solution.py:200
  119.5 6.9 %multiply_convert_fusion = bf16[16,16,64,128]{3,2,1,0:T(8,128)(2,1)S(1)} fusion(f32[16,16]{1,0:T(8,128)S(1)} %select_multiply_fusion, bf16[16,16,32,128]{3,2,1,0:T(8,128)(2,1)S(1)} %bitcast.340, f32[16,16,32,64]{3,2,1,0:T(8,128)} %copy-done.9, f32[16,16,32]{2,1,0:T(8,128)S(1)} %fusion.4, f32[16,16,32]{2,1,0:T(8,128)S(1)} %get-tuple-element.70, ...), kind=kOutput, calls=%fused_computation.5 | convolution fusion | flops 140509184 | bytes 8471552 | tf_op jit(solution)/shard_map/scij,scie->scje/dot_general | solution.py:193
  126.4 3.0 %fusion.33 = (f32[32,64]{0,1:T(8,128)S(1)}, f32[32,64,128]{2,0,1:T(8,128)S(1)}) fusion(f32[32,64,128]{2,1,0:T(8,128)S(1)} %bitcast.345, bf16[16,16,64,128]{3,2,1,0:T(8,128)(2,1)S(1)} %multiply_convert_fusion, pred[16,16,64]{2,0,1:T(8,128)(4,1)S(1)} %fusion.37), kind=kOutput, calls=%fused_computation.59 | convolution fusion | flops 134739968 | bytes 6316032 | tf_op jit(solution)/shard_map/scb,scje->bje/dot_general | solution.py:212
  130.2 6.0 %fusion.34 = (f32[32,64]{0,1:T(8,128)S(1)}, f32[32,64,128]{2,0,1:T(8,128)}) fusion(f32[32,64,128]{2,1,0:T(8,128)S(1)} %bitcast.346, bf16[16,16,64,128]{3,2,1,0:T(8,128)(2,1)} %copy-done.8, pred[16,16,64]{2,0,1:T(8,128)(4,1)S(1)} %fusion.37), kind=kOutput, calls=%fused_computation.61 | convolution fusion | flops 134739968 | bytes 6316032 | tf_op jit(solution)/shard_map/scb,scje->bje/dot_general | solution.py:212
  136.4 2.0 %copy.208 = f32[32,64,128]{2,1,0:T(8,128)S(1)} copy(f32[32,64,128]{2,0,1:T(8,128)} %get-tuple-element.75) | data formatting | bytes 2097152 | tf_op jit(solution)/shard_map/scb,scje->bje/dot_general | solution.py:212
  142.0 12.8 %collective-permute-done.24 = bf16[1,2048,128]{2,1,0:T(8,128)(2,1)S(1)} collective-permute-done((bf16[1,2048,128]{2,1,0:T(8,128)(2,1)S(1)}, bf16[1,2048,128]{2,1,0:T(8,128)(2,1)S(1)}, u32[]{:S(2)}, u32[]{:S(2)}) %collective-permute-start.24) | collective-permute-done | bytes 524320 | tf_op jit(solution)/shard_map/ppermute | solution.py:44
  156.1 5.9 %collective-permute-done.22 = bf16[1,2048,128]{2,1,0:T(8,128)(2,1)S(1)} collective-permute-done((bf16[1,2048,128]{2,1,0:T(8,128)(2,1)S(1)}, bf16[1,2048,128]{2,1,0:T(8,128)(2,1)S(1)}, u32[]{:S(2)}, u32[]{:S(2)}) %collective-permute-start.22) | collective-permute-done | bytes 524320 | tf_op jit(solution)/shard_map/ppermute | solution.py:44
  163.2 4.0 %fusion.58 = (bf16[4,1,2048,256]{3,2,1,0:T(8,128)(2,1)S(1)}, bf16[4,1,2048,256]{3,2,1,0:T(8,128)(2,1)S(1)}) fusion(bf16[4,2,2048,256]{3,2,1,0:T(8,128)(2,1)} %bitcast.331), kind=kLoop, calls=%fused_computation.192 | loop fusion | bytes 16777216 | tf_op jit(solution)/shard_map/slice | solution.py:223
  172.3 1.9 %collective-permute-start.26 = (f32[256,128]{0,1:T(8,128)S(1)}, f32[256,128]{0,1:T(8,128)S(1)}, u32[]{:S(2)}, u32[]{:S(2)}) collective-permute-start(f32[256,128]{0,1:T(8,128)S(1)} %bitcast.353), channel_id=1, source_target_pairs={{0,4},{4,8},{8,12},{12,0},{1,5},{5,9},{9,13},{13,1},{2,6},{6,10},{... | collective-permute-start | bytes 393224 | tf_op jit(solution)/shard_map/ppermute | solution.py:118
  174.9 3.7 %collective-permute-done.28 = f32[256,128]{0,1:T(8,128)S(1)} collective-permute-done((f32[256,128]{0,1:T(8,128)S(1)}, f32[256,128]{0,1:T(8,128)S(1)}, u32[]{:S(2)}, u32[]{:S(2)}) %collective-permute-start.28) | collective-permute-done | bytes 131104 | tf_op jit(solution)/shard_map/ppermute | solution.py:118
  178.5 6.3 %collective-permute-done.27 = f32[256,128]{0,1:T(8,128)S(1)} collective-permute-done((f32[256,128]{0,1:T(8,128)S(1)}, f32[256,128]{0,1:T(8,128)S(1)}, u32[]{:S(2)}, u32[]{:S(2)}) %collective-permute-start.27) | collective-permute-done | bytes 131104 | tf_op jit(solution)/shard_map/ppermute | solution.py:118
  (237 shorter events, 55.9 us)
Async XLA Ops:
  8.9 17.8 %collective-permute-start = (f32[2,1024,128]{2,1,0:T(8,128)S(1)}, f32[2,1024,128]{2,1,0:T(8,128)}, u32[]{:S(2)}, u32[]{:S(2)}) collective-permute-start(f32[2,1024,128]{2,1,0:T(8,128)S(1)} %select_bitcast_fusion.7), channel_id=1, source_target_pairs={{0,1},{1,0},{2,3},{3,2},{4,5},{5,4},{6,7},{7,6},{8,9},{9,8},{10,11... | collective-permute-start | bytes 3145736 | tf_op jit(solution)/shard_map/ppermute | solution.py:44
  9.6 13.5 %collective-permute-start.1 = (bf16[1,8,32,128]{3,2,1,0:T(8,128)(2,1)S(1)}, bf16[1,8,32,128]{3,2,1,0:T(8,128)(2,1)S(1)}, u32[]{:S(2)}, u32[]{:S(2)}) collective-permute-start(bf16[1,8,32,128]{3,2,1,0:T(8,128)(2,1)S(1)} %bitcast.360), channel_id=1, source_target_pairs={{0,2},{1,3},{2,0},{3,1},{4,6},{5,7},{6,4},{7,5},{8,10},{9,11},{10,... | collective-permute-start | bytes 196616 | tf_op jit(solution)/shard_map/ppermute | solution.py:95
  12.6 10.0 %collective-permute-start.3 = (s32[1,8,16]{2,1,0:T(8,128)S(1)}, s32[1,8,16]{2,1,0:T(8,128)S(1)}, u32[]{:S(2)}, u32[]{:S(2)}) collective-permute-start(s32[1,8,16]{2,1,0:T(8,128)S(1)} %bitcast.370), channel_id=1, source_target_pairs={{0,2},{1,3},{2,0},{3,1},{4,6},{5,7},{6,4},{7,5},{8,10},{9,11},{10,... | collective-permute-start | bytes 1544 | tf_op jit(solution)/shard_map/ppermute | solution.py:95
  14.4 18.5 %collective-permute-start.13 = (f32[2,1024,128]{2,1,0:T(8,128)}, f32[2,1024,128]{2,1,0:T(8,128)}, u32[]{:S(2)}, u32[]{:S(2)}) collective-permute-start(f32[2,1024,128]{2,1,0:T(8,128)} %select_bitcast_fusion.4), channel_id=1, source_target_pairs={{0,1},{1,0},{2,3},{3,2},{4,5},{5,4},{6,7},{7,6},{8,9},{9,8},{10,11... | collective-permute-start | bytes 3145736 | tf_op jit(solution)/shard_map/ppermute | solution.py:44
  17.8 19.3 %collective-permute-start.11 = (f32[2,1024,128]{2,1,0:T(8,128)}, f32[2,1024,128]{2,1,0:T(8,128)}, u32[]{:S(2)}, u32[]{:S(2)}) collective-permute-start(f32[2,1024,128]{2,1,0:T(8,128)} %select_bitcast_fusion.5), channel_id=1, source_target_pairs={{0,1},{1,0},{2,3},{3,2},{4,5},{5,4},{6,7},{7,6},{8,9},{9,8},{10,11... | collective-permute-start | bytes 3145736 | tf_op jit(solution)/shard_map/ppermute | solution.py:44
  22.6 17.2 %collective-permute-start.9 = (f32[2,1024,128]{2,1,0:T(8,128)}, f32[2,1024,128]{2,1,0:T(8,128)S(1)}, u32[]{:S(2)}, u32[]{:S(2)}) collective-permute-start(f32[2,1024,128]{2,1,0:T(8,128)} %select_bitcast_fusion.6), channel_id=1, source_target_pairs={{0,1},{1,0},{2,3},{3,2},{4,5},{5,4},{6,7},{7,6},{8,9},{9,8},{10,11... | collective-permute-start | bytes 3145736 | tf_op jit(solution)/shard_map/ppermute | solution.py:44
  23.1 2.2 %collective-permute-start.4 = (s32[2,8,16]{2,1,0:T(8,128)S(1)}, s32[2,8,16]{2,1,0:T(8,128)S(1)}, u32[]{:S(2)}, u32[]{:S(2)}) collective-permute-start(s32[2,8,16]{2,1,0:T(8,128)S(1)} %add_bitcast_fusion.2), channel_id=1, source_target_pairs={{0,1},{1,0},{2,3},{3,2},{4,5},{5,4},{6,7},{7,6},{8,9},{9,8},{10,11... | collective-permute-start | bytes 3080 | tf_op jit(solution)/shard_map/ppermute | solution.py:95
  25.3 1.3 collective-permute-start.2
  29.7 11.8 %collective-permute-start.5 = (s32[1,32,16]{2,1,0:T(8,128)S(1)}, s32[1,32,16]{2,1,0:T(8,128)S(1)}, u32[]{:S(2)}, u32[]{:S(2)}) collective-permute-start(s32[1,32,16]{2,1,0:T(8,128)S(1)} %bitcast.358), channel_id=1, source_target_pairs={{0,8},{4,12},{8,0},{12,4},{1,9},{5,13},{9,1},{13,5},{2,10},{6,14},... | collective-permute-start | bytes 6152 | tf_op jit(solution)/shard_map/ppermute | solution.py:95
  32.8 23.1 %collective-permute-start.7 = (bf16[1,32,32,128]{3,2,1,0:T(8,128)(2,1)S(1)}, bf16[1,32,32,128]{3,2,1,0:T(8,128)(2,1)}, u32[]{:S(2)}, u32[]{:S(2)}) collective-permute-start(bf16[1,32,32,128]{3,2,1,0:T(8,128)(2,1)S(1)} %bitcast.349), channel_id=1, source_target_pairs={{0,8},{4,12},{8,0},{12,4},{1,9},{5,13},{9,1},{13,5},{2,10},{6,14},... | collective-permute-start | bytes 786440 | tf_op jit(solution)/shard_map/ppermute | solution.py:95
  32.8 25.1 %collective-permute-start.15 = (f32[1,1024,128]{2,1,0:T(8,128)}, f32[1,1024,128]{2,1,0:T(8,128)}, u32[]{:S(2)}, u32[]{:S(2)}) collective-permute-start(f32[1,1024,128]{2,1,0:T(8,128)} %select_bitcast_fusion.17), channel_id=1, source_target_pairs={{0,2},{1,3},{2,0},{3,1},{4,6},{5,7},{6,4},{7,5},{8,10},{9,11},{10,... | collective-permute-start | bytes 1572872 | tf_op jit(solution)/shard_map/ppermute | solution.py:44
  37.1 22.2 %collective-permute-start.14 = (f32[1,1024,128]{2,1,0:T(8,128)}, f32[1,1024,128]{2,1,0:T(8,128)}, u32[]{:S(2)}, u32[]{:S(2)}) collective-permute-start(f32[1,1024,128]{2,1,0:T(8,128)} %select_bitcast_fusion.12), channel_id=1, source_target_pairs={{0,2},{1,3},{2,0},{3,1},{4,6},{5,7},{6,4},{7,5},{8,10},{9,11},{10,... | collective-permute-start | bytes 1572872 | tf_op jit(solution)/shard_map/ppermute | solution.py:44
  39.8 30.6 %collective-permute-start.12 = (f32[1,1024,128]{2,1,0:T(8,128)}, f32[1,1024,128]{2,1,0:T(8,128)S(1)}, u32[]{:S(2)}, u32[]{:S(2)}) collective-permute-start(f32[1,1024,128]{2,1,0:T(8,128)} %select_bitcast_fusion.13), channel_id=1, source_target_pairs={{0,2},{1,3},{2,0},{3,1},{4,6},{5,7},{6,4},{7,5},{8,10},{9,11},{10,... | collective-permute-start | bytes 1572872 | tf_op jit(solution)/shard_map/ppermute | solution.py:44
  41.6 6.5 %collective-permute-start.6 = (s32[2,32,16]{2,1,0:T(8,128)S(1)}, s32[2,32,16]{2,1,0:T(8,128)S(1)}, u32[]{:S(2)}, u32[]{:S(2)}) collective-permute-start(s32[2,32,16]{2,1,0:T(8,128)S(1)} %add_bitcast_fusion.1), channel_id=1, source_target_pairs={{0,4},{4,0},{8,12},{12,8},{1,5},{5,1},{9,13},{13,9},{2,6},{6,2},{1... | collective-permute-start | bytes 12296 | tf_op jit(solution)/shard_map/ppermute | solution.py:95
  48.1 32.5 %collective-permute-start.10 = (f32[1,1024,128]{2,1,0:T(8,128)}, f32[1,1024,128]{2,1,0:T(8,128)}, u32[]{:S(2)}, u32[]{:S(2)}) collective-permute-start(f32[1,1024,128]{2,1,0:T(8,128)} %select_bitcast_fusion.14), channel_id=1, source_target_pairs={{0,2},{1,3},{2,0},{3,1},{4,6},{5,7},{6,4},{7,5},{8,10},{9,11},{10,... | collective-permute-start | bytes 1572872 | tf_op jit(solution)/shard_map/ppermute | solution.py:44
  55.6 37.0 %copy-start.29 = (pred[16,16,64]{2,1,0:T(8,128)(4,1)}, pred[16,16,64]{2,1,0:T(8,128)(4,1)S(1)}, u32[]{:S(2)}) copy-start(pred[16,16,64]{2,1,0:T(8,128)(4,1)S(1)} %add_compare_fusion) | copy-start | bytes 49156
  57.9 32.3 %collective-permute-start.8 = (bf16[2,32,32,128]{3,2,1,0:T(8,128)(2,1)}, bf16[2,32,32,128]{3,2,1,0:T(8,128)(2,1)}, u32[]{:S(2)}, u32[]{:S(2)}) collective-permute-start(bf16[2,32,32,128]{3,2,1,0:T(8,128)(2,1)} %maximum_bitcast_fusion.2), channel_id=1, source_target_pairs={{0,4},{4,0},{8,12},{12,8},{1,5},{5,1},{9,13},{13,9},{2,6},{6,2},{1... | collective-permute-start | bytes 1572872 | tf_op jit(solution)/shard_map/ppermute | solution.py:95
  59.2 22.6 %copy-start.20 = (f32[1,1024,128]{2,1,0:T(8,128)}, f32[1,1024,128]{2,1,0:T(8,128)S(1)}, u32[]{:S(2)}) copy-start(f32[1,1024,128]{2,1,0:T(8,128)S(1)} %bitcast_add_fusion.3) | copy-start | bytes 1572868
  60.5 21.2 %copy-start.22 = (f32[1,1024,128]{2,1,0:T(8,128)}, f32[1,1024,128]{2,1,0:T(8,128)S(1)}, u32[]{:S(2)}) copy-start(f32[1,1024,128]{2,1,0:T(8,128)S(1)} %bitcast_add_fusion.4) | copy-start | bytes 1572868
  100.9 1.9 %collective-permute-start.18 = (f32[16,128]{1,0:T(8,128)S(1)}, f32[16,128]{1,0:T(8,128)S(1)}, u32[]{:S(2)}, u32[]{:S(2)}) collective-permute-start(f32[16,128]{1,0:T(8,128)S(1)} %select_reduce_fusion.1), channel_id=1, source_target_pairs={{0,3},{1,0},{2,1},{3,2},{4,7},{5,4},{6,5},{7,6},{8,11},{9,8},{10,9... | collective-permute-start | bytes 24584 | tf_op jit(solution)/shard_map/ppermute | solution.py:118
  100.9 3.7 %collective-permute-start.17 = (f32[16,128]{1,0:T(8,128)S(1)}, f32[16,128]{1,0:T(8,128)S(1)}, u32[]{:S(2)}, u32[]{:S(2)}) collective-permute-start(f32[16,128]{1,0:T(8,128)S(1)} %select_reduce_fusion.1), channel_id=1, source_target_pairs={{0,2},{1,3},{2,0},{3,1},{4,6},{5,7},{6,4},{7,5},{8,10},{9,11},{10,... | collective-permute-start | bytes 24584 | tf_op jit(solution)/shard_map/ppermute | solution.py:118
  102.5 3.1 %collective-permute-start.16 = (f32[16,128]{1,0:T(8,128)S(1)}, f32[16,128]{1,0:T(8,128)S(1)}, u32[]{:S(2)}, u32[]{:S(2)}) collective-permute-start(f32[16,128]{1,0:T(8,128)S(1)} %select_reduce_fusion.1), channel_id=1, source_target_pairs={{0,1},{1,2},{2,3},{3,0},{4,5},{5,6},{6,7},{7,4},{8,9},{9,10},{10,1... | collective-permute-start | bytes 24584 | tf_op jit(solution)/shard_map/ppermute | solution.py:118
  105.6 5.0 %collective-permute-start.21 = (f32[16,128]{1,0:T(8,128)S(1)}, f32[16,128]{1,0:T(8,128)S(1)}, u32[]{:S(2)}, u32[]{:S(2)}) collective-permute-start(f32[16,128]{1,0:T(8,128)S(1)} %fusion.68), channel_id=1, source_target_pairs={{0,12},{4,0},{8,4},{12,8},{1,13},{5,1},{9,5},{13,9},{2,14},{6,2},{... | collective-permute-start | bytes 24584 | tf_op jit(solution)/shard_map/ppermute | solution.py:118
  109.2 4.5 %collective-permute-start.20 = (f32[16,128]{1,0:T(8,128)S(1)}, f32[16,128]{1,0:T(8,128)S(1)}, u32[]{:S(2)}, u32[]{:S(2)}) collective-permute-start(f32[16,128]{1,0:T(8,128)S(1)} %fusion.68), channel_id=1, source_target_pairs={{0,8},{4,12},{8,0},{12,4},{1,9},{5,13},{9,1},{13,5},{2,10},{6,14},... | collective-permute-start | bytes 24584 | tf_op jit(solution)/shard_map/ppermute | solution.py:118
  109.2 5.4 %collective-permute-start.19 = (f32[16,128]{1,0:T(8,128)S(1)}, f32[16,128]{1,0:T(8,128)S(1)}, u32[]{:S(2)}, u32[]{:S(2)}) collective-permute-start(f32[16,128]{1,0:T(8,128)S(1)} %fusion.68), channel_id=1, source_target_pairs={{0,4},{4,8},{8,12},{12,0},{1,5},{5,9},{9,13},{13,1},{2,6},{6,10},{... | collective-permute-start | bytes 24584 | tf_op jit(solution)/shard_map/ppermute | solution.py:118
  139.9 14.9 %collective-permute-start.24 = (bf16[1,2048,128]{2,1,0:T(8,128)(2,1)S(1)}, bf16[1,2048,128]{2,1,0:T(8,128)(2,1)S(1)}, u32[]{:S(2)}, u32[]{:S(2)}) collective-permute-start(bf16[1,2048,128]{2,1,0:T(8,128)(2,1)S(1)} %bitcast.348), channel_id=1, source_target_pairs={{0,2},{1,3},{2,0},{3,1},{4,6},{5,7},{6,4},{7,5},{8,10},{9,11},{10,... | collective-permute-start | bytes 1572872 | tf_op jit(solution)/shard_map/ppermute | solution.py:44
  140.6 21.4 %collective-permute-start.22 = (bf16[1,2048,128]{2,1,0:T(8,128)(2,1)S(1)}, bf16[1,2048,128]{2,1,0:T(8,128)(2,1)S(1)}, u32[]{:S(2)}, u32[]{:S(2)}) collective-permute-start(bf16[1,2048,128]{2,1,0:T(8,128)(2,1)S(1)} %bitcast.347), channel_id=1, source_target_pairs={{0,2},{1,3},{2,0},{3,1},{4,6},{5,7},{6,4},{7,5},{8,10},{9,11},{10,... | collective-permute-start | bytes 1572872 | tf_op jit(solution)/shard_map/ppermute | solution.py:44
  156.1 11.2 %collective-permute-start.25 = (bf16[2,2048,128]{2,1,0:T(8,128)(2,1)}, bf16[2,2048,128]{2,1,0:T(8,128)(2,1)S(1)}, u32[]{:S(2)}, u32[]{:S(2)}) collective-permute-start(bf16[2,2048,128]{2,1,0:T(8,128)(2,1)} %maximum_bitcast_fusion.1), channel_id=1, source_target_pairs={{0,1},{1,0},{2,3},{3,2},{4,5},{5,4},{6,7},{7,6},{8,9},{9,8},{10,11... | collective-permute-start | bytes 3145736 | tf_op jit(solution)/shard_map/ppermute | solution.py:44
  163.2 4.1 %collective-permute-start.23 = (bf16[2,2048,128]{2,1,0:T(8,128)(2,1)}, bf16[2,2048,128]{2,1,0:T(8,128)(2,1)}, u32[]{:S(2)}, u32[]{:S(2)}) collective-permute-start(bf16[2,2048,128]{2,1,0:T(8,128)(2,1)} %maximum_bitcast_fusion), channel_id=1, source_target_pairs={{0,1},{1,0},{2,3},{3,2},{4,5},{5,4},{6,7},{7,6},{8,9},{9,8},{10,11... | collective-permute-start | bytes 3145736 | tf_op jit(solution)/shard_map/ppermute | solution.py:44
  171.3 7.2 %collective-permute-start.28 = (f32[256,128]{0,1:T(8,128)S(1)}, f32[256,128]{0,1:T(8,128)S(1)}, u32[]{:S(2)}, u32[]{:S(2)}) collective-permute-start(f32[256,128]{0,1:T(8,128)S(1)} %bitcast.351), channel_id=1, source_target_pairs={{0,12},{4,0},{8,4},{12,8},{1,13},{5,1},{9,5},{13,9},{2,14},{6,2},{... | collective-permute-start | bytes 393224 | tf_op jit(solution)/shard_map/ppermute | solution.py:118
  171.9 12.9 %collective-permute-start.27 = (f32[256,128]{0,1:T(8,128)S(1)}, f32[256,128]{0,1:T(8,128)S(1)}, u32[]{:S(2)}, u32[]{:S(2)}) collective-permute-start(f32[256,128]{0,1:T(8,128)S(1)} %bitcast.352), channel_id=1, source_target_pairs={{0,8},{4,12},{8,0},{12,4},{1,9},{5,13},{9,1},{13,5},{2,10},{6,14},... | collective-permute-start | bytes 393224 | tf_op jit(solution)/shard_map/ppermute | solution.py:118
  172.3 12.5 %collective-permute-start.26 = (f32[256,128]{0,1:T(8,128)S(1)}, f32[256,128]{0,1:T(8,128)S(1)}, u32[]{:S(2)}, u32[]{:S(2)}) collective-permute-start(f32[256,128]{0,1:T(8,128)S(1)} %bitcast.353), channel_id=1, source_target_pairs={{0,4},{4,8},{8,12},{12,0},{1,5},{5,9},{9,13},{13,1},{2,6},{6,10},{... | collective-permute-start | bytes 393224 | tf_op jit(solution)/shard_map/ppermute | solution.py:118
  (38 other events, 153.1 us)

commit v14 on v12

--- a/solution.py
+++ b/solution.py
@@ -144,7 +144,7 @@
 
     gathered = all_gather_many([queries, candidates], "mp")
 
-    chunks = 4 if row_share % (4 * BLK) == 0 else 1
+    chunks = 8 if row_share % (8 * BLK) == 0 else 1
     split_rows = hidden.reshape(mp_count, chunks, row_share // chunks, hidden.shape[1])
     partials = [
         jnp.dot(split_rows[:, k], proj_w, preferred_element_type=jnp.float32).reshape(

time: 181 us -> 196 us (1.083)
  starting transfers between devices: 23.9 us -> 35.6 us
  other arithmetic: 32 us -> 38.4 us
  matrix products: 24.6 us -> 22 us
    ppermute x8, waiting for transfers between devices: 7.16 us -> 16.9 us  [all_gather_many(): others = lax.ppermute(arrs, axis, [(i, i ^ bit) for i in range(count)])]
    unnamed x2 -> x9, other arithmetic: 0.01 us -> 5.5 us
    select_n x8 -> x16, other arithmetic: 7.16 us -> 12.6 us  [halving_steps(): sends.append(jnp.where(low, acc[:, 1], acc[:, 0]))]
    ppermute x10 -> x18, starting transfers between devices: 6.59 us -> 11.7 us  [xor_perm(): return lax.ppermute(value, axis, [(i, i ^ bit) for i in range(count)])]
    ppermute x10 -> x18, waiting for transfers between devices: 44.6 us -> 39.5 us  [xor_perm(): return lax.ppermute(value, axis, [(i, i ^ bit) for i in range(count)])]
    ppermute x9, waiting for transfers between devices: 16.9 us -> 12.1 us  [all_sum(): lax.ppermute(value, axis, [(i, (i + k) % count) for i in range(count)])]
    add x4 -> x0, other arithmetic: 4.57 us -> none  [local(): pieces = [k + xor_perm(t, 'mp', bit) for k, t in zip(keeps, sends)]]
    ppermute x8, starting transfers between devices: 7.94 us -> 11.9 us  [all_gather_many(): others = lax.ppermute(arrs, axis, [(i, i ^ bit) for i in range(count)])]
  transfers between devices with their start and end apart: 27 -> 35, of which waited for: 14 -> 17; matrix products, arithmetic and copies ran while one was open for 19% -> 19% of each run, Pallas kernels for 0% -> 0%
where the time goes in v14:
time: 196 us; the launch traced here: 195 us
  waiting for transfers between devices  68.6 us (35%)
  other arithmetic  38.4 us (20%)
  starting transfers between devices  35.6 us (18%)
  local copies, waits for them, and re-layouts  28.9 us (15%)
  matrix products  22 us (11%)
    ppermute x18, waiting for transfers between devices, xor_perm(): return lax.ppermute(value, axis, [(i, i ^ bit) for i in range(count)])  39.5 us
    ppermute x8, waiting for transfers between devices, all_gather_many(): others = lax.ppermute(arrs, axis, [(i, i ^ bit) for i in range(count)])  16.9 us
    select_n x16, other arithmetic, halving_steps(): sends.append(jnp.where(low, acc[:, 1], acc[:, 0]))  12.6 us
    ppermute x9, waiting for transfers between devices, all_sum(): lax.ppermute(value, axis, [(i, (i + k) % count) for i in range(count)])  12.1 us
    ppermute x9, starting transfers between devices, all_sum(): lax.ppermute(value, axis, [(i, (i + k) % count) for i in range(count)])  12 us
    ppermute x8, starting transfers between devices, all_gather_many(): others = lax.ppermute(arrs, axis, [(i, i ^ bit) for i in range(count)])  11.9 us
    ppermute x18, starting transfers between devices, xor_perm(): return lax.ppermute(value, axis, [(i, i ^ bit) for i in range(count)])  11.7 us
    unnamed x79, local copies, waits for them, and re-layouts  7.28 us
  transfers between devices with their start and end apart: 35, of which 17 were waited for; matrix products, arithmetic and copies ran while one was open for 19% of the time, Pallas kernels for 0%

profile of v14, /device:TPU:0, one launch (start us, length us, event | category | flops | bytes accessed | tf_op | source)
XLA Modules:
  0.0 195.0 jit_solution(3419688219850909401)
XLA Ops:
  0.7 5.5 %fusion.79 = (bf16[4,1,512,256]{3,2,1,0:T(8,128)(2,1)}, bf16[4,1,512,256]{3,2,1,0:T(8,128)(2,1)}, bf16[4,1,512,256]{3,2,1,0:T(8,128)(2,1)}, bf16[4,1,512,256]{3,...) fusion(bf16[4,8,512,256]{3,2,1,0:T(8,128)(2,1)} %bitcast.395), kind=kLoop, calls=%fused_computation.210 | loop fusion | bytes 16777216 | tf_op jit(solution)/shard_map/slice | solution.py:150
  12.5 3.0 %collective-permute-start.3 = (s32[1,8,16]{2,1,0:T(8,128)S(1)}, s32[1,8,16]{2,1,0:T(8,128)S(1)}, u32[]{:S(2)}, u32[]{:S(2)}) collective-permute-start(s32[1,8,16]{2,1,0:T(8,128)S(1)} %bitcast.436), channel_id=1, source_target_pairs={{0,2},{1,3},{2,0},{3,1},{4,6},{5,7},{6,4},{7,5},{8,10},{9,11},{10,... | collective-permute-start | bytes 1544 | tf_op jit(solution)/shard_map/ppermute | solution.py:95
  15.5 1.7 fusion.20
  24.8 4.1 %collective-permute-done.1 = bf16[1,8,32,128]{3,2,1,0:T(8,128)(2,1)S(1)} collective-permute-done((bf16[1,8,32,128]{3,2,1,0:T(8,128)(2,1)S(1)}, bf16[1,8,32,128]{3,2,1,0:T(8,128)(2,1)S(1)}, u32[]{:S(2)}, u32[]{:S(2)}) %collective-permute-start.1) | collective-permute-done | bytes 65568 | tf_op jit(solution)/shard_map/ppermute | solution.py:95
  39.1 1.8 collective-permute-start.12
  43.8 1.8 collective-permute-start.16
  45.6 2.7 %collective-permute-start.5 = (s32[1,32,16]{2,1,0:T(8,128)S(1)}, s32[1,32,16]{2,1,0:T(8,128)S(1)}, u32[]{:S(2)}, u32[]{:S(2)}) collective-permute-start(s32[1,32,16]{2,1,0:T(8,128)S(1)} %bitcast.426), channel_id=1, source_target_pairs={{0,8},{4,12},{8,0},{12,4},{1,9},{5,13},{9,1},{13,5},{2,10},{6,14},... | collective-permute-start | bytes 6152 | tf_op jit(solution)/shard_map/ppermute | solution.py:95
  50.4 1.6 collective-permute-start.6
  55.5 1.9 gather_fusion.3
  58.1 1.9 gather_fusion
  61.7 1.8 collective-permute-start.20
  66.1 1.8 collective-permute-start.23
  69.0 2.7 %collective-permute-start.7 = (bf16[1,32,32,128]{3,2,1,0:T(8,128)(2,1)S(1)}, bf16[1,32,32,128]{3,2,1,0:T(8,128)(2,1)S(1)}, u32[]{:S(2)}, u32[]{:S(2)}) collective-permute-start(bf16[1,32,32,128]{3,2,1,0:T(8,128)(2,1)S(1)} %bitcast.415), channel_id=1, source_target_pairs={{0,8},{4,12},{8,0},{12,4},{1,9},{5,13},{9,1},{13,5},{2,10},{6,14},... | collective-permute-start | bytes 786440 | tf_op jit(solution)/shard_map/ppermute | solution.py:95
  75.0 5.6 %collective-permute-done.22 = f32[1,512,128]{2,1,0:T(8,128)S(1)} collective-permute-done((f32[1,512,128]{2,1,0:T(8,128)}, f32[1,512,128]{2,1,0:T(8,128)S(1)}, u32[]{:S(2)}, u32[]{:S(2)}) %collective-permute-start.22) | collective-permute-done | bytes 262176 | tf_op jit(solution)/shard_map/ppermute | solution.py:44
  80.6 4.8 %collective-permute-done.23 = f32[1,512,128]{2,1,0:T(8,128)S(1)} collective-permute-done((f32[1,512,128]{2,1,0:T(8,128)}, f32[1,512,128]{2,1,0:T(8,128)S(1)}, u32[]{:S(2)}, u32[]{:S(2)}) %collective-permute-start.23) | collective-permute-done | bytes 262176 | tf_op jit(solution)/shard_map/ppermute | solution.py:44
  89.7 3.1 %gather_fusion.2 = bf16[256,64,128]{2,1,0:T(8,128)(2,1)} fusion(bf16[64,64,128]{2,1,0:T(8,128)(2,1)S(1)} %multiply_convert_fusion.1, s32[1024]{0:T(1024)S(1)} %get-tuple-element.66), kind=kCustom, calls=%fused_computation.2 | custom fusion | bytes 8389632 | tf_op jit(solution)/shard_map/gather | solution.py:188
  92.8 7.8 %collective-permute-done.8 = bf16[2,32,32,128]{3,2,1,0:T(8,128)(2,1)} collective-permute-done((bf16[2,32,32,128]{3,2,1,0:T(8,128)(2,1)}, bf16[2,32,32,128]{3,2,1,0:T(8,128)(2,1)}, u32[]{:S(2)}, u32[]{:S(2)}) %collective-permute-start.8) | collective-permute-done | bytes 524320 | tf_op jit(solution)/shard_map/ppermute | solution.py:95
  102.0 2.2 %gather_fusion.1 = bf16[256,32,128]{2,1,0:T(8,128)(2,1)} fusion(bf16[128,32,128]{2,1,0:T(8,128)(2,1)S(1)} %bitcast.403, s32[1024]{0:T(1024)S(1)} %get-tuple-element.67), kind=kCustom, calls=%fused_computation.1 | custom fusion | bytes 4195328 | tf_op jit(solution)/shard_map/gather | solution.py:181
  104.2 5.2 %select_reduce_fusion = (f32[16,16,32]{2,1,0:T(8,128)S(1)}, f32[16,16,32,64]{3,2,1,0:T(8,128)S(1)}) fusion(pred[16,16,64]{2,1,0:T(8,128)(4,1)S(1)} %add_compare_fusion, bf16[16,16,32,128]{3,2,1,0:T(8,128)(2,1)} %bitcast.405, bf16[16,16,64,128]{3,2,1,0:T(8,128)(2,1)} %bitcast.402), kind=kOutput, calls=%fused_computation.11 | convolution fusion | flops 135258112 | bytes 8437760 | tf_op jit(solution)/shard_map/scie,scje->scij/dot_general | solution.py:190
  109.4 2.4 %fusion.2 = f32[16,16,32]{2,1,0:T(8,128)S(1)} fusion(f32[16,16,32,64]{3,2,1,0:T(8,128)S(1)} %get-tuple-element.63, f32[16,16,32]{2,1,0:T(8,128)S(1)} %get-tuple-element.62, pred[16,16,64]{2,1,0:T(8,128)(4,1)S(1)} %add_compare_fusion), kind=kLoop, calls=%fused_computation.12 | loop fusion | flops 1564672 | bytes 2179072 | tf_op jit(solution)/shard_map/reduce_sum | solution.py:22
  117.5 2.6 %collective-permute-start.28 = (f32[16,128]{1,0:T(8,128)S(1)}, f32[16,128]{1,0:T(8,128)S(1)}, u32[]{:S(2)}, u32[]{:S(2)}) collective-permute-start(f32[16,128]{1,0:T(8,128)S(1)} %fusion.86), channel_id=1, source_target_pairs={{0,8},{4,12},{8,0},{12,4},{1,9},{5,13},{9,1},{13,5},{2,10},{6,14},... | collective-permute-start | bytes 24584 | tf_op jit(solution)/shard_map/ppermute | solution.py:118
  124.4 1.9 gather_fusion.4
  126.4 6.9 %multiply_convert_fusion = bf16[16,16,64,128]{3,2,1,0:T(8,128)(2,1)S(1)} fusion(f32[16,16]{1,0:T(8,128)S(1)} %select_multiply_fusion, bf16[16,16,32,128]{3,2,1,0:T(8,128)(2,1)} %bitcast.406, f32[16,16,32,64]{3,2,1,0:T(8,128)} %copy-done.3, f32[16,16,32]{2,1,0:T(8,128)S(1)} %fusion.2, f32[16,16,32]{2,1,0:T(8,128)S(1)} %get-tuple-element.62, ...), kind=kOutput, calls=%fused_computation.5 | convolution fusion | flops 140509184 | bytes 8471552 | tf_op jit(solution)/shard_map/scij,scie->scje/dot_general | solution.py:193
  133.3 3.7 %fusion.6 = (f32[64,64]{0,1:T(8,128)S(1)}, f32[64,64,128]{2,0,1:T(8,128)S(1)}) fusion(f32[64,64,128]{2,1,0:T(8,128)S(1)} %bitcast.399, bf16[16,16,64,128]{3,2,1,0:T(8,128)(2,1)S(1)} %multiply_convert_fusion, s32[16,16]{0,1:T(8,128)S(1)} %copy.263, pred[16,16]{0,1:T(8,128)(4,1)S(1)} %copy.264), kind=kOutput, calls=%fused_computation.20 | convolution fusion | flops 269512704 | bytes 8406272 | tf_op jit(solution)/shard_map/scb,scje->bje/dot_general | solution.py:204
  137.0 2.6 %copy.267 = f32[64,64,128]{2,1,0:T(8,128)} copy(f32[64,64,128]{2,0,1:T(8,128)S(1)} %get-tuple-element.65) | data formatting | bytes 4194304 | tf_op jit(solution)/shard_map/scb,scje->bje/dot_general | solution.py:204
  139.7 3.6 %fusion.5 = bf16[1,4096,128]{2,1,0:T(8,128)(2,1)S(1)} fusion(f32[4096]{0:T(1024)S(1)} %mul.134, f32[4096]{0:T(1024)S(1)} %multiply_multiply_fusion, f32[4096]{0:T(1024)S(1)} %bitcast.422, f32[1,4096,128]{2,1,0:T(8,128)S(1)} %bitcast.400, f32[1,4096,128]{2,1,0:T(8,128)} %bitcast.404), kind=kLoop, calls=%fused_computation.17 | loop fusion | flops 2621440 | bytes 5292032 | tf_op jit(solution)/shard_map/convert_element_type | solution.py:212
  144.5 23.4 %collective-permute-done.30 = bf16[1,4096,128]{2,1,0:T(8,128)(2,1)S(1)} collective-permute-done((bf16[1,4096,128]{2,1,0:T(8,128)(2,1)S(1)}, bf16[1,4096,128]{2,1,0:T(8,128)(2,1)S(1)}, u32[]{:S(2)}, u32[]{:S(2)}) %collective-permute-start.30) | collective-permute-done | bytes 1048608 | tf_op jit(solution)/shard_map/ppermute | solution.py:44
  169.6 4.5 %collective-permute-done.31 = bf16[2,4096,128]{2,1,0:T(8,128)(2,1)} collective-permute-done((bf16[2,4096,128]{2,1,0:T(8,128)(2,1)}, bf16[2,4096,128]{2,1,0:T(8,128)(2,1)}, u32[]{:S(2)}, u32[]{:S(2)}) %collective-permute-start.31) | collective-permute-done | bytes 2097184 | tf_op jit(solution)/shard_map/ppermute | solution.py:44
  174.1 1.9 select_bitcast_fusion.1
  181.7 3.2 %collective-permute-start.33 = (f32[256,128]{0,1:T(8,128)S(1)}, f32[256,128]{0,1:T(8,128)S(1)}, u32[]{:S(2)}, u32[]{:S(2)}) collective-permute-start(f32[256,128]{0,1:T(8,128)S(1)} %bitcast.418), channel_id=1, source_target_pairs={{0,8},{4,12},{8,0},{12,4},{1,9},{5,13},{9,1},{13,5},{2,10},{6,14},... | collective-permute-start | bytes 393224 | tf_op jit(solution)/shard_map/ppermute | solution.py:118
  186.2 3.2 %collective-permute-done.32 = f32[256,128]{0,1:T(8,128)S(1)} collective-permute-done((f32[256,128]{0,1:T(8,128)S(1)}, f32[256,128]{0,1:T(8,128)S(1)}, u32[]{:S(2)}, u32[]{:S(2)}) %collective-permute-start.32) | collective-permute-done | bytes 131104 | tf_op jit(solution)/shard_map/ppermute | solution.py:118
  189.4 4.8 %collective-permute-done.33 = f32[256,128]{0,1:T(8,128)S(1)} collective-permute-done((f32[256,128]{0,1:T(8,128)S(1)}, f32[256,128]{0,1:T(8,128)S(1)}, u32[]{:S(2)}, u32[]{:S(2)}) %collective-permute-start.33) | collective-permute-done | bytes 131104 | tf_op jit(solution)/shard_map/ppermute | solution.py:118
  (247 shorter events, 68.0 us)
Async XLA Ops:
  7.6 24.1 %collective-permute-start.9 = (f32[2,512,128]{2,1,0:T(8,128)}, f32[2,512,128]{2,1,0:T(8,128)}, u32[]{:S(2)}, u32[]{:S(2)}) collective-permute-start(f32[2,512,128]{2,1,0:T(8,128)} %select_bitcast_fusion.10), channel_id=1, source_target_pairs={{0,1},{1,0},{2,3},{3,2},{4,5},{5,4},{6,7},{7,6},{8,9},{9,8},{10,11... | collective-permute-start | bytes 1572872 | tf_op jit(solution)/shard_map/ppermute | solution.py:44
  9.3 23.9 %collective-permute-start.11 = (f32[2,512,128]{2,1,0:T(8,128)}, f32[2,512,128]{2,1,0:T(8,128)}, u32[]{:S(2)}, u32[]{:S(2)}) collective-permute-start(f32[2,512,128]{2,1,0:T(8,128)} %select_bitcast_fusion.9), channel_id=1, source_target_pairs={{0,1},{1,0},{2,3},{3,2},{4,5},{5,4},{6,7},{7,6},{8,9},{9,8},{10,11... | collective-permute-start | bytes 1572872 | tf_op jit(solution)/shard_map/ppermute | solution.py:44
  10.7 23.8 %collective-permute-start.13 = (f32[2,512,128]{2,1,0:T(8,128)}, f32[2,512,128]{2,1,0:T(8,128)}, u32[]{:S(2)}, u32[]{:S(2)}) collective-permute-start(f32[2,512,128]{2,1,0:T(8,128)} %select_bitcast_fusion.8), channel_id=1, source_target_pairs={{0,1},{1,0},{2,3},{3,2},{4,5},{5,4},{6,7},{7,6},{8,9},{9,8},{10,11... | collective-permute-start | bytes 1572872 | tf_op jit(solution)/shard_map/ppermute | solution.py:44
  12.5 25.3 %collective-permute-start.15 = (f32[2,512,128]{2,1,0:T(8,128)}, f32[2,512,128]{2,1,0:T(8,128)}, u32[]{:S(2)}, u32[]{:S(2)}) collective-permute-start(f32[2,512,128]{2,1,0:T(8,128)} %select_bitcast_fusion.7), channel_id=1, source_target_pairs={{0,1},{1,0},{2,3},{3,2},{4,5},{5,4},{6,7},{7,6},{8,9},{9,8},{10,11... | collective-permute-start | bytes 1572872 | tf_op jit(solution)/shard_map/ppermute | solution.py:44
  12.5 12.0 %collective-permute-start.3 = (s32[1,8,16]{2,1,0:T(8,128)S(1)}, s32[1,8,16]{2,1,0:T(8,128)S(1)}, u32[]{:S(2)}, u32[]{:S(2)}) collective-permute-start(s32[1,8,16]{2,1,0:T(8,128)S(1)} %bitcast.436), channel_id=1, source_target_pairs={{0,2},{1,3},{2,0},{3,1},{4,6},{5,7},{6,4},{7,5},{8,10},{9,11},{10,... | collective-permute-start | bytes 1544 | tf_op jit(solution)/shard_map/ppermute | solution.py:95
  24.5 4.3 %collective-permute-start.1 = (bf16[1,8,32,128]{3,2,1,0:T(8,128)(2,1)S(1)}, bf16[1,8,32,128]{3,2,1,0:T(8,128)(2,1)S(1)}, u32[]{:S(2)}, u32[]{:S(2)}) collective-permute-start(bf16[1,8,32,128]{3,2,1,0:T(8,128)(2,1)S(1)} %bitcast.428), channel_id=1, source_target_pairs={{0,2},{1,3},{2,0},{3,1},{4,6},{5,7},{6,4},{7,5},{8,10},{9,11},{10,... | collective-permute-start | bytes 196616 | tf_op jit(solution)/shard_map/ppermute | solution.py:95
  31.4 7.8 %collective-permute-start.17 = (f32[2,512,128]{2,1,0:T(8,128)}, f32[2,512,128]{2,1,0:T(8,128)S(1)}, u32[]{:S(2)}, u32[]{:S(2)}) collective-permute-start(f32[2,512,128]{2,1,0:T(8,128)} %select_bitcast_fusion.6), channel_id=1, source_target_pairs={{0,1},{1,0},{2,3},{3,2},{4,5},{5,4},{6,7},{7,6},{8,9},{9,8},{10,11... | collective-permute-start | bytes 1572872 | tf_op jit(solution)/shard_map/ppermute | solution.py:44
  31.6 12.2 %collective-permute-start.19 = (f32[2,512,128]{2,1,0:T(8,128)}, f32[2,512,128]{2,1,0:T(8,128)S(1)}, u32[]{:S(2)}, u32[]{:S(2)}) collective-permute-start(f32[2,512,128]{2,1,0:T(8,128)} %select_bitcast_fusion.5), channel_id=1, source_target_pairs={{0,1},{1,0},{2,3},{3,2},{4,5},{5,4},{6,7},{7,6},{8,9},{9,8},{10,11... | collective-permute-start | bytes 1572872 | tf_op jit(solution)/shard_map/ppermute | solution.py:44
  33.2 12.4 %collective-permute-start.21 = (f32[2,512,128]{2,1,0:T(8,128)S(1)}, f32[2,512,128]{2,1,0:T(8,128)S(1)}, u32[]{:S(2)}, u32[]{:S(2)}) collective-permute-start(f32[2,512,128]{2,1,0:T(8,128)S(1)} %copy-done.31), channel_id=1, source_target_pairs={{0,1},{1,0},{2,3},{3,2},{4,5},{5,4},{6,7},{7,6},{8,9},{9,8},{10,11... | collective-permute-start | bytes 1572872 | tf_op jit(solution)/shard_map/ppermute | solution.py:44
  34.6 6.5 %collective-permute-start = (f32[2,512,128]{2,1,0:T(8,128)S(1)}, f32[2,512,128]{2,1,0:T(8,128)S(1)}, u32[]{:S(2)}, u32[]{:S(2)}) collective-permute-start(f32[2,512,128]{2,1,0:T(8,128)S(1)} %copy-done.32), channel_id=1, source_target_pairs={{0,1},{1,0},{2,3},{3,2},{4,5},{5,4},{6,7},{7,6},{8,9},{9,8},{10,11... | collective-permute-start | bytes 1572872 | tf_op jit(solution)/shard_map/ppermute | solution.py:44
  37.7 23.2 %collective-permute-start.10 = (f32[1,512,128]{2,1,0:T(8,128)S(1)}, f32[1,512,128]{2,1,0:T(8,128)S(1)}, u32[]{:S(2)}, u32[]{:S(2)}) collective-permute-start(f32[1,512,128]{2,1,0:T(8,128)S(1)} %select_bitcast_fusion.20), channel_id=1, source_target_pairs={{0,2},{1,3},{2,0},{3,1},{4,6},{5,7},{6,4},{7,5},{8,10},{9,11},{10,... | collective-permute-start | bytes 786440 | tf_op jit(solution)/shard_map/ppermute | solution.py:44
  39.1 25.5 %collective-permute-start.12 = (f32[1,512,128]{2,1,0:T(8,128)}, f32[1,512,128]{2,1,0:T(8,128)}, u32[]{:S(2)}, u32[]{:S(2)}) collective-permute-start(f32[1,512,128]{2,1,0:T(8,128)} %select_bitcast_fusion.19), channel_id=1, source_target_pairs={{0,2},{1,3},{2,0},{3,1},{4,6},{5,7},{6,4},{7,5},{8,10},{9,11},{10,... | collective-permute-start | bytes 786440 | tf_op jit(solution)/shard_map/ppermute | solution.py:44
  41.1 25.0 %collective-permute-start.14 = (f32[1,512,128]{2,1,0:T(8,128)}, f32[1,512,128]{2,1,0:T(8,128)}, u32[]{:S(2)}, u32[]{:S(2)}) collective-permute-start(f32[1,512,128]{2,1,0:T(8,128)} %select_bitcast_fusion.18), channel_id=1, source_target_pairs={{0,2},{1,3},{2,0},{3,1},{4,6},{5,7},{6,4},{7,5},{8,10},{9,11},{10,... | collective-permute-start | bytes 786440 | tf_op jit(solution)/shard_map/ppermute | solution.py:44
  43.8 25.2 %collective-permute-start.16 = (f32[1,512,128]{2,1,0:T(8,128)}, f32[1,512,128]{2,1,0:T(8,128)}, u32[]{:S(2)}, u32[]{:S(2)}) collective-permute-start(f32[1,512,128]{2,1,0:T(8,128)} %select_bitcast_fusion.17), channel_id=1, source_target_pairs={{0,2},{1,3},{2,0},{3,1},{4,6},{5,7},{6,4},{7,5},{8,10},{9,11},{10,... | collective-permute-start | bytes 786440 | tf_op jit(solution)/shard_map/ppermute | solution.py:44
  45.6 4.7 %collective-permute-start.5 = (s32[1,32,16]{2,1,0:T(8,128)S(1)}, s32[1,32,16]{2,1,0:T(8,128)S(1)}, u32[]{:S(2)}, u32[]{:S(2)}) collective-permute-start(s32[1,32,16]{2,1,0:T(8,128)S(1)} %bitcast.426), channel_id=1, source_target_pairs={{0,8},{4,12},{8,0},{12,4},{1,9},{5,13},{9,1},{13,5},{2,10},{6,14},... | collective-permute-start | bytes 6152 | tf_op jit(solution)/shard_map/ppermute | solution.py:95
  50.4 4.0 %collective-permute-start.6 = (s32[2,32,16]{2,1,0:T(8,128)S(1)}, s32[2,32,16]{2,1,0:T(8,128)S(1)}, u32[]{:S(2)}, u32[]{:S(2)}) collective-permute-start(s32[2,32,16]{2,1,0:T(8,128)S(1)} %add_bitcast_fusion.1), channel_id=1, source_target_pairs={{0,4},{4,0},{8,12},{12,8},{1,5},{5,1},{9,13},{13,9},{2,6},{6,2},{1... | collective-permute-start | bytes 12296 | tf_op jit(solution)/shard_map/ppermute | solution.py:95
  54.3 18.4 %collective-permute-start.18 = (f32[1,512,128]{2,1,0:T(8,128)}, f32[1,512,128]{2,1,0:T(8,128)}, u32[]{:S(2)}, u32[]{:S(2)}) collective-permute-start(f32[1,512,128]{2,1,0:T(8,128)} %select_bitcast_fusion.16), channel_id=1, source_target_pairs={{0,2},{1,3},{2,0},{3,1},{4,6},{5,7},{6,4},{7,5},{8,10},{9,11},{10,... | collective-permute-start | bytes 786440 | tf_op jit(solution)/shard_map/ppermute | solution.py:44
  61.7 13.3 %collective-permute-start.20 = (f32[1,512,128]{2,1,0:T(8,128)}, f32[1,512,128]{2,1,0:T(8,128)S(1)}, u32[]{:S(2)}, u32[]{:S(2)}) collective-permute-start(f32[1,512,128]{2,1,0:T(8,128)} %select_bitcast_fusion.15), channel_id=1, source_target_pairs={{0,2},{1,3},{2,0},{3,1},{4,6},{5,7},{6,4},{7,5},{8,10},{9,11},{10,... | collective-permute-start | bytes 786440 | tf_op jit(solution)/shard_map/ppermute | solution.py:44
  64.6 16.0 %collective-permute-start.22 = (f32[1,512,128]{2,1,0:T(8,128)}, f32[1,512,128]{2,1,0:T(8,128)S(1)}, u32[]{:S(2)}, u32[]{:S(2)}) collective-permute-start(f32[1,512,128]{2,1,0:T(8,128)} %select_bitcast_fusion.14), channel_id=1, source_target_pairs={{0,2},{1,3},{2,0},{3,1},{4,6},{5,7},{6,4},{7,5},{8,10},{9,11},{10,... | collective-permute-start | bytes 786440 | tf_op jit(solution)/shard_map/ppermute | solution.py:44
  66.1 19.3 %collective-permute-start.23 = (f32[1,512,128]{2,1,0:T(8,128)}, f32[1,512,128]{2,1,0:T(8,128)S(1)}, u32[]{:S(2)}, u32[]{:S(2)}) collective-permute-start(f32[1,512,128]{2,1,0:T(8,128)} %select_bitcast_fusion.23), channel_id=1, source_target_pairs={{0,2},{1,3},{2,0},{3,1},{4,6},{5,7},{6,4},{7,5},{8,10},{9,11},{10,... | collective-permute-start | bytes 786440 | tf_op jit(solution)/shard_map/ppermute | solution.py:44
  69.0 17.2 %collective-permute-start.7 = (bf16[1,32,32,128]{3,2,1,0:T(8,128)(2,1)S(1)}, bf16[1,32,32,128]{3,2,1,0:T(8,128)(2,1)S(1)}, u32[]{:S(2)}, u32[]{:S(2)}) collective-permute-start(bf16[1,32,32,128]{3,2,1,0:T(8,128)(2,1)S(1)} %bitcast.415), channel_id=1, source_target_pairs={{0,8},{4,12},{8,0},{12,4},{1,9},{5,13},{9,1},{13,5},{2,10},{6,14},... | collective-permute-start | bytes 786440 | tf_op jit(solution)/shard_map/ppermute | solution.py:95
  87.1 13.5 %collective-permute-start.8 = (bf16[2,32,32,128]{3,2,1,0:T(8,128)(2,1)}, bf16[2,32,32,128]{3,2,1,0:T(8,128)(2,1)}, u32[]{:S(2)}, u32[]{:S(2)}) collective-permute-start(bf16[2,32,32,128]{3,2,1,0:T(8,128)(2,1)} %maximum_bitcast_fusion.1), channel_id=1, source_target_pairs={{0,4},{4,0},{8,12},{12,8},{1,5},{5,1},{9,13},{13,9},{2,6},{6,2},{1... | collective-permute-start | bytes 1572872 | tf_op jit(solution)/shard_map/ppermute | solution.py:95
  112.2 3.7 %collective-permute-start.25 = (f32[16,128]{1,0:T(8,128)S(1)}, f32[16,128]{1,0:T(8,128)S(1)}, u32[]{:S(2)}, u32[]{:S(2)}) collective-permute-start(f32[16,128]{1,0:T(8,128)S(1)} %select_reduce_fusion.1), channel_id=1, source_target_pairs={{0,2},{1,3},{2,0},{3,1},{4,6},{5,7},{6,4},{7,5},{8,10},{9,11},{10,... | collective-permute-start | bytes 24584 | tf_op jit(solution)/shard_map/ppermute | solution.py:118
  112.6 3.2 %collective-permute-start.26 = (f32[16,128]{1,0:T(8,128)S(1)}, f32[16,128]{1,0:T(8,128)S(1)}, u32[]{:S(2)}, u32[]{:S(2)}) collective-permute-start(f32[16,128]{1,0:T(8,128)S(1)} %select_reduce_fusion.1), channel_id=1, source_target_pairs={{0,3},{1,0},{2,1},{3,2},{4,7},{5,4},{6,5},{7,6},{8,11},{9,8},{10,9... | collective-permute-start | bytes 24584 | tf_op jit(solution)/shard_map/ppermute | solution.py:118
  115.9 5.6 %collective-permute-start.27 = (f32[16,128]{1,0:T(8,128)S(1)}, f32[16,128]{1,0:T(8,128)S(1)}, u32[]{:S(2)}, u32[]{:S(2)}) collective-permute-start(f32[16,128]{1,0:T(8,128)S(1)} %fusion.86), channel_id=1, source_target_pairs={{0,4},{4,8},{8,12},{12,0},{1,5},{5,9},{9,13},{13,1},{2,6},{6,10},{... | collective-permute-start | bytes 24584 | tf_op jit(solution)/shard_map/ppermute | solution.py:118
  117.5 4.6 %collective-permute-start.28 = (f32[16,128]{1,0:T(8,128)S(1)}, f32[16,128]{1,0:T(8,128)S(1)}, u32[]{:S(2)}, u32[]{:S(2)}) collective-permute-start(f32[16,128]{1,0:T(8,128)S(1)} %fusion.86), channel_id=1, source_target_pairs={{0,8},{4,12},{8,0},{12,4},{1,9},{5,13},{9,1},{13,5},{2,10},{6,14},... | collective-permute-start | bytes 24584 | tf_op jit(solution)/shard_map/ppermute | solution.py:118
  120.1 3.7 %collective-permute-start.29 = (f32[16,128]{1,0:T(8,128)S(1)}, f32[16,128]{1,0:T(8,128)S(1)}, u32[]{:S(2)}, u32[]{:S(2)}) collective-permute-start(f32[16,128]{1,0:T(8,128)S(1)} %fusion.86), channel_id=1, source_target_pairs={{0,12},{4,0},{8,4},{12,8},{1,13},{5,1},{9,5},{13,9},{2,14},{6,2},{... | collective-permute-start | bytes 24584 | tf_op jit(solution)/shard_map/ppermute | solution.py:118
  143.3 24.6 %collective-permute-start.30 = (bf16[1,4096,128]{2,1,0:T(8,128)(2,1)S(1)}, bf16[1,4096,128]{2,1,0:T(8,128)(2,1)S(1)}, u32[]{:S(2)}, u32[]{:S(2)}) collective-permute-start(bf16[1,4096,128]{2,1,0:T(8,128)(2,1)S(1)} %fusion.5), channel_id=1, source_target_pairs={{0,2},{1,3},{2,0},{3,1},{4,6},{5,7},{6,4},{7,5},{8,10},{9,11},{10,... | collective-permute-start | bytes 3145736 | tf_op jit(solution)/shard_map/ppermute | solution.py:44
  169.6 4.5 %collective-permute-start.31 = (bf16[2,4096,128]{2,1,0:T(8,128)(2,1)}, bf16[2,4096,128]{2,1,0:T(8,128)(2,1)}, u32[]{:S(2)}, u32[]{:S(2)}) collective-permute-start(bf16[2,4096,128]{2,1,0:T(8,128)(2,1)} %maximum_bitcast_fusion), channel_id=1, source_target_pairs={{0,1},{1,0},{2,3},{3,2},{4,5},{5,4},{6,7},{7,6},{8,9},{9,8},{10,11... | collective-permute-start | bytes 6291464 | tf_op jit(solution)/shard_map/ppermute | solution.py:44
  181.1 8.3 %collective-permute-start.32 = (f32[256,128]{0,1:T(8,128)S(1)}, f32[256,128]{0,1:T(8,128)S(1)}, u32[]{:S(2)}, u32[]{:S(2)}) collective-permute-start(f32[256,128]{0,1:T(8,128)S(1)} %bitcast.417), channel_id=1, source_target_pairs={{0,4},{4,8},{8,12},{12,0},{1,5},{5,9},{9,13},{13,1},{2,6},{6,10},{... | collective-permute-start | bytes 393224 | tf_op jit(solution)/shard_map/ppermute | solution.py:118
  181.7 12.5 %collective-permute-start.33 = (f32[256,128]{0,1:T(8,128)S(1)}, f32[256,128]{0,1:T(8,128)S(1)}, u32[]{:S(2)}, u32[]{:S(2)}) collective-permute-start(f32[256,128]{0,1:T(8,128)S(1)} %bitcast.418), channel_id=1, source_target_pairs={{0,8},{4,12},{8,0},{12,4},{1,9},{5,13},{9,1},{13,5},{2,10},{6,14},... | collective-permute-start | bytes 393224 | tf_op jit(solution)/shard_map/ppermute | solution.py:118
  184.9 9.3 %collective-permute-start.34 = (f32[256,128]{0,1:T(8,128)S(1)}, f32[256,128]{0,1:T(8,128)S(1)}, u32[]{:S(2)}, u32[]{:S(2)}) collective-permute-start(f32[256,128]{0,1:T(8,128)S(1)} %bitcast.419), channel_id=1, source_target_pairs={{0,12},{4,0},{8,4},{12,8},{1,13},{5,1},{9,5},{13,9},{2,14},{6,2},{... | collective-permute-start | bytes 393224 | tf_op jit(solution)/shard_map/ppermute | solution.py:118
  (41 other events, 215.4 us)

commit v15 on v14

--- a/solution.py
+++ b/solution.py
@@ -144,7 +144,7 @@
 
     gathered = all_gather_many([queries, candidates], "mp")
 
-    chunks = 8 if row_share % (8 * BLK) == 0 else 1
+    chunks = 2 if row_share % (2 * BLK) == 0 else 1
     split_rows = hidden.reshape(mp_count, chunks, row_share // chunks, hidden.shape[1])
     partials = [
         jnp.dot(split_rows[:, k], proj_w, preferred_element_type=jnp.float32).reshape(

time: 196 us -> 175 us (0.89)
  other arithmetic: 38.4 us -> 24.9 us
  starting transfers between devices: 35.6 us -> 25.5 us
  waiting for transfers between devices: 68.6 us -> 71.1 us
    select_n x16 -> x4, other arithmetic: 12.6 us -> 4.15 us  [halving_steps(): sends.append(jnp.where(low, acc[:, 1], acc[:, 0]))]
    ppermute x18 -> x6, starting transfers between devices: 11.7 us -> 4.42 us  [xor_perm(): return lax.ppermute(value, axis, [(i, i ^ bit) for i in range(count)])]
    unnamed x9 -> x2, other arithmetic: 5.5 us -> 0.02 us
    ppermute x9, waiting for transfers between devices: 12.1 us -> 16.9 us  [all_sum(): lax.ppermute(value, axis, [(i, (i + k) % count) for i in range(count)])]
    ppermute x8, waiting for transfers between devices: 16.9 us -> 13.3 us  [all_gather_many(): others = lax.ppermute(arrs, axis, [(i, i ^ bit) for i in range(count)])]
    add x0 -> x2, other arithmetic: none -> 2.92 us  [local(): pieces = [k + xor_perm(t, 'mp', bit) for k, t in zip(keeps, sends)]]
    ppermute x9, starting transfers between devices: 12 us -> 9.44 us  [all_sum(): lax.ppermute(value, axis, [(i, (i + k) % count) for i in range(count)])]
    ppermute x18 -> x6, waiting for transfers between devices: 39.5 us -> 40.9 us  [xor_perm(): return lax.ppermute(value, axis, [(i, i ^ bit) for i in range(count)])]
  transfers between devices with their start and end apart: 35 -> 23, of which waited for: 17 -> 13; matrix products, arithmetic and copies ran while one was open for 19% -> 13% of each run, Pallas kernels for 0% -> 0%
where the time goes in v15:
time: 175 us
  waiting for transfers between devices  71.1 us (41%)
  local copies, waits for them, and re-layouts  28.9 us (17%)
  starting transfers between devices  25.5 us (15%)
  other arithmetic  24.9 us (14%)
  matrix products  23.3 us (13%)
    ppermute x6, waiting for transfers between devices, xor_perm(): return lax.ppermute(value, axis, [(i, i ^ bit) for i in range(count)])  40.9 us
    ppermute x9, waiting for transfers between devices, all_sum(): lax.ppermute(value, axis, [(i, (i + k) % count) for i in range(count)])  16.9 us
    ppermute x8, waiting for transfers between devices, all_gather_many(): others = lax.ppermute(arrs, axis, [(i, i ^ bit) for i in range(count)])  13.3 us
    ppermute x8, starting transfers between devices, all_gather_many(): others = lax.ppermute(arrs, axis, [(i, i ^ bit) for i in range(count)])  11.7 us
    ppermute x9, starting transfers between devices, all_sum(): lax.ppermute(value, axis, [(i, (i + k) % count) for i in range(count)])  9.44 us
    dot_general x1, matrix products, local(): jnp.einsum('scij,scie->scje', weights, q_e, preferred_element_type=jnp.fl...  6.95 us
    unnamed x31, local copies, waits for them, and re-layouts  6.8 us
    slice x1, local copies, waits for them, and re-layouts, local(): split_rows[:, k]  5.76 us
  transfers between devices with their start and end apart: 23, of which 13 were waited for; matrix products, arithmetic and copies ran while one was open for 13% of the time, Pallas kernels for 0%

profile of v15, /device:TPU:0, one launch (start us, length us, event | category | flops | bytes accessed | tf_op | source)
XLA Modules:
  0.0 174.9 jit_solution(11137964644893055575)
XLA Ops:
  0.7 5.8 %fusion.47 = (bf16[4,1,2048,256]{3,2,1,0:T(8,128)(2,1)}, bf16[4,1,2048,256]{3,2,1,0:T(8,128)(2,1)}) fusion(bf16[4,2,2048,256]{3,2,1,0:T(8,128)(2,1)} %bitcast.241), kind=kLoop, calls=%fused_computation.155 | loop fusion | bytes 16777216 | tf_op jit(solution)/shard_map/slice | solution.py:150
  6.4 3.4 %fusion = f32[2,2,2048,128]{3,2,1,0:T(8,128)S(1)} fusion(bf16[256,128]{1,0:T(8,128)(2,1)S(1)} %copy-done, bf16[2,2,2048,256]{3,2,1,0:T(8,128)(2,1)} %bitcast.250), kind=kOutput, calls=%fused_computation.7 | convolution fusion | flops 536870912 | bytes 8454144 | tf_op jit(solution)/shard_map/dot_general | solution.py:150
  10.1 1.9 %copy-done.5 = f32[2,2,2048,128]{3,2,1,0:T(8,128)} copy-done((f32[2,2,2048,128]{3,2,1,0:T(8,128)}, f32[2,2,2048,128]{3,2,1,0:T(8,128)S(1)}, u32[]{:S(2)}) %copy-start.5) | copy-done | bytes 4194328
  12.4 2.5 %collective-permute-start.1 = (bf16[1,8,32,128]{3,2,1,0:T(8,128)(2,1)S(1)}, bf16[1,8,32,128]{3,2,1,0:T(8,128)(2,1)S(1)}, u32[]{:S(2)}, u32[]{:S(2)}) collective-permute-start(bf16[1,8,32,128]{3,2,1,0:T(8,128)(2,1)S(1)} %bitcast.268), channel_id=1, source_target_pairs={{0,2},{1,3},{2,0},{3,1},{4,6},{5,7},{6,4},{7,5},{8,10},{9,11},{10,... | collective-permute-start | bytes 196616 | tf_op jit(solution)/shard_map/ppermute | solution.py:95
  16.3 1.8 %select_bitcast_fusion.2 = f32[2,2048,128]{2,1,0:T(8,128)} fusion(f32[2,2,2048,128]{3,2,0,1:T(8,128)S(1)} %fusion.2, pred[]{:T(512)S(6)} %eq.85), kind=kLoop, calls=%fused_computation.39 | loop fusion | flops 524288 | bytes 6291457 | tf_op jit(solution)/shard_map/jit(_where)/select_n | solution.py:62
  19.8 3.3 %collective-permute-done.4 = s32[2,8,16]{2,1,0:T(8,128)S(1)} collective-permute-done((s32[2,8,16]{2,1,0:T(8,128)S(1)}, s32[2,8,16]{2,1,0:T(8,128)S(1)}, u32[]{:S(2)}, u32[]{:S(2)}) %collective-permute-start.4) | collective-permute-done | bytes 1056 | tf_op jit(solution)/shard_map/ppermute | solution.py:95
  23.3 3.3 %fusion.9 = f32[1,2,2048,128]{3,2,1,0:T(8,128)S(1)} fusion(f32[2,2048,128]{2,1,0:T(8,128)} %collective-permute-done, f32[2,2,2048,128]{3,2,1,0:T(8,128)} %copy-done.5, pred[]{:T(512)S(6)} %eq.85), kind=kLoop, calls=%fused_computation.22 | loop fusion | flops 1048576 | bytes 8388609 | tf_op jit(solution)/shard_map/reshape | solution.py:59
  27.7 2.7 %collective-permute-start.5 = (s32[1,32,16]{2,1,0:T(8,128)S(1)}, s32[1,32,16]{2,1,0:T(8,128)S(1)}, u32[]{:S(2)}, u32[]{:S(2)}) collective-permute-start(s32[1,32,16]{2,1,0:T(8,128)S(1)} %bitcast.266), channel_id=1, source_target_pairs={{0,8},{4,12},{8,0},{12,4},{1,9},{5,13},{9,1},{13,5},{2,10},{6,14},... | collective-permute-start | bytes 6152 | tf_op jit(solution)/shard_map/ppermute | solution.py:95
  32.2 1.9 %fusion.13 = f32[1,2,2048,128]{3,2,1,0:T(8,128)S(1)} fusion(f32[2,2048,128]{2,1,0:T(8,128)} %collective-permute-done.9, f32[2,2,2048,128]{3,2,0,1:T(8,128)S(1)} %copy-done.4, pred[]{:T(512)S(6)} %eq.85), kind=kLoop, calls=%fused_computation.29 | loop fusion | flops 1048576 | bytes 8388609 | tf_op jit(solution)/shard_map/reshape | solution.py:59
  34.1 4.2 %collective-permute-start.6 = (s32[2,32,16]{2,1,0:T(8,128)S(1)}, s32[2,32,16]{2,1,0:T(8,128)S(1)}, u32[]{:S(2)}, u32[]{:S(2)}) collective-permute-start(s32[2,32,16]{2,1,0:T(8,128)S(1)} %add_bitcast_fusion.1), channel_id=1, source_target_pairs={{0,4},{4,0},{8,12},{12,8},{1,5},{5,1},{9,13},{13,9},{2,6},{6,2},{1... | collective-permute-start | bytes 12296 | tf_op jit(solution)/shard_map/ppermute | solution.py:95
  41.8 1.9 %gather_fusion.3 = s32[256]{0:T(256)S(1)} fusion(s32[16,128]{1,0:T(8,128)S(1)} %reshape_reshape_reshape.2, s32[256]{0:T(256)S(1)} %reshape.668), kind=kCustom, calls=%fused_computation.3 | custom fusion | bytes 4096 | tf_op jit(solution)/shard_map/jit(take_along_axis)/gather | solution.py:177
  44.4 1.9 %gather_fusion = s32[256]{0:T(256)S(1)} fusion(s32[256]{0:T(256)S(1)} %copy-done.2, s32[1024]{0:T(1024)S(1)} %pad_clamp_fusion.2), kind=kCustom, calls=%fused_computation | custom fusion | bytes 3072 | tf_op jit(solution)/shard_map/gather | solution.py:15
  49.5 9.8 %collective-permute-done.8 = bf16[2,32,32,128]{3,2,1,0:T(8,128)(2,1)S(1)} collective-permute-done((bf16[2,32,32,128]{3,2,1,0:T(8,128)(2,1)}, bf16[2,32,32,128]{3,2,1,0:T(8,128)(2,1)S(1)}, u32[]{:S(2)}, u32[]{:S(2)}) %collective-permute-start.8) | collective-permute-done | bytes 524320 | tf_op jit(solution)/shard_map/ppermute | solution.py:95
  59.6 2.2 %gather_fusion.1 = bf16[256,32,128]{2,1,0:T(8,128)(2,1)} fusion(bf16[128,32,128]{2,1,0:T(8,128)(2,1)S(1)} %bitcast.251, s32[1024]{0:T(1024)S(1)} %pad_clamp_fusion.1), kind=kCustom, calls=%fused_computation.1 | custom fusion | bytes 4195328 | tf_op jit(solution)/shard_map/gather | solution.py:181
  63.4 15.0 %collective-permute-done.10 = f32[1,2048,128]{2,1,0:T(8,128)} collective-permute-done((f32[1,2048,128]{2,1,0:T(8,128)}, f32[1,2048,128]{2,1,0:T(8,128)}, u32[]{:S(2)}, u32[]{:S(2)}) %collective-permute-start.10) | collective-permute-done | bytes 1048608 | tf_op jit(solution)/shard_map/ppermute | solution.py:44
  81.2 3.0 %gather_fusion.2 = bf16[256,64,128]{2,1,0:T(8,128)(2,1)} fusion(bf16[64,64,128]{2,1,0:T(8,128)(2,1)S(1)} %multiply_convert_fusion.1, s32[1024]{0:T(1024)S(1)} %pad_clamp_fusion), kind=kCustom, calls=%fused_computation.2 | custom fusion | bytes 8389632 | tf_op jit(solution)/shard_map/gather | solution.py:188
  84.3 5.2 %select_reduce_fusion = (f32[16,16,32]{2,1,0:T(8,128)S(1)}, f32[16,16,32,64]{3,2,1,0:T(8,128)S(1)}) fusion(pred[16,16,64]{2,1,0:T(8,128)(4,1)S(1)} %add_compare_fusion, bf16[16,16,32,128]{3,2,1,0:T(8,128)(2,1)} %bitcast.253, bf16[16,16,64,128]{3,2,1,0:T(8,128)(2,1)} %bitcast.248), kind=kOutput, calls=%fused_computation.15 | convolution fusion | flops 135258112 | bytes 8437760 | tf_op jit(solution)/shard_map/scie,scje->scij/dot_general | solution.py:190
  89.5 2.6 %fusion.6 = f32[16,16,32]{2,1,0:T(8,128)S(1)} fusion(f32[16,16,32,64]{3,2,1,0:T(8,128)S(1)} %get-tuple-element.59, f32[16,16,32]{2,1,0:T(8,128)S(1)} %get-tuple-element.58, pred[16,16,64]{2,1,0:T(8,128)(4,1)S(1)} %add_compare_fusion), kind=kLoop, calls=%fused_computation.16 | loop fusion | flops 1564672 | bytes 2179072 | tf_op jit(solution)/shard_map/reduce_sum | solution.py:22
  94.2 2.0 %collective-permute-done.13 = f32[16,128]{1,0:T(8,128)S(1)} collective-permute-done((f32[16,128]{1,0:T(8,128)S(1)}, f32[16,128]{1,0:T(8,128)S(1)}, u32[]{:S(2)}, u32[]{:S(2)}) %collective-permute-start.13) | collective-permute-done | bytes 8224 | tf_op jit(solution)/shard_map/ppermute | solution.py:118
  97.1 3.6 %collective-permute-start.17 = (f32[16,128]{1,0:T(8,128)S(1)}, f32[16,128]{1,0:T(8,128)S(1)}, u32[]{:S(2)}, u32[]{:S(2)}) collective-permute-start(f32[16,128]{1,0:T(8,128)S(1)} %fusion.54), channel_id=1, source_target_pairs={{0,12},{4,0},{8,4},{12,8},{1,13},{5,1},{9,5},{13,9},{2,14},{6,2},{... | collective-permute-start | bytes 24584 | tf_op jit(solution)/shard_map/ppermute | solution.py:118
  102.1 3.2 %collective-permute-done.16 = f32[16,128]{1,0:T(8,128)S(1)} collective-permute-done((f32[16,128]{1,0:T(8,128)S(1)}, f32[16,128]{1,0:T(8,128)S(1)}, u32[]{:S(2)}, u32[]{:S(2)}) %collective-permute-start.16) | collective-permute-done | bytes 8224 | tf_op jit(solution)/shard_map/ppermute | solution.py:118
  106.8 1.9 %gather_fusion.4 = f32[256]{0:T(256)S(1)} fusion(f32[16,128]{1,0:T(8,128)S(1)} %reshape.640, s32[256]{0:T(256)S(1)} %reshape.668), kind=kCustom, calls=%fused_computation.4 | custom fusion | bytes 4096 | tf_op jit(solution)/shard_map/jit(take_along_axis)/gather | solution.py:200
  108.8 6.9 %multiply_convert_fusion = bf16[16,16,64,128]{3,2,1,0:T(8,128)(2,1)S(1)} fusion(f32[16,16]{1,0:T(8,128)S(1)} %select_multiply_fusion, bf16[16,16,32,128]{3,2,1,0:T(8,128)(2,1)} %bitcast.254, f32[16,16,32,64]{3,2,1,0:T(8,128)} %copy-done.8, f32[16,16,32]{2,1,0:T(8,128)S(1)} %fusion.6, f32[16,16,32]{2,1,0:T(8,128)S(1)} %get-tuple-element.58, ...), kind=kOutput, calls=%fused_computation.5 | convolution fusion | flops 140509184 | bytes 8471552 | tf_op jit(solution)/shard_map/scij,scie->scje/dot_general | solution.py:193
  115.8 4.9 %fusion.14 = (f32[64,64]{0,1:T(8,128)S(1)}, f32[64,64,128]{2,0,1:T(8,128)}) fusion(f32[64,64,128]{2,1,0:T(8,128)S(1)} %bitcast.245, bf16[16,16,64,128]{3,2,1,0:T(8,128)(2,1)S(1)} %multiply_convert_fusion, s32[16,16]{0,1:T(8,128)S(1)} %copy.137, pred[16,16]{0,1:T(8,128)(4,1)S(1)} %copy.138), kind=kOutput, calls=%fused_computation.31 | convolution fusion | flops 269512704 | bytes 8406272 | tf_op jit(solution)/shard_map/scb,scje->bje/dot_general | solution.py:204
  120.9 2.8 %copy.141 = f32[64,64,128]{2,1,0:T(8,128)S(1)} copy(f32[64,64,128]{2,0,1:T(8,128)} %get-tuple-element.61) | data formatting | bytes 4194304 | tf_op jit(solution)/shard_map/scb,scje->bje/dot_general | solution.py:204
  123.7 1.9 %fusion.12 = bf16[1,4096,128]{2,1,0:T(8,128)(2,1)S(1)} fusion(f32[4096]{0:T(1024)S(1)} %mul.134, f32[4096]{0:T(1024)S(1)} %multiply_multiply_fusion, f32[4096]{0:T(1024)S(1)} %bitcast.262, f32[1,4096,128]{2,1,0:T(8,128)S(1)} %bitcast.246, f32[1,4096,128]{2,1,0:T(8,128)S(1)} %bitcast.252), kind=kLoop, calls=%fused_computation.26 | loop fusion | flops 2621440 | bytes 5292032 | tf_op jit(solution)/shard_map/convert_element_type | solution.py:212
  126.3 21.4 %collective-permute-done.18 = bf16[1,4096,128]{2,1,0:T(8,128)(2,1)S(1)} collective-permute-done((bf16[1,4096,128]{2,1,0:T(8,128)(2,1)S(1)}, bf16[1,4096,128]{2,1,0:T(8,128)(2,1)S(1)}, u32[]{:S(2)}, u32[]{:S(2)}) %collective-permute-start.18) | collective-permute-done | bytes 1048608 | tf_op jit(solution)/shard_map/ppermute | solution.py:44
  149.4 4.5 %collective-permute-done.19 = bf16[2,4096,128]{2,1,0:T(8,128)(2,1)} collective-permute-done((bf16[2,4096,128]{2,1,0:T(8,128)(2,1)}, bf16[2,4096,128]{2,1,0:T(8,128)(2,1)}, u32[]{:S(2)}, u32[]{:S(2)}) %collective-permute-start.19) | collective-permute-done | bytes 2097184 | tf_op jit(solution)/shard_map/ppermute | solution.py:44
  153.9 1.9 %select_bitcast_fusion.1 = (bf16[2,1,4096,128]{3,2,0,1:T(8,128)(2,1)S(1)}, bf16[2,1,4096,128]{3,2,0,1:T(8,128)(2,1)S(1)}) fusion(bf16[2,4096,128]{2,1,0:T(8,128)(2,1)} %collective-permute-done.19, pred[]{:T(512)S(6)} %eq.85, bf16[1,1,4096,128]{3,2,1,0:T(8,128)(2,1)S(1)} %get-tuple-element.33, bf16[1,1,4096,128]{3,2,1,0:T(8,128)(2,1)S(1)} %get-tuple-element.32), kind=kLoop, calls=%fused_computation.33 | loop fusion | flops 3145728 | bytes 8388609 | tf_op jit(solution)/shard_map/stack | solution.py:81
  161.9 1.9 %collective-permute-start.20 = (f32[256,128]{0,1:T(8,128)S(1)}, f32[256,128]{0,1:T(8,128)S(1)}, u32[]{:S(2)}, u32[]{:S(2)}) collective-permute-start(f32[256,128]{0,1:T(8,128)S(1)} %bitcast.259), channel_id=1, source_target_pairs={{0,4},{4,8},{8,12},{12,0},{1,5},{5,9},{9,13},{13,1},{2,6},{6,10},{... | collective-permute-start | bytes 393224 | tf_op jit(solution)/shard_map/ppermute | solution.py:118
  164.4 3.2 %collective-permute-done.22 = f32[256,128]{0,1:T(8,128)S(1)} collective-permute-done((f32[256,128]{0,1:T(8,128)S(1)}, f32[256,128]{0,1:T(8,128)S(1)}, u32[]{:S(2)}, u32[]{:S(2)}) %collective-permute-start.22) | collective-permute-done | bytes 131104 | tf_op jit(solution)/shard_map/ppermute | solution.py:118
  167.6 6.4 %collective-permute-done.21 = f32[256,128]{0,1:T(8,128)S(1)} collective-permute-done((f32[256,128]{0,1:T(8,128)S(1)}, f32[256,128]{0,1:T(8,128)S(1)}, u32[]{:S(2)}, u32[]{:S(2)}) %collective-permute-start.21) | collective-permute-done | bytes 131104 | tf_op jit(solution)/shard_map/ppermute | solution.py:118
  (146 shorter events, 34.7 us)
Async XLA Ops:
  0.6 5.8 %copy-start = (bf16[256,128]{1,0:T(8,128)(2,1)S(1)}, bf16[256,128]{1,0:T(8,128)(2,1)}, u32[]{:S(2)}) copy-start(bf16[256,128]{1,0:T(8,128)(2,1)} %param.6) | copy-start | bytes 196612
  9.9 5.1 %copy-start.11 = (s32[8,16]{1,0:T(8,128)S(1)}, s32[8,16]{1,0:T(8,128)}, u32[]{:S(2)}) copy-start(s32[8,16]{1,0:T(8,128)} %param.9) | copy-start | bytes 1540
  9.9 5.1 %copy-start.9 = (bf16[4,1,2048,256]{3,2,1,0:T(8,128)(2,1)S(1)}, bf16[4,1,2048,256]{3,2,1,0:T(8,128)(2,1)}, u32[]{:S(2)}) copy-start(bf16[4,1,2048,256]{3,2,1,0:T(8,128)(2,1)} %get-tuple-element.28) | copy-start | bytes 12582916
  12.0 11.3 %collective-permute-start = (f32[2,2048,128]{2,1,0:T(8,128)S(1)}, f32[2,2048,128]{2,1,0:T(8,128)}, u32[]{:S(2)}, u32[]{:S(2)}) collective-permute-start(f32[2,2048,128]{2,1,0:T(8,128)S(1)} %select_bitcast_fusion.3), channel_id=1, source_target_pairs={{0,1},{1,0},{2,3},{3,2},{4,5},{5,4},{6,7},{7,6},{8,9},{9,8},{10,11... | collective-permute-start | bytes 6291464 | tf_op jit(solution)/shard_map/ppermute | solution.py:44
  12.4 7.1 %collective-permute-start.1 = (bf16[1,8,32,128]{3,2,1,0:T(8,128)(2,1)S(1)}, bf16[1,8,32,128]{3,2,1,0:T(8,128)(2,1)S(1)}, u32[]{:S(2)}, u32[]{:S(2)}) collective-permute-start(bf16[1,8,32,128]{3,2,1,0:T(8,128)(2,1)S(1)} %bitcast.268), channel_id=1, source_target_pairs={{0,2},{1,3},{2,0},{3,1},{4,6},{5,7},{6,4},{7,5},{8,10},{9,11},{10,... | collective-permute-start | bytes 196616 | tf_op jit(solution)/shard_map/ppermute | solution.py:95
  14.9 4.2 %collective-permute-start.3 = (s32[1,8,16]{2,1,0:T(8,128)S(1)}, s32[1,8,16]{2,1,0:T(8,128)S(1)}, u32[]{:S(2)}, u32[]{:S(2)}) collective-permute-start(s32[1,8,16]{2,1,0:T(8,128)S(1)} %bitcast.276), channel_id=1, source_target_pairs={{0,2},{1,3},{2,0},{3,1},{4,6},{5,7},{6,4},{7,5},{8,10},{9,11},{10,... | collective-permute-start | bytes 1544 | tf_op jit(solution)/shard_map/ppermute | solution.py:95
  16.3 2.6 %copy-start.3 = (f32[2,2,2048,128]{3,2,0,1:T(8,128)}, f32[2,2,2048,128]{3,2,0,1:T(8,128)S(1)}, u32[]{:S(2)}) copy-start(f32[2,2,2048,128]{3,2,0,1:T(8,128)S(1)} %fusion.2) | copy-start | bytes 12582916
  18.9 13.3 %collective-permute-start.9 = (f32[2,2048,128]{2,1,0:T(8,128)}, f32[2,2048,128]{2,1,0:T(8,128)}, u32[]{:S(2)}, u32[]{:S(2)}) collective-permute-start(f32[2,2048,128]{2,1,0:T(8,128)} %select_bitcast_fusion.2), channel_id=1, source_target_pairs={{0,1},{1,0},{2,3},{3,2},{4,5},{5,4},{6,7},{7,6},{8,9},{9,8},{10,11... | collective-permute-start | bytes 6291464 | tf_op jit(solution)/shard_map/ppermute | solution.py:44
  19.1 3.9 %collective-permute-start.4 = (s32[2,8,16]{2,1,0:T(8,128)S(1)}, s32[2,8,16]{2,1,0:T(8,128)S(1)}, u32[]{:S(2)}, u32[]{:S(2)}) collective-permute-start(s32[2,8,16]{2,1,0:T(8,128)S(1)} %add_bitcast_fusion.2), channel_id=1, source_target_pairs={{0,1},{1,0},{2,3},{3,2},{4,5},{5,4},{6,7},{7,6},{8,9},{9,8},{10,11... | collective-permute-start | bytes 3080 | tf_op jit(solution)/shard_map/ppermute | solution.py:95
  19.5 3.7 %collective-permute-start.2 = (bf16[2,8,32,128]{3,2,1,0:T(8,128)(2,1)S(1)}, bf16[2,8,32,128]{3,2,1,0:T(8,128)(2,1)S(1)}, u32[]{:S(2)}, u32[]{:S(2)}) collective-permute-start(bf16[2,8,32,128]{3,2,1,0:T(8,128)(2,1)S(1)} %maximum_bitcast_fusion.2), channel_id=1, source_target_pairs={{0,1},{1,0},{2,3},{3,2},{4,5},{5,4},{6,7},{7,6},{8,9},{9,8},{10,11... | collective-permute-start | bytes 393224 | tf_op jit(solution)/shard_map/ppermute | solution.py:95
  23.3 8.9 %copy-start.4 = (f32[2,2,2048,128]{3,2,0,1:T(8,128)S(1)}, f32[2,2,2048,128]{3,2,0,1:T(8,128)}, u32[]{:S(2)}) copy-start(f32[2,2,2048,128]{3,2,0,1:T(8,128)} %copy-done.3) | copy-start | bytes 12582916
  27.7 6.4 %collective-permute-start.5 = (s32[1,32,16]{2,1,0:T(8,128)S(1)}, s32[1,32,16]{2,1,0:T(8,128)S(1)}, u32[]{:S(2)}, u32[]{:S(2)}) collective-permute-start(s32[1,32,16]{2,1,0:T(8,128)S(1)} %bitcast.266), channel_id=1, source_target_pairs={{0,8},{4,12},{8,0},{12,4},{1,9},{5,13},{9,1},{13,5},{2,10},{6,14},... | collective-permute-start | bytes 6152 | tf_op jit(solution)/shard_map/ppermute | solution.py:95
  30.4 16.1 %collective-permute-start.7 = (bf16[1,32,32,128]{3,2,1,0:T(8,128)(2,1)S(1)}, bf16[1,32,32,128]{3,2,1,0:T(8,128)(2,1)S(1)}, u32[]{:S(2)}, u32[]{:S(2)}) collective-permute-start(bf16[1,32,32,128]{3,2,1,0:T(8,128)(2,1)S(1)} %bitcast.255), channel_id=1, source_target_pairs={{0,8},{4,12},{8,0},{12,4},{1,9},{5,13},{9,1},{13,5},{2,10},{6,14},... | collective-permute-start | bytes 786440 | tf_op jit(solution)/shard_map/ppermute | solution.py:95
  30.6 31.2 %collective-permute-start.11 = (f32[1,2048,128]{2,1,0:T(8,128)}, f32[1,2048,128]{2,1,0:T(8,128)}, u32[]{:S(2)}, u32[]{:S(2)}) collective-permute-start(f32[1,2048,128]{2,1,0:T(8,128)} %select_bitcast_fusion.7), channel_id=1, source_target_pairs={{0,2},{1,3},{2,0},{3,1},{4,6},{5,7},{6,4},{7,5},{8,10},{9,11},{10,... | collective-permute-start | bytes 3145736 | tf_op jit(solution)/shard_map/ppermute | solution.py:44
  34.1 6.8 %copy-start.6 = (f32[1,2,2048,128]{3,2,1,0:T(8,128)}, f32[1,2,2048,128]{3,2,1,0:T(8,128)S(1)}, u32[]{:S(2)}) copy-start(f32[1,2,2048,128]{3,2,1,0:T(8,128)S(1)} %fusion.13) | copy-start | bytes 6291460
  34.1 6.8 %collective-permute-start.6 = (s32[2,32,16]{2,1,0:T(8,128)S(1)}, s32[2,32,16]{2,1,0:T(8,128)S(1)}, u32[]{:S(2)}, u32[]{:S(2)}) collective-permute-start(s32[2,32,16]{2,1,0:T(8,128)S(1)} %add_bitcast_fusion.1), channel_id=1, source_target_pairs={{0,4},{4,0},{8,12},{12,8},{1,5},{5,1},{9,13},{13,9},{2,6},{6,2},{1... | collective-permute-start | bytes 12296 | tf_op jit(solution)/shard_map/ppermute | solution.py:95
  39.4 39.0 %collective-permute-start.10 = (f32[1,2048,128]{2,1,0:T(8,128)}, f32[1,2048,128]{2,1,0:T(8,128)}, u32[]{:S(2)}, u32[]{:S(2)}) collective-permute-start(f32[1,2048,128]{2,1,0:T(8,128)} %select_bitcast_fusion.6), channel_id=1, source_target_pairs={{0,2},{1,3},{2,0},{3,1},{4,6},{5,7},{6,4},{7,5},{8,10},{9,11},{10,... | collective-permute-start | bytes 3145736 | tf_op jit(solution)/shard_map/ppermute | solution.py:44
  47.4 11.9 %collective-permute-start.8 = (bf16[2,32,32,128]{3,2,1,0:T(8,128)(2,1)}, bf16[2,32,32,128]{3,2,1,0:T(8,128)(2,1)S(1)}, u32[]{:S(2)}, u32[]{:S(2)}) collective-permute-start(bf16[2,32,32,128]{3,2,1,0:T(8,128)(2,1)} %maximum_bitcast_fusion.1), channel_id=1, source_target_pairs={{0,4},{4,0},{8,12},{12,8},{1,5},{5,1},{9,13},{13,9},{2,6},{6,2},{1... | collective-permute-start | bytes 1572872 | tf_op jit(solution)/shard_map/ppermute | solution.py:95
  61.9 16.5 %copy-start.7 = (f32[1,2,2048,128]{3,2,1,0:T(8,128)S(1)}, f32[1,2,2048,128]{3,2,1,0:T(8,128)}, u32[]{:S(2)}) copy-start(f32[1,2,2048,128]{3,2,1,0:T(8,128)} %copy-done.6) | copy-start | bytes 6291460
  92.3 1.8 %collective-permute-start.14 = (f32[16,128]{1,0:T(8,128)S(1)}, f32[16,128]{1,0:T(8,128)S(1)}, u32[]{:S(2)}, u32[]{:S(2)}) collective-permute-start(f32[16,128]{1,0:T(8,128)S(1)} %select_reduce_fusion.1), channel_id=1, source_target_pairs={{0,3},{1,0},{2,1},{3,2},{4,7},{5,4},{6,5},{7,6},{8,11},{9,8},{10,9... | collective-permute-start | bytes 24584 | tf_op jit(solution)/shard_map/ppermute | solution.py:118
  92.5 3.7 %collective-permute-start.13 = (f32[16,128]{1,0:T(8,128)S(1)}, f32[16,128]{1,0:T(8,128)S(1)}, u32[]{:S(2)}, u32[]{:S(2)}) collective-permute-start(f32[16,128]{1,0:T(8,128)S(1)} %select_reduce_fusion.1), channel_id=1, source_target_pairs={{0,2},{1,3},{2,0},{3,1},{4,6},{5,7},{6,4},{7,5},{8,10},{9,11},{10,... | collective-permute-start | bytes 24584 | tf_op jit(solution)/shard_map/ppermute | solution.py:118
  94.0 3.1 %collective-permute-start.12 = (f32[16,128]{1,0:T(8,128)S(1)}, f32[16,128]{1,0:T(8,128)S(1)}, u32[]{:S(2)}, u32[]{:S(2)}) collective-permute-start(f32[16,128]{1,0:T(8,128)S(1)} %select_reduce_fusion.1), channel_id=1, source_target_pairs={{0,1},{1,2},{2,3},{3,0},{4,5},{5,6},{6,7},{7,4},{8,9},{9,10},{10,1... | collective-permute-start | bytes 24584 | tf_op jit(solution)/shard_map/ppermute | solution.py:118
  97.1 5.0 %collective-permute-start.17 = (f32[16,128]{1,0:T(8,128)S(1)}, f32[16,128]{1,0:T(8,128)S(1)}, u32[]{:S(2)}, u32[]{:S(2)}) collective-permute-start(f32[16,128]{1,0:T(8,128)S(1)} %fusion.54), channel_id=1, source_target_pairs={{0,12},{4,0},{8,4},{12,8},{1,13},{5,1},{9,5},{13,9},{2,14},{6,2},{... | collective-permute-start | bytes 24584 | tf_op jit(solution)/shard_map/ppermute | solution.py:118
  100.7 4.5 %collective-permute-start.16 = (f32[16,128]{1,0:T(8,128)S(1)}, f32[16,128]{1,0:T(8,128)S(1)}, u32[]{:S(2)}, u32[]{:S(2)}) collective-permute-start(f32[16,128]{1,0:T(8,128)S(1)} %fusion.54), channel_id=1, source_target_pairs={{0,8},{4,12},{8,0},{12,4},{1,9},{5,13},{9,1},{13,5},{2,10},{6,14},... | collective-permute-start | bytes 24584 | tf_op jit(solution)/shard_map/ppermute | solution.py:118
  100.7 5.4 %collective-permute-start.15 = (f32[16,128]{1,0:T(8,128)S(1)}, f32[16,128]{1,0:T(8,128)S(1)}, u32[]{:S(2)}, u32[]{:S(2)}) collective-permute-start(f32[16,128]{1,0:T(8,128)S(1)} %fusion.54), channel_id=1, source_target_pairs={{0,4},{4,8},{8,12},{12,0},{1,5},{5,9},{9,13},{13,1},{2,6},{6,10},{... | collective-permute-start | bytes 24584 | tf_op jit(solution)/shard_map/ppermute | solution.py:118
  125.6 22.1 %collective-permute-start.18 = (bf16[1,4096,128]{2,1,0:T(8,128)(2,1)S(1)}, bf16[1,4096,128]{2,1,0:T(8,128)(2,1)S(1)}, u32[]{:S(2)}, u32[]{:S(2)}) collective-permute-start(bf16[1,4096,128]{2,1,0:T(8,128)(2,1)S(1)} %fusion.12), channel_id=1, source_target_pairs={{0,2},{1,3},{2,0},{3,1},{4,6},{5,7},{6,4},{7,5},{8,10},{9,11},{10,... | collective-permute-start | bytes 3145736 | tf_op jit(solution)/shard_map/ppermute | solution.py:44
  149.4 4.5 %collective-permute-start.19 = (bf16[2,4096,128]{2,1,0:T(8,128)(2,1)}, bf16[2,4096,128]{2,1,0:T(8,128)(2,1)}, u32[]{:S(2)}, u32[]{:S(2)}) collective-permute-start(bf16[2,4096,128]{2,1,0:T(8,128)(2,1)} %maximum_bitcast_fusion), channel_id=1, source_target_pairs={{0,1},{1,0},{2,3},{3,2},{4,5},{5,4},{6,7},{7,6},{8,9},{9,8},{10,11... | collective-permute-start | bytes 6291464 | tf_op jit(solution)/shard_map/ppermute | solution.py:44
  156.1 3.2 %slice-start.1 = ((s8[8388608]{0:T(1024)(128)(4,1)}), s8[4194304]{0:T(1024)(128)(4,1)S(1)}, s32[]{:S(2)}) async-start(s8[8388608]{0:T(1024)(128)(4,1)} %bitcast.242), calls=%async_computation.1 | async-start | bytes 8388608
  159.3 15.6 %copy-start.1 = (bf16[256,128]{1,0:T(8,128)(2,1)S(1)}, bf16[256,128]{1,0:T(8,128)(2,1)}, u32[]{:S(2)}) copy-start(bf16[256,128]{1,0:T(8,128)(2,1)} %param.6) | copy-start | bytes 196612
  160.8 6.8 %collective-permute-start.22 = (f32[256,128]{0,1:T(8,128)S(1)}, f32[256,128]{0,1:T(8,128)S(1)}, u32[]{:S(2)}, u32[]{:S(2)}) collective-permute-start(f32[256,128]{0,1:T(8,128)S(1)} %bitcast.257), channel_id=1, source_target_pairs={{0,12},{4,0},{8,4},{12,8},{1,13},{5,1},{9,5},{13,9},{2,14},{6,2},{... | collective-permute-start | bytes 393224 | tf_op jit(solution)/shard_map/ppermute | solution.py:118
  161.5 12.5 %collective-permute-start.21 = (f32[256,128]{0,1:T(8,128)S(1)}, f32[256,128]{0,1:T(8,128)S(1)}, u32[]{:S(2)}, u32[]{:S(2)}) collective-permute-start(f32[256,128]{0,1:T(8,128)S(1)} %bitcast.258), channel_id=1, source_target_pairs={{0,8},{4,12},{8,0},{12,4},{1,9},{5,13},{9,1},{13,5},{2,10},{6,14},... | collective-permute-start | bytes 393224 | tf_op jit(solution)/shard_map/ppermute | solution.py:118
  161.9 12.1 %collective-permute-start.20 = (f32[256,128]{0,1:T(8,128)S(1)}, f32[256,128]{0,1:T(8,128)S(1)}, u32[]{:S(2)}, u32[]{:S(2)}) collective-permute-start(f32[256,128]{0,1:T(8,128)S(1)} %bitcast.259), channel_id=1, source_target_pairs={{0,4},{4,8},{8,12},{12,0},{1,5},{5,9},{9,13},{13,1},{2,6},{6,10},{... | collective-permute-start | bytes 393224 | tf_op jit(solution)/shard_map/ppermute | solution.py:118
  (5 other events, 10.2 us)

commit v16 on v15

--- a/solution.py
+++ b/solution.py
@@ -144,7 +144,7 @@
 
     gathered = all_gather_many([queries, candidates], "mp")
 
-    chunks = 2 if row_share % (2 * BLK) == 0 else 1
+    chunks = 1
     split_rows = hidden.reshape(mp_count, chunks, row_share // chunks, hidden.shape[1])
     partials = [
         jnp.dot(split_rows[:, k], proj_w, preferred_element_type=jnp.float32).reshape(

time: 175 us -> 178 us (1.017)
  waiting for transfers between devices: 71.1 us -> 78.7 us
  local copies, waits for them, and re-layouts: 28.9 us -> 24.8 us
    ppermute x8, waiting for transfers between devices: 13.3 us -> 24.6 us  [all_gather_many(): others = lax.ppermute(arrs, axis, [(i, i ^ bit) for i in range(count)])]
    ppermute x9, waiting for transfers between devices: 16.9 us -> 10.6 us  [all_sum(): lax.ppermute(value, axis, [(i, (i + k) % count) for i in range(count)])]
    slice x1 -> x0, local copies, waits for them, and re-layouts: 5.76 us -> none  [local(): split_rows[:, k]]
    ppermute x9, starting transfers between devices: 9.44 us -> 13 us  [all_sum(): lax.ppermute(value, axis, [(i, (i + k) % count) for i in range(count)])]
    unnamed x31 -> x22, local copies, waits for them, and re-layouts: 6.8 us -> 10.3 us
    add x2 -> x0, other arithmetic: 2.92 us -> none  [local(): pieces = [k + xor_perm(t, 'mp', bit) for k, t in zip(keeps, sends)]]
    reduce_sum x1, other arithmetic: 0.63 us -> 3.47 us  [local(): scale = lax.rsqrt(jnp.sum(e_pre * e_pre, -1, keepdims=True) + 1e-06)]
    ppermute x6 -> x4, waiting for transfers between devices: 40.9 us -> 43.5 us  [xor_perm(): return lax.ppermute(value, axis, [(i, i ^ bit) for i in range(count)])]
  transfers between devices with their start and end apart: 23 -> 21, of which waited for: 13 -> 14; matrix products, arithmetic and copies ran while one was open for 13% -> 5% of each run, Pallas kernels for 0% -> 0%
where the time goes in v16:
time: 178 us; the launch traced here: 177 us
  waiting for transfers between devices  78.7 us (44%)
  starting transfers between devices  27.1 us (15%)
  local copies, waits for them, and re-layouts  24.8 us (14%)
  other arithmetic  23.2 us (13%)
  matrix products  22 us (12%)
    ppermute x4, waiting for transfers between devices, xor_perm(): return lax.ppermute(value, axis, [(i, i ^ bit) for i in range(count)])  43.5 us
    ppermute x8, waiting for transfers between devices, all_gather_many(): others = lax.ppermute(arrs, axis, [(i, i ^ bit) for i in range(count)])  24.6 us
    ppermute x9, starting transfers between devices, all_sum(): lax.ppermute(value, axis, [(i, (i + k) % count) for i in range(count)])  13 us
    ppermute x8, starting transfers between devices, all_gather_many(): others = lax.ppermute(arrs, axis, [(i, i ^ bit) for i in range(count)])  11.2 us
    ppermute x9, waiting for transfers between devices, all_sum(): lax.ppermute(value, axis, [(i, (i + k) % count) for i in range(count)])  10.6 us
    unnamed x22, local copies, waits for them, and re-layouts  10.3 us
    dot_general x1, matrix products, local(): jnp.einsum('scij,scie->scje', weights, q_e, preferred_element_type=jnp.fl...  6.94 us
    dot_general x1, matrix products, local(): jnp.dot(split_rows[:, k], proj_w, preferred_element_type=jnp.float32)  5.7 us
  transfers between devices with their start and end apart: 21, of which 14 were waited for; matrix products, arithmetic and copies ran while one was open for 5% of the time, Pallas kernels for 0%

profile of v16, /device:TPU:0, one launch (start us, length us, event | category | flops | bytes accessed | tf_op | source)
XLA Modules:
  0.0 176.9 jit_solution(1687739752520059296)
XLA Ops:
  1.5 5.7 %fusion.22 = f32[2,2,4096,128]{3,2,1,0:T(8,128)S(1)} fusion(bf16[2,2,4096,256]{3,2,1,0:T(8,128)(2,1)} %bitcast.210, bf16[256,128]{1,0:T(8,128)(2,1)S(1)} %copy-done), kind=kOutput, calls=%fused_computation.62 | convolution fusion | flops 1073741824 | bytes 16842752 | tf_op jit(solution)/shard_map/dot_general | solution.py:150
  7.2 2.6 %select_bitcast_fusion = f32[2,4096,128]{2,1,0:T(8,128)} fusion(f32[2,2,4096,128]{3,2,1,0:T(8,128)S(1)} %fusion.22, pred[]{:T(512)S(6)} %eq.81), kind=kLoop, calls=%fused_computation.15 | loop fusion | flops 1048576 | bytes 12582913 | tf_op jit(solution)/shard_map/jit(_where)/select_n | solution.py:62
  12.1 2.5 %collective-permute-start.1 = (bf16[1,8,32,128]{3,2,1,0:T(8,128)(2,1)S(1)}, bf16[1,8,32,128]{3,2,1,0:T(8,128)(2,1)S(1)}, u32[]{:S(2)}, u32[]{:S(2)}) collective-permute-start(bf16[1,8,32,128]{3,2,1,0:T(8,128)(2,1)S(1)} %bitcast.231), channel_id=1, source_target_pairs={{0,2},{1,3},{2,0},{3,1},{4,6},{5,7},{6,4},{7,5},{8,10},{9,11},{10,... | collective-permute-start | bytes 196616 | tf_op jit(solution)/shard_map/ppermute | solution.py:95
  14.7 3.5 %collective-permute-done.3 = s32[1,8,16]{2,1,0:T(8,128)S(1)} collective-permute-done((s32[1,8,16]{2,1,0:T(8,128)S(1)}, s32[1,8,16]{2,1,0:T(8,128)S(1)}, u32[]{:S(2)}, u32[]{:S(2)}) %collective-permute-start.3) | collective-permute-done | bytes 544 | tf_op jit(solution)/shard_map/ppermute | solution.py:95
  20.0 5.2 %fusion.2 = f32[1,2,4096,128]{3,2,1,0:T(8,128)S(1)} fusion(f32[2,4096,128]{2,1,0:T(8,128)} %collective-permute-done, f32[2,2,4096,128]{3,2,1,0:T(8,128)} %copy-done.3, pred[]{:T(512)S(6)} %eq.81), kind=kLoop, calls=%fused_computation.10 | loop fusion | flops 2097152 | bytes 16777216 | tf_op jit(solution)/shard_map/reshape | solution.py:59
  25.2 1.9 %copy-done.4 = f32[1,2,4096,128]{3,2,1,0:T(8,128)} copy-done((f32[1,2,4096,128]{3,2,1,0:T(8,128)}, f32[1,2,4096,128]{3,2,1,0:T(8,128)S(1)}, u32[]{:S(2)}) %copy-start.4) | copy-done | bytes 4194328
  27.4 3.3 %collective-permute-start.5 = (s32[1,32,16]{2,1,0:T(8,128)S(1)}, s32[1,32,16]{2,1,0:T(8,128)S(1)}, u32[]{:S(2)}, u32[]{:S(2)}) collective-permute-start(s32[1,32,16]{2,1,0:T(8,128)S(1)} %bitcast.229), channel_id=1, source_target_pairs={{0,8},{4,12},{8,0},{12,4},{1,9},{5,13},{9,1},{13,5},{2,10},{6,14},... | collective-permute-start | bytes 6152 | tf_op jit(solution)/shard_map/ppermute | solution.py:95
  32.4 2.0 %collective-permute-start.6 = (s32[2,32,16]{2,1,0:T(8,128)S(1)}, s32[2,32,16]{2,1,0:T(8,128)S(1)}, u32[]{:S(2)}, u32[]{:S(2)}) collective-permute-start(s32[2,32,16]{2,1,0:T(8,128)S(1)} %add_bitcast_fusion.1), channel_id=1, source_target_pairs={{0,4},{4,0},{8,12},{12,8},{1,5},{5,1},{9,13},{13,9},{2,6},{6,2},{1... | collective-permute-start | bytes 12296 | tf_op jit(solution)/shard_map/ppermute | solution.py:95
  35.8 2.6 %collective-permute-start.7 = (bf16[1,32,32,128]{3,2,1,0:T(8,128)(2,1)S(1)}, bf16[1,32,32,128]{3,2,1,0:T(8,128)(2,1)S(1)}, u32[]{:S(2)}, u32[]{:S(2)}) collective-permute-start(bf16[1,32,32,128]{3,2,1,0:T(8,128)(2,1)S(1)} %bitcast.220), channel_id=1, source_target_pairs={{0,8},{4,12},{8,0},{12,4},{1,9},{5,13},{9,1},{13,5},{2,10},{6,14},... | collective-permute-start | bytes 786440 | tf_op jit(solution)/shard_map/ppermute | solution.py:95
  39.4 1.9 %gather_fusion.3 = s32[256]{0:T(256)S(1)} fusion(s32[16,128]{1,0:T(8,128)S(1)} %reshape_reshape_reshape.4, s32[256]{0:T(256)S(1)} %reshape.537), kind=kCustom, calls=%fused_computation.3 | custom fusion | bytes 4096 | tf_op jit(solution)/shard_map/jit(take_along_axis)/gather | solution.py:177
  41.8 1.9 %gather_fusion = s32[256]{0:T(256)S(1)} fusion(s32[256]{0:T(256)S(1)} %copy-done.2, s32[1024]{0:T(1024)S(1)} %pad_clamp_fusion.2), kind=kCustom, calls=%fused_computation | custom fusion | bytes 3072 | tf_op jit(solution)/shard_map/gather | solution.py:15
  43.9 5.1 %collective-permute-done.7 = bf16[1,32,32,128]{3,2,1,0:T(8,128)(2,1)S(1)} collective-permute-done((bf16[1,32,32,128]{3,2,1,0:T(8,128)(2,1)S(1)}, bf16[1,32,32,128]{3,2,1,0:T(8,128)(2,1)S(1)}, u32[]{:S(2)}, u32[]{:S(2)}) %collective-permute-start.7) | collective-permute-done | bytes 262176 | tf_op jit(solution)/shard_map/ppermute | solution.py:95
  49.3 13.3 %collective-permute-done.8 = bf16[2,32,32,128]{3,2,1,0:T(8,128)(2,1)S(1)} collective-permute-done((bf16[2,32,32,128]{3,2,1,0:T(8,128)(2,1)S(1)}, bf16[2,32,32,128]{3,2,1,0:T(8,128)(2,1)S(1)}, u32[]{:S(2)}, u32[]{:S(2)}) %collective-permute-start.8) | collective-permute-done | bytes 524320 | tf_op jit(solution)/shard_map/ppermute | solution.py:95
  62.9 2.2 %gather_fusion.1 = bf16[256,32,128]{2,1,0:T(8,128)(2,1)} fusion(bf16[128,32,128]{2,1,0:T(8,128)(2,1)S(1)} %bitcast.217, s32[1024]{0:T(1024)S(1)} %pad_clamp_fusion.1), kind=kCustom, calls=%fused_computation.1 | custom fusion | bytes 4195328 | tf_op jit(solution)/shard_map/gather | solution.py:181
  65.1 15.6 %collective-permute-done.9 = f32[1,4096,128]{2,1,0:T(8,128)} collective-permute-done((f32[1,4096,128]{2,1,0:T(8,128)S(1)}, f32[1,4096,128]{2,1,0:T(8,128)}, u32[]{:S(2)}, u32[]{:S(2)}) %collective-permute-start.9) | collective-permute-done | bytes 2097184 | tf_op jit(solution)/shard_map/ppermute | solution.py:44
  80.7 3.5 %fusion.9 = (f32[4096]{0:T(1024)S(1)}, f32[1,4096,128]{2,1,0:T(8,128)S(1)}) fusion(f32[1,4096,128]{2,1,0:T(8,128)} %collective-permute-done.9, f32[1,2,4096,128]{3,2,1,0:T(8,128)} %copy-done.4, pred[]{:T(512)S(6)} %eq.80), kind=kLoop, calls=%fused_computation.25 | loop fusion | flops 2093056 | bytes 8404993 | tf_op jit(solution)/shard_map/reduce_sum | solution.py:184
  85.0 3.0 %gather_fusion.2 = bf16[256,64,128]{2,1,0:T(8,128)(2,1)} fusion(bf16[64,64,128]{2,1,0:T(8,128)(2,1)S(1)} %multiply_convert_fusion.1, s32[1024]{0:T(1024)S(1)} %pad_clamp_fusion), kind=kCustom, calls=%fused_computation.2 | custom fusion | bytes 8389632 | tf_op jit(solution)/shard_map/gather | solution.py:188
  88.0 5.2 %select_reduce_fusion = (f32[16,16,32]{2,1,0:T(8,128)S(1)}, f32[16,16,32,64]{3,2,1,0:T(8,128)S(1)}) fusion(pred[16,16,64]{2,1,0:T(8,128)(4,1)S(1)} %add_compare_fusion, bf16[16,16,32,128]{3,2,1,0:T(8,128)(2,1)} %bitcast.218, bf16[16,16,64,128]{3,2,1,0:T(8,128)(2,1)} %bitcast.216), kind=kOutput, calls=%fused_computation.16 | convolution fusion | flops 135258112 | bytes 8437760 | tf_op jit(solution)/shard_map/scie,scje->scij/dot_general | solution.py:190
  93.2 1.9 %copy-done.5 = f32[16,16,32,64]{3,2,1,0:T(8,128)} copy-done((f32[16,16,32,64]{3,2,1,0:T(8,128)}, f32[16,16,32,64]{3,2,1,0:T(8,128)S(1)}, u32[]{:S(2)}) %copy-start.5) | copy-done | bytes 2097176
  95.2 2.4 %fusion.5 = f32[16,16,32]{2,1,0:T(8,128)S(1)} fusion(f32[16,16,32,64]{3,2,1,0:T(8,128)S(1)} %get-tuple-element.55, f32[16,16,32]{2,1,0:T(8,128)S(1)} %get-tuple-element.54, pred[16,16,64]{2,1,0:T(8,128)(4,1)S(1)} %add_compare_fusion), kind=kLoop, calls=%fused_computation.17 | loop fusion | flops 1564672 | bytes 2179072 | tf_op jit(solution)/shard_map/reduce_sum | solution.py:22
  102.8 2.6 %collective-permute-start.14 = (f32[16,128]{1,0:T(8,128)S(1)}, f32[16,128]{1,0:T(8,128)S(1)}, u32[]{:S(2)}, u32[]{:S(2)}) collective-permute-start(f32[16,128]{1,0:T(8,128)S(1)} %fusion.48), channel_id=1, source_target_pairs={{0,8},{4,12},{8,0},{12,4},{1,9},{5,13},{9,1},{13,5},{2,10},{6,14},... | collective-permute-start | bytes 24584 | tf_op jit(solution)/shard_map/ppermute | solution.py:118
  105.4 2.4 %collective-permute-start.15 = (f32[16,128]{1,0:T(8,128)S(1)}, f32[16,128]{1,0:T(8,128)S(1)}, u32[]{:S(2)}, u32[]{:S(2)}) collective-permute-start(f32[16,128]{1,0:T(8,128)S(1)} %fusion.48), channel_id=1, source_target_pairs={{0,12},{4,0},{8,4},{12,8},{1,13},{5,1},{9,5},{13,9},{2,14},{6,2},{... | collective-permute-start | bytes 24584 | tf_op jit(solution)/shard_map/ppermute | solution.py:118
  109.9 1.9 %gather_fusion.4 = f32[256]{0:T(256)S(1)} fusion(f32[16,128]{1,0:T(8,128)S(1)} %reshape.509, s32[256]{0:T(256)S(1)} %reshape.537), kind=kCustom, calls=%fused_computation.4 | custom fusion | bytes 4096 | tf_op jit(solution)/shard_map/jit(take_along_axis)/gather | solution.py:200
  111.9 6.9 %multiply_convert_fusion = bf16[16,16,64,128]{3,2,1,0:T(8,128)(2,1)S(1)} fusion(f32[16,16]{1,0:T(8,128)S(1)} %select_multiply_fusion, bf16[16,16,32,128]{3,2,1,0:T(8,128)(2,1)} %bitcast.219, f32[16,16,32,64]{3,2,1,0:T(8,128)} %copy-done.5, f32[16,16,32]{2,1,0:T(8,128)S(1)} %fusion.5, f32[16,16,32]{2,1,0:T(8,128)S(1)} %get-tuple-element.54, ...), kind=kOutput, calls=%fused_computation.5 | convolution fusion | flops 140509184 | bytes 8471552 | tf_op jit(solution)/shard_map/scij,scie->scje/dot_general | solution.py:193
  118.8 2.6 %fusion.14 = f32[64,64,128]{2,0,1:T(8,128)S(1)} fusion(bf16[16,16,64,128]{3,2,1,0:T(8,128)(2,1)S(1)} %multiply_convert_fusion, s32[16,16]{0,1:T(8,128)S(1)} %copy.91, pred[16,16]{0,1:T(8,128)(4,1)S(1)} %copy.92), kind=kOutput, calls=%fused_computation.35 | convolution fusion | flops 268468224 | bytes 6292736 | tf_op jit(solution)/shard_map/scb,scje->bje/dot_general | solution.py:204
  123.3 1.9 %fusion.8 = bf16[1,4096,128]{2,1,0:T(8,128)(2,1)S(1)} fusion(f32[1,4096,128]{2,1,0:T(8,128)S(1)} %get-tuple-element.25, f32[4096]{0:T(1024)S(1)} %fusion.6, f32[4096]{0:T(1024)S(1)} %get-tuple-element.44, f32[4096]{0:T(1024)S(1)} %get-tuple-element.45, f32[1,4096,128]{2,1,0:T(8,128)S(1)} %bitcast.215), kind=kLoop, calls=%fused_computation.23 | loop fusion | flops 2621440 | bytes 5292032 | tf_op jit(solution)/shard_map/convert_element_type | solution.py:212
  126.2 23.4 %collective-permute-done.16 = bf16[1,4096,128]{2,1,0:T(8,128)(2,1)S(1)} collective-permute-done((bf16[1,4096,128]{2,1,0:T(8,128)(2,1)S(1)}, bf16[1,4096,128]{2,1,0:T(8,128)(2,1)S(1)}, u32[]{:S(2)}, u32[]{:S(2)}) %collective-permute-start.16) | collective-permute-done | bytes 1048608 | tf_op jit(solution)/shard_map/ppermute | solution.py:44
  151.3 4.5 %collective-permute-done.17 = bf16[2,4096,128]{2,1,0:T(8,128)(2,1)} collective-permute-done((bf16[2,4096,128]{2,1,0:T(8,128)(2,1)}, bf16[2,4096,128]{2,1,0:T(8,128)(2,1)}, u32[]{:S(2)}, u32[]{:S(2)}) %collective-permute-start.17) | collective-permute-done | bytes 2097184 | tf_op jit(solution)/shard_map/ppermute | solution.py:44
  155.8 1.9 %select_bitcast_fusion.2 = (bf16[2,1,4096,128]{3,2,0,1:T(8,128)(2,1)S(1)}, bf16[2,1,4096,128]{3,2,0,1:T(8,128)(2,1)S(1)}) fusion(bf16[2,4096,128]{2,1,0:T(8,128)(2,1)} %collective-permute-done.17, pred[]{:T(512)S(6)} %eq.81, bf16[1,1,4096,128]{3,2,1,0:T(8,128)(2,1)S(1)} %get-tuple-element.31, bf16[1,1,4096,128]{3,2,1,0:T(8,128)(2,1)S(1)} %get-tuple-element.30), kind=kLoop, calls=%fused_computation.28 | loop fusion | flops 3145728 | bytes 8388609 | tf_op jit(solution)/shard_map/stack | solution.py:81
  163.7 3.5 %collective-permute-start.19 = (f32[256,128]{0,1:T(8,128)S(1)}, f32[256,128]{0,1:T(8,128)S(1)}, u32[]{:S(2)}, u32[]{:S(2)}) collective-permute-start(f32[256,128]{0,1:T(8,128)S(1)} %bitcast.223), channel_id=1, source_target_pairs={{0,8},{4,12},{8,0},{12,4},{1,9},{5,13},{9,1},{13,5},{2,10},{6,14},... | collective-permute-start | bytes 393224 | tf_op jit(solution)/shard_map/ppermute | solution.py:118
  167.7 3.3 %collective-permute-done.18 = f32[256,128]{0,1:T(8,128)S(1)} collective-permute-done((f32[256,128]{0,1:T(8,128)S(1)}, f32[256,128]{0,1:T(8,128)S(1)}, u32[]{:S(2)}, u32[]{:S(2)}) %collective-permute-start.18) | collective-permute-done | bytes 131104 | tf_op jit(solution)/shard_map/ppermute | solution.py:118
  171.0 5.1 %collective-permute-done.19 = f32[256,128]{0,1:T(8,128)S(1)} collective-permute-done((f32[256,128]{0,1:T(8,128)S(1)}, f32[256,128]{0,1:T(8,128)S(1)}, u32[]{:S(2)}, u32[]{:S(2)}) %collective-permute-start.19) | collective-permute-done | bytes 131104 | tf_op jit(solution)/shard_map/ppermute | solution.py:118
  (124 shorter events, 30.2 us)
Async XLA Ops:
  0.6 0.8 copy-start
  7.2 4.5 %copy-start.3 = (f32[2,2,4096,128]{3,2,1,0:T(8,128)}, f32[2,2,4096,128]{3,2,1,0:T(8,128)S(1)}, u32[]{:S(2)}) copy-start(f32[2,2,4096,128]{3,2,1,0:T(8,128)S(1)} %fusion.22) | copy-start | bytes 25165828
  7.2 4.9 %copy-start.6 = (bf16[8,32,128]{2,1,0:T(8,128)(2,1)S(1)}, bf16[8,32,128]{2,1,0:T(8,128)(2,1)}, u32[]{:S(2)}) copy-start(bf16[8,32,128]{2,1,0:T(8,128)(2,1)} %param.7) | copy-start | bytes 196612
  7.2 7.4 %copy-start.7 = (s32[8,16]{1,0:T(8,128)S(1)}, s32[8,16]{1,0:T(8,128)}, u32[]{:S(2)}) copy-start(s32[8,16]{1,0:T(8,128)} %param.9) | copy-start | bytes 1540
  11.7 8.3 %collective-permute-start = (f32[2,4096,128]{2,1,0:T(8,128)}, f32[2,4096,128]{2,1,0:T(8,128)}, u32[]{:S(2)}, u32[]{:S(2)}) collective-permute-start(f32[2,4096,128]{2,1,0:T(8,128)} %select_bitcast_fusion), channel_id=1, source_target_pairs={{0,1},{1,0},{2,3},{3,2},{4,5},{5,4},{6,7},{7,6},{8,9},{9,8},{10,11... | collective-permute-start | bytes 12582920 | tf_op jit(solution)/shard_map/ppermute | solution.py:44
  12.1 6.2 %collective-permute-start.1 = (bf16[1,8,32,128]{3,2,1,0:T(8,128)(2,1)S(1)}, bf16[1,8,32,128]{3,2,1,0:T(8,128)(2,1)S(1)}, u32[]{:S(2)}, u32[]{:S(2)}) collective-permute-start(bf16[1,8,32,128]{3,2,1,0:T(8,128)(2,1)S(1)} %bitcast.231), channel_id=1, source_target_pairs={{0,2},{1,3},{2,0},{3,1},{4,6},{5,7},{6,4},{7,5},{8,10},{9,11},{10,... | collective-permute-start | bytes 196616 | tf_op jit(solution)/shard_map/ppermute | solution.py:95
  14.6 3.6 %collective-permute-start.3 = (s32[1,8,16]{2,1,0:T(8,128)S(1)}, s32[1,8,16]{2,1,0:T(8,128)S(1)}, u32[]{:S(2)}, u32[]{:S(2)}) collective-permute-start(s32[1,8,16]{2,1,0:T(8,128)S(1)} %bitcast.239), channel_id=1, source_target_pairs={{0,2},{1,3},{2,0},{3,1},{4,6},{5,7},{6,4},{7,5},{8,10},{9,11},{10,... | collective-permute-start | bytes 1544 | tf_op jit(solution)/shard_map/ppermute | solution.py:95
  18.2 1.2 collective-permute-start.4
  18.4 1.5 collective-permute-start.2
  25.2 1.9 %copy-start.4 = (f32[1,2,4096,128]{3,2,1,0:T(8,128)}, f32[1,2,4096,128]{3,2,1,0:T(8,128)S(1)}, u32[]{:S(2)}) copy-start(f32[1,2,4096,128]{3,2,1,0:T(8,128)S(1)} %fusion.2) | copy-start | bytes 12582916
  27.4 5.0 %collective-permute-start.5 = (s32[1,32,16]{2,1,0:T(8,128)S(1)}, s32[1,32,16]{2,1,0:T(8,128)S(1)}, u32[]{:S(2)}, u32[]{:S(2)}) collective-permute-start(s32[1,32,16]{2,1,0:T(8,128)S(1)} %bitcast.229), channel_id=1, source_target_pairs={{0,8},{4,12},{8,0},{12,4},{1,9},{5,13},{9,1},{13,5},{2,10},{6,14},... | collective-permute-start | bytes 6152 | tf_op jit(solution)/shard_map/ppermute | solution.py:95
  32.4 6.1 %collective-permute-start.6 = (s32[2,32,16]{2,1,0:T(8,128)S(1)}, s32[2,32,16]{2,1,0:T(8,128)S(1)}, u32[]{:S(2)}, u32[]{:S(2)}) collective-permute-start(s32[2,32,16]{2,1,0:T(8,128)S(1)} %add_bitcast_fusion.1), channel_id=1, source_target_pairs={{0,4},{4,0},{8,12},{12,8},{1,5},{5,1},{9,13},{13,9},{2,6},{6,2},{1... | collective-permute-start | bytes 12296 | tf_op jit(solution)/shard_map/ppermute | solution.py:95
  34.4 46.3 %collective-permute-start.9 = (f32[1,4096,128]{2,1,0:T(8,128)S(1)}, f32[1,4096,128]{2,1,0:T(8,128)}, u32[]{:S(2)}, u32[]{:S(2)}) collective-permute-start(f32[1,4096,128]{2,1,0:T(8,128)S(1)} %select_bitcast_fusion.3), channel_id=1, source_target_pairs={{0,2},{1,3},{2,0},{3,1},{4,6},{5,7},{6,4},{7,5},{8,10},{9,11},{10,... | collective-permute-start | bytes 6291464 | tf_op jit(solution)/shard_map/ppermute | solution.py:44
  35.8 13.1 %collective-permute-start.7 = (bf16[1,32,32,128]{3,2,1,0:T(8,128)(2,1)S(1)}, bf16[1,32,32,128]{3,2,1,0:T(8,128)(2,1)S(1)}, u32[]{:S(2)}, u32[]{:S(2)}) collective-permute-start(bf16[1,32,32,128]{3,2,1,0:T(8,128)(2,1)S(1)} %bitcast.220), channel_id=1, source_target_pairs={{0,8},{4,12},{8,0},{12,4},{1,9},{5,13},{9,1},{13,5},{2,10},{6,14},... | collective-permute-start | bytes 786440 | tf_op jit(solution)/shard_map/ppermute | solution.py:95
  39.4 2.4 %copy-start.2 = (s32[256]{0:T(256)S(1)}, s32[256]{0:T(256)}, u32[]{:S(2)}) copy-start(s32[256]{0:T(256)} %param.8) | copy-start | bytes 3076
  49.0 13.6 %collective-permute-start.8 = (bf16[2,32,32,128]{3,2,1,0:T(8,128)(2,1)S(1)}, bf16[2,32,32,128]{3,2,1,0:T(8,128)(2,1)S(1)}, u32[]{:S(2)}, u32[]{:S(2)}) collective-permute-start(bf16[2,32,32,128]{3,2,1,0:T(8,128)(2,1)S(1)} %maximum_bitcast_fusion.1), channel_id=1, source_target_pairs={{0,4},{4,0},{8,12},{12,8},{1,5},{5,1},{9,13},{13,9},{2,6},{6,2},{1... | collective-permute-start | bytes 1572872 | tf_op jit(solution)/shard_map/ppermute | solution.py:95
  93.2 2.0 %copy-start.5 = (f32[16,16,32,64]{3,2,1,0:T(8,128)}, f32[16,16,32,64]{3,2,1,0:T(8,128)S(1)}, u32[]{:S(2)}) copy-start(f32[16,16,32,64]{3,2,1,0:T(8,128)S(1)} %get-tuple-element.55) | copy-start | bytes 6291460
  97.8 3.5 %collective-permute-start.10 = (f32[16,128]{1,0:T(8,128)S(1)}, f32[16,128]{1,0:T(8,128)S(1)}, u32[]{:S(2)}, u32[]{:S(2)}) collective-permute-start(f32[16,128]{1,0:T(8,128)S(1)} %select_reduce_fusion.1), channel_id=1, source_target_pairs={{0,1},{1,2},{2,3},{3,0},{4,5},{5,6},{6,7},{7,4},{8,9},{9,10},{10,1... | collective-permute-start | bytes 24584 | tf_op jit(solution)/shard_map/ppermute | solution.py:118
  97.9 3.7 %collective-permute-start.11 = (f32[16,128]{1,0:T(8,128)S(1)}, f32[16,128]{1,0:T(8,128)S(1)}, u32[]{:S(2)}, u32[]{:S(2)}) collective-permute-start(f32[16,128]{1,0:T(8,128)S(1)} %select_reduce_fusion.1), channel_id=1, source_target_pairs={{0,2},{1,3},{2,0},{3,1},{4,6},{5,7},{6,4},{7,5},{8,10},{9,11},{10,... | collective-permute-start | bytes 24584 | tf_op jit(solution)/shard_map/ppermute | solution.py:118
  99.5 2.8 %collective-permute-start.12 = (f32[16,128]{1,0:T(8,128)S(1)}, f32[16,128]{1,0:T(8,128)S(1)}, u32[]{:S(2)}, u32[]{:S(2)}) collective-permute-start(f32[16,128]{1,0:T(8,128)S(1)} %select_reduce_fusion.1), channel_id=1, source_target_pairs={{0,3},{1,0},{2,1},{3,2},{4,7},{5,4},{6,5},{7,6},{8,11},{9,8},{10,9... | collective-permute-start | bytes 24584 | tf_op jit(solution)/shard_map/ppermute | solution.py:118
  102.2 5.6 %collective-permute-start.13 = (f32[16,128]{1,0:T(8,128)S(1)}, f32[16,128]{1,0:T(8,128)S(1)}, u32[]{:S(2)}, u32[]{:S(2)}) collective-permute-start(f32[16,128]{1,0:T(8,128)S(1)} %fusion.48), channel_id=1, source_target_pairs={{0,4},{4,8},{8,12},{12,0},{1,5},{5,9},{9,13},{13,1},{2,6},{6,10},{... | collective-permute-start | bytes 24584 | tf_op jit(solution)/shard_map/ppermute | solution.py:118
  102.8 5.1 %collective-permute-start.14 = (f32[16,128]{1,0:T(8,128)S(1)}, f32[16,128]{1,0:T(8,128)S(1)}, u32[]{:S(2)}, u32[]{:S(2)}) collective-permute-start(f32[16,128]{1,0:T(8,128)S(1)} %fusion.48), channel_id=1, source_target_pairs={{0,8},{4,12},{8,0},{12,4},{1,9},{5,13},{9,1},{13,5},{2,10},{6,14},... | collective-permute-start | bytes 24584 | tf_op jit(solution)/shard_map/ppermute | solution.py:118
  105.4 3.8 %collective-permute-start.15 = (f32[16,128]{1,0:T(8,128)S(1)}, f32[16,128]{1,0:T(8,128)S(1)}, u32[]{:S(2)}, u32[]{:S(2)}) collective-permute-start(f32[16,128]{1,0:T(8,128)S(1)} %fusion.48), channel_id=1, source_target_pairs={{0,12},{4,0},{8,4},{12,8},{1,13},{5,1},{9,5},{13,9},{2,14},{6,2},{... | collective-permute-start | bytes 24584 | tf_op jit(solution)/shard_map/ppermute | solution.py:118
  125.2 24.3 %collective-permute-start.16 = (bf16[1,4096,128]{2,1,0:T(8,128)(2,1)S(1)}, bf16[1,4096,128]{2,1,0:T(8,128)(2,1)S(1)}, u32[]{:S(2)}, u32[]{:S(2)}) collective-permute-start(bf16[1,4096,128]{2,1,0:T(8,128)(2,1)S(1)} %fusion.8), channel_id=1, source_target_pairs={{0,2},{1,3},{2,0},{3,1},{4,6},{5,7},{6,4},{7,5},{8,10},{9,11},{10,... | collective-permute-start | bytes 3145736 | tf_op jit(solution)/shard_map/ppermute | solution.py:44
  151.3 4.5 %collective-permute-start.17 = (bf16[2,4096,128]{2,1,0:T(8,128)(2,1)}, bf16[2,4096,128]{2,1,0:T(8,128)(2,1)}, u32[]{:S(2)}, u32[]{:S(2)}) collective-permute-start(bf16[2,4096,128]{2,1,0:T(8,128)(2,1)} %maximum_bitcast_fusion), channel_id=1, source_target_pairs={{0,1},{1,0},{2,3},{3,2},{4,5},{5,4},{6,7},{7,6},{8,9},{9,8},{10,11... | collective-permute-start | bytes 6291464 | tf_op jit(solution)/shard_map/ppermute | solution.py:44
  157.6 2.2 %slice-start = ((s8[8388608]{0:T(1024)(128)(4,1)}), s8[4194304]{0:T(1024)(128)(4,1)S(1)}, s32[]{:S(2)}) async-start(s8[8388608]{0:T(1024)(128)(4,1)} %bitcast.211), calls=%async_computation | async-start | bytes 8388608
  158.0 3.2 %slice-start.1 = ((s8[8388608]{0:T(1024)(128)(4,1)}), s8[4194304]{0:T(1024)(128)(4,1)S(1)}, s32[]{:S(2)}) async-start(s8[8388608]{0:T(1024)(128)(4,1)} %bitcast.211), calls=%async_computation.1 | async-start | bytes 8388608
  161.2 15.7 %copy-start.1 = (bf16[256,128]{1,0:T(8,128)(2,1)S(1)}, bf16[256,128]{1,0:T(8,128)(2,1)}, u32[]{:S(2)}) copy-start(bf16[256,128]{1,0:T(8,128)(2,1)} %param.6) | copy-start | bytes 196612
  162.7 8.3 %collective-permute-start.18 = (f32[256,128]{0,1:T(8,128)S(1)}, f32[256,128]{0,1:T(8,128)S(1)}, u32[]{:S(2)}, u32[]{:S(2)}) collective-permute-start(f32[256,128]{0,1:T(8,128)S(1)} %bitcast.222), channel_id=1, source_target_pairs={{0,4},{4,8},{8,12},{12,0},{1,5},{5,9},{9,13},{13,1},{2,6},{6,10},{... | collective-permute-start | bytes 393224 | tf_op jit(solution)/shard_map/ppermute | solution.py:118
  163.7 12.4 %collective-permute-start.19 = (f32[256,128]{0,1:T(8,128)S(1)}, f32[256,128]{0,1:T(8,128)S(1)}, u32[]{:S(2)}, u32[]{:S(2)}) collective-permute-start(f32[256,128]{0,1:T(8,128)S(1)} %bitcast.223), channel_id=1, source_target_pairs={{0,8},{4,12},{8,0},{12,4},{1,9},{5,13},{9,1},{13,5},{2,10},{6,14},... | collective-permute-start | bytes 393224 | tf_op jit(solution)/shard_map/ppermute | solution.py:118
  167.1 8.9 %collective-permute-start.20 = (f32[256,128]{0,1:T(8,128)S(1)}, f32[256,128]{0,1:T(8,128)S(1)}, u32[]{:S(2)}, u32[]{:S(2)}) collective-permute-start(f32[256,128]{0,1:T(8,128)S(1)} %bitcast.224), channel_id=1, source_target_pairs={{0,12},{4,0},{8,4},{12,8},{1,13},{5,1},{9,5},{13,9},{2,14},{6,2},{... | collective-permute-start | bytes 393224 | tf_op jit(solution)/shard_map/ppermute | solution.py:118

commit v17 on v15

--- a/solution.py
+++ b/solution.py
@@ -154,8 +154,8 @@
     ]
     if is_pow2(mp_count) and mp_count > 1:
         keeps, sends, bit = halving_steps(partials, "mp")
-        last, gathered = lax.optimization_barrier((sends[-1], gathered))
-        sends = sends[:-1] + [last]
+        first, gathered = lax.optimization_barrier((sends[0], gathered))
+        sends = [first] + sends[1:]
         pieces = [k + xor_perm(t, "mp", bit) for k, t in zip(keeps, sends)]
         pieces = [p.reshape(-1, emb_width) for p in pieces]
     else:

time: 175 us -> 169 us (0.966)
  matrix products: 23.3 us -> 19.8 us
  waiting for transfers between devices: 71.1 us -> 67.8 us
  local copies, waits for them, and re-layouts: 28.9 us -> 26.5 us
    ppermute x8, waiting for transfers between devices: 13.3 us -> 22.4 us  [all_gather_many(): others = lax.ppermute(arrs, axis, [(i, i ^ bit) for i in range(count)])]
    ppermute x6, waiting for transfers between devices: 40.9 us -> 33.5 us  [xor_perm(): return lax.ppermute(value, axis, [(i, i ^ bit) for i in range(count)])]
    ppermute x9, waiting for transfers between devices: 16.9 us -> 11.9 us  [all_sum(): lax.ppermute(value, axis, [(i, (i + k) % count) for i in range(count)])]
    ppermute x9, starting transfers between devices: 9.44 us -> 13 us  [all_sum(): lax.ppermute(value, axis, [(i, (i + k) % count) for i in range(count)])]
    dot_general x2, matrix products: 4.67 us -> 2.48 us  [local(): jnp.dot(split_rows[:, k], proj_w, preferred_element_type=jnp.float32)]
    slice x1, local copies, waits for them, and re-layouts: 5.76 us -> 3.78 us  [local(): split_rows[:, k]]
    unnamed x31 -> x29, local copies, waits for them, and re-layouts: 6.8 us -> 6.63 us
  transfers between devices with their start and end apart: 23 -> 23, of which waited for: 13 -> 14; matrix products, arithmetic and copies ran while one was open for 13% -> 13% of each run, Pallas kernels for 0% -> 0%
where the time goes in v17:
time: 169 us
  waiting for transfers between devices  67.8 us (40%)
  starting transfers between devices  26.9 us (16%)
  other arithmetic  26.6 us (16%)
  local copies, waits for them, and re-layouts  26.5 us (16%)
  matrix products  19.8 us (12%)
    ppermute x6, waiting for transfers between devices, xor_perm(): return lax.ppermute(value, axis, [(i, i ^ bit) for i in range(count)])  33.5 us
    ppermute x8, waiting for transfers between devices, all_gather_many(): others = lax.ppermute(arrs, axis, [(i, i ^ bit) for i in range(count)])  22.4 us
    ppermute x9, starting transfers between devices, all_sum(): lax.ppermute(value, axis, [(i, (i + k) % count) for i in range(count)])  13 us
    ppermute x9, waiting for transfers between devices, all_sum(): lax.ppermute(value, axis, [(i, (i + k) % count) for i in range(count)])  11.9 us
    ppermute x8, starting transfers between devices, all_gather_many(): others = lax.ppermute(arrs, axis, [(i, i ^ bit) for i in range(count)])  10.1 us
    dot_general x1, matrix products, local(): jnp.einsum('scij,scie->scje', weights, q_e, preferred_element_type=jnp.fl...  6.95 us
    unnamed x29, local copies, waits for them, and re-layouts  6.63 us
    dot_general x1, matrix products, local(): jnp.einsum('scie,scje->scij', q_e, tiles, preferred_element_type=jnp.floa...  5.2 us
  transfers between devices with their start and end apart: 23, of which 14 were waited for; matrix products, arithmetic and copies ran while one was open for 13% of the time, Pallas kernels for 0%

profile of v17, /device:TPU:0, one launch (start us, length us, event | category | flops | bytes accessed | tf_op | source)
XLA Modules:
  0.0 168.7 jit_solution(12280879939047116277)
XLA Ops:
  0.7 3.8 %fusion.47 = (bf16[4,1,2048,256]{3,2,1,0:T(8,128)(2,1)S(1)}, bf16[4,1,2048,256]{3,2,1,0:T(8,128)(2,1)S(1)}) fusion(bf16[4,2,2048,256]{3,2,1,0:T(8,128)(2,1)} %bitcast.241), kind=kLoop, calls=%fused_computation.155 | loop fusion | bytes 16777216 | tf_op jit(solution)/shard_map/slice | solution.py:150
  6.0 1.8 %copy-done.3 = f32[2,2,2048,128]{3,2,1,0:T(8,128)} copy-done((f32[2,2,2048,128]{3,2,1,0:T(8,128)}, f32[2,2,2048,128]{3,2,1,0:T(8,128)S(1)}, u32[]{:S(2)}) %copy-start.3) | copy-done | bytes 4194328
  8.2 2.5 %collective-permute-start.1 = (bf16[1,8,32,128]{3,2,1,0:T(8,128)(2,1)S(1)}, bf16[1,8,32,128]{3,2,1,0:T(8,128)(2,1)S(1)}, u32[]{:S(2)}, u32[]{:S(2)}) collective-permute-start(bf16[1,8,32,128]{3,2,1,0:T(8,128)(2,1)S(1)} %bitcast.268), channel_id=1, source_target_pairs={{0,2},{1,3},{2,0},{3,1},{4,6},{5,7},{6,4},{7,5},{8,10},{9,11},{10,... | collective-permute-start | bytes 196616 | tf_op jit(solution)/shard_map/ppermute | solution.py:95
  12.0 1.8 %select_bitcast_fusion.2 = f32[2,2048,128]{2,1,0:T(8,128)} fusion(f32[2,2,2048,128]{3,2,0,1:T(8,128)S(1)} %fusion.2, pred[]{:T(512)S(6)} %eq.85), kind=kLoop, calls=%fused_computation.39 | loop fusion | flops 524288 | bytes 6291457 | tf_op jit(solution)/shard_map/jit(_where)/select_n | solution.py:62
  15.6 3.2 %collective-permute-done.4 = s32[2,8,16]{2,1,0:T(8,128)S(1)} collective-permute-done((s32[2,8,16]{2,1,0:T(8,128)S(1)}, s32[2,8,16]{2,1,0:T(8,128)S(1)}, u32[]{:S(2)}, u32[]{:S(2)}) %collective-permute-start.4) | collective-permute-done | bytes 1056 | tf_op jit(solution)/shard_map/ppermute | solution.py:95
  19.1 3.3 %fusion.9 = f32[1,2,2048,128]{3,2,1,0:T(8,128)S(1)} fusion(f32[2,2048,128]{2,1,0:T(8,128)} %collective-permute-done, f32[2,2,2048,128]{3,2,1,0:T(8,128)} %copy-done.3, pred[]{:T(512)S(6)} %eq.85), kind=kLoop, calls=%fused_computation.22 | loop fusion | flops 1048576 | bytes 8388609 | tf_op jit(solution)/shard_map/reshape | solution.py:59
  25.1 2.6 %collective-permute-start.5 = (s32[1,32,16]{2,1,0:T(8,128)S(1)}, s32[1,32,16]{2,1,0:T(8,128)S(1)}, u32[]{:S(2)}, u32[]{:S(2)}) collective-permute-start(s32[1,32,16]{2,1,0:T(8,128)S(1)} %bitcast.266), channel_id=1, source_target_pairs={{0,8},{4,12},{8,0},{12,4},{1,9},{5,13},{9,1},{13,5},{2,10},{6,14},... | collective-permute-start | bytes 6152 | tf_op jit(solution)/shard_map/ppermute | solution.py:95
  27.6 1.9 %fusion.13 = f32[1,2,2048,128]{3,2,1,0:T(8,128)S(1)} fusion(f32[2,2048,128]{2,1,0:T(8,128)} %collective-permute-done.10, f32[2,2,2048,128]{3,2,0,1:T(8,128)S(1)} %copy-done.5, pred[]{:T(512)S(6)} %eq.85), kind=kLoop, calls=%fused_computation.29 | loop fusion | flops 1048576 | bytes 8388609 | tf_op jit(solution)/shard_map/reshape | solution.py:59
  33.0 2.7 %collective-permute-start.7 = (bf16[1,32,32,128]{3,2,1,0:T(8,128)(2,1)S(1)}, bf16[1,32,32,128]{3,2,1,0:T(8,128)(2,1)S(1)}, u32[]{:S(2)}, u32[]{:S(2)}) collective-permute-start(bf16[1,32,32,128]{3,2,1,0:T(8,128)(2,1)S(1)} %bitcast.255), channel_id=1, source_target_pairs={{0,8},{4,12},{8,0},{12,4},{1,9},{5,13},{9,1},{13,5},{2,10},{6,14},... | collective-permute-start | bytes 786440 | tf_op jit(solution)/shard_map/ppermute | solution.py:95
  36.5 1.9 %gather_fusion.3 = s32[256]{0:T(256)S(1)} fusion(s32[16,128]{1,0:T(8,128)S(1)} %reshape_reshape_reshape.2, s32[256]{0:T(256)S(1)} %reshape.668), kind=kCustom, calls=%fused_computation.3 | custom fusion | bytes 4096 | tf_op jit(solution)/shard_map/jit(take_along_axis)/gather | solution.py:177
  39.1 1.9 %gather_fusion = s32[256]{0:T(256)S(1)} fusion(s32[256]{0:T(256)S(1)} %copy-done.2, s32[1024]{0:T(1024)S(1)} %pad_clamp_fusion.2), kind=kCustom, calls=%fused_computation | custom fusion | bytes 3072 | tf_op jit(solution)/shard_map/gather | solution.py:15
  41.2 5.6 %collective-permute-done.7 = bf16[1,32,32,128]{3,2,1,0:T(8,128)(2,1)S(1)} collective-permute-done((bf16[1,32,32,128]{3,2,1,0:T(8,128)(2,1)S(1)}, bf16[1,32,32,128]{3,2,1,0:T(8,128)(2,1)S(1)}, u32[]{:S(2)}, u32[]{:S(2)}) %collective-permute-start.7) | collective-permute-done | bytes 262176 | tf_op jit(solution)/shard_map/ppermute | solution.py:95
  48.5 13.1 %collective-permute-done.8 = bf16[2,32,32,128]{3,2,1,0:T(8,128)(2,1)S(1)} collective-permute-done((bf16[2,32,32,128]{3,2,1,0:T(8,128)(2,1)}, bf16[2,32,32,128]{3,2,1,0:T(8,128)(2,1)S(1)}, u32[]{:S(2)}, u32[]{:S(2)}) %collective-permute-start.8) | collective-permute-done | bytes 524320 | tf_op jit(solution)/shard_map/ppermute | solution.py:95
  61.9 2.2 %gather_fusion.1 = bf16[256,32,128]{2,1,0:T(8,128)(2,1)} fusion(bf16[128,32,128]{2,1,0:T(8,128)(2,1)S(1)} %bitcast.251, s32[1024]{0:T(1024)S(1)} %pad_clamp_fusion.1), kind=kCustom, calls=%fused_computation.1 | custom fusion | bytes 4195328 | tf_op jit(solution)/shard_map/gather | solution.py:181
  65.6 5.9 %collective-permute-done.11 = f32[1,2048,128]{2,1,0:T(8,128)} collective-permute-done((f32[1,2048,128]{2,1,0:T(8,128)}, f32[1,2048,128]{2,1,0:T(8,128)}, u32[]{:S(2)}, u32[]{:S(2)}) %collective-permute-start.11) | collective-permute-done | bytes 1048608 | tf_op jit(solution)/shard_map/ppermute | solution.py:44
  74.4 3.0 %gather_fusion.2 = bf16[256,64,128]{2,1,0:T(8,128)(2,1)} fusion(bf16[64,64,128]{2,1,0:T(8,128)(2,1)S(1)} %multiply_convert_fusion.1, s32[1024]{0:T(1024)S(1)} %pad_clamp_fusion), kind=kCustom, calls=%fused_computation.2 | custom fusion | bytes 8389632 | tf_op jit(solution)/shard_map/gather | solution.py:188
  77.4 5.2 %select_reduce_fusion = (f32[16,16,32]{2,1,0:T(8,128)S(1)}, f32[16,16,32,64]{3,2,1,0:T(8,128)S(1)}) fusion(pred[16,16,64]{2,1,0:T(8,128)(4,1)S(1)} %add_compare_fusion, bf16[16,16,32,128]{3,2,1,0:T(8,128)(2,1)} %bitcast.253, bf16[16,16,64,128]{3,2,1,0:T(8,128)(2,1)} %bitcast.248), kind=kOutput, calls=%fused_computation.15 | convolution fusion | flops 135258112 | bytes 8437760 | tf_op jit(solution)/shard_map/scie,scje->scij/dot_general | solution.py:190
  82.6 2.6 %fusion.6 = f32[16,16,32]{2,1,0:T(8,128)S(1)} fusion(f32[16,16,32,64]{3,2,1,0:T(8,128)S(1)} %get-tuple-element.59, f32[16,16,32]{2,1,0:T(8,128)S(1)} %get-tuple-element.58, pred[16,16,64]{2,1,0:T(8,128)(4,1)S(1)} %add_compare_fusion), kind=kLoop, calls=%fused_computation.16 | loop fusion | flops 1564672 | bytes 2179072 | tf_op jit(solution)/shard_map/reduce_sum | solution.py:22
  85.6 1.8 %collective-permute-start.13 = (f32[16,128]{1,0:T(8,128)S(1)}, f32[16,128]{1,0:T(8,128)S(1)}, u32[]{:S(2)}, u32[]{:S(2)}) collective-permute-start(f32[16,128]{1,0:T(8,128)S(1)} %select_reduce_fusion.1), channel_id=1, source_target_pairs={{0,2},{1,3},{2,0},{3,1},{4,6},{5,7},{6,4},{7,5},{8,10},{9,11},{10,... | collective-permute-start | bytes 24584 | tf_op jit(solution)/shard_map/ppermute | solution.py:118
  91.8 2.6 %collective-permute-start.16 = (f32[16,128]{1,0:T(8,128)S(1)}, f32[16,128]{1,0:T(8,128)S(1)}, u32[]{:S(2)}, u32[]{:S(2)}) collective-permute-start(f32[16,128]{1,0:T(8,128)S(1)} %fusion.54), channel_id=1, source_target_pairs={{0,8},{4,12},{8,0},{12,4},{1,9},{5,13},{9,1},{13,5},{2,10},{6,14},... | collective-permute-start | bytes 24584 | tf_op jit(solution)/shard_map/ppermute | solution.py:118
  96.3 1.7 %collective-permute-done.17 = f32[16,128]{1,0:T(8,128)S(1)} collective-permute-done((f32[16,128]{1,0:T(8,128)S(1)}, f32[16,128]{1,0:T(8,128)S(1)}, u32[]{:S(2)}, u32[]{:S(2)}) %collective-permute-start.17) | collective-permute-done | bytes 8224 | tf_op jit(solution)/shard_map/ppermute | solution.py:118
  98.6 1.9 %gather_fusion.4 = f32[256]{0:T(256)S(1)} fusion(f32[16,128]{1,0:T(8,128)S(1)} %reshape.640, s32[256]{0:T(256)S(1)} %reshape.668), kind=kCustom, calls=%fused_computation.4 | custom fusion | bytes 4096 | tf_op jit(solution)/shard_map/jit(take_along_axis)/gather | solution.py:200
  100.6 6.9 %multiply_convert_fusion = bf16[16,16,64,128]{3,2,1,0:T(8,128)(2,1)S(1)} fusion(f32[16,16]{1,0:T(8,128)S(1)} %select_multiply_fusion, bf16[16,16,32,128]{3,2,1,0:T(8,128)(2,1)} %bitcast.254, f32[16,16,32,64]{3,2,1,0:T(8,128)} %copy-done.8, f32[16,16,32]{2,1,0:T(8,128)S(1)} %fusion.6, f32[16,16,32]{2,1,0:T(8,128)S(1)} %get-tuple-element.58, ...), kind=kOutput, calls=%fused_computation.5 | convolution fusion | flops 140509184 | bytes 8471552 | tf_op jit(solution)/shard_map/scij,scie->scje/dot_general | solution.py:193
  107.6 3.7 %fusion.14 = (f32[64,64]{0,1:T(8,128)S(1)}, f32[64,64,128]{2,0,1:T(8,128)S(1)}) fusion(f32[64,64,128]{2,1,0:T(8,128)S(1)} %bitcast.245, bf16[16,16,64,128]{3,2,1,0:T(8,128)(2,1)S(1)} %multiply_convert_fusion, s32[16,16]{0,1:T(8,128)S(1)} %copy.137, pred[16,16]{0,1:T(8,128)(4,1)S(1)} %copy.138), kind=kOutput, calls=%fused_computation.31 | convolution fusion | flops 269512704 | bytes 8406272 | tf_op jit(solution)/shard_map/scb,scje->bje/dot_general | solution.py:204
  111.3 2.6 %copy.141 = f32[64,64,128]{2,1,0:T(8,128)} copy(f32[64,64,128]{2,0,1:T(8,128)S(1)} %get-tuple-element.61) | data formatting | bytes 4194304 | tf_op jit(solution)/shard_map/scb,scje->bje/dot_general | solution.py:204
  114.0 3.6 %fusion.12 = bf16[1,4096,128]{2,1,0:T(8,128)(2,1)S(1)} fusion(f32[4096]{0:T(1024)S(1)} %mul.134, f32[4096]{0:T(1024)S(1)} %multiply_multiply_fusion, f32[4096]{0:T(1024)S(1)} %bitcast.262, f32[1,4096,128]{2,1,0:T(8,128)S(1)} %bitcast.246, f32[1,4096,128]{2,1,0:T(8,128)} %bitcast.252), kind=kLoop, calls=%fused_computation.26 | loop fusion | flops 2621440 | bytes 5292032 | tf_op jit(solution)/shard_map/convert_element_type | solution.py:212
  118.5 23.1 %collective-permute-done.18 = bf16[1,4096,128]{2,1,0:T(8,128)(2,1)S(1)} collective-permute-done((bf16[1,4096,128]{2,1,0:T(8,128)(2,1)S(1)}, bf16[1,4096,128]{2,1,0:T(8,128)(2,1)S(1)}, u32[]{:S(2)}, u32[]{:S(2)}) %collective-permute-start.18) | collective-permute-done | bytes 1048608 | tf_op jit(solution)/shard_map/ppermute | solution.py:44
  143.3 4.5 %collective-permute-done.19 = bf16[2,4096,128]{2,1,0:T(8,128)(2,1)} collective-permute-done((bf16[2,4096,128]{2,1,0:T(8,128)(2,1)}, bf16[2,4096,128]{2,1,0:T(8,128)(2,1)}, u32[]{:S(2)}, u32[]{:S(2)}) %collective-permute-start.19) | collective-permute-done | bytes 2097184 | tf_op jit(solution)/shard_map/ppermute | solution.py:44
  147.8 1.9 %select_bitcast_fusion.1 = (bf16[2,1,4096,128]{3,2,0,1:T(8,128)(2,1)S(1)}, bf16[2,1,4096,128]{3,2,0,1:T(8,128)(2,1)S(1)}) fusion(bf16[2,4096,128]{2,1,0:T(8,128)(2,1)} %collective-permute-done.19, pred[]{:T(512)S(6)} %eq.85, bf16[1,1,4096,128]{3,2,1,0:T(8,128)(2,1)S(1)} %get-tuple-element.33, bf16[1,1,4096,128]{3,2,1,0:T(8,128)(2,1)S(1)} %get-tuple-element.32), kind=kLoop, calls=%fused_computation.33 | loop fusion | flops 3145728 | bytes 8388609 | tf_op jit(solution)/shard_map/stack | solution.py:81
  155.5 3.1 %collective-permute-start.21 = (f32[256,128]{0,1:T(8,128)S(1)}, f32[256,128]{0,1:T(8,128)S(1)}, u32[]{:S(2)}, u32[]{:S(2)}) collective-permute-start(f32[256,128]{0,1:T(8,128)S(1)} %bitcast.258), channel_id=1, source_target_pairs={{0,8},{4,12},{8,0},{12,4},{1,9},{5,13},{9,1},{13,5},{2,10},{6,14},... | collective-permute-start | bytes 393224 | tf_op jit(solution)/shard_map/ppermute | solution.py:118
  159.6 3.5 %collective-permute-done.20 = f32[256,128]{0,1:T(8,128)S(1)} collective-permute-done((f32[256,128]{0,1:T(8,128)S(1)}, f32[256,128]{0,1:T(8,128)S(1)}, u32[]{:S(2)}, u32[]{:S(2)}) %collective-permute-start.20) | collective-permute-done | bytes 131104 | tf_op jit(solution)/shard_map/ppermute | solution.py:118
  163.0 4.8 %collective-permute-done.21 = f32[256,128]{0,1:T(8,128)S(1)} collective-permute-done((f32[256,128]{0,1:T(8,128)S(1)}, f32[256,128]{0,1:T(8,128)S(1)}, u32[]{:S(2)}, u32[]{:S(2)}) %collective-permute-start.21) | collective-permute-done | bytes 131104 | tf_op jit(solution)/shard_map/ppermute | solution.py:118
  (144 shorter events, 37.0 us)
Async XLA Ops:
  0.6 3.8 %copy-start = (bf16[256,128]{1,0:T(8,128)(2,1)S(1)}, bf16[256,128]{1,0:T(8,128)(2,1)}, u32[]{:S(2)}) copy-start(bf16[256,128]{1,0:T(8,128)(2,1)} %param.6) | copy-start | bytes 196612
  5.7 4.9 %copy-start.10 = (s32[8,16]{1,0:T(8,128)S(1)}, s32[8,16]{1,0:T(8,128)}, u32[]{:S(2)}) copy-start(s32[8,16]{1,0:T(8,128)} %param.9) | copy-start | bytes 1540
  7.7 11.4 %collective-permute-start = (f32[2,2048,128]{2,1,0:T(8,128)S(1)}, f32[2,2048,128]{2,1,0:T(8,128)}, u32[]{:S(2)}, u32[]{:S(2)}) collective-permute-start(f32[2,2048,128]{2,1,0:T(8,128)S(1)} %select_bitcast_fusion.3), channel_id=1, source_target_pairs={{0,1},{1,0},{2,3},{3,2},{4,5},{5,4},{6,7},{7,6},{8,9},{9,8},{10,11... | collective-permute-start | bytes 6291464 | tf_op jit(solution)/shard_map/ppermute | solution.py:44
  8.2 7.1 %collective-permute-start.1 = (bf16[1,8,32,128]{3,2,1,0:T(8,128)(2,1)S(1)}, bf16[1,8,32,128]{3,2,1,0:T(8,128)(2,1)S(1)}, u32[]{:S(2)}, u32[]{:S(2)}) collective-permute-start(bf16[1,8,32,128]{3,2,1,0:T(8,128)(2,1)S(1)} %bitcast.268), channel_id=1, source_target_pairs={{0,2},{1,3},{2,0},{3,1},{4,6},{5,7},{6,4},{7,5},{8,10},{9,11},{10,... | collective-permute-start | bytes 196616 | tf_op jit(solution)/shard_map/ppermute | solution.py:95
  10.7 4.2 %collective-permute-start.3 = (s32[1,8,16]{2,1,0:T(8,128)S(1)}, s32[1,8,16]{2,1,0:T(8,128)S(1)}, u32[]{:S(2)}, u32[]{:S(2)}) collective-permute-start(s32[1,8,16]{2,1,0:T(8,128)S(1)} %bitcast.276), channel_id=1, source_target_pairs={{0,2},{1,3},{2,0},{3,1},{4,6},{5,7},{6,4},{7,5},{8,10},{9,11},{10,... | collective-permute-start | bytes 1544 | tf_op jit(solution)/shard_map/ppermute | solution.py:95
  12.0 2.7 %copy-start.4 = (f32[2,2,2048,128]{3,2,0,1:T(8,128)}, f32[2,2,2048,128]{3,2,0,1:T(8,128)S(1)}, u32[]{:S(2)}) copy-start(f32[2,2,2048,128]{3,2,0,1:T(8,128)S(1)} %fusion.2) | copy-start | bytes 12582916
  14.6 13.0 %collective-permute-start.10 = (f32[2,2048,128]{2,1,0:T(8,128)}, f32[2,2048,128]{2,1,0:T(8,128)}, u32[]{:S(2)}, u32[]{:S(2)}) collective-permute-start(f32[2,2048,128]{2,1,0:T(8,128)} %select_bitcast_fusion.2), channel_id=1, source_target_pairs={{0,1},{1,0},{2,3},{3,2},{4,5},{5,4},{6,7},{7,6},{8,9},{9,8},{10,11... | collective-permute-start | bytes 6291464 | tf_op jit(solution)/shard_map/ppermute | solution.py:44
  14.9 3.9 %collective-permute-start.4 = (s32[2,8,16]{2,1,0:T(8,128)S(1)}, s32[2,8,16]{2,1,0:T(8,128)S(1)}, u32[]{:S(2)}, u32[]{:S(2)}) collective-permute-start(s32[2,8,16]{2,1,0:T(8,128)S(1)} %add_bitcast_fusion.2), channel_id=1, source_target_pairs={{0,1},{1,0},{2,3},{3,2},{4,5},{5,4},{6,7},{7,6},{8,9},{9,8},{10,11... | collective-permute-start | bytes 3080 | tf_op jit(solution)/shard_map/ppermute | solution.py:95
  15.3 3.7 %collective-permute-start.2 = (bf16[2,8,32,128]{3,2,1,0:T(8,128)(2,1)S(1)}, bf16[2,8,32,128]{3,2,1,0:T(8,128)(2,1)S(1)}, u32[]{:S(2)}, u32[]{:S(2)}) collective-permute-start(bf16[2,8,32,128]{3,2,1,0:T(8,128)(2,1)S(1)} %maximum_bitcast_fusion.2), channel_id=1, source_target_pairs={{0,1},{1,0},{2,3},{3,2},{4,5},{5,4},{6,7},{7,6},{8,9},{9,8},{10,11... | collective-permute-start | bytes 393224 | tf_op jit(solution)/shard_map/ppermute | solution.py:95
  19.1 8.6 %copy-start.5 = (f32[2,2,2048,128]{3,2,0,1:T(8,128)S(1)}, f32[2,2,2048,128]{3,2,0,1:T(8,128)}, u32[]{:S(2)}) copy-start(f32[2,2,2048,128]{3,2,0,1:T(8,128)} %copy-done.4) | copy-start | bytes 12582916
  23.5 40.6 %collective-permute-start.9 = (f32[1,2048,128]{2,1,0:T(8,128)}, f32[1,2048,128]{2,1,0:T(8,128)}, u32[]{:S(2)}, u32[]{:S(2)}) collective-permute-start(f32[1,2048,128]{2,1,0:T(8,128)} %select_bitcast_fusion.7), channel_id=1, source_target_pairs={{0,2},{1,3},{2,0},{3,1},{4,6},{5,7},{6,4},{7,5},{8,10},{9,11},{10,... | collective-permute-start | bytes 3145736 | tf_op jit(solution)/shard_map/ppermute | solution.py:44
  25.1 4.6 %collective-permute-start.5 = (s32[1,32,16]{2,1,0:T(8,128)S(1)}, s32[1,32,16]{2,1,0:T(8,128)S(1)}, u32[]{:S(2)}, u32[]{:S(2)}) collective-permute-start(s32[1,32,16]{2,1,0:T(8,128)S(1)} %bitcast.266), channel_id=1, source_target_pairs={{0,8},{4,12},{8,0},{12,4},{1,9},{5,13},{9,1},{13,5},{2,10},{6,14},... | collective-permute-start | bytes 6152 | tf_op jit(solution)/shard_map/ppermute | solution.py:95
  29.5 6.1 %copy-start.6 = (f32[1,2,2048,128]{3,2,1,0:T(8,128)}, f32[1,2,2048,128]{3,2,1,0:T(8,128)S(1)}, u32[]{:S(2)}) copy-start(f32[1,2,2048,128]{3,2,1,0:T(8,128)S(1)} %fusion.13) | copy-start | bytes 6291460
  29.7 5.9 %collective-permute-start.6 = (s32[2,32,16]{2,1,0:T(8,128)S(1)}, s32[2,32,16]{2,1,0:T(8,128)S(1)}, u32[]{:S(2)}, u32[]{:S(2)}) collective-permute-start(s32[2,32,16]{2,1,0:T(8,128)S(1)} %add_bitcast_fusion.1), channel_id=1, source_target_pairs={{0,4},{4,0},{8,12},{12,8},{1,5},{5,1},{9,13},{13,9},{2,6},{6,2},{1... | collective-permute-start | bytes 12296 | tf_op jit(solution)/shard_map/ppermute | solution.py:95
  32.4 39.1 %collective-permute-start.11 = (f32[1,2048,128]{2,1,0:T(8,128)}, f32[1,2048,128]{2,1,0:T(8,128)}, u32[]{:S(2)}, u32[]{:S(2)}) collective-permute-start(f32[1,2048,128]{2,1,0:T(8,128)} %select_bitcast_fusion.6), channel_id=1, source_target_pairs={{0,2},{1,3},{2,0},{3,1},{4,6},{5,7},{6,4},{7,5},{8,10},{9,11},{10,... | collective-permute-start | bytes 3145736 | tf_op jit(solution)/shard_map/ppermute | solution.py:44
  33.0 13.8 %collective-permute-start.7 = (bf16[1,32,32,128]{3,2,1,0:T(8,128)(2,1)S(1)}, bf16[1,32,32,128]{3,2,1,0:T(8,128)(2,1)S(1)}, u32[]{:S(2)}, u32[]{:S(2)}) collective-permute-start(bf16[1,32,32,128]{3,2,1,0:T(8,128)(2,1)S(1)} %bitcast.255), channel_id=1, source_target_pairs={{0,8},{4,12},{8,0},{12,4},{1,9},{5,13},{9,1},{13,5},{2,10},{6,14},... | collective-permute-start | bytes 786440 | tf_op jit(solution)/shard_map/ppermute | solution.py:95
  47.7 13.9 %collective-permute-start.8 = (bf16[2,32,32,128]{3,2,1,0:T(8,128)(2,1)}, bf16[2,32,32,128]{3,2,1,0:T(8,128)(2,1)S(1)}, u32[]{:S(2)}, u32[]{:S(2)}) collective-permute-start(bf16[2,32,32,128]{3,2,1,0:T(8,128)(2,1)} %maximum_bitcast_fusion.1), channel_id=1, source_target_pairs={{0,4},{4,0},{8,12},{12,8},{1,5},{5,1},{9,13},{13,9},{2,6},{6,2},{1... | collective-permute-start | bytes 1572872 | tf_op jit(solution)/shard_map/ppermute | solution.py:95
  64.1 7.5 %copy-start.7 = (f32[1,2,2048,128]{3,2,1,0:T(8,128)S(1)}, f32[1,2,2048,128]{3,2,1,0:T(8,128)}, u32[]{:S(2)}) copy-start(f32[1,2,2048,128]{3,2,1,0:T(8,128)} %copy-done.6) | copy-start | bytes 6291460
  82.6 2.6 %copy-start.8 = (f32[16,16,32,64]{3,2,1,0:T(8,128)}, f32[16,16,32,64]{3,2,1,0:T(8,128)S(1)}, u32[]{:S(2)}) copy-start(f32[16,16,32,64]{3,2,1,0:T(8,128)S(1)} %get-tuple-element.59) | copy-start | bytes 6291460
  85.5 3.3 %collective-permute-start.12 = (f32[16,128]{1,0:T(8,128)S(1)}, f32[16,128]{1,0:T(8,128)S(1)}, u32[]{:S(2)}, u32[]{:S(2)}) collective-permute-start(f32[16,128]{1,0:T(8,128)S(1)} %select_reduce_fusion.1), channel_id=1, source_target_pairs={{0,1},{1,2},{2,3},{3,0},{4,5},{5,6},{6,7},{7,4},{8,9},{9,10},{10,1... | collective-permute-start | bytes 24584 | tf_op jit(solution)/shard_map/ppermute | solution.py:118
  85.6 3.7 %collective-permute-start.13 = (f32[16,128]{1,0:T(8,128)S(1)}, f32[16,128]{1,0:T(8,128)S(1)}, u32[]{:S(2)}, u32[]{:S(2)}) collective-permute-start(f32[16,128]{1,0:T(8,128)S(1)} %select_reduce_fusion.1), channel_id=1, source_target_pairs={{0,2},{1,3},{2,0},{3,1},{4,6},{5,7},{6,4},{7,5},{8,10},{9,11},{10,... | collective-permute-start | bytes 24584 | tf_op jit(solution)/shard_map/ppermute | solution.py:118
  87.4 2.8 %collective-permute-start.14 = (f32[16,128]{1,0:T(8,128)S(1)}, f32[16,128]{1,0:T(8,128)S(1)}, u32[]{:S(2)}, u32[]{:S(2)}) collective-permute-start(f32[16,128]{1,0:T(8,128)S(1)} %select_reduce_fusion.1), channel_id=1, source_target_pairs={{0,3},{1,0},{2,1},{3,2},{4,7},{5,4},{6,5},{7,6},{8,11},{9,8},{10,9... | collective-permute-start | bytes 24584 | tf_op jit(solution)/shard_map/ppermute | solution.py:118
  90.1 5.6 %collective-permute-start.15 = (f32[16,128]{1,0:T(8,128)S(1)}, f32[16,128]{1,0:T(8,128)S(1)}, u32[]{:S(2)}, u32[]{:S(2)}) collective-permute-start(f32[16,128]{1,0:T(8,128)S(1)} %fusion.54), channel_id=1, source_target_pairs={{0,4},{4,8},{8,12},{12,0},{1,5},{5,9},{9,13},{13,1},{2,6},{6,10},{... | collective-permute-start | bytes 24584 | tf_op jit(solution)/shard_map/ppermute | solution.py:118
  91.8 4.5 %collective-permute-start.16 = (f32[16,128]{1,0:T(8,128)S(1)}, f32[16,128]{1,0:T(8,128)S(1)}, u32[]{:S(2)}, u32[]{:S(2)}) collective-permute-start(f32[16,128]{1,0:T(8,128)S(1)} %fusion.54), channel_id=1, source_target_pairs={{0,8},{4,12},{8,0},{12,4},{1,9},{5,13},{9,1},{13,5},{2,10},{6,14},... | collective-permute-start | bytes 24584 | tf_op jit(solution)/shard_map/ppermute | solution.py:118
  94.3 3.7 %collective-permute-start.17 = (f32[16,128]{1,0:T(8,128)S(1)}, f32[16,128]{1,0:T(8,128)S(1)}, u32[]{:S(2)}, u32[]{:S(2)}) collective-permute-start(f32[16,128]{1,0:T(8,128)S(1)} %fusion.54), channel_id=1, source_target_pairs={{0,12},{4,0},{8,4},{12,8},{1,13},{5,1},{9,5},{13,9},{2,14},{6,2},{... | collective-permute-start | bytes 24584 | tf_op jit(solution)/shard_map/ppermute | solution.py:118
  117.6 24.0 %collective-permute-start.18 = (bf16[1,4096,128]{2,1,0:T(8,128)(2,1)S(1)}, bf16[1,4096,128]{2,1,0:T(8,128)(2,1)S(1)}, u32[]{:S(2)}, u32[]{:S(2)}) collective-permute-start(bf16[1,4096,128]{2,1,0:T(8,128)(2,1)S(1)} %fusion.12), channel_id=1, source_target_pairs={{0,2},{1,3},{2,0},{3,1},{4,6},{5,7},{6,4},{7,5},{8,10},{9,11},{10,... | collective-permute-start | bytes 3145736 | tf_op jit(solution)/shard_map/ppermute | solution.py:44
  143.3 4.5 %collective-permute-start.19 = (bf16[2,4096,128]{2,1,0:T(8,128)(2,1)}, bf16[2,4096,128]{2,1,0:T(8,128)(2,1)}, u32[]{:S(2)}, u32[]{:S(2)}) collective-permute-start(bf16[2,4096,128]{2,1,0:T(8,128)(2,1)} %maximum_bitcast_fusion), channel_id=1, source_target_pairs={{0,1},{1,0},{2,3},{3,2},{4,5},{5,4},{6,7},{7,6},{8,9},{9,8},{10,11... | collective-permute-start | bytes 6291464 | tf_op jit(solution)/shard_map/ppermute | solution.py:44
  150.0 3.2 %slice-start.1 = ((s8[8388608]{0:T(1024)(128)(4,1)}), s8[4194304]{0:T(1024)(128)(4,1)S(1)}, s32[]{:S(2)}) async-start(s8[8388608]{0:T(1024)(128)(4,1)} %bitcast.242), calls=%async_computation.1 | async-start | bytes 8388608
  153.2 15.5 %copy-start.1 = (bf16[256,128]{1,0:T(8,128)(2,1)S(1)}, bf16[256,128]{1,0:T(8,128)(2,1)}, u32[]{:S(2)}) copy-start(bf16[256,128]{1,0:T(8,128)(2,1)} %param.6) | copy-start | bytes 196612
  154.8 8.3 %collective-permute-start.20 = (f32[256,128]{0,1:T(8,128)S(1)}, f32[256,128]{0,1:T(8,128)S(1)}, u32[]{:S(2)}, u32[]{:S(2)}) collective-permute-start(f32[256,128]{0,1:T(8,128)S(1)} %bitcast.257), channel_id=1, source_target_pairs={{0,4},{4,8},{8,12},{12,0},{1,5},{5,9},{9,13},{13,1},{2,6},{6,10},{... | collective-permute-start | bytes 393224 | tf_op jit(solution)/shard_map/ppermute | solution.py:118
  155.5 12.4 %collective-permute-start.21 = (f32[256,128]{0,1:T(8,128)S(1)}, f32[256,128]{0,1:T(8,128)S(1)}, u32[]{:S(2)}, u32[]{:S(2)}) collective-permute-start(f32[256,128]{0,1:T(8,128)S(1)} %bitcast.258), channel_id=1, source_target_pairs={{0,8},{4,12},{8,0},{12,4},{1,9},{5,13},{9,1},{13,5},{2,10},{6,14},... | collective-permute-start | bytes 393224 | tf_op jit(solution)/shard_map/ppermute | solution.py:118
  158.5 9.3 %collective-permute-start.22 = (f32[256,128]{0,1:T(8,128)S(1)}, f32[256,128]{0,1:T(8,128)S(1)}, u32[]{:S(2)}, u32[]{:S(2)}) collective-permute-start(f32[256,128]{0,1:T(8,128)S(1)} %bitcast.259), channel_id=1, source_target_pairs={{0,12},{4,0},{8,4},{12,8},{1,13},{5,1},{9,5},{13,9},{2,14},{6,2},{... | collective-permute-start | bytes 393224 | tf_op jit(solution)/shard_map/ppermute | solution.py:118
  (4 other events, 7.3 us)

commit v18 on v17

--- a/solution.py
+++ b/solution.py
@@ -154,8 +154,6 @@
     ]
     if is_pow2(mp_count) and mp_count > 1:
         keeps, sends, bit = halving_steps(partials, "mp")
-        first, gathered = lax.optimization_barrier((sends[0], gathered))
-        sends = [first] + sends[1:]
         pieces = [k + xor_perm(t, "mp", bit) for k, t in zip(keeps, sends)]
         pieces = [p.reshape(-1, emb_width) for p in pieces]
     else:

time: 169 us -> 198 us (1.17)
  waiting for transfers between devices: 67.8 us -> 93.3 us
  starting transfers between devices: 26.9 us -> 29.3 us
    ppermute x6, waiting for transfers between devices: 33.5 us -> 63 us  [xor_perm(): return lax.ppermute(value, axis, [(i, i ^ bit) for i in range(count)])]
    ppermute x8, waiting for transfers between devices: 22.4 us -> 19.2 us  [all_gather_many(): others = lax.ppermute(arrs, axis, [(i, i ^ bit) for i in range(count)])]
  transfers between devices with their start and end apart: 23 -> 23, of which waited for: 14 -> 17; matrix products, arithmetic and copies ran while one was open for 13% -> 11% of each run, Pallas kernels for 0% -> 0%
where the time goes in v18:
time: 198 us
  waiting for transfers between devices  93.3 us (47%)
  starting transfers between devices  29.3 us (15%)
  local copies, waits for them, and re-layouts  27.5 us (14%)
  other arithmetic  26.4 us (13%)
  matrix products  19.8 us (10%)
    ppermute x6, waiting for transfers between devices, xor_perm(): return lax.ppermute(value, axis, [(i, i ^ bit) for i in range(count)])  63 us
    ppermute x8, waiting for transfers between devices, all_gather_many(): others = lax.ppermute(arrs, axis, [(i, i ^ bit) for i in range(count)])  19.2 us
    ppermute x9, starting transfers between devices, all_sum(): lax.ppermute(value, axis, [(i, (i + k) % count) for i in range(count)])  13.8 us
    ppermute x8, starting transfers between devices, all_gather_many(): others = lax.ppermute(arrs, axis, [(i, i ^ bit) for i in range(count)])  12 us
    ppermute x9, waiting for transfers between devices, all_sum(): lax.ppermute(value, axis, [(i, (i + k) % count) for i in range(count)])  11.1 us
    unnamed x29, local copies, waits for them, and re-layouts  7.7 us
    dot_general x1, matrix products, local(): jnp.einsum('scij,scie->scje', weights, q_e, preferred_element_type=jnp.fl...  6.95 us
    dot_general x1, matrix products, local(): jnp.einsum('scie,scje->scij', q_e, tiles, preferred_element_type=jnp.floa...  5.2 us
  transfers between devices with their start and end apart: 23, of which 17 were waited for; matrix products, arithmetic and copies ran while one was open for 11% of the time, Pallas kernels for 0%

profile of v18, /device:TPU:0, one launch (start us, length us, event | category | flops | bytes accessed | tf_op | source)
XLA Modules:
  0.0 197.6 jit_solution(4422563724619209590)
XLA Ops:
  0.7 3.8 %fusion.47 = (bf16[4,1,2048,256]{3,2,1,0:T(8,128)(2,1)S(1)}, bf16[4,1,2048,256]{3,2,1,0:T(8,128)(2,1)S(1)}) fusion(bf16[4,2,2048,256]{3,2,1,0:T(8,128)(2,1)} %bitcast.235), kind=kLoop, calls=%fused_computation.155 | loop fusion | bytes 16777216 | tf_op jit(solution)/shard_map/slice | solution.py:150
  9.4 1.8 select_bitcast_fusion.2
  12.1 2.9 %collective-permute-start = (s32[1,8,16]{2,1,0:T(8,128)S(1)}, s32[1,8,16]{2,1,0:T(8,128)S(1)}, u32[]{:S(2)}, u32[]{:S(2)}) collective-permute-start(s32[1,8,16]{2,1,0:T(8,128)S(1)} %bitcast.270), channel_id=1, source_target_pairs={{0,2},{1,3},{2,0},{3,1},{4,6},{5,7},{6,4},{7,5},{8,10},{9,11},{10,... | collective-permute-start | bytes 1544 | tf_op jit(solution)/shard_map/ppermute | solution.py:95
  17.9 3.2 %collective-permute-start.2 = (s32[1,32,16]{2,1,0:T(8,128)S(1)}, s32[1,32,16]{2,1,0:T(8,128)S(1)}, u32[]{:S(2)}, u32[]{:S(2)}) collective-permute-start(s32[1,32,16]{2,1,0:T(8,128)S(1)} %bitcast.260), channel_id=1, source_target_pairs={{0,8},{4,12},{8,0},{12,4},{1,9},{5,13},{9,1},{13,5},{2,10},{6,14},... | collective-permute-start | bytes 6152 | tf_op jit(solution)/shard_map/ppermute | solution.py:95
  22.8 2.0 collective-permute-start.3
  24.8 2.0 %collective-permute-done.3 = s32[2,32,16]{2,1,0:T(8,128)S(1)} collective-permute-done((s32[2,32,16]{2,1,0:T(8,128)S(1)}, s32[2,32,16]{2,1,0:T(8,128)S(1)}, u32[]{:S(2)}, u32[]{:S(2)}) %collective-permute-start.3) | collective-permute-done | bytes 4128 | tf_op jit(solution)/shard_map/ppermute | solution.py:95
  27.7 1.9 gather_fusion.3
  31.4 3.0 %collective-permute-start.6 = (bf16[1,32,32,128]{3,2,1,0:T(8,128)(2,1)S(1)}, bf16[1,32,32,128]{3,2,1,0:T(8,128)(2,1)S(1)}, u32[]{:S(2)}, u32[]{:S(2)}) collective-permute-start(bf16[1,32,32,128]{3,2,1,0:T(8,128)(2,1)S(1)} %bitcast.249), channel_id=1, source_target_pairs={{0,8},{4,12},{8,0},{12,4},{1,9},{5,13},{9,1},{13,5},{2,10},{6,14},... | collective-permute-start | bytes 786440 | tf_op jit(solution)/shard_map/ppermute | solution.py:95
  34.5 1.9 gather_fusion
  36.7 10.0 %collective-permute-done.6 = bf16[1,32,32,128]{3,2,1,0:T(8,128)(2,1)S(1)} collective-permute-done((bf16[1,32,32,128]{3,2,1,0:T(8,128)(2,1)S(1)}, bf16[1,32,32,128]{3,2,1,0:T(8,128)(2,1)S(1)}, u32[]{:S(2)}, u32[]{:S(2)}) %collective-permute-start.6) | collective-permute-done | bytes 262176 | tf_op jit(solution)/shard_map/ppermute | solution.py:95
  48.3 3.3 %fusion.9 = f32[1,2,2048,128]{3,2,1,0:T(8,128)S(1)} fusion(f32[2,2048,128]{2,1,0:T(8,128)} %collective-permute-done.8, f32[2,2,2048,128]{3,2,1,0:T(8,128)} %copy-done.5, pred[]{:T(512)S(6)} %eq.84), kind=kLoop, calls=%fused_computation.22 | loop fusion | flops 1048576 | bytes 8388609 | tf_op jit(solution)/shard_map/reshape | solution.py:59
  54.1 1.9 fusion.13
  59.2 2.0 %collective-permute-done.7 = bf16[2,32,32,128]{3,2,1,0:T(8,128)(2,1)S(1)} collective-permute-done((bf16[2,32,32,128]{3,2,1,0:T(8,128)(2,1)}, bf16[2,32,32,128]{3,2,1,0:T(8,128)(2,1)S(1)}, u32[]{:S(2)}, u32[]{:S(2)}) %collective-permute-start.7) | collective-permute-done | bytes 524320 | tf_op jit(solution)/shard_map/ppermute | solution.py:95
  61.5 2.2 %gather_fusion.1 = bf16[256,32,128]{2,1,0:T(8,128)(2,1)} fusion(bf16[128,32,128]{2,1,0:T(8,128)(2,1)S(1)} %bitcast.245, s32[1024]{0:T(1024)S(1)} %pad_clamp_fusion.1), kind=kCustom, calls=%fused_computation.1 | custom fusion | bytes 4195328 | tf_op jit(solution)/shard_map/gather | solution.py:179
  63.7 15.3 %collective-permute-done.9 = f32[1,2048,128]{2,1,0:T(8,128)} collective-permute-done((f32[1,2048,128]{2,1,0:T(8,128)}, f32[1,2048,128]{2,1,0:T(8,128)}, u32[]{:S(2)}, u32[]{:S(2)}) %collective-permute-start.9) | collective-permute-done | bytes 1048608 | tf_op jit(solution)/shard_map/ppermute | solution.py:44
  80.4 19.8 %collective-permute-done.11 = f32[1,2048,128]{2,1,0:T(8,128)} collective-permute-done((f32[1,2048,128]{2,1,0:T(8,128)}, f32[1,2048,128]{2,1,0:T(8,128)}, u32[]{:S(2)}, u32[]{:S(2)}) %collective-permute-start.11) | collective-permute-done | bytes 1048608 | tf_op jit(solution)/shard_map/ppermute | solution.py:44
  103.1 3.0 %gather_fusion.2 = bf16[256,64,128]{2,1,0:T(8,128)(2,1)} fusion(bf16[64,64,128]{2,1,0:T(8,128)(2,1)S(1)} %multiply_convert_fusion.1, s32[1024]{0:T(1024)S(1)} %pad_clamp_fusion), kind=kCustom, calls=%fused_computation.2 | custom fusion | bytes 8389632 | tf_op jit(solution)/shard_map/gather | solution.py:186
  106.1 5.2 %select_reduce_fusion = (f32[16,16,32]{2,1,0:T(8,128)S(1)}, f32[16,16,32,64]{3,2,1,0:T(8,128)S(1)}) fusion(pred[16,16,64]{2,1,0:T(8,128)(4,1)S(1)} %add_compare_fusion, bf16[16,16,32,128]{3,2,1,0:T(8,128)(2,1)} %bitcast.247, bf16[16,16,64,128]{3,2,1,0:T(8,128)(2,1)} %bitcast.242), kind=kOutput, calls=%fused_computation.15 | convolution fusion | flops 135258112 | bytes 8437760 | tf_op jit(solution)/shard_map/scie,scje->scij/dot_general | solution.py:188
  111.4 2.6 %fusion.6 = f32[16,16,32]{2,1,0:T(8,128)S(1)} fusion(f32[16,16,32,64]{3,2,1,0:T(8,128)S(1)} %get-tuple-element.53, f32[16,16,32]{2,1,0:T(8,128)S(1)} %get-tuple-element.52, pred[16,16,64]{2,1,0:T(8,128)(4,1)S(1)} %add_compare_fusion), kind=kLoop, calls=%fused_computation.16 | loop fusion | flops 1564672 | bytes 2179072 | tf_op jit(solution)/shard_map/reduce_sum | solution.py:22
  119.3 3.0 %collective-permute-start.16 = (f32[16,128]{1,0:T(8,128)S(1)}, f32[16,128]{1,0:T(8,128)S(1)}, u32[]{:S(2)}, u32[]{:S(2)}) collective-permute-start(f32[16,128]{1,0:T(8,128)S(1)} %fusion.54), channel_id=1, source_target_pairs={{0,8},{4,12},{8,0},{12,4},{1,9},{5,13},{9,1},{13,5},{2,10},{6,14},... | collective-permute-start | bytes 24584 | tf_op jit(solution)/shard_map/ppermute | solution.py:118
  122.3 2.6 %collective-permute-start.17 = (f32[16,128]{1,0:T(8,128)S(1)}, f32[16,128]{1,0:T(8,128)S(1)}, u32[]{:S(2)}, u32[]{:S(2)}) collective-permute-start(f32[16,128]{1,0:T(8,128)S(1)} %fusion.54), channel_id=1, source_target_pairs={{0,12},{4,0},{8,4},{12,8},{1,13},{5,1},{9,5},{13,9},{2,14},{6,2},{... | collective-permute-start | bytes 24584 | tf_op jit(solution)/shard_map/ppermute | solution.py:118
  127.0 1.9 gather_fusion.4
  129.0 6.9 %multiply_convert_fusion = bf16[16,16,64,128]{3,2,1,0:T(8,128)(2,1)S(1)} fusion(f32[16,16]{1,0:T(8,128)S(1)} %select_multiply_fusion, bf16[16,16,32,128]{3,2,1,0:T(8,128)(2,1)} %bitcast.248, f32[16,16,32,64]{3,2,1,0:T(8,128)} %copy-done.8, f32[16,16,32]{2,1,0:T(8,128)S(1)} %fusion.6, f32[16,16,32]{2,1,0:T(8,128)S(1)} %get-tuple-element.52, ...), kind=kOutput, calls=%fused_computation.5 | convolution fusion | flops 140509184 | bytes 8471552 | tf_op jit(solution)/shard_map/scij,scie->scje/dot_general | solution.py:191
  135.9 3.7 %fusion.14 = (f32[64,64]{0,1:T(8,128)S(1)}, f32[64,64,128]{2,0,1:T(8,128)S(1)}) fusion(f32[64,64,128]{2,1,0:T(8,128)S(1)} %bitcast.239, bf16[16,16,64,128]{3,2,1,0:T(8,128)(2,1)S(1)} %multiply_convert_fusion, s32[16,16]{0,1:T(8,128)S(1)} %copy.137, pred[16,16]{0,1:T(8,128)(4,1)S(1)} %copy.138), kind=kOutput, calls=%fused_computation.31 | convolution fusion | flops 269512704 | bytes 8406272 | tf_op jit(solution)/shard_map/scb,scje->bje/dot_general | solution.py:202
  139.6 2.6 %copy.141 = f32[64,64,128]{2,1,0:T(8,128)} copy(f32[64,64,128]{2,0,1:T(8,128)S(1)} %get-tuple-element.55) | data formatting | bytes 4194304 | tf_op jit(solution)/shard_map/scb,scje->bje/dot_general | solution.py:202
  142.3 3.6 %fusion.12 = bf16[1,4096,128]{2,1,0:T(8,128)(2,1)S(1)} fusion(f32[4096]{0:T(1024)S(1)} %mul.134, f32[4096]{0:T(1024)S(1)} %multiply_multiply_fusion, f32[4096]{0:T(1024)S(1)} %bitcast.256, f32[1,4096,128]{2,1,0:T(8,128)S(1)} %bitcast.240, f32[1,4096,128]{2,1,0:T(8,128)} %bitcast.246), kind=kLoop, calls=%fused_computation.26 | loop fusion | flops 2621440 | bytes 5292032 | tf_op jit(solution)/shard_map/convert_element_type | solution.py:210
  146.9 23.4 %collective-permute-done.18 = bf16[1,4096,128]{2,1,0:T(8,128)(2,1)S(1)} collective-permute-done((bf16[1,4096,128]{2,1,0:T(8,128)(2,1)S(1)}, bf16[1,4096,128]{2,1,0:T(8,128)(2,1)S(1)}, u32[]{:S(2)}, u32[]{:S(2)}) %collective-permute-start.18) | collective-permute-done | bytes 1048608 | tf_op jit(solution)/shard_map/ppermute | solution.py:44
  171.9 4.5 %collective-permute-done.19 = bf16[2,4096,128]{2,1,0:T(8,128)(2,1)} collective-permute-done((bf16[2,4096,128]{2,1,0:T(8,128)(2,1)}, bf16[2,4096,128]{2,1,0:T(8,128)(2,1)}, u32[]{:S(2)}, u32[]{:S(2)}) %collective-permute-start.19) | collective-permute-done | bytes 2097184 | tf_op jit(solution)/shard_map/ppermute | solution.py:44
  176.4 1.9 select_bitcast_fusion.1
  184.3 3.5 %collective-permute-start.21 = (f32[256,128]{0,1:T(8,128)S(1)}, f32[256,128]{0,1:T(8,128)S(1)}, u32[]{:S(2)}, u32[]{:S(2)}) collective-permute-start(f32[256,128]{0,1:T(8,128)S(1)} %bitcast.252), channel_id=1, source_target_pairs={{0,8},{4,12},{8,0},{12,4},{1,9},{5,13},{9,1},{13,5},{2,10},{6,14},... | collective-permute-start | bytes 393224 | tf_op jit(solution)/shard_map/ppermute | solution.py:118
  188.4 3.3 %collective-permute-done.20 = f32[256,128]{0,1:T(8,128)S(1)} collective-permute-done((f32[256,128]{0,1:T(8,128)S(1)}, f32[256,128]{0,1:T(8,128)S(1)}, u32[]{:S(2)}, u32[]{:S(2)}) %collective-permute-start.20) | collective-permute-done | bytes 131104 | tf_op jit(solution)/shard_map/ppermute | solution.py:118
  191.6 5.1 %collective-permute-done.21 = f32[256,128]{0,1:T(8,128)S(1)} collective-permute-done((f32[256,128]{0,1:T(8,128)S(1)}, f32[256,128]{0,1:T(8,128)S(1)}, u32[]{:S(2)}, u32[]{:S(2)}) %collective-permute-start.21) | collective-permute-done | bytes 131104 | tf_op jit(solution)/shard_map/ppermute | solution.py:118
  (144 shorter events, 42.7 us)
Async XLA Ops:
  0.6 3.8 %copy-start = (bf16[256,128]{1,0:T(8,128)(2,1)S(1)}, bf16[256,128]{1,0:T(8,128)(2,1)}, u32[]{:S(2)}) copy-start(bf16[256,128]{1,0:T(8,128)(2,1)} %param.6) | copy-start | bytes 196612
  7.7 40.6 %collective-permute-start.8 = (f32[2,2048,128]{2,1,0:T(8,128)S(1)}, f32[2,2048,128]{2,1,0:T(8,128)}, u32[]{:S(2)}, u32[]{:S(2)}) collective-permute-start(f32[2,2048,128]{2,1,0:T(8,128)S(1)} %select_bitcast_fusion.3), channel_id=1, source_target_pairs={{0,1},{1,0},{2,3},{3,2},{4,5},{5,4},{6,7},{7,6},{8,9},{9,8},{10,11... | collective-permute-start | bytes 6291464 | tf_op jit(solution)/shard_map/ppermute | solution.py:44
  9.4 2.7 %copy-start.3 = (f32[2,2,2048,128]{3,2,0,1:T(8,128)}, f32[2,2,2048,128]{3,2,0,1:T(8,128)S(1)}, u32[]{:S(2)}) copy-start(f32[2,2,2048,128]{3,2,0,1:T(8,128)S(1)} %fusion.2) | copy-start | bytes 12582916
  9.4 2.7 %copy-start.10 = (s32[8,16]{1,0:T(8,128)S(1)}, s32[8,16]{1,0:T(8,128)}, u32[]{:S(2)}) copy-start(s32[8,16]{1,0:T(8,128)} %param.9) | copy-start | bytes 1540
  9.4 5.6 %copy-start.9 = (bf16[8,32,128]{2,1,0:T(8,128)(2,1)S(1)}, bf16[8,32,128]{2,1,0:T(8,128)(2,1)}, u32[]{:S(2)}) copy-start(bf16[8,32,128]{2,1,0:T(8,128)(2,1)} %param.7) | copy-start | bytes 196612
  12.1 42.1 %collective-permute-start.10 = (f32[2,2048,128]{2,1,0:T(8,128)}, f32[2,2048,128]{2,1,0:T(8,128)}, u32[]{:S(2)}, u32[]{:S(2)}) collective-permute-start(f32[2,2048,128]{2,1,0:T(8,128)} %select_bitcast_fusion.2), channel_id=1, source_target_pairs={{0,1},{1,0},{2,3},{3,2},{4,5},{5,4},{6,7},{7,6},{8,9},{9,8},{10,11... | collective-permute-start | bytes 6291464 | tf_op jit(solution)/shard_map/ppermute | solution.py:44
  12.1 4.5 %collective-permute-start = (s32[1,8,16]{2,1,0:T(8,128)S(1)}, s32[1,8,16]{2,1,0:T(8,128)S(1)}, u32[]{:S(2)}, u32[]{:S(2)}) collective-permute-start(s32[1,8,16]{2,1,0:T(8,128)S(1)} %bitcast.270), channel_id=1, source_target_pairs={{0,2},{1,3},{2,0},{3,1},{4,6},{5,7},{6,4},{7,5},{8,10},{9,11},{10,... | collective-permute-start | bytes 1544 | tf_op jit(solution)/shard_map/ppermute | solution.py:95
  15.1 14.8 %collective-permute-start.4 = (bf16[1,8,32,128]{3,2,1,0:T(8,128)(2,1)S(1)}, bf16[1,8,32,128]{3,2,1,0:T(8,128)(2,1)S(1)}, u32[]{:S(2)}, u32[]{:S(2)}) collective-permute-start(bf16[1,8,32,128]{3,2,1,0:T(8,128)(2,1)S(1)} %bitcast.262), channel_id=1, source_target_pairs={{0,2},{1,3},{2,0},{3,1},{4,6},{5,7},{6,4},{7,5},{8,10},{9,11},{10,... | collective-permute-start | bytes 196616 | tf_op jit(solution)/shard_map/ppermute | solution.py:95
  16.7 1.2 collective-permute-start.1
  17.9 4.9 %collective-permute-start.2 = (s32[1,32,16]{2,1,0:T(8,128)S(1)}, s32[1,32,16]{2,1,0:T(8,128)S(1)}, u32[]{:S(2)}, u32[]{:S(2)}) collective-permute-start(s32[1,32,16]{2,1,0:T(8,128)S(1)} %bitcast.260), channel_id=1, source_target_pairs={{0,8},{4,12},{8,0},{12,4},{1,9},{5,13},{9,1},{13,5},{2,10},{6,14},... | collective-permute-start | bytes 6152 | tf_op jit(solution)/shard_map/ppermute | solution.py:95
  22.8 4.0 %collective-permute-start.3 = (s32[2,32,16]{2,1,0:T(8,128)S(1)}, s32[2,32,16]{2,1,0:T(8,128)S(1)}, u32[]{:S(2)}, u32[]{:S(2)}) collective-permute-start(s32[2,32,16]{2,1,0:T(8,128)S(1)} %add_bitcast_fusion.1), channel_id=1, source_target_pairs={{0,4},{4,0},{8,12},{12,8},{1,5},{5,1},{9,13},{13,9},{2,6},{6,2},{1... | collective-permute-start | bytes 12296 | tf_op jit(solution)/shard_map/ppermute | solution.py:95
  29.6 4.9 %copy-start.2 = (s32[256]{0:T(256)S(1)}, s32[256]{0:T(256)}, u32[]{:S(2)}) copy-start(s32[256]{0:T(256)} %param.8) | copy-start | bytes 3076
  29.9 1.4 collective-permute-start.5
  31.4 15.2 %collective-permute-start.6 = (bf16[1,32,32,128]{3,2,1,0:T(8,128)(2,1)S(1)}, bf16[1,32,32,128]{3,2,1,0:T(8,128)(2,1)S(1)}, u32[]{:S(2)}, u32[]{:S(2)}) collective-permute-start(bf16[1,32,32,128]{3,2,1,0:T(8,128)(2,1)S(1)} %bitcast.249), channel_id=1, source_target_pairs={{0,8},{4,12},{8,0},{12,4},{1,9},{5,13},{9,1},{13,5},{2,10},{6,14},... | collective-permute-start | bytes 786440 | tf_op jit(solution)/shard_map/ppermute | solution.py:95
  47.5 13.7 %collective-permute-start.7 = (bf16[2,32,32,128]{3,2,1,0:T(8,128)(2,1)}, bf16[2,32,32,128]{3,2,1,0:T(8,128)(2,1)S(1)}, u32[]{:S(2)}, u32[]{:S(2)}) collective-permute-start(bf16[2,32,32,128]{3,2,1,0:T(8,128)(2,1)} %maximum_bitcast_fusion.1), channel_id=1, source_target_pairs={{0,4},{4,0},{8,12},{12,8},{1,5},{5,1},{9,13},{13,9},{2,6},{6,2},{1... | collective-permute-start | bytes 1572872 | tf_op jit(solution)/shard_map/ppermute | solution.py:95
  48.3 5.9 %copy-start.4 = (f32[2,2,2048,128]{3,2,0,1:T(8,128)S(1)}, f32[2,2,2048,128]{3,2,0,1:T(8,128)}, u32[]{:S(2)}) copy-start(f32[2,2,2048,128]{3,2,0,1:T(8,128)} %copy-done.3) | copy-start | bytes 12582916
  52.6 26.4 %collective-permute-start.9 = (f32[1,2048,128]{2,1,0:T(8,128)}, f32[1,2048,128]{2,1,0:T(8,128)}, u32[]{:S(2)}, u32[]{:S(2)}) collective-permute-start(f32[1,2048,128]{2,1,0:T(8,128)} %select_bitcast_fusion.7), channel_id=1, source_target_pairs={{0,2},{1,3},{2,0},{3,1},{4,6},{5,7},{6,4},{7,5},{8,10},{9,11},{10,... | collective-permute-start | bytes 3145736 | tf_op jit(solution)/shard_map/ppermute | solution.py:44
  58.4 41.8 %collective-permute-start.11 = (f32[1,2048,128]{2,1,0:T(8,128)}, f32[1,2048,128]{2,1,0:T(8,128)}, u32[]{:S(2)}, u32[]{:S(2)}) collective-permute-start(f32[1,2048,128]{2,1,0:T(8,128)} %select_bitcast_fusion.6), channel_id=1, source_target_pairs={{0,2},{1,3},{2,0},{3,1},{4,6},{5,7},{6,4},{7,5},{8,10},{9,11},{10,... | collective-permute-start | bytes 3145736 | tf_op jit(solution)/shard_map/ppermute | solution.py:44
  63.7 36.5 %copy-start.7 = (f32[1,2,2048,128]{3,2,1,0:T(8,128)S(1)}, f32[1,2,2048,128]{3,2,1,0:T(8,128)}, u32[]{:S(2)}) copy-start(f32[1,2,2048,128]{3,2,1,0:T(8,128)} %copy-done.6) | copy-start | bytes 6291460
  114.2 3.1 %collective-permute-start.12 = (f32[16,128]{1,0:T(8,128)S(1)}, f32[16,128]{1,0:T(8,128)S(1)}, u32[]{:S(2)}, u32[]{:S(2)}) collective-permute-start(f32[16,128]{1,0:T(8,128)S(1)} %select_reduce_fusion.1), channel_id=1, source_target_pairs={{0,1},{1,2},{2,3},{3,0},{4,5},{5,6},{6,7},{7,4},{8,9},{9,10},{10,1... | collective-permute-start | bytes 24584 | tf_op jit(solution)/shard_map/ppermute | solution.py:118
  114.3 3.7 %collective-permute-start.13 = (f32[16,128]{1,0:T(8,128)S(1)}, f32[16,128]{1,0:T(8,128)S(1)}, u32[]{:S(2)}, u32[]{:S(2)}) collective-permute-start(f32[16,128]{1,0:T(8,128)S(1)} %select_reduce_fusion.1), channel_id=1, source_target_pairs={{0,2},{1,3},{2,0},{3,1},{4,6},{5,7},{6,4},{7,5},{8,10},{9,11},{10,... | collective-permute-start | bytes 24584 | tf_op jit(solution)/shard_map/ppermute | solution.py:118
  115.8 2.8 %collective-permute-start.14 = (f32[16,128]{1,0:T(8,128)S(1)}, f32[16,128]{1,0:T(8,128)S(1)}, u32[]{:S(2)}, u32[]{:S(2)}) collective-permute-start(f32[16,128]{1,0:T(8,128)S(1)} %select_reduce_fusion.1), channel_id=1, source_target_pairs={{0,3},{1,0},{2,1},{3,2},{4,7},{5,4},{6,5},{7,6},{8,11},{9,8},{10,9... | collective-permute-start | bytes 24584 | tf_op jit(solution)/shard_map/ppermute | solution.py:118
  118.6 6.4 %collective-permute-start.15 = (f32[16,128]{1,0:T(8,128)S(1)}, f32[16,128]{1,0:T(8,128)S(1)}, u32[]{:S(2)}, u32[]{:S(2)}) collective-permute-start(f32[16,128]{1,0:T(8,128)S(1)} %fusion.54), channel_id=1, source_target_pairs={{0,4},{4,8},{8,12},{12,0},{1,5},{5,9},{9,13},{13,1},{2,6},{6,10},{... | collective-permute-start | bytes 24584 | tf_op jit(solution)/shard_map/ppermute | solution.py:118
  119.3 5.7 %collective-permute-start.16 = (f32[16,128]{1,0:T(8,128)S(1)}, f32[16,128]{1,0:T(8,128)S(1)}, u32[]{:S(2)}, u32[]{:S(2)}) collective-permute-start(f32[16,128]{1,0:T(8,128)S(1)} %fusion.54), channel_id=1, source_target_pairs={{0,8},{4,12},{8,0},{12,4},{1,9},{5,13},{9,1},{13,5},{2,10},{6,14},... | collective-permute-start | bytes 24584 | tf_op jit(solution)/shard_map/ppermute | solution.py:118
  122.3 4.0 %collective-permute-start.17 = (f32[16,128]{1,0:T(8,128)S(1)}, f32[16,128]{1,0:T(8,128)S(1)}, u32[]{:S(2)}, u32[]{:S(2)}) collective-permute-start(f32[16,128]{1,0:T(8,128)S(1)} %fusion.54), channel_id=1, source_target_pairs={{0,12},{4,0},{8,4},{12,8},{1,13},{5,1},{9,5},{13,9},{2,14},{6,2},{... | collective-permute-start | bytes 24584 | tf_op jit(solution)/shard_map/ppermute | solution.py:118
  145.9 24.3 %collective-permute-start.18 = (bf16[1,4096,128]{2,1,0:T(8,128)(2,1)S(1)}, bf16[1,4096,128]{2,1,0:T(8,128)(2,1)S(1)}, u32[]{:S(2)}, u32[]{:S(2)}) collective-permute-start(bf16[1,4096,128]{2,1,0:T(8,128)(2,1)S(1)} %fusion.12), channel_id=1, source_target_pairs={{0,2},{1,3},{2,0},{3,1},{4,6},{5,7},{6,4},{7,5},{8,10},{9,11},{10,... | collective-permute-start | bytes 3145736 | tf_op jit(solution)/shard_map/ppermute | solution.py:44
  171.9 4.5 %collective-permute-start.19 = (bf16[2,4096,128]{2,1,0:T(8,128)(2,1)}, bf16[2,4096,128]{2,1,0:T(8,128)(2,1)}, u32[]{:S(2)}, u32[]{:S(2)}) collective-permute-start(bf16[2,4096,128]{2,1,0:T(8,128)(2,1)} %maximum_bitcast_fusion), channel_id=1, source_target_pairs={{0,1},{1,0},{2,3},{3,2},{4,5},{5,4},{6,7},{7,6},{8,9},{9,8},{10,11... | collective-permute-start | bytes 6291464 | tf_op jit(solution)/shard_map/ppermute | solution.py:44
  178.7 3.2 %slice-start.1 = ((s8[8388608]{0:T(1024)(128)(4,1)}), s8[4194304]{0:T(1024)(128)(4,1)S(1)}, s32[]{:S(2)}) async-start(s8[8388608]{0:T(1024)(128)(4,1)} %bitcast.236), calls=%async_computation.1 | async-start | bytes 8388608
  181.8 15.7 %copy-start.1 = (bf16[256,128]{1,0:T(8,128)(2,1)S(1)}, bf16[256,128]{1,0:T(8,128)(2,1)}, u32[]{:S(2)}) copy-start(bf16[256,128]{1,0:T(8,128)(2,1)} %param.6) | copy-start | bytes 196612
  183.4 8.3 %collective-permute-start.20 = (f32[256,128]{0,1:T(8,128)S(1)}, f32[256,128]{0,1:T(8,128)S(1)}, u32[]{:S(2)}, u32[]{:S(2)}) collective-permute-start(f32[256,128]{0,1:T(8,128)S(1)} %bitcast.251), channel_id=1, source_target_pairs={{0,4},{4,8},{8,12},{12,0},{1,5},{5,9},{9,13},{13,1},{2,6},{6,10},{... | collective-permute-start | bytes 393224 | tf_op jit(solution)/shard_map/ppermute | solution.py:118
  184.3 12.4 %collective-permute-start.21 = (f32[256,128]{0,1:T(8,128)S(1)}, f32[256,128]{0,1:T(8,128)S(1)}, u32[]{:S(2)}, u32[]{:S(2)}) collective-permute-start(f32[256,128]{0,1:T(8,128)S(1)} %bitcast.252), channel_id=1, source_target_pairs={{0,8},{4,12},{8,0},{12,4},{1,9},{5,13},{9,1},{13,5},{2,10},{6,14},... | collective-permute-start | bytes 393224 | tf_op jit(solution)/shard_map/ppermute | solution.py:118
  187.8 8.9 %collective-permute-start.22 = (f32[256,128]{0,1:T(8,128)S(1)}, f32[256,128]{0,1:T(8,128)S(1)}, u32[]{:S(2)}, u32[]{:S(2)}) collective-permute-start(f32[256,128]{0,1:T(8,128)S(1)} %bitcast.253), channel_id=1, source_target_pairs={{0,12},{4,0},{8,4},{12,8},{1,13},{5,1},{9,5},{13,9},{2,14},{6,2},{... | collective-permute-start | bytes 393224 | tf_op jit(solution)/shard_map/ppermute | solution.py:118
  (4 other events, 8.1 us)

commit v19 on v17

--- a/solution.py
+++ b/solution.py
@@ -144,7 +144,7 @@
 
     gathered = all_gather_many([queries, candidates], "mp")
 
-    chunks = 2 if row_share % (2 * BLK) == 0 else 1
+    chunks = 4 if row_share % (4 * BLK) == 0 else 1
     split_rows = hidden.reshape(mp_count, chunks, row_share // chunks, hidden.shape[1])
     partials = [
         jnp.dot(split_rows[:, k], proj_w, preferred_element_type=jnp.float32).reshape(

time: 169 us -> 184 us (1.089)
  other arithmetic: 26.6 us -> 31.7 us
  matrix products: 19.8 us -> 24.6 us
  local copies, waits for them, and re-layouts: 26.5 us -> 30.2 us
  waiting for transfers between devices: 67.8 us -> 70.8 us
  starting transfers between devices: 26.9 us -> 24.4 us
    ppermute x8, waiting for transfers between devices: 22.4 us -> 6.78 us  [all_gather_many(): others = lax.ppermute(arrs, axis, [(i, i ^ bit) for i in range(count)])]
    ppermute x6 -> x10, waiting for transfers between devices: 33.5 us -> 47.1 us  [xor_perm(): return lax.ppermute(value, axis, [(i, i ^ bit) for i in range(count)])]
    ppermute x9, waiting for transfers between devices: 11.9 us -> 16.9 us  [all_sum(): lax.ppermute(value, axis, [(i, (i + k) % count) for i in range(count)])]
    ppermute x9, starting transfers between devices: 13 us -> 9.43 us  [all_sum(): lax.ppermute(value, axis, [(i, (i + k) % count) for i in range(count)])]
    dot_general x2 -> x4, matrix products: 2.48 us -> 5.95 us  [local(): jnp.dot(split_rows[:, k], proj_w, preferred_element_type=jnp.float32)]
    ppermute x6 -> x10, starting transfers between devices: 3.77 us -> 6.78 us  [xor_perm(): return lax.ppermute(value, axis, [(i, i ^ bit) for i in range(count)])]
    select_n x4 -> x8, other arithmetic: 4.15 us -> 7.11 us  [halving_steps(): sends.append(jnp.where(low, acc[:, 1], acc[:, 0]))]
    another operation x12, other arithmetic: 0.32 us -> 2.54 us  [all_gather_many(): jnp.stack([jnp.where(low, a, o), jnp.where(low, o, a)], axis=1)]
  transfers between devices with their start and end apart: 23 -> 27, of which waited for: 14 -> 15; matrix products, arithmetic and copies ran while one was open for 13% -> 18% of each run, Pallas kernels for 0% -> 0%
where the time goes in v19:
time: 184 us; the launch traced here: 183 us
  waiting for transfers between devices  70.8 us (38%)
  other arithmetic  31.7 us (17%)
  local copies, waits for them, and re-layouts  30.2 us (16%)
  matrix products  24.6 us (13%)
  starting transfers between devices  24.4 us (13%)
    ppermute x10, waiting for transfers between devices, xor_perm(): return lax.ppermute(value, axis, [(i, i ^ bit) for i in range(count)])  47.1 us
    ppermute x9, waiting for transfers between devices, all_sum(): lax.ppermute(value, axis, [(i, (i + k) % count) for i in range(count)])  16.9 us
    ppermute x9, starting transfers between devices, all_sum(): lax.ppermute(value, axis, [(i, (i + k) % count) for i in range(count)])  9.43 us
    ppermute x8, starting transfers between devices, all_gather_many(): others = lax.ppermute(arrs, axis, [(i, i ^ bit) for i in range(count)])  8.23 us
    unnamed x47, local copies, waits for them, and re-layouts  8.06 us
    select_n x8, other arithmetic, halving_steps(): sends.append(jnp.where(low, acc[:, 1], acc[:, 0]))  7.11 us
    dot_general x1, matrix products, local(): jnp.einsum('scij,scie->scje', weights, q_e, preferred_element_type=jnp.fl...  6.95 us
    ppermute x10, starting transfers between devices, xor_perm(): return lax.ppermute(value, axis, [(i, i ^ bit) for i in range(count)])  6.78 us
  transfers between devices with their start and end apart: 27, of which 15 were waited for; matrix products, arithmetic and copies ran while one was open for 18% of the time, Pallas kernels for 0%

profile of v19, /device:TPU:0, one launch (start us, length us, event | category | flops | bytes accessed | tf_op | source)
XLA Modules:
  0.0 183.0 jit_solution(15149697009437184432)
XLA Ops:
  0.7 5.8 %fusion.55 = (bf16[4,1,1024,256]{3,2,1,0:T(8,128)(2,1)}, bf16[4,1,1024,256]{3,2,1,0:T(8,128)(2,1)}, bf16[4,1,1024,256]{3,2,1,0:T(8,128)(2,1)}, bf16[4,1,1024,256]{3,2,1,0:T(8,128)(2,1)S(1)}) fusion(bf16[4,4,1024,256]{3,2,1,0:T(8,128)(2,1)} %bitcast.291), kind=kLoop, calls=%fused_computation.172 | loop fusion | bytes 16777216 | tf_op jit(solution)/shard_map/slice | solution.py:150
  6.4 2.3 %fusion.3 = f32[2,2,1024,128]{3,2,1,0:T(8,128)S(1)} fusion(bf16[256,128]{1,0:T(8,128)(2,1)S(1)} %copy-done, bf16[2,2,1024,256]{3,2,1,0:T(8,128)(2,1)} %bitcast.306), kind=kOutput, calls=%fused_computation.15 | convolution fusion | flops 268435456 | bytes 4259840 | tf_op jit(solution)/shard_map/dot_general | solution.py:150
  9.6 2.9 %collective-permute-start.1 = (bf16[1,8,32,128]{3,2,1,0:T(8,128)(2,1)S(1)}, bf16[1,8,32,128]{3,2,1,0:T(8,128)(2,1)S(1)}, u32[]{:S(2)}, u32[]{:S(2)}) collective-permute-start(bf16[1,8,32,128]{3,2,1,0:T(8,128)(2,1)S(1)} %bitcast.319), channel_id=1, source_target_pairs={{0,2},{1,3},{2,0},{3,1},{4,6},{5,7},{6,4},{7,5},{8,10},{9,11},{10,... | collective-permute-start | bytes 196616 | tf_op jit(solution)/shard_map/ppermute | solution.py:95
  17.9 2.3 %fusion.12 = f32[2,2,1024,128]{3,2,0,1:T(8,128)S(1)} fusion(bf16[256,128]{1,0:T(8,128)(2,1)S(1)} %copy-done, bf16[2,2,1024,256]{3,2,1,0:T(8,128)(2,1)} %bitcast.303), kind=kOutput, calls=%fused_computation.26 | convolution fusion | flops 268435456 | bytes 4259840 | tf_op jit(solution)/shard_map/dot_general | solution.py:150
  23.3 2.0 %collective-permute-done.4 = s32[2,8,16]{2,1,0:T(8,128)S(1)} collective-permute-done((s32[2,8,16]{2,1,0:T(8,128)S(1)}, s32[2,8,16]{2,1,0:T(8,128)S(1)}, u32[]{:S(2)}, u32[]{:S(2)}) %collective-permute-start.4) | collective-permute-done | bytes 1056 | tf_op jit(solution)/shard_map/ppermute | solution.py:95
  26.7 2.1 %fusion.24 = f32[1,2,1024,128]{3,2,1,0:T(8,128)S(1)} fusion(f32[2,1024,128]{2,1,0:T(8,128)} %collective-permute-done, f32[2,2,1024,128]{3,2,1,0:T(8,128)} %copy-done.5, pred[]{:T(512)S(6)} %eq.93), kind=kLoop, calls=%fused_computation.43 | loop fusion | flops 524288 | bytes 4194305 | tf_op jit(solution)/shard_map/reshape | solution.py:59
  29.8 3.1 %collective-permute-start.5 = (s32[1,32,16]{2,1,0:T(8,128)S(1)}, s32[1,32,16]{2,1,0:T(8,128)S(1)}, u32[]{:S(2)}, u32[]{:S(2)}) collective-permute-start(s32[1,32,16]{2,1,0:T(8,128)S(1)} %bitcast.317), channel_id=1, source_target_pairs={{0,8},{4,12},{8,0},{12,4},{1,9},{5,13},{9,1},{13,5},{2,10},{6,14},... | collective-permute-start | bytes 6152 | tf_op jit(solution)/shard_map/ppermute | solution.py:95
  40.1 1.9 %collective-permute-start.6 = (s32[2,32,16]{2,1,0:T(8,128)S(1)}, s32[2,32,16]{2,1,0:T(8,128)S(1)}, u32[]{:S(2)}, u32[]{:S(2)}) collective-permute-start(s32[2,32,16]{2,1,0:T(8,128)S(1)} %add_bitcast_fusion.1), channel_id=1, source_target_pairs={{0,4},{4,0},{8,12},{12,8},{1,5},{5,1},{9,13},{13,9},{2,6},{6,2},{1... | collective-permute-start | bytes 12296 | tf_op jit(solution)/shard_map/ppermute | solution.py:95
  44.3 3.6 %collective-permute-done.6 = s32[2,32,16]{2,1,0:T(8,128)S(1)} collective-permute-done((s32[2,32,16]{2,1,0:T(8,128)S(1)}, s32[2,32,16]{2,1,0:T(8,128)S(1)}, u32[]{:S(2)}, u32[]{:S(2)}) %collective-permute-start.6) | collective-permute-done | bytes 4128 | tf_op jit(solution)/shard_map/ppermute | solution.py:95
  50.2 1.9 %gather_fusion.3 = s32[256]{0:T(256)S(1)} fusion(s32[16,128]{1,0:T(8,128)S(1)} %reshape_reshape_reshape.2, s32[256]{0:T(256)S(1)} %reshape.776), kind=kCustom, calls=%fused_computation.3 | custom fusion | bytes 4096 | tf_op jit(solution)/shard_map/jit(take_along_axis)/gather | solution.py:177
  52.8 1.9 %gather_fusion = s32[256]{0:T(256)S(1)} fusion(s32[256]{0:T(256)S(1)} %copy-done.2, s32[1024]{0:T(1024)S(1)} %pad_clamp_fusion.2), kind=kCustom, calls=%fused_computation | custom fusion | bytes 3072 | tf_op jit(solution)/shard_map/gather | solution.py:15
  59.7 2.0 %collective-permute-done.13 = f32[1,1024,128]{2,1,0:T(8,128)} collective-permute-done((f32[1,1024,128]{2,1,0:T(8,128)}, f32[1,1024,128]{2,1,0:T(8,128)}, u32[]{:S(2)}, u32[]{:S(2)}) %collective-permute-start.13) | collective-permute-done | bytes 524320 | tf_op jit(solution)/shard_map/ppermute | solution.py:44
  62.8 10.1 %collective-permute-done.11 = f32[1,1024,128]{2,1,0:T(8,128)} collective-permute-done((f32[1,1024,128]{2,1,0:T(8,128)}, f32[1,1024,128]{2,1,0:T(8,128)}, u32[]{:S(2)}, u32[]{:S(2)}) %collective-permute-start.11) | collective-permute-done | bytes 524320 | tf_op jit(solution)/shard_map/ppermute | solution.py:44
  74.1 9.0 %collective-permute-done.9 = f32[1,1024,128]{2,1,0:T(8,128)} collective-permute-done((f32[1,1024,128]{2,1,0:T(8,128)}, f32[1,1024,128]{2,1,0:T(8,128)}, u32[]{:S(2)}, u32[]{:S(2)}) %collective-permute-start.9) | collective-permute-done | bytes 524320 | tf_op jit(solution)/shard_map/ppermute | solution.py:44
  85.6 3.1 %gather_fusion.2 = bf16[256,64,128]{2,1,0:T(8,128)(2,1)} fusion(bf16[64,64,128]{2,1,0:T(8,128)(2,1)S(1)} %multiply_convert_fusion.1, s32[1024]{0:T(1024)S(1)} %pad_clamp_fusion), kind=kCustom, calls=%fused_computation.2 | custom fusion | bytes 8389632 | tf_op jit(solution)/shard_map/gather | solution.py:188
  90.1 2.2 %gather_fusion.1 = bf16[256,32,128]{2,1,0:T(8,128)(2,1)} fusion(bf16[128,32,128]{2,1,0:T(8,128)(2,1)S(1)} %bitcast.299, s32[1024]{0:T(1024)S(1)} %pad_clamp_fusion.1), kind=kCustom, calls=%fused_computation.1 | custom fusion | bytes 4195328 | tf_op jit(solution)/shard_map/gather | solution.py:181
  92.3 5.2 %select_reduce_fusion = (f32[16,16,32]{2,1,0:T(8,128)S(1)}, f32[16,16,32,64]{3,2,1,0:T(8,128)S(1)}) fusion(pred[16,16,64]{2,1,0:T(8,128)(4,1)S(1)} %add_compare_fusion, bf16[16,16,32,128]{3,2,1,0:T(8,128)(2,1)} %bitcast.301, bf16[16,16,64,128]{3,2,1,0:T(8,128)(2,1)} %bitcast.298), kind=kOutput, calls=%fused_computation.11 | convolution fusion | flops 135258112 | bytes 8437760 | tf_op jit(solution)/shard_map/scie,scje->scij/dot_general | solution.py:190
  97.5 2.6 %fusion.2 = f32[16,16,32]{2,1,0:T(8,128)S(1)} fusion(f32[16,16,32,64]{3,2,1,0:T(8,128)S(1)} %get-tuple-element.61, f32[16,16,32]{2,1,0:T(8,128)S(1)} %get-tuple-element.60, pred[16,16,64]{2,1,0:T(8,128)(4,1)S(1)} %add_compare_fusion), kind=kLoop, calls=%fused_computation.12 | loop fusion | flops 1564672 | bytes 2179072 | tf_op jit(solution)/shard_map/reduce_sum | solution.py:22
  102.2 2.0 %collective-permute-done.17 = f32[16,128]{1,0:T(8,128)S(1)} collective-permute-done((f32[16,128]{1,0:T(8,128)S(1)}, f32[16,128]{1,0:T(8,128)S(1)}, u32[]{:S(2)}, u32[]{:S(2)}) %collective-permute-start.17) | collective-permute-done | bytes 8224 | tf_op jit(solution)/shard_map/ppermute | solution.py:118
  105.1 3.7 %collective-permute-start.21 = (f32[16,128]{1,0:T(8,128)S(1)}, f32[16,128]{1,0:T(8,128)S(1)}, u32[]{:S(2)}, u32[]{:S(2)}) collective-permute-start(f32[16,128]{1,0:T(8,128)S(1)} %fusion.62), channel_id=1, source_target_pairs={{0,12},{4,0},{8,4},{12,8},{1,13},{5,1},{9,5},{13,9},{2,14},{6,2},{... | collective-permute-start | bytes 24584 | tf_op jit(solution)/shard_map/ppermute | solution.py:118
  110.2 3.2 %collective-permute-done.20 = f32[16,128]{1,0:T(8,128)S(1)} collective-permute-done((f32[16,128]{1,0:T(8,128)S(1)}, f32[16,128]{1,0:T(8,128)S(1)}, u32[]{:S(2)}, u32[]{:S(2)}) %collective-permute-start.20) | collective-permute-done | bytes 8224 | tf_op jit(solution)/shard_map/ppermute | solution.py:118
  114.9 1.9 %gather_fusion.4 = f32[256]{0:T(256)S(1)} fusion(f32[16,128]{1,0:T(8,128)S(1)} %reshape.748, s32[256]{0:T(256)S(1)} %reshape.776), kind=kCustom, calls=%fused_computation.4 | custom fusion | bytes 4096 | tf_op jit(solution)/shard_map/jit(take_along_axis)/gather | solution.py:200
  116.9 6.9 %multiply_convert_fusion = bf16[16,16,64,128]{3,2,1,0:T(8,128)(2,1)S(1)} fusion(f32[16,16]{1,0:T(8,128)S(1)} %select_multiply_fusion, bf16[16,16,32,128]{3,2,1,0:T(8,128)(2,1)} %bitcast.302, f32[16,16,32,64]{3,2,1,0:T(8,128)} %copy-done.8, f32[16,16,32]{2,1,0:T(8,128)S(1)} %fusion.2, f32[16,16,32]{2,1,0:T(8,128)S(1)} %get-tuple-element.60, ...), kind=kOutput, calls=%fused_computation.5 | convolution fusion | flops 140509184 | bytes 8471552 | tf_op jit(solution)/shard_map/scij,scie->scje/dot_general | solution.py:193
  123.8 5.0 %fusion.14 = (f32[64,64]{0,1:T(8,128)S(1)}, f32[64,64,128]{2,0,1:T(8,128)}) fusion(f32[64,64,128]{2,1,0:T(8,128)S(1)} %bitcast.295, bf16[16,16,64,128]{3,2,1,0:T(8,128)(2,1)S(1)} %multiply_convert_fusion, s32[16,16]{0,1:T(8,128)S(1)} %copy.179, pred[16,16]{0,1:T(8,128)(4,1)S(1)} %copy.180), kind=kOutput, calls=%fused_computation.29 | convolution fusion | flops 269512704 | bytes 8406272 | tf_op jit(solution)/shard_map/scb,scje->bje/dot_general | solution.py:204
  128.9 2.8 %copy.183 = f32[64,64,128]{2,1,0:T(8,128)S(1)} copy(f32[64,64,128]{2,0,1:T(8,128)} %get-tuple-element.63) | data formatting | bytes 4194304 | tf_op jit(solution)/shard_map/scb,scje->bje/dot_general | solution.py:204
  131.8 1.9 %fusion.7 = bf16[1,4096,128]{2,1,0:T(8,128)(2,1)S(1)} fusion(f32[4096]{0:T(1024)S(1)} %mul.134, f32[4096]{0:T(1024)S(1)} %multiply_multiply_fusion, f32[4096]{0:T(1024)S(1)} %bitcast.316, f32[1,4096,128]{2,1,0:T(8,128)S(1)} %bitcast.296, f32[1,4096,128]{2,1,0:T(8,128)S(1)} %bitcast.300), kind=kLoop, calls=%fused_computation.20 | loop fusion | flops 2621440 | bytes 5292032 | tf_op jit(solution)/shard_map/convert_element_type | solution.py:212
  134.4 21.4 %collective-permute-done.22 = bf16[1,4096,128]{2,1,0:T(8,128)(2,1)S(1)} collective-permute-done((bf16[1,4096,128]{2,1,0:T(8,128)(2,1)S(1)}, bf16[1,4096,128]{2,1,0:T(8,128)(2,1)S(1)}, u32[]{:S(2)}, u32[]{:S(2)}) %collective-permute-start.22) | collective-permute-done | bytes 1048608 | tf_op jit(solution)/shard_map/ppermute | solution.py:44
  157.5 4.5 %collective-permute-done.23 = bf16[2,4096,128]{2,1,0:T(8,128)(2,1)} collective-permute-done((bf16[2,4096,128]{2,1,0:T(8,128)(2,1)}, bf16[2,4096,128]{2,1,0:T(8,128)(2,1)}, u32[]{:S(2)}, u32[]{:S(2)}) %collective-permute-start.23) | collective-permute-done | bytes 2097184 | tf_op jit(solution)/shard_map/ppermute | solution.py:44
  162.0 1.9 %select_bitcast_fusion.1 = (bf16[2,1,4096,128]{3,2,0,1:T(8,128)(2,1)S(1)}, bf16[2,1,4096,128]{3,2,0,1:T(8,128)(2,1)S(1)}) fusion(bf16[2,4096,128]{2,1,0:T(8,128)(2,1)} %collective-permute-done.23, pred[]{:T(512)S(6)} %eq.93, bf16[1,1,4096,128]{3,2,1,0:T(8,128)(2,1)S(1)} %get-tuple-element.35, bf16[1,1,4096,128]{3,2,1,0:T(8,128)(2,1)S(1)} %get-tuple-element.34), kind=kLoop, calls=%fused_computation.31 | loop fusion | flops 3145728 | bytes 8388609 | tf_op jit(solution)/shard_map/stack | solution.py:81
  170.0 1.9 %collective-permute-start.24 = (f32[256,128]{0,1:T(8,128)S(1)}, f32[256,128]{0,1:T(8,128)S(1)}, u32[]{:S(2)}, u32[]{:S(2)}) collective-permute-start(f32[256,128]{0,1:T(8,128)S(1)} %bitcast.311), channel_id=1, source_target_pairs={{0,4},{4,8},{8,12},{12,0},{1,5},{5,9},{9,13},{13,1},{2,6},{6,10},{... | collective-permute-start | bytes 393224 | tf_op jit(solution)/shard_map/ppermute | solution.py:118
  172.5 3.2 %collective-permute-done.26 = f32[256,128]{0,1:T(8,128)S(1)} collective-permute-done((f32[256,128]{0,1:T(8,128)S(1)}, f32[256,128]{0,1:T(8,128)S(1)}, u32[]{:S(2)}, u32[]{:S(2)}) %collective-permute-start.26) | collective-permute-done | bytes 131104 | tf_op jit(solution)/shard_map/ppermute | solution.py:118
  175.7 6.4 %collective-permute-done.25 = f32[256,128]{0,1:T(8,128)S(1)} collective-permute-done((f32[256,128]{0,1:T(8,128)S(1)}, f32[256,128]{0,1:T(8,128)S(1)}, u32[]{:S(2)}, u32[]{:S(2)}) %collective-permute-start.25) | collective-permute-done | bytes 131104 | tf_op jit(solution)/shard_map/ppermute | solution.py:118
  (180 shorter events, 50.9 us)
Async XLA Ops:
  8.9 17.9 %collective-permute-start = (f32[2,1024,128]{2,1,0:T(8,128)S(1)}, f32[2,1024,128]{2,1,0:T(8,128)}, u32[]{:S(2)}, u32[]{:S(2)}) collective-permute-start(f32[2,1024,128]{2,1,0:T(8,128)S(1)} %select_bitcast_fusion.7), channel_id=1, source_target_pairs={{0,1},{1,0},{2,3},{3,2},{4,5},{5,4},{6,7},{7,6},{8,9},{9,8},{10,11... | collective-permute-start | bytes 3145736 | tf_op jit(solution)/shard_map/ppermute | solution.py:44
  9.6 13.5 %collective-permute-start.1 = (bf16[1,8,32,128]{3,2,1,0:T(8,128)(2,1)S(1)}, bf16[1,8,32,128]{3,2,1,0:T(8,128)(2,1)S(1)}, u32[]{:S(2)}, u32[]{:S(2)}) collective-permute-start(bf16[1,8,32,128]{3,2,1,0:T(8,128)(2,1)S(1)} %bitcast.319), channel_id=1, source_target_pairs={{0,2},{1,3},{2,0},{3,1},{4,6},{5,7},{6,4},{7,5},{8,10},{9,11},{10,... | collective-permute-start | bytes 196616 | tf_op jit(solution)/shard_map/ppermute | solution.py:95
  12.6 10.1 %collective-permute-start.3 = (s32[1,8,16]{2,1,0:T(8,128)S(1)}, s32[1,8,16]{2,1,0:T(8,128)S(1)}, u32[]{:S(2)}, u32[]{:S(2)}) collective-permute-start(s32[1,8,16]{2,1,0:T(8,128)S(1)} %bitcast.327), channel_id=1, source_target_pairs={{0,2},{1,3},{2,0},{3,1},{4,6},{5,7},{6,4},{7,5},{8,10},{9,11},{10,... | collective-permute-start | bytes 1544 | tf_op jit(solution)/shard_map/ppermute | solution.py:95
  14.4 18.5 %collective-permute-start.14 = (f32[2,1024,128]{2,1,0:T(8,128)}, f32[2,1024,128]{2,1,0:T(8,128)}, u32[]{:S(2)}, u32[]{:S(2)}) collective-permute-start(f32[2,1024,128]{2,1,0:T(8,128)} %select_bitcast_fusion.4), channel_id=1, source_target_pairs={{0,1},{1,0},{2,3},{3,2},{4,5},{5,4},{6,7},{7,6},{8,9},{9,8},{10,11... | collective-permute-start | bytes 3145736 | tf_op jit(solution)/shard_map/ppermute | solution.py:44
  17.9 19.2 %collective-permute-start.12 = (f32[2,1024,128]{2,1,0:T(8,128)}, f32[2,1024,128]{2,1,0:T(8,128)}, u32[]{:S(2)}, u32[]{:S(2)}) collective-permute-start(f32[2,1024,128]{2,1,0:T(8,128)} %select_bitcast_fusion.5), channel_id=1, source_target_pairs={{0,1},{1,0},{2,3},{3,2},{4,5},{5,4},{6,7},{7,6},{8,9},{9,8},{10,11... | collective-permute-start | bytes 3145736 | tf_op jit(solution)/shard_map/ppermute | solution.py:44
  22.6 17.2 %collective-permute-start.10 = (f32[2,1024,128]{2,1,0:T(8,128)}, f32[2,1024,128]{2,1,0:T(8,128)S(1)}, u32[]{:S(2)}, u32[]{:S(2)}) collective-permute-start(f32[2,1024,128]{2,1,0:T(8,128)} %select_bitcast_fusion.6), channel_id=1, source_target_pairs={{0,1},{1,0},{2,3},{3,2},{4,5},{5,4},{6,7},{7,6},{8,9},{9,8},{10,11... | collective-permute-start | bytes 3145736 | tf_op jit(solution)/shard_map/ppermute | solution.py:44
  23.2 2.1 %collective-permute-start.4 = (s32[2,8,16]{2,1,0:T(8,128)S(1)}, s32[2,8,16]{2,1,0:T(8,128)S(1)}, u32[]{:S(2)}, u32[]{:S(2)}) collective-permute-start(s32[2,8,16]{2,1,0:T(8,128)S(1)} %add_bitcast_fusion.2), channel_id=1, source_target_pairs={{0,1},{1,0},{2,3},{3,2},{4,5},{5,4},{6,7},{7,6},{8,9},{9,8},{10,11... | collective-permute-start | bytes 3080 | tf_op jit(solution)/shard_map/ppermute | solution.py:95
  25.3 1.3 collective-permute-start.2
  26.7 6.2 %copy-start.17 = (bf16[2,2,8,32,128]{4,3,2,1,0:T(8,128)(2,1)}, bf16[2,2,8,32,128]{4,3,2,1,0:T(8,128)(2,1)S(1)}, u32[]{:S(2)}) copy-start(bf16[2,2,8,32,128]{4,3,2,1,0:T(8,128)(2,1)S(1)} %pad_maximum_fusion.4) | copy-start | bytes 786436
  26.7 6.2 %copy-start.4 = (f32[2,2,1024,128]{3,2,0,1:T(8,128)S(1)}, f32[2,2,1024,128]{3,2,0,1:T(8,128)}, u32[]{:S(2)}) copy-start(f32[2,2,1024,128]{3,2,0,1:T(8,128)} %copy-done.3) | copy-start | bytes 6291460
  29.8 10.2 %collective-permute-start.5 = (s32[1,32,16]{2,1,0:T(8,128)S(1)}, s32[1,32,16]{2,1,0:T(8,128)S(1)}, u32[]{:S(2)}, u32[]{:S(2)}) collective-permute-start(s32[1,32,16]{2,1,0:T(8,128)S(1)} %bitcast.317), channel_id=1, source_target_pairs={{0,8},{4,12},{8,0},{12,4},{1,9},{5,13},{9,1},{13,5},{2,10},{6,14},... | collective-permute-start | bytes 6152 | tf_op jit(solution)/shard_map/ppermute | solution.py:95
  32.9 22.9 %collective-permute-start.7 = (bf16[1,32,32,128]{3,2,1,0:T(8,128)(2,1)S(1)}, bf16[1,32,32,128]{3,2,1,0:T(8,128)(2,1)}, u32[]{:S(2)}, u32[]{:S(2)}) collective-permute-start(bf16[1,32,32,128]{3,2,1,0:T(8,128)(2,1)S(1)} %bitcast.307), channel_id=1, source_target_pairs={{0,8},{4,12},{8,0},{12,4},{1,9},{5,13},{9,1},{13,5},{2,10},{6,14},... | collective-permute-start | bytes 786440 | tf_op jit(solution)/shard_map/ppermute | solution.py:95
  35.4 23.1 %collective-permute-start.15 = (f32[1,1024,128]{2,1,0:T(8,128)}, f32[1,1024,128]{2,1,0:T(8,128)}, u32[]{:S(2)}, u32[]{:S(2)}) collective-permute-start(f32[1,1024,128]{2,1,0:T(8,128)} %select_bitcast_fusion.8), channel_id=1, source_target_pairs={{0,2},{1,3},{2,0},{3,1},{4,6},{5,7},{6,4},{7,5},{8,10},{9,11},{10,... | collective-permute-start | bytes 1572872 | tf_op jit(solution)/shard_map/ppermute | solution.py:44
  39.5 22.2 %collective-permute-start.13 = (f32[1,1024,128]{2,1,0:T(8,128)}, f32[1,1024,128]{2,1,0:T(8,128)}, u32[]{:S(2)}, u32[]{:S(2)}) collective-permute-start(f32[1,1024,128]{2,1,0:T(8,128)} %select_bitcast_fusion.9), channel_id=1, source_target_pairs={{0,2},{1,3},{2,0},{3,1},{4,6},{5,7},{6,4},{7,5},{8,10},{9,11},{10,... | collective-permute-start | bytes 1572872 | tf_op jit(solution)/shard_map/ppermute | solution.py:44
  40.0 9.3 %copy-start.13 = (f32[1,2,1024,128]{3,2,1,0:T(8,128)}, f32[1,2,1024,128]{3,2,1,0:T(8,128)S(1)}, u32[]{:S(2)}) copy-start(f32[1,2,1024,128]{3,2,1,0:T(8,128)S(1)} %fusion.27) | copy-start | bytes 3145732
  40.1 7.8 %collective-permute-start.6 = (s32[2,32,16]{2,1,0:T(8,128)S(1)}, s32[2,32,16]{2,1,0:T(8,128)S(1)}, u32[]{:S(2)}, u32[]{:S(2)}) collective-permute-start(s32[2,32,16]{2,1,0:T(8,128)S(1)} %add_bitcast_fusion.1), channel_id=1, source_target_pairs={{0,4},{4,0},{8,12},{12,8},{1,5},{5,1},{9,13},{13,9},{2,6},{6,2},{1... | collective-permute-start | bytes 12296 | tf_op jit(solution)/shard_map/ppermute | solution.py:95
  42.9 30.1 %collective-permute-start.11 = (f32[1,1024,128]{2,1,0:T(8,128)}, f32[1,1024,128]{2,1,0:T(8,128)}, u32[]{:S(2)}, u32[]{:S(2)}) collective-permute-start(f32[1,1024,128]{2,1,0:T(8,128)} %select_bitcast_fusion.10), channel_id=1, source_target_pairs={{0,2},{1,3},{2,0},{3,1},{4,6},{5,7},{6,4},{7,5},{8,10},{9,11},{10,... | collective-permute-start | bytes 1572872 | tf_op jit(solution)/shard_map/ppermute | solution.py:44
  47.8 35.3 %collective-permute-start.9 = (f32[1,1024,128]{2,1,0:T(8,128)}, f32[1,1024,128]{2,1,0:T(8,128)}, u32[]{:S(2)}, u32[]{:S(2)}) collective-permute-start(f32[1,1024,128]{2,1,0:T(8,128)} %select_bitcast_fusion.13), channel_id=1, source_target_pairs={{0,2},{1,3},{2,0},{3,1},{4,6},{5,7},{6,4},{7,5},{8,10},{9,11},{10,... | collective-permute-start | bytes 1572872 | tf_op jit(solution)/shard_map/ppermute | solution.py:44
  58.5 14.5 %copy-start.14 = (f32[1,2,1024,128]{3,2,1,0:T(8,128)S(1)}, f32[1,2,1024,128]{3,2,1,0:T(8,128)}, u32[]{:S(2)}) copy-start(f32[1,2,1024,128]{3,2,1,0:T(8,128)} %copy-done.13) | copy-start | bytes 3145732
  58.5 30.2 %collective-permute-start.8 = (bf16[2,32,32,128]{3,2,1,0:T(8,128)(2,1)}, bf16[2,32,32,128]{3,2,1,0:T(8,128)(2,1)}, u32[]{:S(2)}, u32[]{:S(2)}) collective-permute-start(bf16[2,32,32,128]{3,2,1,0:T(8,128)(2,1)} %maximum_bitcast_fusion.1), channel_id=1, source_target_pairs={{0,4},{4,0},{8,12},{12,8},{1,5},{5,1},{9,13},{13,9},{2,6},{6,2},{1... | collective-permute-start | bytes 1572872 | tf_op jit(solution)/shard_map/ppermute | solution.py:95
  100.4 1.8 collective-permute-start.18
  100.5 3.7 %collective-permute-start.17 = (f32[16,128]{1,0:T(8,128)S(1)}, f32[16,128]{1,0:T(8,128)S(1)}, u32[]{:S(2)}, u32[]{:S(2)}) collective-permute-start(f32[16,128]{1,0:T(8,128)S(1)} %select_reduce_fusion.1), channel_id=1, source_target_pairs={{0,2},{1,3},{2,0},{3,1},{4,6},{5,7},{6,4},{7,5},{8,10},{9,11},{10,... | collective-permute-start | bytes 24584 | tf_op jit(solution)/shard_map/ppermute | solution.py:118
  102.0 3.1 %collective-permute-start.16 = (f32[16,128]{1,0:T(8,128)S(1)}, f32[16,128]{1,0:T(8,128)S(1)}, u32[]{:S(2)}, u32[]{:S(2)}) collective-permute-start(f32[16,128]{1,0:T(8,128)S(1)} %select_reduce_fusion.1), channel_id=1, source_target_pairs={{0,1},{1,2},{2,3},{3,0},{4,5},{5,6},{6,7},{7,4},{8,9},{9,10},{10,1... | collective-permute-start | bytes 24584 | tf_op jit(solution)/shard_map/ppermute | solution.py:118
  105.1 5.0 %collective-permute-start.21 = (f32[16,128]{1,0:T(8,128)S(1)}, f32[16,128]{1,0:T(8,128)S(1)}, u32[]{:S(2)}, u32[]{:S(2)}) collective-permute-start(f32[16,128]{1,0:T(8,128)S(1)} %fusion.62), channel_id=1, source_target_pairs={{0,12},{4,0},{8,4},{12,8},{1,13},{5,1},{9,5},{13,9},{2,14},{6,2},{... | collective-permute-start | bytes 24584 | tf_op jit(solution)/shard_map/ppermute | solution.py:118
  108.8 4.5 %collective-permute-start.20 = (f32[16,128]{1,0:T(8,128)S(1)}, f32[16,128]{1,0:T(8,128)S(1)}, u32[]{:S(2)}, u32[]{:S(2)}) collective-permute-start(f32[16,128]{1,0:T(8,128)S(1)} %fusion.62), channel_id=1, source_target_pairs={{0,8},{4,12},{8,0},{12,4},{1,9},{5,13},{9,1},{13,5},{2,10},{6,14},... | collective-permute-start | bytes 24584 | tf_op jit(solution)/shard_map/ppermute | solution.py:118
  108.8 5.4 %collective-permute-start.19 = (f32[16,128]{1,0:T(8,128)S(1)}, f32[16,128]{1,0:T(8,128)S(1)}, u32[]{:S(2)}, u32[]{:S(2)}) collective-permute-start(f32[16,128]{1,0:T(8,128)S(1)} %fusion.62), channel_id=1, source_target_pairs={{0,4},{4,8},{8,12},{12,0},{1,5},{5,9},{9,13},{13,1},{2,6},{6,10},{... | collective-permute-start | bytes 24584 | tf_op jit(solution)/shard_map/ppermute | solution.py:118
  133.7 22.1 %collective-permute-start.22 = (bf16[1,4096,128]{2,1,0:T(8,128)(2,1)S(1)}, bf16[1,4096,128]{2,1,0:T(8,128)(2,1)S(1)}, u32[]{:S(2)}, u32[]{:S(2)}) collective-permute-start(bf16[1,4096,128]{2,1,0:T(8,128)(2,1)S(1)} %fusion.7), channel_id=1, source_target_pairs={{0,2},{1,3},{2,0},{3,1},{4,6},{5,7},{6,4},{7,5},{8,10},{9,11},{10,... | collective-permute-start | bytes 3145736 | tf_op jit(solution)/shard_map/ppermute | solution.py:44
  157.5 4.5 %collective-permute-start.23 = (bf16[2,4096,128]{2,1,0:T(8,128)(2,1)}, bf16[2,4096,128]{2,1,0:T(8,128)(2,1)}, u32[]{:S(2)}, u32[]{:S(2)}) collective-permute-start(bf16[2,4096,128]{2,1,0:T(8,128)(2,1)} %maximum_bitcast_fusion), channel_id=1, source_target_pairs={{0,1},{1,0},{2,3},{3,2},{4,5},{5,4},{6,7},{7,6},{8,9},{9,8},{10,11... | collective-permute-start | bytes 6291464 | tf_op jit(solution)/shard_map/ppermute | solution.py:44
  167.4 15.6 %copy-start.1 = (bf16[256,128]{1,0:T(8,128)(2,1)S(1)}, bf16[256,128]{1,0:T(8,128)(2,1)}, u32[]{:S(2)}) copy-start(bf16[256,128]{1,0:T(8,128)(2,1)} %param.6) | copy-start | bytes 196612
  168.9 6.8 %collective-permute-start.26 = (f32[256,128]{0,1:T(8,128)S(1)}, f32[256,128]{0,1:T(8,128)S(1)}, u32[]{:S(2)}, u32[]{:S(2)}) collective-permute-start(f32[256,128]{0,1:T(8,128)S(1)} %bitcast.309), channel_id=1, source_target_pairs={{0,12},{4,0},{8,4},{12,8},{1,13},{5,1},{9,5},{13,9},{2,14},{6,2},{... | collective-permute-start | bytes 393224 | tf_op jit(solution)/shard_map/ppermute | solution.py:118
  169.6 12.5 %collective-permute-start.25 = (f32[256,128]{0,1:T(8,128)S(1)}, f32[256,128]{0,1:T(8,128)S(1)}, u32[]{:S(2)}, u32[]{:S(2)}) collective-permute-start(f32[256,128]{0,1:T(8,128)S(1)} %bitcast.310), channel_id=1, source_target_pairs={{0,8},{4,12},{8,0},{12,4},{1,9},{5,13},{9,1},{13,5},{2,10},{6,14},... | collective-permute-start | bytes 393224 | tf_op jit(solution)/shard_map/ppermute | solution.py:118
  170.0 12.1 %collective-permute-start.24 = (f32[256,128]{0,1:T(8,128)S(1)}, f32[256,128]{0,1:T(8,128)S(1)}, u32[]{:S(2)}, u32[]{:S(2)}) collective-permute-start(f32[256,128]{0,1:T(8,128)S(1)} %bitcast.311), channel_id=1, source_target_pairs={{0,4},{4,8},{8,12},{12,0},{1,5},{5,9},{9,13},{13,1},{2,6},{6,10},{... | collective-permute-start | bytes 393224 | tf_op jit(solution)/shard_map/ppermute | solution.py:118
  (17 other events, 51.1 us)

commit v20 on v17

--- a/solution.py
+++ b/solution.py
@@ -103,9 +103,9 @@
     return [a.reshape((-1,) + v.shape[1:]) for a, v in zip(arrs, values)]
 
 
-def all_sum(value, axis):
-    count = lax.axis_size(axis)
-    if count > 4:
+def all_sum(value, axis, one_step=True):
+    count = lax.axis_size(axis)
+    if count > 4 or not one_step:
         if not is_pow2(count):
             return lax.psum(value, axis)
         bit = 1
@@ -211,7 +211,7 @@
     dot_e = jnp.sum(e_pre * grad_flat, -1, keepdims=True)
     de_pre = (scale * grad_flat - e_pre * (scale * scale * scale) * dot_e).astype(jnp.bfloat16)
     partial_w = left_product(hidden, all_gather_rows(de_pre, "mp"))
-    grad_w = all_sum(partial_w, "enc")
+    grad_w = all_sum(partial_w, "enc", one_step=False)
     return (losses, grad_w)
 
 

time: 169 us -> 167 us (0.988)
  other arithmetic: 26.6 us -> 23.6 us
  waiting for transfers between devices: 67.8 us -> 69.9 us
    ppermute x6 -> x8, waiting for transfers between devices: 33.5 us -> 43.9 us  [xor_perm(): return lax.ppermute(value, axis, [(i, i ^ bit) for i in range(count)])]
    ppermute x9 -> x6, waiting for transfers between devices: 11.9 us -> 3.64 us  [all_sum(): lax.ppermute(value, axis, [(i, (i + k) % count) for i in range(count)])]
    ppermute x9 -> x6, starting transfers between devices: 13 us -> 8.8 us  [all_sum(): lax.ppermute(value, axis, [(i, (i + k) % count) for i in range(count)])]
    ppermute x6 -> x8, starting transfers between devices: 3.77 us -> 6.6 us  [xor_perm(): return lax.ppermute(value, axis, [(i, i ^ bit) for i in range(count)])]
  transfers between devices with their start and end apart: 23 -> 22, of which waited for: 14 -> 14; matrix products, arithmetic and copies ran while one was open for 13% -> 13% of each run, Pallas kernels for 0% -> 0%
where the time goes in v20:
time: 167 us; the launch traced here: 166 us
  waiting for transfers between devices  69.9 us (42%)
  local copies, waits for them, and re-layouts  26.5 us (16%)
  starting transfers between devices  25.5 us (15%)
  other arithmetic  23.6 us (14%)
  matrix products  19.8 us (12%)
    ppermute x8, waiting for transfers between devices, xor_perm(): return lax.ppermute(value, axis, [(i, i ^ bit) for i in range(count)])  43.9 us
    ppermute x8, waiting for transfers between devices, all_gather_many(): others = lax.ppermute(arrs, axis, [(i, i ^ bit) for i in range(count)])  22.4 us
    ppermute x8, starting transfers between devices, all_gather_many(): others = lax.ppermute(arrs, axis, [(i, i ^ bit) for i in range(count)])  10.1 us
    ppermute x6, starting transfers between devices, all_sum(): lax.ppermute(value, axis, [(i, (i + k) % count) for i in range(count)])  8.8 us
    dot_general x1, matrix products, local(): jnp.einsum('scij,scie->scje', weights, q_e, preferred_element_type=jnp.fl...  6.94 us
    unnamed x29, local copies, waits for them, and re-layouts  6.62 us
    ppermute x8, starting transfers between devices, xor_perm(): return lax.ppermute(value, axis, [(i, i ^ bit) for i in range(count)])  6.6 us
    dot_general x1, matrix products, local(): jnp.einsum('scie,scje->scij', q_e, tiles, preferred_element_type=jnp.floa...  5.2 us
  transfers between devices with their start and end apart: 22, of which 14 were waited for; matrix products, arithmetic and copies ran while one was open for 13% of the time, Pallas kernels for 0%

profile of v20, /device:TPU:0, one launch (start us, length us, event | category | flops | bytes accessed | tf_op | source)
XLA Modules:
  0.0 166.4 jit_solution(15010554346463831425)
XLA Ops:
  0.7 3.8 %fusion.47 = (bf16[4,1,2048,256]{3,2,1,0:T(8,128)(2,1)S(1)}, bf16[4,1,2048,256]{3,2,1,0:T(8,128)(2,1)S(1)}) fusion(bf16[4,2,2048,256]{3,2,1,0:T(8,128)(2,1)} %bitcast.235), kind=kLoop, calls=%fused_computation.154 | loop fusion | bytes 16777216 | tf_op jit(solution)/shard_map/slice | solution.py:150
  6.0 1.7 %copy-done.3 = f32[2,2,2048,128]{3,2,1,0:T(8,128)} copy-done((f32[2,2,2048,128]{3,2,1,0:T(8,128)}, f32[2,2,2048,128]{3,2,1,0:T(8,128)S(1)}, u32[]{:S(2)}) %copy-start.3) | copy-done | bytes 4194328
  8.2 2.5 %collective-permute-start.1 = (bf16[1,8,32,128]{3,2,1,0:T(8,128)(2,1)S(1)}, bf16[1,8,32,128]{3,2,1,0:T(8,128)(2,1)S(1)}, u32[]{:S(2)}, u32[]{:S(2)}) collective-permute-start(bf16[1,8,32,128]{3,2,1,0:T(8,128)(2,1)S(1)} %bitcast.255), channel_id=1, source_target_pairs={{0,2},{1,3},{2,0},{3,1},{4,6},{5,7},{6,4},{7,5},{8,10},{9,11},{10,... | collective-permute-start | bytes 196616 | tf_op jit(solution)/shard_map/ppermute | solution.py:95
  12.0 1.8 %select_bitcast_fusion.2 = f32[2,2048,128]{2,1,0:T(8,128)} fusion(f32[2,2,2048,128]{3,2,0,1:T(8,128)S(1)} %fusion.2, pred[]{:T(512)S(6)} %eq.81), kind=kLoop, calls=%fused_computation.39 | loop fusion | flops 524288 | bytes 6291457 | tf_op jit(solution)/shard_map/jit(_where)/select_n | solution.py:62
  15.6 3.2 %collective-permute-done.4 = s32[2,8,16]{2,1,0:T(8,128)S(1)} collective-permute-done((s32[2,8,16]{2,1,0:T(8,128)S(1)}, s32[2,8,16]{2,1,0:T(8,128)S(1)}, u32[]{:S(2)}, u32[]{:S(2)}) %collective-permute-start.4) | collective-permute-done | bytes 1056 | tf_op jit(solution)/shard_map/ppermute | solution.py:95
  19.1 3.3 %fusion.9 = f32[1,2,2048,128]{3,2,1,0:T(8,128)S(1)} fusion(f32[2,2048,128]{2,1,0:T(8,128)} %collective-permute-done, f32[2,2,2048,128]{3,2,1,0:T(8,128)} %copy-done.3, pred[]{:T(512)S(6)} %eq.81), kind=kLoop, calls=%fused_computation.22 | loop fusion | flops 1048576 | bytes 8388609 | tf_op jit(solution)/shard_map/reshape | solution.py:59
  25.0 2.6 %collective-permute-start.5 = (s32[1,32,16]{2,1,0:T(8,128)S(1)}, s32[1,32,16]{2,1,0:T(8,128)S(1)}, u32[]{:S(2)}, u32[]{:S(2)}) collective-permute-start(s32[1,32,16]{2,1,0:T(8,128)S(1)} %bitcast.253), channel_id=1, source_target_pairs={{0,8},{4,12},{8,0},{12,4},{1,9},{5,13},{9,1},{13,5},{2,10},{6,14},... | collective-permute-start | bytes 6152 | tf_op jit(solution)/shard_map/ppermute | solution.py:95
  27.6 1.9 %fusion.13 = f32[1,2,2048,128]{3,2,1,0:T(8,128)S(1)} fusion(f32[2,2048,128]{2,1,0:T(8,128)} %collective-permute-done.10, f32[2,2,2048,128]{3,2,0,1:T(8,128)S(1)} %copy-done.5, pred[]{:T(512)S(6)} %eq.81), kind=kLoop, calls=%fused_computation.29 | loop fusion | flops 1048576 | bytes 8388609 | tf_op jit(solution)/shard_map/reshape | solution.py:59
  29.7 1.6 collective-permute-start.6
  33.0 2.6 %collective-permute-start.7 = (bf16[1,32,32,128]{3,2,1,0:T(8,128)(2,1)S(1)}, bf16[1,32,32,128]{3,2,1,0:T(8,128)(2,1)S(1)}, u32[]{:S(2)}, u32[]{:S(2)}) collective-permute-start(bf16[1,32,32,128]{3,2,1,0:T(8,128)(2,1)S(1)} %bitcast.249), channel_id=1, source_target_pairs={{0,8},{4,12},{8,0},{12,4},{1,9},{5,13},{9,1},{13,5},{2,10},{6,14},... | collective-permute-start | bytes 786440 | tf_op jit(solution)/shard_map/ppermute | solution.py:95
  36.5 1.9 %gather_fusion.3 = s32[256]{0:T(256)S(1)} fusion(s32[16,128]{1,0:T(8,128)S(1)} %reshape_reshape_reshape.2, s32[256]{0:T(256)S(1)} %reshape.665), kind=kCustom, calls=%fused_computation.3 | custom fusion | bytes 4096 | tf_op jit(solution)/shard_map/jit(take_along_axis)/gather | solution.py:177
  39.1 1.9 %gather_fusion = s32[256]{0:T(256)S(1)} fusion(s32[256]{0:T(256)S(1)} %copy-done.2, s32[1024]{0:T(1024)S(1)} %pad_clamp_fusion.2), kind=kCustom, calls=%fused_computation | custom fusion | bytes 3072 | tf_op jit(solution)/shard_map/gather | solution.py:15
  41.1 5.6 %collective-permute-done.7 = bf16[1,32,32,128]{3,2,1,0:T(8,128)(2,1)S(1)} collective-permute-done((bf16[1,32,32,128]{3,2,1,0:T(8,128)(2,1)S(1)}, bf16[1,32,32,128]{3,2,1,0:T(8,128)(2,1)S(1)}, u32[]{:S(2)}, u32[]{:S(2)}) %collective-permute-start.7) | collective-permute-done | bytes 262176 | tf_op jit(solution)/shard_map/ppermute | solution.py:95
  48.4 13.1 %collective-permute-done.8 = bf16[2,32,32,128]{3,2,1,0:T(8,128)(2,1)S(1)} collective-permute-done((bf16[2,32,32,128]{3,2,1,0:T(8,128)(2,1)}, bf16[2,32,32,128]{3,2,1,0:T(8,128)(2,1)S(1)}, u32[]{:S(2)}, u32[]{:S(2)}) %collective-permute-start.8) | collective-permute-done | bytes 524320 | tf_op jit(solution)/shard_map/ppermute | solution.py:95
  61.9 2.2 %gather_fusion.1 = bf16[256,32,128]{2,1,0:T(8,128)(2,1)} fusion(bf16[128,32,128]{2,1,0:T(8,128)(2,1)S(1)} %bitcast.245, s32[1024]{0:T(1024)S(1)} %pad_clamp_fusion.1), kind=kCustom, calls=%fused_computation.1 | custom fusion | bytes 4195328 | tf_op jit(solution)/shard_map/gather | solution.py:181
  65.6 5.9 %collective-permute-done.11 = f32[1,2048,128]{2,1,0:T(8,128)} collective-permute-done((f32[1,2048,128]{2,1,0:T(8,128)}, f32[1,2048,128]{2,1,0:T(8,128)}, u32[]{:S(2)}, u32[]{:S(2)}) %collective-permute-start.11) | collective-permute-done | bytes 1048608 | tf_op jit(solution)/shard_map/ppermute | solution.py:44
  74.4 3.0 %gather_fusion.2 = bf16[256,64,128]{2,1,0:T(8,128)(2,1)} fusion(bf16[64,64,128]{2,1,0:T(8,128)(2,1)S(1)} %multiply_convert_fusion.1, s32[1024]{0:T(1024)S(1)} %pad_clamp_fusion), kind=kCustom, calls=%fused_computation.2 | custom fusion | bytes 8389632 | tf_op jit(solution)/shard_map/gather | solution.py:188
  77.4 5.2 %select_reduce_fusion = (f32[16,16,32]{2,1,0:T(8,128)S(1)}, f32[16,16,32,64]{3,2,1,0:T(8,128)S(1)}) fusion(pred[16,16,64]{2,1,0:T(8,128)(4,1)S(1)} %add_compare_fusion, bf16[16,16,32,128]{3,2,1,0:T(8,128)(2,1)} %bitcast.247, bf16[16,16,64,128]{3,2,1,0:T(8,128)(2,1)} %bitcast.242), kind=kOutput, calls=%fused_computation.15 | convolution fusion | flops 135258112 | bytes 8437760 | tf_op jit(solution)/shard_map/scie,scje->scij/dot_general | solution.py:190
  82.6 2.6 %fusion.6 = f32[16,16,32]{2,1,0:T(8,128)S(1)} fusion(f32[16,16,32,64]{3,2,1,0:T(8,128)S(1)} %get-tuple-element.59, f32[16,16,32]{2,1,0:T(8,128)S(1)} %get-tuple-element.58, pred[16,16,64]{2,1,0:T(8,128)(4,1)S(1)} %add_compare_fusion), kind=kLoop, calls=%fused_computation.16 | loop fusion | flops 1564672 | bytes 2179072 | tf_op jit(solution)/shard_map/reduce_sum | solution.py:22
  85.6 1.8 %collective-permute-start.13 = (f32[16,128]{1,0:T(8,128)S(1)}, f32[16,128]{1,0:T(8,128)S(1)}, u32[]{:S(2)}, u32[]{:S(2)}) collective-permute-start(f32[16,128]{1,0:T(8,128)S(1)} %select_reduce_fusion.1), channel_id=1, source_target_pairs={{0,2},{1,3},{2,0},{3,1},{4,6},{5,7},{6,4},{7,5},{8,10},{9,11},{10,... | collective-permute-start | bytes 24584 | tf_op jit(solution)/shard_map/ppermute | solution.py:118
  91.8 2.6 %collective-permute-start.16 = (f32[16,128]{1,0:T(8,128)S(1)}, f32[16,128]{1,0:T(8,128)S(1)}, u32[]{:S(2)}, u32[]{:S(2)}) collective-permute-start(f32[16,128]{1,0:T(8,128)S(1)} %fusion.53), channel_id=1, source_target_pairs={{0,8},{4,12},{8,0},{12,4},{1,9},{5,13},{9,1},{13,5},{2,10},{6,14},... | collective-permute-start | bytes 24584 | tf_op jit(solution)/shard_map/ppermute | solution.py:118
  96.3 1.7 %collective-permute-done.17 = f32[16,128]{1,0:T(8,128)S(1)} collective-permute-done((f32[16,128]{1,0:T(8,128)S(1)}, f32[16,128]{1,0:T(8,128)S(1)}, u32[]{:S(2)}, u32[]{:S(2)}) %collective-permute-start.17) | collective-permute-done | bytes 8224 | tf_op jit(solution)/shard_map/ppermute | solution.py:118
  98.6 1.9 %gather_fusion.4 = f32[256]{0:T(256)S(1)} fusion(f32[16,128]{1,0:T(8,128)S(1)} %reshape.637, s32[256]{0:T(256)S(1)} %reshape.665), kind=kCustom, calls=%fused_computation.4 | custom fusion | bytes 4096 | tf_op jit(solution)/shard_map/jit(take_along_axis)/gather | solution.py:200
  100.6 6.9 %multiply_convert_fusion = bf16[16,16,64,128]{3,2,1,0:T(8,128)(2,1)S(1)} fusion(f32[16,16]{1,0:T(8,128)S(1)} %select_multiply_fusion, bf16[16,16,32,128]{3,2,1,0:T(8,128)(2,1)} %bitcast.248, f32[16,16,32,64]{3,2,1,0:T(8,128)} %copy-done.8, f32[16,16,32]{2,1,0:T(8,128)S(1)} %fusion.6, f32[16,16,32]{2,1,0:T(8,128)S(1)} %get-tuple-element.58, ...), kind=kOutput, calls=%fused_computation.5 | convolution fusion | flops 140509184 | bytes 8471552 | tf_op jit(solution)/shard_map/scij,scie->scje/dot_general | solution.py:193
  107.6 3.7 %fusion.14 = (f32[64,64]{0,1:T(8,128)S(1)}, f32[64,64,128]{2,0,1:T(8,128)S(1)}) fusion(f32[64,64,128]{2,1,0:T(8,128)S(1)} %bitcast.239, bf16[16,16,64,128]{3,2,1,0:T(8,128)(2,1)S(1)} %multiply_convert_fusion, s32[16,16]{0,1:T(8,128)S(1)} %copy.137, pred[16,16]{0,1:T(8,128)(4,1)S(1)} %copy.138), kind=kOutput, calls=%fused_computation.31 | convolution fusion | flops 269512704 | bytes 8406272 | tf_op jit(solution)/shard_map/scb,scje->bje/dot_general | solution.py:204
  111.3 2.6 %copy.141 = f32[64,64,128]{2,1,0:T(8,128)} copy(f32[64,64,128]{2,0,1:T(8,128)S(1)} %get-tuple-element.61) | data formatting | bytes 4194304 | tf_op jit(solution)/shard_map/scb,scje->bje/dot_general | solution.py:204
  114.0 3.6 %fusion.12 = bf16[1,4096,128]{2,1,0:T(8,128)(2,1)S(1)} fusion(f32[4096]{0:T(1024)S(1)} %mul.134, f32[4096]{0:T(1024)S(1)} %multiply_multiply_fusion, f32[4096]{0:T(1024)S(1)} %bitcast.252, f32[1,4096,128]{2,1,0:T(8,128)S(1)} %bitcast.240, f32[1,4096,128]{2,1,0:T(8,128)} %bitcast.246), kind=kLoop, calls=%fused_computation.26 | loop fusion | flops 2621440 | bytes 5292032 | tf_op jit(solution)/shard_map/convert_element_type | solution.py:212
  118.5 23.1 %collective-permute-done.18 = bf16[1,4096,128]{2,1,0:T(8,128)(2,1)S(1)} collective-permute-done((bf16[1,4096,128]{2,1,0:T(8,128)(2,1)S(1)}, bf16[1,4096,128]{2,1,0:T(8,128)(2,1)S(1)}, u32[]{:S(2)}, u32[]{:S(2)}) %collective-permute-start.18) | collective-permute-done | bytes 1048608 | tf_op jit(solution)/shard_map/ppermute | solution.py:44
  142.0 4.1 %collective-permute-done.19 = bf16[2,4096,128]{2,1,0:T(8,128)(2,1)S(1)} collective-permute-done((bf16[2,4096,128]{2,1,0:T(8,128)(2,1)S(1)}, bf16[2,4096,128]{2,1,0:T(8,128)(2,1)S(1)}, u32[]{:S(2)}, u32[]{:S(2)}) %collective-permute-start.19) | collective-permute-done | bytes 2097184 | tf_op jit(solution)/shard_map/ppermute | solution.py:44
  152.3 4.9 %collective-permute-done.20 = f32[256,128]{0,1:T(8,128)S(1)} collective-permute-done((f32[256,128]{0,1:T(8,128)S(1)}, f32[256,128]{0,1:T(8,128)S(1)}, u32[]{:S(2)}, u32[]{:S(2)}) %collective-permute-start.20) | collective-permute-done | bytes 131104 | tf_op jit(solution)/shard_map/ppermute | solution.py:44
  157.2 2.0 %collective-permute-start.21 = (f32[256,128]{0,1:T(8,128)S(1)}, f32[256,128]{0,1:T(8,128)S(1)}, u32[]{:S(2)}, u32[]{:S(2)}) collective-permute-start(f32[256,128]{0,1:T(8,128)S(1)} %add.387), channel_id=1, source_target_pairs={{0,8},{4,12},{8,0},{12,4},{1,9},{5,13},{9,1},{13,5},{2,10},{6,14},... | collective-permute-start | bytes 393224 | tf_op jit(solution)/shard_map/ppermute | solution.py:44
  159.8 5.9 %collective-permute-done.21 = f32[256,128]{0,1:T(8,128)S(1)} collective-permute-done((f32[256,128]{0,1:T(8,128)S(1)}, f32[256,128]{0,1:T(8,128)S(1)}, u32[]{:S(2)}, u32[]{:S(2)}) %collective-permute-start.21) | collective-permute-done | bytes 131104 | tf_op jit(solution)/shard_map/ppermute | solution.py:44
  (142 shorter events, 33.9 us)
Async XLA Ops:
  0.6 3.8 %copy-start = (bf16[256,128]{1,0:T(8,128)(2,1)S(1)}, bf16[256,128]{1,0:T(8,128)(2,1)}, u32[]{:S(2)}) copy-start(bf16[256,128]{1,0:T(8,128)(2,1)} %param.6) | copy-start | bytes 196612
  5.7 2.4 %copy-start.9 = (bf16[8,32,128]{2,1,0:T(8,128)(2,1)S(1)}, bf16[8,32,128]{2,1,0:T(8,128)(2,1)}, u32[]{:S(2)}) copy-start(bf16[8,32,128]{2,1,0:T(8,128)(2,1)} %param.7) | copy-start | bytes 196612
  5.7 4.9 %copy-start.10 = (s32[8,16]{1,0:T(8,128)S(1)}, s32[8,16]{1,0:T(8,128)}, u32[]{:S(2)}) copy-start(s32[8,16]{1,0:T(8,128)} %param.9) | copy-start | bytes 1540
  7.7 11.4 %collective-permute-start = (f32[2,2048,128]{2,1,0:T(8,128)S(1)}, f32[2,2048,128]{2,1,0:T(8,128)}, u32[]{:S(2)}, u32[]{:S(2)}) collective-permute-start(f32[2,2048,128]{2,1,0:T(8,128)S(1)} %select_bitcast_fusion.3), channel_id=1, source_target_pairs={{0,1},{1,0},{2,3},{3,2},{4,5},{5,4},{6,7},{7,6},{8,9},{9,8},{10,11... | collective-permute-start | bytes 6291464 | tf_op jit(solution)/shard_map/ppermute | solution.py:44
  8.2 7.1 %collective-permute-start.1 = (bf16[1,8,32,128]{3,2,1,0:T(8,128)(2,1)S(1)}, bf16[1,8,32,128]{3,2,1,0:T(8,128)(2,1)S(1)}, u32[]{:S(2)}, u32[]{:S(2)}) collective-permute-start(bf16[1,8,32,128]{3,2,1,0:T(8,128)(2,1)S(1)} %bitcast.255), channel_id=1, source_target_pairs={{0,2},{1,3},{2,0},{3,1},{4,6},{5,7},{6,4},{7,5},{8,10},{9,11},{10,... | collective-permute-start | bytes 196616 | tf_op jit(solution)/shard_map/ppermute | solution.py:95
  10.6 4.2 %collective-permute-start.3 = (s32[1,8,16]{2,1,0:T(8,128)S(1)}, s32[1,8,16]{2,1,0:T(8,128)S(1)}, u32[]{:S(2)}, u32[]{:S(2)}) collective-permute-start(s32[1,8,16]{2,1,0:T(8,128)S(1)} %bitcast.263), channel_id=1, source_target_pairs={{0,2},{1,3},{2,0},{3,1},{4,6},{5,7},{6,4},{7,5},{8,10},{9,11},{10,... | collective-permute-start | bytes 1544 | tf_op jit(solution)/shard_map/ppermute | solution.py:95
  12.0 2.7 %copy-start.4 = (f32[2,2,2048,128]{3,2,0,1:T(8,128)}, f32[2,2,2048,128]{3,2,0,1:T(8,128)S(1)}, u32[]{:S(2)}) copy-start(f32[2,2,2048,128]{3,2,0,1:T(8,128)S(1)} %fusion.2) | copy-start | bytes 12582916
  14.6 13.0 %collective-permute-start.10 = (f32[2,2048,128]{2,1,0:T(8,128)}, f32[2,2048,128]{2,1,0:T(8,128)}, u32[]{:S(2)}, u32[]{:S(2)}) collective-permute-start(f32[2,2048,128]{2,1,0:T(8,128)} %select_bitcast_fusion.2), channel_id=1, source_target_pairs={{0,1},{1,0},{2,3},{3,2},{4,5},{5,4},{6,7},{7,6},{8,9},{9,8},{10,11... | collective-permute-start | bytes 6291464 | tf_op jit(solution)/shard_map/ppermute | solution.py:44
  14.9 3.9 %collective-permute-start.4 = (s32[2,8,16]{2,1,0:T(8,128)S(1)}, s32[2,8,16]{2,1,0:T(8,128)S(1)}, u32[]{:S(2)}, u32[]{:S(2)}) collective-permute-start(s32[2,8,16]{2,1,0:T(8,128)S(1)} %add_bitcast_fusion.1), channel_id=1, source_target_pairs={{0,1},{1,0},{2,3},{3,2},{4,5},{5,4},{6,7},{7,6},{8,9},{9,8},{10,11... | collective-permute-start | bytes 3080 | tf_op jit(solution)/shard_map/ppermute | solution.py:95
  15.3 3.7 %collective-permute-start.2 = (bf16[2,8,32,128]{3,2,1,0:T(8,128)(2,1)S(1)}, bf16[2,8,32,128]{3,2,1,0:T(8,128)(2,1)S(1)}, u32[]{:S(2)}, u32[]{:S(2)}) collective-permute-start(bf16[2,8,32,128]{3,2,1,0:T(8,128)(2,1)S(1)} %maximum_bitcast_fusion.2), channel_id=1, source_target_pairs={{0,1},{1,0},{2,3},{3,2},{4,5},{5,4},{6,7},{7,6},{8,9},{9,8},{10,11... | collective-permute-start | bytes 393224 | tf_op jit(solution)/shard_map/ppermute | solution.py:95
  19.1 8.6 %copy-start.5 = (f32[2,2,2048,128]{3,2,0,1:T(8,128)S(1)}, f32[2,2,2048,128]{3,2,0,1:T(8,128)}, u32[]{:S(2)}) copy-start(f32[2,2,2048,128]{3,2,0,1:T(8,128)} %copy-done.4) | copy-start | bytes 12582916
  23.4 40.6 %collective-permute-start.9 = (f32[1,2048,128]{2,1,0:T(8,128)}, f32[1,2048,128]{2,1,0:T(8,128)}, u32[]{:S(2)}, u32[]{:S(2)}) collective-permute-start(f32[1,2048,128]{2,1,0:T(8,128)} %select_bitcast_fusion.7), channel_id=1, source_target_pairs={{0,2},{1,3},{2,0},{3,1},{4,6},{5,7},{6,4},{7,5},{8,10},{9,11},{10,... | collective-permute-start | bytes 3145736 | tf_op jit(solution)/shard_map/ppermute | solution.py:44
  25.0 4.6 %collective-permute-start.5 = (s32[1,32,16]{2,1,0:T(8,128)S(1)}, s32[1,32,16]{2,1,0:T(8,128)S(1)}, u32[]{:S(2)}, u32[]{:S(2)}) collective-permute-start(s32[1,32,16]{2,1,0:T(8,128)S(1)} %bitcast.253), channel_id=1, source_target_pairs={{0,8},{4,12},{8,0},{12,4},{1,9},{5,13},{9,1},{13,5},{2,10},{6,14},... | collective-permute-start | bytes 6152 | tf_op jit(solution)/shard_map/ppermute | solution.py:95
  29.5 6.1 %copy-start.6 = (f32[1,2,2048,128]{3,2,1,0:T(8,128)}, f32[1,2,2048,128]{3,2,1,0:T(8,128)S(1)}, u32[]{:S(2)}) copy-start(f32[1,2,2048,128]{3,2,1,0:T(8,128)S(1)} %fusion.13) | copy-start | bytes 6291460
  29.7 5.9 %collective-permute-start.6 = (s32[2,32,16]{2,1,0:T(8,128)S(1)}, s32[2,32,16]{2,1,0:T(8,128)S(1)}, u32[]{:S(2)}, u32[]{:S(2)}) collective-permute-start(s32[2,32,16]{2,1,0:T(8,128)S(1)} %add_bitcast_fusion), channel_id=1, source_target_pairs={{0,4},{4,0},{8,12},{12,8},{1,5},{5,1},{9,13},{13,9},{2,6},{6,2},{1... | collective-permute-start | bytes 12296 | tf_op jit(solution)/shard_map/ppermute | solution.py:95
  32.4 39.1 %collective-permute-start.11 = (f32[1,2048,128]{2,1,0:T(8,128)}, f32[1,2048,128]{2,1,0:T(8,128)}, u32[]{:S(2)}, u32[]{:S(2)}) collective-permute-start(f32[1,2048,128]{2,1,0:T(8,128)} %select_bitcast_fusion.6), channel_id=1, source_target_pairs={{0,2},{1,3},{2,0},{3,1},{4,6},{5,7},{6,4},{7,5},{8,10},{9,11},{10,... | collective-permute-start | bytes 3145736 | tf_op jit(solution)/shard_map/ppermute | solution.py:44
  33.0 13.8 %collective-permute-start.7 = (bf16[1,32,32,128]{3,2,1,0:T(8,128)(2,1)S(1)}, bf16[1,32,32,128]{3,2,1,0:T(8,128)(2,1)S(1)}, u32[]{:S(2)}, u32[]{:S(2)}) collective-permute-start(bf16[1,32,32,128]{3,2,1,0:T(8,128)(2,1)S(1)} %bitcast.249), channel_id=1, source_target_pairs={{0,8},{4,12},{8,0},{12,4},{1,9},{5,13},{9,1},{13,5},{2,10},{6,14},... | collective-permute-start | bytes 786440 | tf_op jit(solution)/shard_map/ppermute | solution.py:95
  47.7 13.9 %collective-permute-start.8 = (bf16[2,32,32,128]{3,2,1,0:T(8,128)(2,1)}, bf16[2,32,32,128]{3,2,1,0:T(8,128)(2,1)S(1)}, u32[]{:S(2)}, u32[]{:S(2)}) collective-permute-start(bf16[2,32,32,128]{3,2,1,0:T(8,128)(2,1)} %maximum_bitcast_fusion.1), channel_id=1, source_target_pairs={{0,4},{4,0},{8,12},{12,8},{1,5},{5,1},{9,13},{13,9},{2,6},{6,2},{1... | collective-permute-start | bytes 1572872 | tf_op jit(solution)/shard_map/ppermute | solution.py:95
  64.1 7.5 %copy-start.7 = (f32[1,2,2048,128]{3,2,1,0:T(8,128)S(1)}, f32[1,2,2048,128]{3,2,1,0:T(8,128)}, u32[]{:S(2)}) copy-start(f32[1,2,2048,128]{3,2,1,0:T(8,128)} %copy-done.6) | copy-start | bytes 6291460
  82.6 2.6 %copy-start.8 = (f32[16,16,32,64]{3,2,1,0:T(8,128)}, f32[16,16,32,64]{3,2,1,0:T(8,128)S(1)}, u32[]{:S(2)}) copy-start(f32[16,16,32,64]{3,2,1,0:T(8,128)S(1)} %get-tuple-element.59) | copy-start | bytes 6291460
  85.5 3.3 %collective-permute-start.12 = (f32[16,128]{1,0:T(8,128)S(1)}, f32[16,128]{1,0:T(8,128)S(1)}, u32[]{:S(2)}, u32[]{:S(2)}) collective-permute-start(f32[16,128]{1,0:T(8,128)S(1)} %select_reduce_fusion.1), channel_id=1, source_target_pairs={{0,1},{1,2},{2,3},{3,0},{4,5},{5,6},{6,7},{7,4},{8,9},{9,10},{10,1... | collective-permute-start | bytes 24584 | tf_op jit(solution)/shard_map/ppermute | solution.py:118
  85.6 3.7 %collective-permute-start.13 = (f32[16,128]{1,0:T(8,128)S(1)}, f32[16,128]{1,0:T(8,128)S(1)}, u32[]{:S(2)}, u32[]{:S(2)}) collective-permute-start(f32[16,128]{1,0:T(8,128)S(1)} %select_reduce_fusion.1), channel_id=1, source_target_pairs={{0,2},{1,3},{2,0},{3,1},{4,6},{5,7},{6,4},{7,5},{8,10},{9,11},{10,... | collective-permute-start | bytes 24584 | tf_op jit(solution)/shard_map/ppermute | solution.py:118
  87.4 2.8 %collective-permute-start.14 = (f32[16,128]{1,0:T(8,128)S(1)}, f32[16,128]{1,0:T(8,128)S(1)}, u32[]{:S(2)}, u32[]{:S(2)}) collective-permute-start(f32[16,128]{1,0:T(8,128)S(1)} %select_reduce_fusion.1), channel_id=1, source_target_pairs={{0,3},{1,0},{2,1},{3,2},{4,7},{5,4},{6,5},{7,6},{8,11},{9,8},{10,9... | collective-permute-start | bytes 24584 | tf_op jit(solution)/shard_map/ppermute | solution.py:118
  90.1 5.6 %collective-permute-start.15 = (f32[16,128]{1,0:T(8,128)S(1)}, f32[16,128]{1,0:T(8,128)S(1)}, u32[]{:S(2)}, u32[]{:S(2)}) collective-permute-start(f32[16,128]{1,0:T(8,128)S(1)} %fusion.53), channel_id=1, source_target_pairs={{0,4},{4,8},{8,12},{12,0},{1,5},{5,9},{9,13},{13,1},{2,6},{6,10},{... | collective-permute-start | bytes 24584 | tf_op jit(solution)/shard_map/ppermute | solution.py:118
  91.8 4.5 %collective-permute-start.16 = (f32[16,128]{1,0:T(8,128)S(1)}, f32[16,128]{1,0:T(8,128)S(1)}, u32[]{:S(2)}, u32[]{:S(2)}) collective-permute-start(f32[16,128]{1,0:T(8,128)S(1)} %fusion.53), channel_id=1, source_target_pairs={{0,8},{4,12},{8,0},{12,4},{1,9},{5,13},{9,1},{13,5},{2,10},{6,14},... | collective-permute-start | bytes 24584 | tf_op jit(solution)/shard_map/ppermute | solution.py:118
  94.3 3.7 %collective-permute-start.17 = (f32[16,128]{1,0:T(8,128)S(1)}, f32[16,128]{1,0:T(8,128)S(1)}, u32[]{:S(2)}, u32[]{:S(2)}) collective-permute-start(f32[16,128]{1,0:T(8,128)S(1)} %fusion.53), channel_id=1, source_target_pairs={{0,12},{4,0},{8,4},{12,8},{1,13},{5,1},{9,5},{13,9},{2,14},{6,2},{... | collective-permute-start | bytes 24584 | tf_op jit(solution)/shard_map/ppermute | solution.py:118
  117.6 24.0 %collective-permute-start.18 = (bf16[1,4096,128]{2,1,0:T(8,128)(2,1)S(1)}, bf16[1,4096,128]{2,1,0:T(8,128)(2,1)S(1)}, u32[]{:S(2)}, u32[]{:S(2)}) collective-permute-start(bf16[1,4096,128]{2,1,0:T(8,128)(2,1)S(1)} %fusion.12), channel_id=1, source_target_pairs={{0,2},{1,3},{2,0},{3,1},{4,6},{5,7},{6,4},{7,5},{8,10},{9,11},{10,... | collective-permute-start | bytes 3145736 | tf_op jit(solution)/shard_map/ppermute | solution.py:44
  141.9 4.2 %collective-permute-start.19 = (bf16[2,4096,128]{2,1,0:T(8,128)(2,1)S(1)}, bf16[2,4096,128]{2,1,0:T(8,128)(2,1)S(1)}, u32[]{:S(2)}, u32[]{:S(2)}) collective-permute-start(bf16[2,4096,128]{2,1,0:T(8,128)(2,1)S(1)} %maximum_bitcast_fusion), channel_id=1, source_target_pairs={{0,1},{1,0},{2,3},{3,2},{4,5},{5,4},{6,7},{7,6},{8,9},{9,8},{10,11... | collective-permute-start | bytes 6291464 | tf_op jit(solution)/shard_map/ppermute | solution.py:44
  146.9 3.2 %slice-start.1 = ((s8[8388608]{0:T(1024)(128)(4,1)}), s8[4194304]{0:T(1024)(128)(4,1)S(1)}, s32[]{:S(2)}) async-start(s8[8388608]{0:T(1024)(128)(4,1)} %bitcast.236), calls=%async_computation.1 | async-start | bytes 8388608
  150.0 16.4 %copy-start.1 = (bf16[256,128]{1,0:T(8,128)(2,1)S(1)}, bf16[256,128]{1,0:T(8,128)(2,1)}, u32[]{:S(2)}) copy-start(bf16[256,128]{1,0:T(8,128)(2,1)} %param.6) | copy-start | bytes 196612
  151.6 5.6 %collective-permute-start.20 = (f32[256,128]{0,1:T(8,128)S(1)}, f32[256,128]{0,1:T(8,128)S(1)}, u32[]{:S(2)}, u32[]{:S(2)}) collective-permute-start(f32[256,128]{0,1:T(8,128)S(1)} %convolution_bitcast_fusion), channel_id=1, source_target_pairs={{0,4},{4,0},{8,12},{12,8},{1,5},{5,1},{9,13},{13,9},{2,6},{6,2},{1... | collective-permute-start | bytes 393224 | tf_op jit(solution)/shard_map/ppermute | solution.py:44
  157.2 8.5 %collective-permute-start.21 = (f32[256,128]{0,1:T(8,128)S(1)}, f32[256,128]{0,1:T(8,128)S(1)}, u32[]{:S(2)}, u32[]{:S(2)}) collective-permute-start(f32[256,128]{0,1:T(8,128)S(1)} %add.387), channel_id=1, source_target_pairs={{0,8},{4,12},{8,0},{12,4},{1,9},{5,13},{9,1},{13,5},{2,10},{6,14},... | collective-permute-start | bytes 393224 | tf_op jit(solution)/shard_map/ppermute | solution.py:44
  (3 other events, 4.9 us)

commit v21 on v20

--- a/solution.py
+++ b/solution.py
@@ -193,7 +193,7 @@
     occ_raw = jnp.einsum("scij,scie->scje", weights, q_e, preferred_element_type=jnp.float32)
 
     placed = jnp.sum(jnp.where(pick, scores[:, :, None], jnp.float32(0)), axis=1)
-    all_scores = all_sum(all_sum(placed, "mp"), "enc").reshape(owners * qry_dev, cand_count)
+    all_scores = all_sum(all_sum(placed, "mp", one_step=False), "enc", one_step=False).reshape(owners * qry_dev, cand_count)
     all_losses, d_score = loss_terms(all_scores)
     losses = lax.dynamic_slice_in_dim(all_losses, me * qry_dev, qry_dev)
 

time: 167 us -> 166 us (level)
    ppermute x8 -> x12, starting transfers between devices: 6.6 us -> 15.5 us  [xor_perm(): return lax.ppermute(value, axis, [(i, i ^ bit) for i in range(count)])]
    ppermute x6 -> x0, starting transfers between devices: 8.8 us -> none  [all_sum(): lax.ppermute(value, axis, [(i, (i + k) % count) for i in range(count)])]
    ppermute x6 -> x0, waiting for transfers between devices: 3.64 us -> none  [all_sum(): lax.ppermute(value, axis, [(i, (i + k) % count) for i in range(count)])]
    ppermute x8 -> x12, waiting for transfers between devices: 43.9 us -> 45.5 us  [xor_perm(): return lax.ppermute(value, axis, [(i, i ^ bit) for i in range(count)])]
  transfers between devices with their start and end apart: 22 -> 20, of which waited for: 14 -> 14; matrix products, arithmetic and copies ran while one was open for 13% -> 13% of each run, Pallas kernels for 0% -> 0%
where the time goes in v21:
time: 166 us; the launch traced here: 165 us
  waiting for transfers between devices  68.6 us (41%)
  local copies, waits for them, and re-layouts  26.3 us (16%)
  starting transfers between devices  25.6 us (15%)
  other arithmetic  23.8 us (14%)
  matrix products  19.8 us (12%)
    ppermute x12, waiting for transfers between devices, xor_perm(): return lax.ppermute(value, axis, [(i, i ^ bit) for i in range(count)])  45.5 us
    ppermute x8, waiting for transfers between devices, all_gather_many(): others = lax.ppermute(arrs, axis, [(i, i ^ bit) for i in range(count)])  23.1 us
    ppermute x12, starting transfers between devices, xor_perm(): return lax.ppermute(value, axis, [(i, i ^ bit) for i in range(count)])  15.5 us
    ppermute x8, starting transfers between devices, all_gather_many(): others = lax.ppermute(arrs, axis, [(i, i ^ bit) for i in range(count)])  10.1 us
    dot_general x1, matrix products, local(): jnp.einsum('scij,scie->scje', weights, q_e, preferred_element_type=jnp.fl...  6.95 us
    unnamed x29, local copies, waits for them, and re-layouts  6.43 us
    dot_general x1, matrix products, local(): jnp.einsum('scie,scje->scij', q_e, tiles, preferred_element_type=jnp.floa...  5.2 us
    reshape x2, other arithmetic, halving_steps(): acc = acc.reshape((acc.shape[0] // 2, 2) + acc.shape[1:])  5.15 us
  transfers between devices with their start and end apart: 20, of which 14 were waited for; matrix products, arithmetic and copies ran while one was open for 13% of the time, Pallas kernels for 0%

profile of v21, /device:TPU:0, one launch (start us, length us, event | category | flops | bytes accessed | tf_op | source)
XLA Modules:
  0.0 165.3 jit_solution(17127226180943793034)
XLA Ops:
  0.7 3.8 %fusion.47 = (bf16[4,1,2048,256]{3,2,1,0:T(8,128)(2,1)S(1)}, bf16[4,1,2048,256]{3,2,1,0:T(8,128)(2,1)S(1)}) fusion(bf16[4,2,2048,256]{3,2,1,0:T(8,128)(2,1)} %bitcast.226), kind=kLoop, calls=%fused_computation.150 | loop fusion | bytes 16777216 | tf_op jit(solution)/shard_map/slice | solution.py:150
  6.0 1.7 %copy-done.3 = f32[2,2,2048,128]{3,2,1,0:T(8,128)} copy-done((f32[2,2,2048,128]{3,2,1,0:T(8,128)}, f32[2,2,2048,128]{3,2,1,0:T(8,128)S(1)}, u32[]{:S(2)}) %copy-start.3) | copy-done | bytes 4194328
  8.2 2.5 %collective-permute-start.1 = (bf16[1,8,32,128]{3,2,1,0:T(8,128)(2,1)S(1)}, bf16[1,8,32,128]{3,2,1,0:T(8,128)(2,1)S(1)}, u32[]{:S(2)}, u32[]{:S(2)}) collective-permute-start(bf16[1,8,32,128]{3,2,1,0:T(8,128)(2,1)S(1)} %bitcast.246), channel_id=1, source_target_pairs={{0,2},{1,3},{2,0},{3,1},{4,6},{5,7},{6,4},{7,5},{8,10},{9,11},{10,... | collective-permute-start | bytes 196616 | tf_op jit(solution)/shard_map/ppermute | solution.py:95
  15.6 3.2 %collective-permute-done.4 = s32[2,8,16]{2,1,0:T(8,128)S(1)} collective-permute-done((s32[2,8,16]{2,1,0:T(8,128)S(1)}, s32[2,8,16]{2,1,0:T(8,128)S(1)}, u32[]{:S(2)}, u32[]{:S(2)}) %collective-permute-start.4) | collective-permute-done | bytes 1056 | tf_op jit(solution)/shard_map/ppermute | solution.py:95
  19.1 3.3 %fusion.9 = f32[1,2,2048,128]{3,2,1,0:T(8,128)S(1)} fusion(f32[2,2048,128]{2,1,0:T(8,128)} %collective-permute-done, f32[2,2,2048,128]{3,2,1,0:T(8,128)} %copy-done.3, pred[]{:T(512)S(6)} %eq.73), kind=kLoop, calls=%fused_computation.22 | loop fusion | flops 1048576 | bytes 8388609 | tf_op jit(solution)/shard_map/reshape | solution.py:59
  25.1 2.6 %collective-permute-start.5 = (s32[1,32,16]{2,1,0:T(8,128)S(1)}, s32[1,32,16]{2,1,0:T(8,128)S(1)}, u32[]{:S(2)}, u32[]{:S(2)}) collective-permute-start(s32[1,32,16]{2,1,0:T(8,128)S(1)} %bitcast.244), channel_id=1, source_target_pairs={{0,8},{4,12},{8,0},{12,4},{1,9},{5,13},{9,1},{13,5},{2,10},{6,14},... | collective-permute-start | bytes 6152 | tf_op jit(solution)/shard_map/ppermute | solution.py:95
  27.6 1.9 %fusion.13 = f32[1,2,2048,128]{3,2,1,0:T(8,128)S(1)} fusion(f32[2,2048,128]{2,1,0:T(8,128)} %collective-permute-done.10, f32[2,2,2048,128]{3,2,0,1:T(8,128)S(1)} %copy-done.5, pred[]{:T(512)S(6)} %eq.73), kind=kLoop, calls=%fused_computation.29 | loop fusion | flops 1048576 | bytes 8388609 | tf_op jit(solution)/shard_map/reshape | solution.py:59
  33.0 2.7 %collective-permute-start.7 = (bf16[1,32,32,128]{3,2,1,0:T(8,128)(2,1)S(1)}, bf16[1,32,32,128]{3,2,1,0:T(8,128)(2,1)S(1)}, u32[]{:S(2)}, u32[]{:S(2)}) collective-permute-start(bf16[1,32,32,128]{3,2,1,0:T(8,128)(2,1)S(1)} %bitcast.240), channel_id=1, source_target_pairs={{0,8},{4,12},{8,0},{12,4},{1,9},{5,13},{9,1},{13,5},{2,10},{6,14},... | collective-permute-start | bytes 786440 | tf_op jit(solution)/shard_map/ppermute | solution.py:95
  36.5 1.9 %gather_fusion.3 = s32[256]{0:T(256)S(1)} fusion(s32[16,128]{1,0:T(8,128)S(1)} %reshape_reshape_reshape.2, s32[256]{0:T(256)S(1)} %reshape.658), kind=kCustom, calls=%fused_computation.3 | custom fusion | bytes 4096 | tf_op jit(solution)/shard_map/jit(take_along_axis)/gather | solution.py:177
  38.9 7.9 %collective-permute-done.7 = bf16[1,32,32,128]{3,2,1,0:T(8,128)(2,1)S(1)} collective-permute-done((bf16[1,32,32,128]{3,2,1,0:T(8,128)(2,1)S(1)}, bf16[1,32,32,128]{3,2,1,0:T(8,128)(2,1)S(1)}, u32[]{:S(2)}, u32[]{:S(2)}) %collective-permute-start.7) | collective-permute-done | bytes 262176 | tf_op jit(solution)/shard_map/ppermute | solution.py:95
  47.7 1.9 %gather_fusion = s32[256]{0:T(256)S(1)} fusion(s32[256]{0:T(256)S(1)} %copy-done.2, s32[1024]{0:T(1024)S(1)} %pad_clamp_fusion.2), kind=kCustom, calls=%fused_computation | custom fusion | bytes 3072 | tf_op jit(solution)/shard_map/gather | solution.py:15
  50.0 11.6 %collective-permute-done.8 = bf16[2,32,32,128]{3,2,1,0:T(8,128)(2,1)S(1)} collective-permute-done((bf16[2,32,32,128]{3,2,1,0:T(8,128)(2,1)}, bf16[2,32,32,128]{3,2,1,0:T(8,128)(2,1)S(1)}, u32[]{:S(2)}, u32[]{:S(2)}) %collective-permute-start.8) | collective-permute-done | bytes 524320 | tf_op jit(solution)/shard_map/ppermute | solution.py:95
  61.9 2.2 %gather_fusion.1 = bf16[256,32,128]{2,1,0:T(8,128)(2,1)} fusion(bf16[128,32,128]{2,1,0:T(8,128)(2,1)S(1)} %bitcast.236, s32[1024]{0:T(1024)S(1)} %pad_clamp_fusion.1), kind=kCustom, calls=%fused_computation.1 | custom fusion | bytes 4195328 | tf_op jit(solution)/shard_map/gather | solution.py:181
  65.7 5.9 %collective-permute-done.11 = f32[1,2048,128]{2,1,0:T(8,128)} collective-permute-done((f32[1,2048,128]{2,1,0:T(8,128)}, f32[1,2048,128]{2,1,0:T(8,128)}, u32[]{:S(2)}, u32[]{:S(2)}) %collective-permute-start.11) | collective-permute-done | bytes 1048608 | tf_op jit(solution)/shard_map/ppermute | solution.py:44
  74.4 3.1 %gather_fusion.2 = bf16[256,64,128]{2,1,0:T(8,128)(2,1)} fusion(bf16[64,64,128]{2,1,0:T(8,128)(2,1)S(1)} %multiply_convert_fusion.1, s32[1024]{0:T(1024)S(1)} %pad_clamp_fusion), kind=kCustom, calls=%fused_computation.2 | custom fusion | bytes 8389632 | tf_op jit(solution)/shard_map/gather | solution.py:188
  77.4 5.2 %select_reduce_fusion = (f32[16,16,32]{2,1,0:T(8,128)S(1)}, f32[16,16,32,64]{3,2,1,0:T(8,128)S(1)}) fusion(pred[16,16,64]{2,1,0:T(8,128)(4,1)S(1)} %add_compare_fusion, bf16[16,16,32,128]{3,2,1,0:T(8,128)(2,1)} %bitcast.238, bf16[16,16,64,128]{3,2,1,0:T(8,128)(2,1)} %bitcast.233), kind=kOutput, calls=%fused_computation.15 | convolution fusion | flops 135258112 | bytes 8437760 | tf_op jit(solution)/shard_map/scie,scje->scij/dot_general | solution.py:190
  82.7 2.6 %fusion.6 = f32[16,16,32]{2,1,0:T(8,128)S(1)} fusion(f32[16,16,32,64]{3,2,1,0:T(8,128)S(1)} %get-tuple-element.59, f32[16,16,32]{2,1,0:T(8,128)S(1)} %get-tuple-element.58, pred[16,16,64]{2,1,0:T(8,128)(4,1)S(1)} %add_compare_fusion), kind=kLoop, calls=%fused_computation.16 | loop fusion | flops 1564672 | bytes 2179072 | tf_op jit(solution)/shard_map/reduce_sum | solution.py:22
  86.8 1.7 %collective-permute-start.13 = (f32[16,128]{1,0:T(8,128)S(1)}, f32[16,128]{1,0:T(8,128)S(1)}, u32[]{:S(2)}, u32[]{:S(2)}) collective-permute-start(f32[16,128]{1,0:T(8,128)S(1)} %add.281), channel_id=1, source_target_pairs={{0,2},{1,3},{2,0},{3,1},{4,6},{5,7},{6,4},{7,5},{8,10},{9,11},{10,... | collective-permute-start | bytes 24584 | tf_op jit(solution)/shard_map/ppermute | solution.py:44
  88.5 1.9 %collective-permute-done.13 = f32[16,128]{1,0:T(8,128)S(1)} collective-permute-done((f32[16,128]{1,0:T(8,128)S(1)}, f32[16,128]{1,0:T(8,128)S(1)}, u32[]{:S(2)}, u32[]{:S(2)}) %collective-permute-start.13) | collective-permute-done | bytes 8224 | tf_op jit(solution)/shard_map/ppermute | solution.py:44
  90.4 1.8 %collective-permute-start.14 = (f32[16,128]{1,0:T(8,128)S(1)}, f32[16,128]{1,0:T(8,128)S(1)}, u32[]{:S(2)}, u32[]{:S(2)}) collective-permute-start(f32[16,128]{1,0:T(8,128)S(1)} %add.282), channel_id=1, source_target_pairs={{0,4},{4,0},{8,12},{12,8},{1,5},{5,1},{9,13},{13,9},{2,6},{6,2},{1... | collective-permute-start | bytes 24584 | tf_op jit(solution)/shard_map/ppermute | solution.py:44
  94.1 2.8 %collective-permute-start.15 = (f32[16,128]{1,0:T(8,128)S(1)}, f32[16,128]{1,0:T(8,128)S(1)}, u32[]{:S(2)}, u32[]{:S(2)}) collective-permute-start(f32[16,128]{1,0:T(8,128)S(1)} %add.283), channel_id=1, source_target_pairs={{0,8},{4,12},{8,0},{12,4},{1,9},{5,13},{9,1},{13,5},{2,10},{6,14},... | collective-permute-start | bytes 24584 | tf_op jit(solution)/shard_map/ppermute | solution.py:44
  99.3 1.9 %gather_fusion.4 = f32[256]{0:T(256)S(1)} fusion(f32[16,128]{1,0:T(8,128)S(1)} %reshape.630, s32[256]{0:T(256)S(1)} %reshape.658), kind=kCustom, calls=%fused_computation.4 | custom fusion | bytes 4096 | tf_op jit(solution)/shard_map/jit(take_along_axis)/gather | solution.py:200
  101.3 6.9 %multiply_convert_fusion = bf16[16,16,64,128]{3,2,1,0:T(8,128)(2,1)S(1)} fusion(f32[16,16]{1,0:T(8,128)S(1)} %select_multiply_fusion, bf16[16,16,32,128]{3,2,1,0:T(8,128)(2,1)} %bitcast.239, f32[16,16,32,64]{3,2,1,0:T(8,128)} %copy-done.8, f32[16,16,32]{2,1,0:T(8,128)S(1)} %fusion.6, f32[16,16,32]{2,1,0:T(8,128)S(1)} %get-tuple-element.58, ...), kind=kOutput, calls=%fused_computation.5 | convolution fusion | flops 140509184 | bytes 8471552 | tf_op jit(solution)/shard_map/scij,scie->scje/dot_general | solution.py:193
  108.2 3.7 %fusion.14 = (f32[64,64]{0,1:T(8,128)S(1)}, f32[64,64,128]{2,0,1:T(8,128)S(1)}) fusion(f32[64,64,128]{2,1,0:T(8,128)S(1)} %bitcast.230, bf16[16,16,64,128]{3,2,1,0:T(8,128)(2,1)S(1)} %multiply_convert_fusion, s32[16,16]{0,1:T(8,128)S(1)} %copy.137, pred[16,16]{0,1:T(8,128)(4,1)S(1)} %copy.138), kind=kOutput, calls=%fused_computation.31 | convolution fusion | flops 269512704 | bytes 8406272 | tf_op jit(solution)/shard_map/scb,scje->bje/dot_general | solution.py:204
  111.9 2.6 %copy.141 = f32[64,64,128]{2,1,0:T(8,128)} copy(f32[64,64,128]{2,0,1:T(8,128)S(1)} %get-tuple-element.61) | data formatting | bytes 4194304 | tf_op jit(solution)/shard_map/scb,scje->bje/dot_general | solution.py:204
  114.6 3.8 %fusion.12 = bf16[1,4096,128]{2,1,0:T(8,128)(2,1)S(1)} fusion(f32[4096]{0:T(1024)S(1)} %mul.134, f32[4096]{0:T(1024)S(1)} %multiply_multiply_fusion, f32[4096]{0:T(1024)S(1)} %bitcast.243, f32[1,4096,128]{2,1,0:T(8,128)S(1)} %bitcast.231, f32[1,4096,128]{2,1,0:T(8,128)} %bitcast.237), kind=kLoop, calls=%fused_computation.26 | loop fusion | flops 2621440 | bytes 5292032 | tf_op jit(solution)/shard_map/convert_element_type | solution.py:212
  118.4 1.8 %collective-permute-start.16 = (bf16[1,4096,128]{2,1,0:T(8,128)(2,1)S(1)}, bf16[1,4096,128]{2,1,0:T(8,128)(2,1)S(1)}, u32[]{:S(2)}, u32[]{:S(2)}) collective-permute-start(bf16[1,4096,128]{2,1,0:T(8,128)(2,1)S(1)} %fusion.12), channel_id=1, source_target_pairs={{0,2},{1,3},{2,0},{3,1},{4,6},{5,7},{6,4},{7,5},{8,10},{9,11},{10,... | collective-permute-start | bytes 3145736 | tf_op jit(solution)/shard_map/ppermute | solution.py:44
  120.2 20.2 %collective-permute-done.16 = bf16[1,4096,128]{2,1,0:T(8,128)(2,1)S(1)} collective-permute-done((bf16[1,4096,128]{2,1,0:T(8,128)(2,1)S(1)}, bf16[1,4096,128]{2,1,0:T(8,128)(2,1)S(1)}, u32[]{:S(2)}, u32[]{:S(2)}) %collective-permute-start.16) | collective-permute-done | bytes 1048608 | tf_op jit(solution)/shard_map/ppermute | solution.py:44
  140.9 4.1 %collective-permute-done.17 = bf16[2,4096,128]{2,1,0:T(8,128)(2,1)S(1)} collective-permute-done((bf16[2,4096,128]{2,1,0:T(8,128)(2,1)S(1)}, bf16[2,4096,128]{2,1,0:T(8,128)(2,1)S(1)}, u32[]{:S(2)}, u32[]{:S(2)}) %collective-permute-start.17) | collective-permute-done | bytes 2097184 | tf_op jit(solution)/shard_map/ppermute | solution.py:44
  152.1 3.9 %collective-permute-done.18 = f32[256,128]{0,1:T(8,128)S(1)} collective-permute-done((f32[256,128]{0,1:T(8,128)S(1)}, f32[256,128]{0,1:T(8,128)S(1)}, u32[]{:S(2)}, u32[]{:S(2)}) %collective-permute-start.18) | collective-permute-done | bytes 131104 | tf_op jit(solution)/shard_map/ppermute | solution.py:44
  156.0 2.7 %collective-permute-start.19 = (f32[256,128]{0,1:T(8,128)S(1)}, f32[256,128]{0,1:T(8,128)S(1)}, u32[]{:S(2)}, u32[]{:S(2)}) collective-permute-start(f32[256,128]{0,1:T(8,128)S(1)} %add.290), channel_id=1, source_target_pairs={{0,8},{4,12},{8,0},{12,4},{1,9},{5,13},{9,1},{13,5},{2,10},{6,14},... | collective-permute-start | bytes 393224 | tf_op jit(solution)/shard_map/ppermute | solution.py:44
  159.3 5.2 %collective-permute-done.19 = f32[256,128]{0,1:T(8,128)S(1)} collective-permute-done((f32[256,128]{0,1:T(8,128)S(1)}, f32[256,128]{0,1:T(8,128)S(1)}, u32[]{:S(2)}, u32[]{:S(2)}) %collective-permute-start.19) | collective-permute-done | bytes 131104 | tf_op jit(solution)/shard_map/ppermute | solution.py:44
  (137 shorter events, 35.0 us)
Async XLA Ops:
  0.6 3.8 %copy-start = (bf16[256,128]{1,0:T(8,128)(2,1)S(1)}, bf16[256,128]{1,0:T(8,128)(2,1)}, u32[]{:S(2)}) copy-start(bf16[256,128]{1,0:T(8,128)(2,1)} %param.6) | copy-start | bytes 196612
  5.7 2.4 %copy-start.9 = (bf16[8,32,128]{2,1,0:T(8,128)(2,1)S(1)}, bf16[8,32,128]{2,1,0:T(8,128)(2,1)}, u32[]{:S(2)}) copy-start(bf16[8,32,128]{2,1,0:T(8,128)(2,1)} %param.7) | copy-start | bytes 196612
  5.7 4.9 %copy-start.10 = (s32[8,16]{1,0:T(8,128)S(1)}, s32[8,16]{1,0:T(8,128)}, u32[]{:S(2)}) copy-start(s32[8,16]{1,0:T(8,128)} %param.9) | copy-start | bytes 1540
  7.7 11.4 %collective-permute-start = (f32[2,2048,128]{2,1,0:T(8,128)S(1)}, f32[2,2048,128]{2,1,0:T(8,128)}, u32[]{:S(2)}, u32[]{:S(2)}) collective-permute-start(f32[2,2048,128]{2,1,0:T(8,128)S(1)} %select_bitcast_fusion.3), channel_id=1, source_target_pairs={{0,1},{1,0},{2,3},{3,2},{4,5},{5,4},{6,7},{7,6},{8,9},{9,8},{10,11... | collective-permute-start | bytes 6291464 | tf_op jit(solution)/shard_map/ppermute | solution.py:44
  8.2 7.1 %collective-permute-start.1 = (bf16[1,8,32,128]{3,2,1,0:T(8,128)(2,1)S(1)}, bf16[1,8,32,128]{3,2,1,0:T(8,128)(2,1)S(1)}, u32[]{:S(2)}, u32[]{:S(2)}) collective-permute-start(bf16[1,8,32,128]{3,2,1,0:T(8,128)(2,1)S(1)} %bitcast.246), channel_id=1, source_target_pairs={{0,2},{1,3},{2,0},{3,1},{4,6},{5,7},{6,4},{7,5},{8,10},{9,11},{10,... | collective-permute-start | bytes 196616 | tf_op jit(solution)/shard_map/ppermute | solution.py:95
  10.7 4.2 %collective-permute-start.3 = (s32[1,8,16]{2,1,0:T(8,128)S(1)}, s32[1,8,16]{2,1,0:T(8,128)S(1)}, u32[]{:S(2)}, u32[]{:S(2)}) collective-permute-start(s32[1,8,16]{2,1,0:T(8,128)S(1)} %bitcast.247), channel_id=1, source_target_pairs={{0,2},{1,3},{2,0},{3,1},{4,6},{5,7},{6,4},{7,5},{8,10},{9,11},{10,... | collective-permute-start | bytes 1544 | tf_op jit(solution)/shard_map/ppermute | solution.py:95
  12.0 2.7 %copy-start.4 = (f32[2,2,2048,128]{3,2,0,1:T(8,128)}, f32[2,2,2048,128]{3,2,0,1:T(8,128)S(1)}, u32[]{:S(2)}) copy-start(f32[2,2,2048,128]{3,2,0,1:T(8,128)S(1)} %fusion.2) | copy-start | bytes 12582916
  14.6 13.0 %collective-permute-start.10 = (f32[2,2048,128]{2,1,0:T(8,128)}, f32[2,2048,128]{2,1,0:T(8,128)}, u32[]{:S(2)}, u32[]{:S(2)}) collective-permute-start(f32[2,2048,128]{2,1,0:T(8,128)} %select_bitcast_fusion.2), channel_id=1, source_target_pairs={{0,1},{1,0},{2,3},{3,2},{4,5},{5,4},{6,7},{7,6},{8,9},{9,8},{10,11... | collective-permute-start | bytes 6291464 | tf_op jit(solution)/shard_map/ppermute | solution.py:44
  14.9 3.9 %collective-permute-start.4 = (s32[2,8,16]{2,1,0:T(8,128)S(1)}, s32[2,8,16]{2,1,0:T(8,128)S(1)}, u32[]{:S(2)}, u32[]{:S(2)}) collective-permute-start(s32[2,8,16]{2,1,0:T(8,128)S(1)} %add_bitcast_fusion.1), channel_id=1, source_target_pairs={{0,1},{1,0},{2,3},{3,2},{4,5},{5,4},{6,7},{7,6},{8,9},{9,8},{10,11... | collective-permute-start | bytes 3080 | tf_op jit(solution)/shard_map/ppermute | solution.py:95
  15.3 3.7 %collective-permute-start.2 = (bf16[2,8,32,128]{3,2,1,0:T(8,128)(2,1)S(1)}, bf16[2,8,32,128]{3,2,1,0:T(8,128)(2,1)S(1)}, u32[]{:S(2)}, u32[]{:S(2)}) collective-permute-start(bf16[2,8,32,128]{3,2,1,0:T(8,128)(2,1)S(1)} %maximum_bitcast_fusion.2), channel_id=1, source_target_pairs={{0,1},{1,0},{2,3},{3,2},{4,5},{5,4},{6,7},{7,6},{8,9},{9,8},{10,11... | collective-permute-start | bytes 393224 | tf_op jit(solution)/shard_map/ppermute | solution.py:95
  19.1 8.6 %copy-start.5 = (f32[2,2,2048,128]{3,2,0,1:T(8,128)S(1)}, f32[2,2,2048,128]{3,2,0,1:T(8,128)}, u32[]{:S(2)}) copy-start(f32[2,2,2048,128]{3,2,0,1:T(8,128)} %copy-done.4) | copy-start | bytes 12582916
  23.5 40.7 %collective-permute-start.9 = (f32[1,2048,128]{2,1,0:T(8,128)}, f32[1,2048,128]{2,1,0:T(8,128)}, u32[]{:S(2)}, u32[]{:S(2)}) collective-permute-start(f32[1,2048,128]{2,1,0:T(8,128)} %select_bitcast_fusion.7), channel_id=1, source_target_pairs={{0,2},{1,3},{2,0},{3,1},{4,6},{5,7},{6,4},{7,5},{8,10},{9,11},{10,... | collective-permute-start | bytes 3145736 | tf_op jit(solution)/shard_map/ppermute | solution.py:44
  25.1 4.6 %collective-permute-start.5 = (s32[1,32,16]{2,1,0:T(8,128)S(1)}, s32[1,32,16]{2,1,0:T(8,128)S(1)}, u32[]{:S(2)}, u32[]{:S(2)}) collective-permute-start(s32[1,32,16]{2,1,0:T(8,128)S(1)} %bitcast.244), channel_id=1, source_target_pairs={{0,8},{4,12},{8,0},{12,4},{1,9},{5,13},{9,1},{13,5},{2,10},{6,14},... | collective-permute-start | bytes 6152 | tf_op jit(solution)/shard_map/ppermute | solution.py:95
  29.5 6.2 %copy-start.6 = (f32[1,2,2048,128]{3,2,1,0:T(8,128)}, f32[1,2,2048,128]{3,2,1,0:T(8,128)S(1)}, u32[]{:S(2)}) copy-start(f32[1,2,2048,128]{3,2,1,0:T(8,128)S(1)} %fusion.13) | copy-start | bytes 6291460
  29.7 5.9 %collective-permute-start.6 = (s32[2,32,16]{2,1,0:T(8,128)S(1)}, s32[2,32,16]{2,1,0:T(8,128)S(1)}, u32[]{:S(2)}, u32[]{:S(2)}) collective-permute-start(s32[2,32,16]{2,1,0:T(8,128)S(1)} %add_bitcast_fusion), channel_id=1, source_target_pairs={{0,4},{4,0},{8,12},{12,8},{1,5},{5,1},{9,13},{13,9},{2,6},{6,2},{1... | collective-permute-start | bytes 12296 | tf_op jit(solution)/shard_map/ppermute | solution.py:95
  32.5 39.1 %collective-permute-start.11 = (f32[1,2048,128]{2,1,0:T(8,128)}, f32[1,2048,128]{2,1,0:T(8,128)}, u32[]{:S(2)}, u32[]{:S(2)}) collective-permute-start(f32[1,2048,128]{2,1,0:T(8,128)} %select_bitcast_fusion.6), channel_id=1, source_target_pairs={{0,2},{1,3},{2,0},{3,1},{4,6},{5,7},{6,4},{7,5},{8,10},{9,11},{10,... | collective-permute-start | bytes 3145736 | tf_op jit(solution)/shard_map/ppermute | solution.py:44
  33.0 13.8 %collective-permute-start.7 = (bf16[1,32,32,128]{3,2,1,0:T(8,128)(2,1)S(1)}, bf16[1,32,32,128]{3,2,1,0:T(8,128)(2,1)S(1)}, u32[]{:S(2)}, u32[]{:S(2)}) collective-permute-start(bf16[1,32,32,128]{3,2,1,0:T(8,128)(2,1)S(1)} %bitcast.240), channel_id=1, source_target_pairs={{0,8},{4,12},{8,0},{12,4},{1,9},{5,13},{9,1},{13,5},{2,10},{6,14},... | collective-permute-start | bytes 786440 | tf_op jit(solution)/shard_map/ppermute | solution.py:95
  38.4 9.3 %copy-start.2 = (s32[256]{0:T(256)S(1)}, s32[256]{0:T(256)}, u32[]{:S(2)}) copy-start(s32[256]{0:T(256)} %param.8) | copy-start | bytes 3076
  47.7 13.9 %collective-permute-start.8 = (bf16[2,32,32,128]{3,2,1,0:T(8,128)(2,1)}, bf16[2,32,32,128]{3,2,1,0:T(8,128)(2,1)S(1)}, u32[]{:S(2)}, u32[]{:S(2)}) collective-permute-start(bf16[2,32,32,128]{3,2,1,0:T(8,128)(2,1)} %maximum_bitcast_fusion.1), channel_id=1, source_target_pairs={{0,4},{4,0},{8,12},{12,8},{1,5},{5,1},{9,13},{13,9},{2,6},{6,2},{1... | collective-permute-start | bytes 1572872 | tf_op jit(solution)/shard_map/ppermute | solution.py:95
  64.1 7.4 %copy-start.7 = (f32[1,2,2048,128]{3,2,1,0:T(8,128)S(1)}, f32[1,2,2048,128]{3,2,1,0:T(8,128)}, u32[]{:S(2)}) copy-start(f32[1,2,2048,128]{3,2,1,0:T(8,128)} %copy-done.6) | copy-start | bytes 6291460
  82.6 2.6 %copy-start.8 = (f32[16,16,32,64]{3,2,1,0:T(8,128)}, f32[16,16,32,64]{3,2,1,0:T(8,128)S(1)}, u32[]{:S(2)}) copy-start(f32[16,16,32,64]{3,2,1,0:T(8,128)S(1)} %get-tuple-element.59) | copy-start | bytes 6291460
  85.5 1.2 collective-permute-start.12
  86.8 3.7 %collective-permute-start.13 = (f32[16,128]{1,0:T(8,128)S(1)}, f32[16,128]{1,0:T(8,128)S(1)}, u32[]{:S(2)}, u32[]{:S(2)}) collective-permute-start(f32[16,128]{1,0:T(8,128)S(1)} %add.281), channel_id=1, source_target_pairs={{0,2},{1,3},{2,0},{3,1},{4,6},{5,7},{6,4},{7,5},{8,10},{9,11},{10,... | collective-permute-start | bytes 24584 | tf_op jit(solution)/shard_map/ppermute | solution.py:44
  90.4 3.7 %collective-permute-start.14 = (f32[16,128]{1,0:T(8,128)S(1)}, f32[16,128]{1,0:T(8,128)S(1)}, u32[]{:S(2)}, u32[]{:S(2)}) collective-permute-start(f32[16,128]{1,0:T(8,128)S(1)} %add.282), channel_id=1, source_target_pairs={{0,4},{4,0},{8,12},{12,8},{1,5},{5,1},{9,13},{13,9},{2,6},{6,2},{1... | collective-permute-start | bytes 24584 | tf_op jit(solution)/shard_map/ppermute | solution.py:44
  94.1 4.5 %collective-permute-start.15 = (f32[16,128]{1,0:T(8,128)S(1)}, f32[16,128]{1,0:T(8,128)S(1)}, u32[]{:S(2)}, u32[]{:S(2)}) collective-permute-start(f32[16,128]{1,0:T(8,128)S(1)} %add.283), channel_id=1, source_target_pairs={{0,8},{4,12},{8,0},{12,4},{1,9},{5,13},{9,1},{13,5},{2,10},{6,14},... | collective-permute-start | bytes 24584 | tf_op jit(solution)/shard_map/ppermute | solution.py:44
  118.4 22.0 %collective-permute-start.16 = (bf16[1,4096,128]{2,1,0:T(8,128)(2,1)S(1)}, bf16[1,4096,128]{2,1,0:T(8,128)(2,1)S(1)}, u32[]{:S(2)}, u32[]{:S(2)}) collective-permute-start(bf16[1,4096,128]{2,1,0:T(8,128)(2,1)S(1)} %fusion.12), channel_id=1, source_target_pairs={{0,2},{1,3},{2,0},{3,1},{4,6},{5,7},{6,4},{7,5},{8,10},{9,11},{10,... | collective-permute-start | bytes 3145736 | tf_op jit(solution)/shard_map/ppermute | solution.py:44
  140.8 4.2 %collective-permute-start.17 = (bf16[2,4096,128]{2,1,0:T(8,128)(2,1)S(1)}, bf16[2,4096,128]{2,1,0:T(8,128)(2,1)S(1)}, u32[]{:S(2)}, u32[]{:S(2)}) collective-permute-start(bf16[2,4096,128]{2,1,0:T(8,128)(2,1)S(1)} %maximum_bitcast_fusion), channel_id=1, source_target_pairs={{0,1},{1,0},{2,3},{3,2},{4,5},{5,4},{6,7},{7,6},{8,9},{9,8},{10,11... | collective-permute-start | bytes 6291464 | tf_op jit(solution)/shard_map/ppermute | solution.py:44
  145.3 2.2 %slice-start = ((s8[8388608]{0:T(1024)(128)(4,1)}), s8[4194304]{0:T(1024)(128)(4,1)S(1)}, s32[]{:S(2)}) async-start(s8[8388608]{0:T(1024)(128)(4,1)} %bitcast.227), calls=%async_computation | async-start | bytes 8388608
  145.7 3.2 %slice-start.1 = ((s8[8388608]{0:T(1024)(128)(4,1)}), s8[4194304]{0:T(1024)(128)(4,1)S(1)}, s32[]{:S(2)}) async-start(s8[8388608]{0:T(1024)(128)(4,1)} %bitcast.227), calls=%async_computation.1 | async-start | bytes 8388608
  148.9 16.4 %copy-start.1 = (bf16[256,128]{1,0:T(8,128)(2,1)S(1)}, bf16[256,128]{1,0:T(8,128)(2,1)}, u32[]{:S(2)}) copy-start(bf16[256,128]{1,0:T(8,128)(2,1)} %param.6) | copy-start | bytes 196612
  150.4 5.6 %collective-permute-start.18 = (f32[256,128]{0,1:T(8,128)S(1)}, f32[256,128]{0,1:T(8,128)S(1)}, u32[]{:S(2)}, u32[]{:S(2)}) collective-permute-start(f32[256,128]{0,1:T(8,128)S(1)} %convolution_bitcast_fusion), channel_id=1, source_target_pairs={{0,4},{4,0},{8,12},{12,8},{1,5},{5,1},{9,13},{13,9},{2,6},{6,2},{1... | collective-permute-start | bytes 393224 | tf_op jit(solution)/shard_map/ppermute | solution.py:44
  156.0 8.5 %collective-permute-start.19 = (f32[256,128]{0,1:T(8,128)S(1)}, f32[256,128]{0,1:T(8,128)S(1)}, u32[]{:S(2)}, u32[]{:S(2)}) collective-permute-start(f32[256,128]{0,1:T(8,128)S(1)} %add.290), channel_id=1, source_target_pairs={{0,8},{4,12},{8,0},{12,4},{1,9},{5,13},{9,1},{13,5},{2,10},{6,14},... | collective-permute-start | bytes 393224 | tf_op jit(solution)/shard_map/ppermute | solution.py:44
  (1 other events, 2.0 us)

commit v22 on v21

--- a/solution.py
+++ b/solution.py
@@ -210,7 +210,24 @@
     grad_flat = grad_emb.reshape(row_share, emb_width)
     dot_e = jnp.sum(e_pre * grad_flat, -1, keepdims=True)
     de_pre = (scale * grad_flat - e_pre * (scale * scale * scale) * dot_e).astype(jnp.bfloat16)
-    partial_w = left_product(hidden, all_gather_rows(de_pre, "mp"))
+    if mp_count == 4:
+        low_bit = lax.axis_index("mp") % 2
+        far_low = (lax.axis_index("mp") // 2) % 2 == 0
+        rows_by = hidden.reshape(2, 2, row_share, hidden.shape[1])
+        mine = de_pre[None]
+        other = xor_perm(mine, "mp", 2)
+        pair = jnp.concatenate(
+            [jnp.where(far_low, mine, other), jnp.where(far_low, other, mine)], axis=0
+        )
+        near = lax.dynamic_index_in_dim(rows_by, low_bit, 1, keepdims=False)
+        partial_w = left_product(near.reshape(-1, hidden.shape[1]), pair.reshape(-1, emb_width))
+        partner_pair = xor_perm(pair, "mp", 1)
+        away = lax.dynamic_index_in_dim(rows_by, 1 - low_bit, 1, keepdims=False)
+        partial_w = partial_w + left_product(
+            away.reshape(-1, hidden.shape[1]), partner_pair.reshape(-1, emb_width)
+        )
+    else:
+        partial_w = left_product(hidden, all_gather_rows(de_pre, "mp"))
     grad_w = all_sum(partial_w, "enc", one_step=False)
     return (losses, grad_w)
 

time: 166 us -> 165 us (level)
  waiting for transfers between devices: 68.6 us -> 65 us
  matrix products: 19.8 us -> 22.5 us
    dynamic_slice x0 -> x1, local copies, waits for them, and re-layouts: none -> 4.02 us  [local(): near = lax.dynamic_index_in_dim(rows_by, low_bit, 1, keepdims=False)]
    unnamed x29 -> x24, local copies, waits for them, and re-layouts: 6.43 us -> 2.76 us
    ppermute x12, waiting for transfers between devices: 45.5 us -> 41.9 us  [xor_perm(): return lax.ppermute(value, axis, [(i, i ^ bit) for i in range(count)])]
    dot_general x1 -> x2, matrix products: 1.53 us -> 4.18 us  [left_product(): lax.dot_general(left, right, (((0,), (0,)), ((), ())), preferred_element_...]
  transfers between devices with their start and end apart: 20 -> 20, of which waited for: 14 -> 14; matrix products, arithmetic and copies ran while one was open for 13% -> 16% of each run, Pallas kernels for 0% -> 0%
where the time goes in v22:
time: 165 us; the launch traced here: 164 us
  waiting for transfers between devices  65 us (39%)
  local copies, waits for them, and re-layouts  26.3 us (16%)
  starting transfers between devices  25.6 us (16%)
  other arithmetic  23.8 us (14%)
  matrix products  22.5 us (14%)
    ppermute x12, waiting for transfers between devices, xor_perm(): return lax.ppermute(value, axis, [(i, i ^ bit) for i in range(count)])  41.9 us
    ppermute x8, waiting for transfers between devices, all_gather_many(): others = lax.ppermute(arrs, axis, [(i, i ^ bit) for i in range(count)])  23.1 us
    ppermute x12, starting transfers between devices, xor_perm(): return lax.ppermute(value, axis, [(i, i ^ bit) for i in range(count)])  15.5 us
    ppermute x8, starting transfers between devices, all_gather_many(): others = lax.ppermute(arrs, axis, [(i, i ^ bit) for i in range(count)])  10.1 us
    dot_general x1, matrix products, local(): jnp.einsum('scij,scie->scje', weights, q_e, preferred_element_type=jnp.fl...  6.95 us
    dot_general x1, matrix products, local(): jnp.einsum('scie,scje->scij', q_e, tiles, preferred_element_type=jnp.floa...  5.2 us
    reshape x2, other arithmetic, halving_steps(): acc = acc.reshape((acc.shape[0] // 2, 2) + acc.shape[1:])  5.15 us
    dot_general x2, matrix products, left_product(): lax.dot_general(left, right, (((0,), (0,)), ((), ())), preferred_element_...  4.18 us
  transfers between devices with their start and end apart: 20, of which 14 were waited for; matrix products, arithmetic and copies ran while one was open for 16% of the time, Pallas kernels for 0%

profile of v22, /device:TPU:0, one launch (start us, length us, event | category | flops | bytes accessed | tf_op | source)
XLA Modules:
  0.0 164.3 jit_solution(8186866772537411003)
XLA Ops:
  0.7 3.8 %fusion.47 = (bf16[4,1,2048,256]{3,2,1,0:T(8,128)(2,1)S(1)}, bf16[4,1,2048,256]{3,2,1,0:T(8,128)(2,1)S(1)}) fusion(bf16[4,2,2048,256]{3,2,1,0:T(8,128)(2,1)} %bitcast.216), kind=kLoop, calls=%fused_computation.149 | loop fusion | bytes 16777216 | tf_op jit(solution)/shard_map/slice | solution.py:150
  8.1 2.5 %collective-permute-start.1 = (bf16[1,8,32,128]{3,2,1,0:T(8,128)(2,1)S(1)}, bf16[1,8,32,128]{3,2,1,0:T(8,128)(2,1)S(1)}, u32[]{:S(2)}, u32[]{:S(2)}) collective-permute-start(bf16[1,8,32,128]{3,2,1,0:T(8,128)(2,1)S(1)} %bitcast.237), channel_id=1, source_target_pairs={{0,2},{1,3},{2,0},{3,1},{4,6},{5,7},{6,4},{7,5},{8,10},{9,11},{10,... | collective-permute-start | bytes 196616 | tf_op jit(solution)/shard_map/ppermute | solution.py:95
  15.5 3.2 %collective-permute-done.4 = s32[2,8,16]{2,1,0:T(8,128)S(1)} collective-permute-done((s32[2,8,16]{2,1,0:T(8,128)S(1)}, s32[2,8,16]{2,1,0:T(8,128)S(1)}, u32[]{:S(2)}, u32[]{:S(2)}) %collective-permute-start.4) | collective-permute-done | bytes 1056 | tf_op jit(solution)/shard_map/ppermute | solution.py:95
  19.0 3.3 %fusion.9 = f32[1,2,2048,128]{3,2,1,0:T(8,128)S(1)} fusion(f32[2,2048,128]{2,1,0:T(8,128)} %collective-permute-done, f32[2,2,2048,128]{3,2,1,0:T(8,128)} %copy-done.5, pred[]{:T(512)S(6)} %eq.72), kind=kLoop, calls=%fused_computation.21 | loop fusion | flops 1048576 | bytes 8388609 | tf_op jit(solution)/shard_map/reshape | solution.py:59
  25.0 2.6 %collective-permute-start.5 = (s32[1,32,16]{2,1,0:T(8,128)S(1)}, s32[1,32,16]{2,1,0:T(8,128)S(1)}, u32[]{:S(2)}, u32[]{:S(2)}) collective-permute-start(s32[1,32,16]{2,1,0:T(8,128)S(1)} %bitcast.235), channel_id=1, source_target_pairs={{0,8},{4,12},{8,0},{12,4},{1,9},{5,13},{9,1},{13,5},{2,10},{6,14},... | collective-permute-start | bytes 6152 | tf_op jit(solution)/shard_map/ppermute | solution.py:95
  27.6 1.9 %fusion.13 = f32[1,2,2048,128]{3,2,1,0:T(8,128)S(1)} fusion(f32[2,2048,128]{2,1,0:T(8,128)} %collective-permute-done.10, f32[2,2,2048,128]{3,2,0,1:T(8,128)S(1)} %copy-done.4, pred[]{:T(512)S(6)} %eq.72), kind=kLoop, calls=%fused_computation.28 | loop fusion | flops 1048576 | bytes 8388609 | tf_op jit(solution)/shard_map/reshape | solution.py:59
  32.9 2.6 %collective-permute-start.7 = (bf16[1,32,32,128]{3,2,1,0:T(8,128)(2,1)S(1)}, bf16[1,32,32,128]{3,2,1,0:T(8,128)(2,1)S(1)}, u32[]{:S(2)}, u32[]{:S(2)}) collective-permute-start(bf16[1,32,32,128]{3,2,1,0:T(8,128)(2,1)S(1)} %bitcast.231), channel_id=1, source_target_pairs={{0,8},{4,12},{8,0},{12,4},{1,9},{5,13},{9,1},{13,5},{2,10},{6,14},... | collective-permute-start | bytes 786440 | tf_op jit(solution)/shard_map/ppermute | solution.py:95
  36.5 1.9 %gather_fusion.3 = s32[256]{0:T(256)S(1)} fusion(s32[16,128]{1,0:T(8,128)S(1)} %reshape_reshape_reshape.2, s32[256]{0:T(256)S(1)} %reshape.676), kind=kCustom, calls=%fused_computation.3 | custom fusion | bytes 4096 | tf_op jit(solution)/shard_map/jit(take_along_axis)/gather | solution.py:177
  38.8 7.9 %collective-permute-done.7 = bf16[1,32,32,128]{3,2,1,0:T(8,128)(2,1)S(1)} collective-permute-done((bf16[1,32,32,128]{3,2,1,0:T(8,128)(2,1)S(1)}, bf16[1,32,32,128]{3,2,1,0:T(8,128)(2,1)S(1)}, u32[]{:S(2)}, u32[]{:S(2)}) %collective-permute-start.7) | collective-permute-done | bytes 262176 | tf_op jit(solution)/shard_map/ppermute | solution.py:95
  47.7 1.9 %gather_fusion = s32[256]{0:T(256)S(1)} fusion(s32[256]{0:T(256)S(1)} %copy-done.2, s32[1024]{0:T(1024)S(1)} %pad_clamp_fusion.2), kind=kCustom, calls=%fused_computation | custom fusion | bytes 3072 | tf_op jit(solution)/shard_map/gather | solution.py:15
  50.0 11.6 %collective-permute-done.8 = bf16[2,32,32,128]{3,2,1,0:T(8,128)(2,1)S(1)} collective-permute-done((bf16[2,32,32,128]{3,2,1,0:T(8,128)(2,1)}, bf16[2,32,32,128]{3,2,1,0:T(8,128)(2,1)S(1)}, u32[]{:S(2)}, u32[]{:S(2)}) %collective-permute-start.8) | collective-permute-done | bytes 524320 | tf_op jit(solution)/shard_map/ppermute | solution.py:95
  61.8 2.2 %gather_fusion.1 = bf16[256,32,128]{2,1,0:T(8,128)(2,1)} fusion(bf16[128,32,128]{2,1,0:T(8,128)(2,1)S(1)} %bitcast.226, s32[1024]{0:T(1024)S(1)} %pad_clamp_fusion.1), kind=kCustom, calls=%fused_computation.1 | custom fusion | bytes 4195328 | tf_op jit(solution)/shard_map/gather | solution.py:181
  65.6 5.9 %collective-permute-done.11 = f32[1,2048,128]{2,1,0:T(8,128)} collective-permute-done((f32[1,2048,128]{2,1,0:T(8,128)}, f32[1,2048,128]{2,1,0:T(8,128)}, u32[]{:S(2)}, u32[]{:S(2)}) %collective-permute-start.11) | collective-permute-done | bytes 1048608 | tf_op jit(solution)/shard_map/ppermute | solution.py:44
  74.4 3.0 %gather_fusion.2 = bf16[256,64,128]{2,1,0:T(8,128)(2,1)} fusion(bf16[64,64,128]{2,1,0:T(8,128)(2,1)S(1)} %multiply_convert_fusion.1, s32[1024]{0:T(1024)S(1)} %pad_clamp_fusion), kind=kCustom, calls=%fused_computation.2 | custom fusion | bytes 8389632 | tf_op jit(solution)/shard_map/gather | solution.py:188
  77.4 5.2 %select_reduce_fusion = (f32[16,16,32]{2,1,0:T(8,128)S(1)}, f32[16,16,32,64]{3,2,1,0:T(8,128)S(1)}) fusion(pred[16,16,64]{2,1,0:T(8,128)(4,1)S(1)} %add_compare_fusion, bf16[16,16,32,128]{3,2,1,0:T(8,128)(2,1)} %bitcast.229, bf16[16,16,64,128]{3,2,1,0:T(8,128)(2,1)} %bitcast.221), kind=kOutput, calls=%fused_computation.14 | convolution fusion | flops 135258112 | bytes 8437760 | tf_op jit(solution)/shard_map/scie,scje->scij/dot_general | solution.py:190
  82.6 2.6 %fusion.6 = f32[16,16,32]{2,1,0:T(8,128)S(1)} fusion(f32[16,16,32,64]{3,2,1,0:T(8,128)S(1)} %get-tuple-element.45, f32[16,16,32]{2,1,0:T(8,128)S(1)} %get-tuple-element.44, pred[16,16,64]{2,1,0:T(8,128)(4,1)S(1)} %add_compare_fusion), kind=kLoop, calls=%fused_computation.15 | loop fusion | flops 1564672 | bytes 2179072 | tf_op jit(solution)/shard_map/reduce_sum | solution.py:22
  86.7 1.7 %collective-permute-start.13 = (f32[16,128]{1,0:T(8,128)S(1)}, f32[16,128]{1,0:T(8,128)S(1)}, u32[]{:S(2)}, u32[]{:S(2)}) collective-permute-start(f32[16,128]{1,0:T(8,128)S(1)} %add.292), channel_id=1, source_target_pairs={{0,2},{1,3},{2,0},{3,1},{4,6},{5,7},{6,4},{7,5},{8,10},{9,11},{10,... | collective-permute-start | bytes 24584 | tf_op jit(solution)/shard_map/ppermute | solution.py:44
  88.5 1.9 %collective-permute-done.13 = f32[16,128]{1,0:T(8,128)S(1)} collective-permute-done((f32[16,128]{1,0:T(8,128)S(1)}, f32[16,128]{1,0:T(8,128)S(1)}, u32[]{:S(2)}, u32[]{:S(2)}) %collective-permute-start.13) | collective-permute-done | bytes 8224 | tf_op jit(solution)/shard_map/ppermute | solution.py:44
  90.4 1.8 %collective-permute-start.14 = (f32[16,128]{1,0:T(8,128)S(1)}, f32[16,128]{1,0:T(8,128)S(1)}, u32[]{:S(2)}, u32[]{:S(2)}) collective-permute-start(f32[16,128]{1,0:T(8,128)S(1)} %add.293), channel_id=1, source_target_pairs={{0,4},{4,0},{8,12},{12,8},{1,5},{5,1},{9,13},{13,9},{2,6},{6,2},{1... | collective-permute-start | bytes 24584 | tf_op jit(solution)/shard_map/ppermute | solution.py:44
  94.0 2.8 %collective-permute-start.15 = (f32[16,128]{1,0:T(8,128)S(1)}, f32[16,128]{1,0:T(8,128)S(1)}, u32[]{:S(2)}, u32[]{:S(2)}) collective-permute-start(f32[16,128]{1,0:T(8,128)S(1)} %add.294), channel_id=1, source_target_pairs={{0,8},{4,12},{8,0},{12,4},{1,9},{5,13},{9,1},{13,5},{2,10},{6,14},... | collective-permute-start | bytes 24584 | tf_op jit(solution)/shard_map/ppermute | solution.py:44
  99.2 1.9 %gather_fusion.4 = f32[256]{0:T(256)S(1)} fusion(f32[16,128]{1,0:T(8,128)S(1)} %reshape.646, s32[256]{0:T(256)S(1)} %reshape.676), kind=kCustom, calls=%fused_computation.4 | custom fusion | bytes 4096 | tf_op jit(solution)/shard_map/jit(take_along_axis)/gather | solution.py:200
  101.2 6.9 %multiply_convert_fusion = bf16[16,16,64,128]{3,2,1,0:T(8,128)(2,1)S(1)} fusion(f32[16,16]{1,0:T(8,128)S(1)} %select_multiply_fusion, bf16[16,16,32,128]{3,2,1,0:T(8,128)(2,1)} %bitcast.230, f32[16,16,32,64]{3,2,1,0:T(8,128)} %copy-done.8, f32[16,16,32]{2,1,0:T(8,128)S(1)} %fusion.6, f32[16,16,32]{2,1,0:T(8,128)S(1)} %get-tuple-element.44, ...), kind=kOutput, calls=%fused_computation.5 | convolution fusion | flops 140509184 | bytes 8471552 | tf_op jit(solution)/shard_map/scij,scie->scje/dot_general | solution.py:193
  108.2 3.7 %fusion.14 = (f32[64,64]{0,1:T(8,128)S(1)}, f32[64,64,128]{2,0,1:T(8,128)S(1)}) fusion(f32[64,64,128]{2,1,0:T(8,128)S(1)} %bitcast.219, bf16[16,16,64,128]{3,2,1,0:T(8,128)(2,1)S(1)} %multiply_convert_fusion, s32[16,16]{0,1:T(8,128)S(1)} %copy.126, pred[16,16]{0,1:T(8,128)(4,1)S(1)} %copy.127), kind=kOutput, calls=%fused_computation.30 | convolution fusion | flops 269512704 | bytes 8406272 | tf_op jit(solution)/shard_map/scb,scje->bje/dot_general | solution.py:204
  111.9 2.6 %copy.130 = f32[64,64,128]{2,1,0:T(8,128)} copy(f32[64,64,128]{2,0,1:T(8,128)S(1)} %get-tuple-element.47) | data formatting | bytes 4194304 | tf_op jit(solution)/shard_map/scb,scje->bje/dot_general | solution.py:204
  114.6 3.8 %fusion.12 = bf16[1,4096,128]{2,1,0:T(8,128)(2,1)S(1)} fusion(f32[4096]{0:T(1024)S(1)} %mul.134, f32[4096]{0:T(1024)S(1)} %multiply_multiply_fusion, f32[4096]{0:T(1024)S(1)} %bitcast.234, f32[1,4096,128]{2,1,0:T(8,128)S(1)} %bitcast.220, f32[1,4096,128]{2,1,0:T(8,128)} %bitcast.228), kind=kLoop, calls=%fused_computation.25 | loop fusion | flops 2621440 | bytes 5292032 | tf_op jit(solution)/shard_map/convert_element_type | solution.py:212
  118.4 1.8 %collective-permute-start.16 = (bf16[1,4096,128]{2,1,0:T(8,128)(2,1)S(1)}, bf16[1,4096,128]{2,1,0:T(8,128)(2,1)S(1)}, u32[]{:S(2)}, u32[]{:S(2)}) collective-permute-start(bf16[1,4096,128]{2,1,0:T(8,128)(2,1)S(1)} %fusion.12), channel_id=1, source_target_pairs={{0,2},{1,3},{2,0},{3,1},{4,6},{5,7},{6,4},{7,5},{8,10},{9,11},{10,... | collective-permute-start | bytes 3145736 | tf_op jit(solution)/shard_map/ppermute | solution.py:44
  120.2 20.2 %collective-permute-done.16 = bf16[1,4096,128]{2,1,0:T(8,128)(2,1)S(1)} collective-permute-done((bf16[1,4096,128]{2,1,0:T(8,128)(2,1)S(1)}, bf16[1,4096,128]{2,1,0:T(8,128)(2,1)S(1)}, u32[]{:S(2)}, u32[]{:S(2)}) %collective-permute-start.16) | collective-permute-done | bytes 1048608 | tf_op jit(solution)/shard_map/ppermute | solution.py:44
  140.8 4.0 %constant_dynamic-slice_fusion.1 = (bf16[2,1,4096,256]{3,2,1,0:T(8,128)(2,1)S(1)}, bf16[2,1,4096,256]{3,2,1,0:T(8,128)(2,1)S(1)}) fusion(bf16[2,2,4096,256]{3,2,1,0:T(8,128)(2,1)} %bitcast.217, s32[]{:T(128)S(6)} %select_n.505, s32[]{:T(128)S(6)} %select_n.512), kind=kLoop, calls=%fused_computation.143 | loop fusion | bytes 16777224 | tf_op jit(solution)/shard_map/jit(dynamic_index_in_dim)/dynamic_slice | solution.py:222
  145.1 2.9 %fusion.48 = f32[256,128]{1,0:T(8,128)S(1)} fusion(bf16[8192,256]{1,0:T(8,128)(2,1)S(1)} %bitcast.224, bf16[8192,128]{1,0:T(8,128)(2,1)} %bitcast.60), kind=kOutput, calls=%fused_computation.150 | convolution fusion | flops 536870912 | bytes 6422528 | tf_op jit(solution)/shard_map/dot_general | solution.py:37
  151.0 4.0 %collective-permute-done.18 = f32[256,128]{1,0:T(8,128)S(1)} collective-permute-done((f32[256,128]{1,0:T(8,128)S(1)}, f32[256,128]{1,0:T(8,128)S(1)}, u32[]{:S(2)}, u32[]{:S(2)}) %collective-permute-start.18) | collective-permute-done | bytes 131104 | tf_op jit(solution)/shard_map/ppermute | solution.py:44
  155.0 2.7 %collective-permute-start.19 = (f32[256,128]{1,0:T(8,128)S(1)}, f32[256,128]{1,0:T(8,128)S(1)}, u32[]{:S(2)}, u32[]{:S(2)}) collective-permute-start(f32[256,128]{1,0:T(8,128)S(1)} %add.304), channel_id=1, source_target_pairs={{0,8},{4,12},{8,0},{12,4},{1,9},{5,13},{9,1},{13,5},{2,10},{6,14},... | collective-permute-start | bytes 393224 | tf_op jit(solution)/shard_map/ppermute | solution.py:44
  158.3 5.3 %collective-permute-done.19 = f32[256,128]{1,0:T(8,128)S(1)} collective-permute-done((f32[256,128]{1,0:T(8,128)S(1)}, f32[256,128]{1,0:T(8,128)S(1)}, u32[]{:S(2)}, u32[]{:S(2)}) %collective-permute-start.19) | collective-permute-done | bytes 131104 | tf_op jit(solution)/shard_map/ppermute | solution.py:44
  (130 shorter events, 32.8 us)
Async XLA Ops:
  0.6 3.8 %copy-start = (bf16[256,128]{1,0:T(8,128)(2,1)S(1)}, bf16[256,128]{1,0:T(8,128)(2,1)}, u32[]{:S(2)}) copy-start(bf16[256,128]{1,0:T(8,128)(2,1)} %param.6) | copy-start | bytes 196612
  5.7 2.0 %copy-start.5 = (f32[2,2,2048,128]{3,2,1,0:T(8,128)}, f32[2,2,2048,128]{3,2,1,0:T(8,128)S(1)}, u32[]{:S(2)}) copy-start(f32[2,2,2048,128]{3,2,1,0:T(8,128)S(1)} %fusion) | copy-start | bytes 12582916
  5.7 2.4 %copy-start.9 = (bf16[8,32,128]{2,1,0:T(8,128)(2,1)S(1)}, bf16[8,32,128]{2,1,0:T(8,128)(2,1)}, u32[]{:S(2)}) copy-start(bf16[8,32,128]{2,1,0:T(8,128)(2,1)} %param.7) | copy-start | bytes 196612
  5.7 4.9 %copy-start.10 = (s32[8,16]{1,0:T(8,128)S(1)}, s32[8,16]{1,0:T(8,128)}, u32[]{:S(2)}) copy-start(s32[8,16]{1,0:T(8,128)} %param.9) | copy-start | bytes 1540
  7.7 11.3 %collective-permute-start = (f32[2,2048,128]{2,1,0:T(8,128)S(1)}, f32[2,2048,128]{2,1,0:T(8,128)}, u32[]{:S(2)}, u32[]{:S(2)}) collective-permute-start(f32[2,2048,128]{2,1,0:T(8,128)S(1)} %select_bitcast_fusion.1), channel_id=1, source_target_pairs={{0,1},{1,0},{2,3},{3,2},{4,5},{5,4},{6,7},{7,6},{8,9},{9,8},{10,11... | collective-permute-start | bytes 6291464 | tf_op jit(solution)/shard_map/ppermute | solution.py:44
  8.1 7.0 %collective-permute-start.1 = (bf16[1,8,32,128]{3,2,1,0:T(8,128)(2,1)S(1)}, bf16[1,8,32,128]{3,2,1,0:T(8,128)(2,1)S(1)}, u32[]{:S(2)}, u32[]{:S(2)}) collective-permute-start(bf16[1,8,32,128]{3,2,1,0:T(8,128)(2,1)S(1)} %bitcast.237), channel_id=1, source_target_pairs={{0,2},{1,3},{2,0},{3,1},{4,6},{5,7},{6,4},{7,5},{8,10},{9,11},{10,... | collective-permute-start | bytes 196616 | tf_op jit(solution)/shard_map/ppermute | solution.py:95
  10.6 4.2 %collective-permute-start.3 = (s32[1,8,16]{2,1,0:T(8,128)S(1)}, s32[1,8,16]{2,1,0:T(8,128)S(1)}, u32[]{:S(2)}, u32[]{:S(2)}) collective-permute-start(s32[1,8,16]{2,1,0:T(8,128)S(1)} %bitcast.238), channel_id=1, source_target_pairs={{0,2},{1,3},{2,0},{3,1},{4,6},{5,7},{6,4},{7,5},{8,10},{9,11},{10,... | collective-permute-start | bytes 1544 | tf_op jit(solution)/shard_map/ppermute | solution.py:95
  12.0 2.6 %copy-start.3 = (f32[2,2,2048,128]{3,2,0,1:T(8,128)}, f32[2,2,2048,128]{3,2,0,1:T(8,128)S(1)}, u32[]{:S(2)}) copy-start(f32[2,2,2048,128]{3,2,0,1:T(8,128)S(1)} %fusion.2) | copy-start | bytes 12582916
  14.6 13.0 %collective-permute-start.10 = (f32[2,2048,128]{2,1,0:T(8,128)}, f32[2,2048,128]{2,1,0:T(8,128)}, u32[]{:S(2)}, u32[]{:S(2)}) collective-permute-start(f32[2,2048,128]{2,1,0:T(8,128)} %select_bitcast_fusion), channel_id=1, source_target_pairs={{0,1},{1,0},{2,3},{3,2},{4,5},{5,4},{6,7},{7,6},{8,9},{9,8},{10,11... | collective-permute-start | bytes 6291464 | tf_op jit(solution)/shard_map/ppermute | solution.py:44
  14.8 3.9 %collective-permute-start.4 = (s32[2,8,16]{2,1,0:T(8,128)S(1)}, s32[2,8,16]{2,1,0:T(8,128)S(1)}, u32[]{:S(2)}, u32[]{:S(2)}) collective-permute-start(s32[2,8,16]{2,1,0:T(8,128)S(1)} %add_bitcast_fusion.1), channel_id=1, source_target_pairs={{0,1},{1,0},{2,3},{3,2},{4,5},{5,4},{6,7},{7,6},{8,9},{9,8},{10,11... | collective-permute-start | bytes 3080 | tf_op jit(solution)/shard_map/ppermute | solution.py:95
  15.2 3.7 %collective-permute-start.2 = (bf16[2,8,32,128]{3,2,1,0:T(8,128)(2,1)S(1)}, bf16[2,8,32,128]{3,2,1,0:T(8,128)(2,1)S(1)}, u32[]{:S(2)}, u32[]{:S(2)}) collective-permute-start(bf16[2,8,32,128]{3,2,1,0:T(8,128)(2,1)S(1)} %maximum_bitcast_fusion.1), channel_id=1, source_target_pairs={{0,1},{1,0},{2,3},{3,2},{4,5},{5,4},{6,7},{7,6},{8,9},{9,8},{10,11... | collective-permute-start | bytes 393224 | tf_op jit(solution)/shard_map/ppermute | solution.py:95
  19.0 8.6 %copy-start.4 = (f32[2,2,2048,128]{3,2,0,1:T(8,128)S(1)}, f32[2,2,2048,128]{3,2,0,1:T(8,128)}, u32[]{:S(2)}) copy-start(f32[2,2,2048,128]{3,2,0,1:T(8,128)} %copy-done.3) | copy-start | bytes 12582916
  23.4 40.6 %collective-permute-start.9 = (f32[1,2048,128]{2,1,0:T(8,128)}, f32[1,2048,128]{2,1,0:T(8,128)}, u32[]{:S(2)}, u32[]{:S(2)}) collective-permute-start(f32[1,2048,128]{2,1,0:T(8,128)} %select_bitcast_fusion.3), channel_id=1, source_target_pairs={{0,2},{1,3},{2,0},{3,1},{4,6},{5,7},{6,4},{7,5},{8,10},{9,11},{10,... | collective-permute-start | bytes 3145736 | tf_op jit(solution)/shard_map/ppermute | solution.py:44
  25.0 4.6 %collective-permute-start.5 = (s32[1,32,16]{2,1,0:T(8,128)S(1)}, s32[1,32,16]{2,1,0:T(8,128)S(1)}, u32[]{:S(2)}, u32[]{:S(2)}) collective-permute-start(s32[1,32,16]{2,1,0:T(8,128)S(1)} %bitcast.235), channel_id=1, source_target_pairs={{0,8},{4,12},{8,0},{12,4},{1,9},{5,13},{9,1},{13,5},{2,10},{6,14},... | collective-permute-start | bytes 6152 | tf_op jit(solution)/shard_map/ppermute | solution.py:95
  29.5 6.1 %copy-start.6 = (f32[1,2,2048,128]{3,2,1,0:T(8,128)}, f32[1,2,2048,128]{3,2,1,0:T(8,128)S(1)}, u32[]{:S(2)}) copy-start(f32[1,2,2048,128]{3,2,1,0:T(8,128)S(1)} %fusion.13) | copy-start | bytes 6291460
  29.7 5.9 %collective-permute-start.6 = (s32[2,32,16]{2,1,0:T(8,128)S(1)}, s32[2,32,16]{2,1,0:T(8,128)S(1)}, u32[]{:S(2)}, u32[]{:S(2)}) collective-permute-start(s32[2,32,16]{2,1,0:T(8,128)S(1)} %add_bitcast_fusion), channel_id=1, source_target_pairs={{0,4},{4,0},{8,12},{12,8},{1,5},{5,1},{9,13},{13,9},{2,6},{6,2},{1... | collective-permute-start | bytes 12296 | tf_op jit(solution)/shard_map/ppermute | solution.py:95
  32.4 39.1 %collective-permute-start.11 = (f32[1,2048,128]{2,1,0:T(8,128)}, f32[1,2048,128]{2,1,0:T(8,128)}, u32[]{:S(2)}, u32[]{:S(2)}) collective-permute-start(f32[1,2048,128]{2,1,0:T(8,128)} %select_bitcast_fusion.2), channel_id=1, source_target_pairs={{0,2},{1,3},{2,0},{3,1},{4,6},{5,7},{6,4},{7,5},{8,10},{9,11},{10,... | collective-permute-start | bytes 3145736 | tf_op jit(solution)/shard_map/ppermute | solution.py:44
  32.9 13.8 %collective-permute-start.7 = (bf16[1,32,32,128]{3,2,1,0:T(8,128)(2,1)S(1)}, bf16[1,32,32,128]{3,2,1,0:T(8,128)(2,1)S(1)}, u32[]{:S(2)}, u32[]{:S(2)}) collective-permute-start(bf16[1,32,32,128]{3,2,1,0:T(8,128)(2,1)S(1)} %bitcast.231), channel_id=1, source_target_pairs={{0,8},{4,12},{8,0},{12,4},{1,9},{5,13},{9,1},{13,5},{2,10},{6,14},... | collective-permute-start | bytes 786440 | tf_op jit(solution)/shard_map/ppermute | solution.py:95
  38.4 9.3 %copy-start.2 = (s32[256]{0:T(256)S(1)}, s32[256]{0:T(256)}, u32[]{:S(2)}) copy-start(s32[256]{0:T(256)} %param.8) | copy-start | bytes 3076
  47.7 13.9 %collective-permute-start.8 = (bf16[2,32,32,128]{3,2,1,0:T(8,128)(2,1)}, bf16[2,32,32,128]{3,2,1,0:T(8,128)(2,1)S(1)}, u32[]{:S(2)}, u32[]{:S(2)}) collective-permute-start(bf16[2,32,32,128]{3,2,1,0:T(8,128)(2,1)} %maximum_bitcast_fusion), channel_id=1, source_target_pairs={{0,4},{4,0},{8,12},{12,8},{1,5},{5,1},{9,13},{13,9},{2,6},{6,2},{1... | collective-permute-start | bytes 1572872 | tf_op jit(solution)/shard_map/ppermute | solution.py:95
  64.0 7.5 %copy-start.7 = (f32[1,2,2048,128]{3,2,1,0:T(8,128)S(1)}, f32[1,2,2048,128]{3,2,1,0:T(8,128)}, u32[]{:S(2)}) copy-start(f32[1,2,2048,128]{3,2,1,0:T(8,128)} %copy-done.6) | copy-start | bytes 6291460
  82.6 2.6 %copy-start.8 = (f32[16,16,32,64]{3,2,1,0:T(8,128)}, f32[16,16,32,64]{3,2,1,0:T(8,128)S(1)}, u32[]{:S(2)}) copy-start(f32[16,16,32,64]{3,2,1,0:T(8,128)S(1)} %get-tuple-element.45) | copy-start | bytes 6291460
  85.5 1.2 collective-permute-start.12
  86.7 3.7 %collective-permute-start.13 = (f32[16,128]{1,0:T(8,128)S(1)}, f32[16,128]{1,0:T(8,128)S(1)}, u32[]{:S(2)}, u32[]{:S(2)}) collective-permute-start(f32[16,128]{1,0:T(8,128)S(1)} %add.292), channel_id=1, source_target_pairs={{0,2},{1,3},{2,0},{3,1},{4,6},{5,7},{6,4},{7,5},{8,10},{9,11},{10,... | collective-permute-start | bytes 24584 | tf_op jit(solution)/shard_map/ppermute | solution.py:44
  90.4 3.7 %collective-permute-start.14 = (f32[16,128]{1,0:T(8,128)S(1)}, f32[16,128]{1,0:T(8,128)S(1)}, u32[]{:S(2)}, u32[]{:S(2)}) collective-permute-start(f32[16,128]{1,0:T(8,128)S(1)} %add.293), channel_id=1, source_target_pairs={{0,4},{4,0},{8,12},{12,8},{1,5},{5,1},{9,13},{13,9},{2,6},{6,2},{1... | collective-permute-start | bytes 24584 | tf_op jit(solution)/shard_map/ppermute | solution.py:44
  94.0 4.5 %collective-permute-start.15 = (f32[16,128]{1,0:T(8,128)S(1)}, f32[16,128]{1,0:T(8,128)S(1)}, u32[]{:S(2)}, u32[]{:S(2)}) collective-permute-start(f32[16,128]{1,0:T(8,128)S(1)} %add.294), channel_id=1, source_target_pairs={{0,8},{4,12},{8,0},{12,4},{1,9},{5,13},{9,1},{13,5},{2,10},{6,14},... | collective-permute-start | bytes 24584 | tf_op jit(solution)/shard_map/ppermute | solution.py:44
  118.4 22.0 %collective-permute-start.16 = (bf16[1,4096,128]{2,1,0:T(8,128)(2,1)S(1)}, bf16[1,4096,128]{2,1,0:T(8,128)(2,1)S(1)}, u32[]{:S(2)}, u32[]{:S(2)}) collective-permute-start(bf16[1,4096,128]{2,1,0:T(8,128)(2,1)S(1)} %fusion.12), channel_id=1, source_target_pairs={{0,2},{1,3},{2,0},{3,1},{4,6},{5,7},{6,4},{7,5},{8,10},{9,11},{10,... | collective-permute-start | bytes 3145736 | tf_op jit(solution)/shard_map/ppermute | solution.py:44
  140.7 4.4 %collective-permute-start.17 = (bf16[2,4096,128]{2,1,0:T(8,128)(2,1)S(1)}, bf16[2,4096,128]{2,1,0:T(8,128)(2,1)}, u32[]{:S(2)}, u32[]{:S(2)}) collective-permute-start(bf16[2,4096,128]{2,1,0:T(8,128)(2,1)S(1)} %pad_maximum_fusion.1), channel_id=1, source_target_pairs={{0,1},{1,0},{2,3},{3,2},{4,5},{5,4},{6,7},{7,6},{8,9},{9,8},{10,11... | collective-permute-start | bytes 6291464 | tf_op jit(solution)/shard_map/ppermute | solution.py:44
  148.0 16.3 %copy-start.1 = (bf16[256,128]{1,0:T(8,128)(2,1)S(1)}, bf16[256,128]{1,0:T(8,128)(2,1)}, u32[]{:S(2)}) copy-start(bf16[256,128]{1,0:T(8,128)(2,1)} %param.6) | copy-start | bytes 196612
  149.3 5.7 %collective-permute-start.18 = (f32[256,128]{1,0:T(8,128)S(1)}, f32[256,128]{1,0:T(8,128)S(1)}, u32[]{:S(2)}, u32[]{:S(2)}) collective-permute-start(f32[256,128]{1,0:T(8,128)S(1)} %convolution_add_fusion), channel_id=1, source_target_pairs={{0,4},{4,0},{8,12},{12,8},{1,5},{5,1},{9,13},{13,9},{2,6},{6,2},{1... | collective-permute-start | bytes 393224 | tf_op jit(solution)/shard_map/ppermute | solution.py:44
  155.0 8.6 %collective-permute-start.19 = (f32[256,128]{1,0:T(8,128)S(1)}, f32[256,128]{1,0:T(8,128)S(1)}, u32[]{:S(2)}, u32[]{:S(2)}) collective-permute-start(f32[256,128]{1,0:T(8,128)S(1)} %add.304), channel_id=1, source_target_pairs={{0,8},{4,12},{8,0},{12,4},{1,9},{5,13},{9,1},{13,5},{2,10},{6,14},... | collective-permute-start | bytes 393224 | tf_op jit(solution)/shard_map/ppermute | solution.py:44

commit v23 on v22

--- a/solution.py
+++ b/solution.py
@@ -108,10 +108,10 @@
     if count > 4 or not one_step:
         if not is_pow2(count):
             return lax.psum(value, axis)
-        bit = 1
-        while bit < count:
+        bit = count // 2
+        while bit >= 1:
             value = value + xor_perm(value, axis, bit)
-            bit *= 2
+            bit //= 2
         return value
     me = lax.axis_index(axis)
     got = [value] + [

time: 165 us -> 166 us (level)
  waiting for transfers between devices: 65 us -> 67.2 us
    ppermute x12, waiting for transfers between devices: 41.9 us -> 44.1 us  [xor_perm(): return lax.ppermute(value, axis, [(i, i ^ bit) for i in range(count)])]
where the time goes in v23:
time: 166 us
  waiting for transfers between devices  67.2 us (40%)
  local copies, waits for them, and re-layouts  26.3 us (16%)
  starting transfers between devices  24.7 us (15%)
  other arithmetic  23.8 us (14%)
  matrix products  22.5 us (14%)
    ppermute x12, waiting for transfers between devices, xor_perm(): return lax.ppermute(value, axis, [(i, i ^ bit) for i in range(count)])  44.1 us
    ppermute x8, waiting for transfers between devices, all_gather_many(): others = lax.ppermute(arrs, axis, [(i, i ^ bit) for i in range(count)])  23.1 us
    ppermute x12, starting transfers between devices, xor_perm(): return lax.ppermute(value, axis, [(i, i ^ bit) for i in range(count)])  14.6 us
    ppermute x8, starting transfers between devices, all_gather_many(): others = lax.ppermute(arrs, axis, [(i, i ^ bit) for i in range(count)])  10.1 us
    dot_general x1, matrix products, local(): jnp.einsum('scij,scie->scje', weights, q_e, preferred_element_type=jnp.fl...  6.95 us
    dot_general x1, matrix products, local(): jnp.einsum('scie,scje->scij', q_e, tiles, preferred_element_type=jnp.floa...  5.2 us
    reshape x2, other arithmetic, halving_steps(): acc = acc.reshape((acc.shape[0] // 2, 2) + acc.shape[1:])  5.15 us
    dot_general x2, matrix products, left_product(): lax.dot_general(left, right, (((0,), (0,)), ((), ())), preferred_element_...  4.18 us
  transfers between devices with their start and end apart: 20, of which 14 were waited for; matrix products, arithmetic and copies ran while one was open for 16% of the time, Pallas kernels for 0%

profile of v23, /device:TPU:0, one launch (start us, length us, event | category | flops | bytes accessed | tf_op | source)
XLA Modules:
  0.0 165.6 jit_solution(9857252127864321018)
XLA Ops:
  0.7 3.8 %fusion.47 = (bf16[4,1,2048,256]{3,2,1,0:T(8,128)(2,1)S(1)}, bf16[4,1,2048,256]{3,2,1,0:T(8,128)(2,1)S(1)}) fusion(bf16[4,2,2048,256]{3,2,1,0:T(8,128)(2,1)} %bitcast.216), kind=kLoop, calls=%fused_computation.149 | loop fusion | bytes 16777216 | tf_op jit(solution)/shard_map/slice | solution.py:150
  8.1 2.5 %collective-permute-start.1 = (bf16[1,8,32,128]{3,2,1,0:T(8,128)(2,1)S(1)}, bf16[1,8,32,128]{3,2,1,0:T(8,128)(2,1)S(1)}, u32[]{:S(2)}, u32[]{:S(2)}) collective-permute-start(bf16[1,8,32,128]{3,2,1,0:T(8,128)(2,1)S(1)} %bitcast.237), channel_id=1, source_target_pairs={{0,2},{1,3},{2,0},{3,1},{4,6},{5,7},{6,4},{7,5},{8,10},{9,11},{10,... | collective-permute-start | bytes 196616 | tf_op jit(solution)/shard_map/ppermute | solution.py:95
  15.5 3.2 %collective-permute-done.4 = s32[2,8,16]{2,1,0:T(8,128)S(1)} collective-permute-done((s32[2,8,16]{2,1,0:T(8,128)S(1)}, s32[2,8,16]{2,1,0:T(8,128)S(1)}, u32[]{:S(2)}, u32[]{:S(2)}) %collective-permute-start.4) | collective-permute-done | bytes 1056 | tf_op jit(solution)/shard_map/ppermute | solution.py:95
  19.0 3.3 %fusion.9 = f32[1,2,2048,128]{3,2,1,0:T(8,128)S(1)} fusion(f32[2,2048,128]{2,1,0:T(8,128)} %collective-permute-done, f32[2,2,2048,128]{3,2,1,0:T(8,128)} %copy-done.5, pred[]{:T(512)S(6)} %eq.72), kind=kLoop, calls=%fused_computation.21 | loop fusion | flops 1048576 | bytes 8388609 | tf_op jit(solution)/shard_map/reshape | solution.py:59
  25.0 2.6 %collective-permute-start.5 = (s32[1,32,16]{2,1,0:T(8,128)S(1)}, s32[1,32,16]{2,1,0:T(8,128)S(1)}, u32[]{:S(2)}, u32[]{:S(2)}) collective-permute-start(s32[1,32,16]{2,1,0:T(8,128)S(1)} %bitcast.235), channel_id=1, source_target_pairs={{0,8},{4,12},{8,0},{12,4},{1,9},{5,13},{9,1},{13,5},{2,10},{6,14},... | collective-permute-start | bytes 6152 | tf_op jit(solution)/shard_map/ppermute | solution.py:95
  27.6 1.9 %fusion.13 = f32[1,2,2048,128]{3,2,1,0:T(8,128)S(1)} fusion(f32[2,2048,128]{2,1,0:T(8,128)} %collective-permute-done.10, f32[2,2,2048,128]{3,2,0,1:T(8,128)S(1)} %copy-done.4, pred[]{:T(512)S(6)} %eq.72), kind=kLoop, calls=%fused_computation.28 | loop fusion | flops 1048576 | bytes 8388609 | tf_op jit(solution)/shard_map/reshape | solution.py:59
  32.9 2.6 %collective-permute-start.7 = (bf16[1,32,32,128]{3,2,1,0:T(8,128)(2,1)S(1)}, bf16[1,32,32,128]{3,2,1,0:T(8,128)(2,1)S(1)}, u32[]{:S(2)}, u32[]{:S(2)}) collective-permute-start(bf16[1,32,32,128]{3,2,1,0:T(8,128)(2,1)S(1)} %bitcast.231), channel_id=1, source_target_pairs={{0,8},{4,12},{8,0},{12,4},{1,9},{5,13},{9,1},{13,5},{2,10},{6,14},... | collective-permute-start | bytes 786440 | tf_op jit(solution)/shard_map/ppermute | solution.py:95
  36.5 1.9 %gather_fusion.3 = s32[256]{0:T(256)S(1)} fusion(s32[16,128]{1,0:T(8,128)S(1)} %reshape_reshape_reshape.2, s32[256]{0:T(256)S(1)} %reshape.676), kind=kCustom, calls=%fused_computation.3 | custom fusion | bytes 4096 | tf_op jit(solution)/shard_map/jit(take_along_axis)/gather | solution.py:177
  38.8 7.9 %collective-permute-done.7 = bf16[1,32,32,128]{3,2,1,0:T(8,128)(2,1)S(1)} collective-permute-done((bf16[1,32,32,128]{3,2,1,0:T(8,128)(2,1)S(1)}, bf16[1,32,32,128]{3,2,1,0:T(8,128)(2,1)S(1)}, u32[]{:S(2)}, u32[]{:S(2)}) %collective-permute-start.7) | collective-permute-done | bytes 262176 | tf_op jit(solution)/shard_map/ppermute | solution.py:95
  47.7 1.9 %gather_fusion = s32[256]{0:T(256)S(1)} fusion(s32[256]{0:T(256)S(1)} %copy-done.2, s32[1024]{0:T(1024)S(1)} %pad_clamp_fusion.2), kind=kCustom, calls=%fused_computation | custom fusion | bytes 3072 | tf_op jit(solution)/shard_map/gather | solution.py:15
  50.0 11.6 %collective-permute-done.8 = bf16[2,32,32,128]{3,2,1,0:T(8,128)(2,1)S(1)} collective-permute-done((bf16[2,32,32,128]{3,2,1,0:T(8,128)(2,1)}, bf16[2,32,32,128]{3,2,1,0:T(8,128)(2,1)S(1)}, u32[]{:S(2)}, u32[]{:S(2)}) %collective-permute-start.8) | collective-permute-done | bytes 524320 | tf_op jit(solution)/shard_map/ppermute | solution.py:95
  61.8 2.2 %gather_fusion.1 = bf16[256,32,128]{2,1,0:T(8,128)(2,1)} fusion(bf16[128,32,128]{2,1,0:T(8,128)(2,1)S(1)} %bitcast.226, s32[1024]{0:T(1024)S(1)} %pad_clamp_fusion.1), kind=kCustom, calls=%fused_computation.1 | custom fusion | bytes 4195328 | tf_op jit(solution)/shard_map/gather | solution.py:181
  65.6 5.9 %collective-permute-done.11 = f32[1,2048,128]{2,1,0:T(8,128)} collective-permute-done((f32[1,2048,128]{2,1,0:T(8,128)}, f32[1,2048,128]{2,1,0:T(8,128)}, u32[]{:S(2)}, u32[]{:S(2)}) %collective-permute-start.11) | collective-permute-done | bytes 1048608 | tf_op jit(solution)/shard_map/ppermute | solution.py:44
  74.4 3.0 %gather_fusion.2 = bf16[256,64,128]{2,1,0:T(8,128)(2,1)} fusion(bf16[64,64,128]{2,1,0:T(8,128)(2,1)S(1)} %multiply_convert_fusion.1, s32[1024]{0:T(1024)S(1)} %pad_clamp_fusion), kind=kCustom, calls=%fused_computation.2 | custom fusion | bytes 8389632 | tf_op jit(solution)/shard_map/gather | solution.py:188
  77.4 5.2 %select_reduce_fusion = (f32[16,16,32]{2,1,0:T(8,128)S(1)}, f32[16,16,32,64]{3,2,1,0:T(8,128)S(1)}) fusion(pred[16,16,64]{2,1,0:T(8,128)(4,1)S(1)} %add_compare_fusion, bf16[16,16,32,128]{3,2,1,0:T(8,128)(2,1)} %bitcast.229, bf16[16,16,64,128]{3,2,1,0:T(8,128)(2,1)} %bitcast.221), kind=kOutput, calls=%fused_computation.14 | convolution fusion | flops 135258112 | bytes 8437760 | tf_op jit(solution)/shard_map/scie,scje->scij/dot_general | solution.py:190
  82.6 2.6 %fusion.6 = f32[16,16,32]{2,1,0:T(8,128)S(1)} fusion(f32[16,16,32,64]{3,2,1,0:T(8,128)S(1)} %get-tuple-element.45, f32[16,16,32]{2,1,0:T(8,128)S(1)} %get-tuple-element.44, pred[16,16,64]{2,1,0:T(8,128)(4,1)S(1)} %add_compare_fusion), kind=kLoop, calls=%fused_computation.15 | loop fusion | flops 1564672 | bytes 2179072 | tf_op jit(solution)/shard_map/reduce_sum | solution.py:22
  87.3 1.9 %collective-permute-done.12 = f32[16,128]{1,0:T(8,128)S(1)} collective-permute-done((f32[16,128]{1,0:T(8,128)S(1)}, f32[16,128]{1,0:T(8,128)S(1)}, u32[]{:S(2)}, u32[]{:S(2)}) %collective-permute-start.12) | collective-permute-done | bytes 8224 | tf_op jit(solution)/shard_map/ppermute | solution.py:44
  90.4 2.8 %collective-permute-start.14 = (f32[16,128]{1,0:T(8,128)S(1)}, f32[16,128]{1,0:T(8,128)S(1)}, u32[]{:S(2)}, u32[]{:S(2)}) collective-permute-start(f32[16,128]{1,0:T(8,128)S(1)} %add.293), channel_id=1, source_target_pairs={{0,8},{4,12},{8,0},{12,4},{1,9},{5,13},{9,1},{13,5},{2,10},{6,14},... | collective-permute-start | bytes 24584 | tf_op jit(solution)/shard_map/ppermute | solution.py:44
  94.9 1.8 %collective-permute-start.15 = (f32[16,128]{1,0:T(8,128)S(1)}, f32[16,128]{1,0:T(8,128)S(1)}, u32[]{:S(2)}, u32[]{:S(2)}) collective-permute-start(f32[16,128]{1,0:T(8,128)S(1)} %add.294), channel_id=1, source_target_pairs={{0,4},{4,0},{8,12},{12,8},{1,5},{5,1},{9,13},{13,9},{2,6},{6,2},{1... | collective-permute-start | bytes 24584 | tf_op jit(solution)/shard_map/ppermute | solution.py:44
  96.8 1.8 %collective-permute-done.15 = f32[16,128]{1,0:T(8,128)S(1)} collective-permute-done((f32[16,128]{1,0:T(8,128)S(1)}, f32[16,128]{1,0:T(8,128)S(1)}, u32[]{:S(2)}, u32[]{:S(2)}) %collective-permute-start.15) | collective-permute-done | bytes 8224 | tf_op jit(solution)/shard_map/ppermute | solution.py:44
  99.2 1.9 %gather_fusion.4 = f32[256]{0:T(256)S(1)} fusion(f32[16,128]{1,0:T(8,128)S(1)} %reshape.646, s32[256]{0:T(256)S(1)} %reshape.676), kind=kCustom, calls=%fused_computation.4 | custom fusion | bytes 4096 | tf_op jit(solution)/shard_map/jit(take_along_axis)/gather | solution.py:200
  101.2 6.9 %multiply_convert_fusion = bf16[16,16,64,128]{3,2,1,0:T(8,128)(2,1)S(1)} fusion(f32[16,16]{1,0:T(8,128)S(1)} %select_multiply_fusion, bf16[16,16,32,128]{3,2,1,0:T(8,128)(2,1)} %bitcast.230, f32[16,16,32,64]{3,2,1,0:T(8,128)} %copy-done.8, f32[16,16,32]{2,1,0:T(8,128)S(1)} %fusion.6, f32[16,16,32]{2,1,0:T(8,128)S(1)} %get-tuple-element.44, ...), kind=kOutput, calls=%fused_computation.5 | convolution fusion | flops 140509184 | bytes 8471552 | tf_op jit(solution)/shard_map/scij,scie->scje/dot_general | solution.py:193
  108.2 3.7 %fusion.14 = (f32[64,64]{0,1:T(8,128)S(1)}, f32[64,64,128]{2,0,1:T(8,128)S(1)}) fusion(f32[64,64,128]{2,1,0:T(8,128)S(1)} %bitcast.219, bf16[16,16,64,128]{3,2,1,0:T(8,128)(2,1)S(1)} %multiply_convert_fusion, s32[16,16]{0,1:T(8,128)S(1)} %copy.126, pred[16,16]{0,1:T(8,128)(4,1)S(1)} %copy.127), kind=kOutput, calls=%fused_computation.30 | convolution fusion | flops 269512704 | bytes 8406272 | tf_op jit(solution)/shard_map/scb,scje->bje/dot_general | solution.py:204
  111.9 2.6 %copy.130 = f32[64,64,128]{2,1,0:T(8,128)} copy(f32[64,64,128]{2,0,1:T(8,128)S(1)} %get-tuple-element.47) | data formatting | bytes 4194304 | tf_op jit(solution)/shard_map/scb,scje->bje/dot_general | solution.py:204
  114.6 3.8 %fusion.12 = bf16[1,4096,128]{2,1,0:T(8,128)(2,1)S(1)} fusion(f32[4096]{0:T(1024)S(1)} %mul.134, f32[4096]{0:T(1024)S(1)} %multiply_multiply_fusion, f32[4096]{0:T(1024)S(1)} %bitcast.234, f32[1,4096,128]{2,1,0:T(8,128)S(1)} %bitcast.220, f32[1,4096,128]{2,1,0:T(8,128)} %bitcast.228), kind=kLoop, calls=%fused_computation.25 | loop fusion | flops 2621440 | bytes 5292032 | tf_op jit(solution)/shard_map/convert_element_type | solution.py:212
  118.4 1.8 %collective-permute-start.16 = (bf16[1,4096,128]{2,1,0:T(8,128)(2,1)S(1)}, bf16[1,4096,128]{2,1,0:T(8,128)(2,1)S(1)}, u32[]{:S(2)}, u32[]{:S(2)}) collective-permute-start(bf16[1,4096,128]{2,1,0:T(8,128)(2,1)S(1)} %fusion.12), channel_id=1, source_target_pairs={{0,2},{1,3},{2,0},{3,1},{4,6},{5,7},{6,4},{7,5},{8,10},{9,11},{10,... | collective-permute-start | bytes 3145736 | tf_op jit(solution)/shard_map/ppermute | solution.py:44
  120.2 21.4 %collective-permute-done.16 = bf16[1,4096,128]{2,1,0:T(8,128)(2,1)S(1)} collective-permute-done((bf16[1,4096,128]{2,1,0:T(8,128)(2,1)S(1)}, bf16[1,4096,128]{2,1,0:T(8,128)(2,1)S(1)}, u32[]{:S(2)}, u32[]{:S(2)}) %collective-permute-start.16) | collective-permute-done | bytes 1048608 | tf_op jit(solution)/shard_map/ppermute | solution.py:44
  142.0 4.0 %constant_dynamic-slice_fusion.1 = (bf16[2,1,4096,256]{3,2,1,0:T(8,128)(2,1)S(1)}, bf16[2,1,4096,256]{3,2,1,0:T(8,128)(2,1)S(1)}) fusion(bf16[2,2,4096,256]{3,2,1,0:T(8,128)(2,1)} %bitcast.217, s32[]{:T(128)S(6)} %select_n.505, s32[]{:T(128)S(6)} %select_n.512), kind=kLoop, calls=%fused_computation.143 | loop fusion | bytes 16777224 | tf_op jit(solution)/shard_map/jit(dynamic_index_in_dim)/dynamic_slice | solution.py:222
  146.2 2.9 %fusion.48 = f32[256,128]{1,0:T(8,128)S(1)} fusion(bf16[8192,256]{1,0:T(8,128)(2,1)S(1)} %bitcast.224, bf16[8192,128]{1,0:T(8,128)(2,1)} %bitcast.60), kind=kOutput, calls=%fused_computation.150 | convolution fusion | flops 536870912 | bytes 6422528 | tf_op jit(solution)/shard_map/dot_general | solution.py:37
  150.4 2.7 %collective-permute-start.18 = (f32[256,128]{1,0:T(8,128)S(1)}, f32[256,128]{1,0:T(8,128)S(1)}, u32[]{:S(2)}, u32[]{:S(2)}) collective-permute-start(f32[256,128]{1,0:T(8,128)S(1)} %convolution_add_fusion), channel_id=1, source_target_pairs={{0,8},{4,12},{8,0},{12,4},{1,9},{5,13},{9,1},{13,5},{2,10},{6,14},... | collective-permute-start | bytes 393224 | tf_op jit(solution)/shard_map/ppermute | solution.py:44
  153.2 6.7 %collective-permute-done.18 = f32[256,128]{1,0:T(8,128)S(1)} collective-permute-done((f32[256,128]{1,0:T(8,128)S(1)}, f32[256,128]{1,0:T(8,128)S(1)}, u32[]{:S(2)}, u32[]{:S(2)}) %collective-permute-start.18) | collective-permute-done | bytes 131104 | tf_op jit(solution)/shard_map/ppermute | solution.py:44
  161.3 3.7 %collective-permute-done.19 = f32[256,128]{1,0:T(8,128)S(1)} collective-permute-done((f32[256,128]{1,0:T(8,128)S(1)}, f32[256,128]{1,0:T(8,128)S(1)}, u32[]{:S(2)}, u32[]{:S(2)}) %collective-permute-start.19) | collective-permute-done | bytes 131104 | tf_op jit(solution)/shard_map/ppermute | solution.py:44
  (130 shorter events, 31.8 us)
Async XLA Ops:
  0.6 3.8 %copy-start = (bf16[256,128]{1,0:T(8,128)(2,1)S(1)}, bf16[256,128]{1,0:T(8,128)(2,1)}, u32[]{:S(2)}) copy-start(bf16[256,128]{1,0:T(8,128)(2,1)} %param.6) | copy-start | bytes 196612
  5.7 2.0 %copy-start.5 = (f32[2,2,2048,128]{3,2,1,0:T(8,128)}, f32[2,2,2048,128]{3,2,1,0:T(8,128)S(1)}, u32[]{:S(2)}) copy-start(f32[2,2,2048,128]{3,2,1,0:T(8,128)S(1)} %fusion) | copy-start | bytes 12582916
  5.7 2.4 %copy-start.9 = (bf16[8,32,128]{2,1,0:T(8,128)(2,1)S(1)}, bf16[8,32,128]{2,1,0:T(8,128)(2,1)}, u32[]{:S(2)}) copy-start(bf16[8,32,128]{2,1,0:T(8,128)(2,1)} %param.7) | copy-start | bytes 196612
  5.7 4.9 %copy-start.10 = (s32[8,16]{1,0:T(8,128)S(1)}, s32[8,16]{1,0:T(8,128)}, u32[]{:S(2)}) copy-start(s32[8,16]{1,0:T(8,128)} %param.9) | copy-start | bytes 1540
  7.7 11.3 %collective-permute-start = (f32[2,2048,128]{2,1,0:T(8,128)S(1)}, f32[2,2048,128]{2,1,0:T(8,128)}, u32[]{:S(2)}, u32[]{:S(2)}) collective-permute-start(f32[2,2048,128]{2,1,0:T(8,128)S(1)} %select_bitcast_fusion.1), channel_id=1, source_target_pairs={{0,1},{1,0},{2,3},{3,2},{4,5},{5,4},{6,7},{7,6},{8,9},{9,8},{10,11... | collective-permute-start | bytes 6291464 | tf_op jit(solution)/shard_map/ppermute | solution.py:44
  8.1 7.0 %collective-permute-start.1 = (bf16[1,8,32,128]{3,2,1,0:T(8,128)(2,1)S(1)}, bf16[1,8,32,128]{3,2,1,0:T(8,128)(2,1)S(1)}, u32[]{:S(2)}, u32[]{:S(2)}) collective-permute-start(bf16[1,8,32,128]{3,2,1,0:T(8,128)(2,1)S(1)} %bitcast.237), channel_id=1, source_target_pairs={{0,2},{1,3},{2,0},{3,1},{4,6},{5,7},{6,4},{7,5},{8,10},{9,11},{10,... | collective-permute-start | bytes 196616 | tf_op jit(solution)/shard_map/ppermute | solution.py:95
  10.6 4.2 %collective-permute-start.3 = (s32[1,8,16]{2,1,0:T(8,128)S(1)}, s32[1,8,16]{2,1,0:T(8,128)S(1)}, u32[]{:S(2)}, u32[]{:S(2)}) collective-permute-start(s32[1,8,16]{2,1,0:T(8,128)S(1)} %bitcast.238), channel_id=1, source_target_pairs={{0,2},{1,3},{2,0},{3,1},{4,6},{5,7},{6,4},{7,5},{8,10},{9,11},{10,... | collective-permute-start | bytes 1544 | tf_op jit(solution)/shard_map/ppermute | solution.py:95
  12.0 2.6 %copy-start.3 = (f32[2,2,2048,128]{3,2,0,1:T(8,128)}, f32[2,2,2048,128]{3,2,0,1:T(8,128)S(1)}, u32[]{:S(2)}) copy-start(f32[2,2,2048,128]{3,2,0,1:T(8,128)S(1)} %fusion.2) | copy-start | bytes 12582916
  14.6 13.0 %collective-permute-start.10 = (f32[2,2048,128]{2,1,0:T(8,128)}, f32[2,2048,128]{2,1,0:T(8,128)}, u32[]{:S(2)}, u32[]{:S(2)}) collective-permute-start(f32[2,2048,128]{2,1,0:T(8,128)} %select_bitcast_fusion), channel_id=1, source_target_pairs={{0,1},{1,0},{2,3},{3,2},{4,5},{5,4},{6,7},{7,6},{8,9},{9,8},{10,11... | collective-permute-start | bytes 6291464 | tf_op jit(solution)/shard_map/ppermute | solution.py:44
  14.8 3.9 %collective-permute-start.4 = (s32[2,8,16]{2,1,0:T(8,128)S(1)}, s32[2,8,16]{2,1,0:T(8,128)S(1)}, u32[]{:S(2)}, u32[]{:S(2)}) collective-permute-start(s32[2,8,16]{2,1,0:T(8,128)S(1)} %add_bitcast_fusion.1), channel_id=1, source_target_pairs={{0,1},{1,0},{2,3},{3,2},{4,5},{5,4},{6,7},{7,6},{8,9},{9,8},{10,11... | collective-permute-start | bytes 3080 | tf_op jit(solution)/shard_map/ppermute | solution.py:95
  15.2 3.7 %collective-permute-start.2 = (bf16[2,8,32,128]{3,2,1,0:T(8,128)(2,1)S(1)}, bf16[2,8,32,128]{3,2,1,0:T(8,128)(2,1)S(1)}, u32[]{:S(2)}, u32[]{:S(2)}) collective-permute-start(bf16[2,8,32,128]{3,2,1,0:T(8,128)(2,1)S(1)} %maximum_bitcast_fusion.1), channel_id=1, source_target_pairs={{0,1},{1,0},{2,3},{3,2},{4,5},{5,4},{6,7},{7,6},{8,9},{9,8},{10,11... | collective-permute-start | bytes 393224 | tf_op jit(solution)/shard_map/ppermute | solution.py:95
  19.0 8.6 %copy-start.4 = (f32[2,2,2048,128]{3,2,0,1:T(8,128)S(1)}, f32[2,2,2048,128]{3,2,0,1:T(8,128)}, u32[]{:S(2)}) copy-start(f32[2,2,2048,128]{3,2,0,1:T(8,128)} %copy-done.3) | copy-start | bytes 12582916
  23.4 40.6 %collective-permute-start.9 = (f32[1,2048,128]{2,1,0:T(8,128)}, f32[1,2048,128]{2,1,0:T(8,128)}, u32[]{:S(2)}, u32[]{:S(2)}) collective-permute-start(f32[1,2048,128]{2,1,0:T(8,128)} %select_bitcast_fusion.3), channel_id=1, source_target_pairs={{0,2},{1,3},{2,0},{3,1},{4,6},{5,7},{6,4},{7,5},{8,10},{9,11},{10,... | collective-permute-start | bytes 3145736 | tf_op jit(solution)/shard_map/ppermute | solution.py:44
  25.0 4.6 %collective-permute-start.5 = (s32[1,32,16]{2,1,0:T(8,128)S(1)}, s32[1,32,16]{2,1,0:T(8,128)S(1)}, u32[]{:S(2)}, u32[]{:S(2)}) collective-permute-start(s32[1,32,16]{2,1,0:T(8,128)S(1)} %bitcast.235), channel_id=1, source_target_pairs={{0,8},{4,12},{8,0},{12,4},{1,9},{5,13},{9,1},{13,5},{2,10},{6,14},... | collective-permute-start | bytes 6152 | tf_op jit(solution)/shard_map/ppermute | solution.py:95
  29.5 6.1 %copy-start.6 = (f32[1,2,2048,128]{3,2,1,0:T(8,128)}, f32[1,2,2048,128]{3,2,1,0:T(8,128)S(1)}, u32[]{:S(2)}) copy-start(f32[1,2,2048,128]{3,2,1,0:T(8,128)S(1)} %fusion.13) | copy-start | bytes 6291460
  29.7 5.9 %collective-permute-start.6 = (s32[2,32,16]{2,1,0:T(8,128)S(1)}, s32[2,32,16]{2,1,0:T(8,128)S(1)}, u32[]{:S(2)}, u32[]{:S(2)}) collective-permute-start(s32[2,32,16]{2,1,0:T(8,128)S(1)} %add_bitcast_fusion), channel_id=1, source_target_pairs={{0,4},{4,0},{8,12},{12,8},{1,5},{5,1},{9,13},{13,9},{2,6},{6,2},{1... | collective-permute-start | bytes 12296 | tf_op jit(solution)/shard_map/ppermute | solution.py:95
  32.4 39.1 %collective-permute-start.11 = (f32[1,2048,128]{2,1,0:T(8,128)}, f32[1,2048,128]{2,1,0:T(8,128)}, u32[]{:S(2)}, u32[]{:S(2)}) collective-permute-start(f32[1,2048,128]{2,1,0:T(8,128)} %select_bitcast_fusion.2), channel_id=1, source_target_pairs={{0,2},{1,3},{2,0},{3,1},{4,6},{5,7},{6,4},{7,5},{8,10},{9,11},{10,... | collective-permute-start | bytes 3145736 | tf_op jit(solution)/shard_map/ppermute | solution.py:44
  32.9 13.8 %collective-permute-start.7 = (bf16[1,32,32,128]{3,2,1,0:T(8,128)(2,1)S(1)}, bf16[1,32,32,128]{3,2,1,0:T(8,128)(2,1)S(1)}, u32[]{:S(2)}, u32[]{:S(2)}) collective-permute-start(bf16[1,32,32,128]{3,2,1,0:T(8,128)(2,1)S(1)} %bitcast.231), channel_id=1, source_target_pairs={{0,8},{4,12},{8,0},{12,4},{1,9},{5,13},{9,1},{13,5},{2,10},{6,14},... | collective-permute-start | bytes 786440 | tf_op jit(solution)/shard_map/ppermute | solution.py:95
  38.4 9.3 %copy-start.2 = (s32[256]{0:T(256)S(1)}, s32[256]{0:T(256)}, u32[]{:S(2)}) copy-start(s32[256]{0:T(256)} %param.8) | copy-start | bytes 3076
  47.7 13.9 %collective-permute-start.8 = (bf16[2,32,32,128]{3,2,1,0:T(8,128)(2,1)}, bf16[2,32,32,128]{3,2,1,0:T(8,128)(2,1)S(1)}, u32[]{:S(2)}, u32[]{:S(2)}) collective-permute-start(bf16[2,32,32,128]{3,2,1,0:T(8,128)(2,1)} %maximum_bitcast_fusion), channel_id=1, source_target_pairs={{0,4},{4,0},{8,12},{12,8},{1,5},{5,1},{9,13},{13,9},{2,6},{6,2},{1... | collective-permute-start | bytes 1572872 | tf_op jit(solution)/shard_map/ppermute | solution.py:95
  64.0 7.5 %copy-start.7 = (f32[1,2,2048,128]{3,2,1,0:T(8,128)S(1)}, f32[1,2,2048,128]{3,2,1,0:T(8,128)}, u32[]{:S(2)}) copy-start(f32[1,2,2048,128]{3,2,1,0:T(8,128)} %copy-done.6) | copy-start | bytes 6291460
  82.6 2.6 %copy-start.8 = (f32[16,16,32,64]{3,2,1,0:T(8,128)}, f32[16,16,32,64]{3,2,1,0:T(8,128)S(1)}, u32[]{:S(2)}) copy-start(f32[16,16,32,64]{3,2,1,0:T(8,128)S(1)} %get-tuple-element.45) | copy-start | bytes 6291460
  85.5 3.7 %collective-permute-start.12 = (f32[16,128]{1,0:T(8,128)S(1)}, f32[16,128]{1,0:T(8,128)S(1)}, u32[]{:S(2)}, u32[]{:S(2)}) collective-permute-start(f32[16,128]{1,0:T(8,128)S(1)} %select_reduce_fusion.1), channel_id=1, source_target_pairs={{0,2},{1,3},{2,0},{3,1},{4,6},{5,7},{6,4},{7,5},{8,10},{9,11},{10,... | collective-permute-start | bytes 24584 | tf_op jit(solution)/shard_map/ppermute | solution.py:44
  89.2 1.2 collective-permute-start.13
  90.4 4.5 %collective-permute-start.14 = (f32[16,128]{1,0:T(8,128)S(1)}, f32[16,128]{1,0:T(8,128)S(1)}, u32[]{:S(2)}, u32[]{:S(2)}) collective-permute-start(f32[16,128]{1,0:T(8,128)S(1)} %add.293), channel_id=1, source_target_pairs={{0,8},{4,12},{8,0},{12,4},{1,9},{5,13},{9,1},{13,5},{2,10},{6,14},... | collective-permute-start | bytes 24584 | tf_op jit(solution)/shard_map/ppermute | solution.py:44
  94.9 3.7 %collective-permute-start.15 = (f32[16,128]{1,0:T(8,128)S(1)}, f32[16,128]{1,0:T(8,128)S(1)}, u32[]{:S(2)}, u32[]{:S(2)}) collective-permute-start(f32[16,128]{1,0:T(8,128)S(1)} %add.294), channel_id=1, source_target_pairs={{0,4},{4,0},{8,12},{12,8},{1,5},{5,1},{9,13},{13,9},{2,6},{6,2},{1... | collective-permute-start | bytes 24584 | tf_op jit(solution)/shard_map/ppermute | solution.py:44
  118.4 23.2 %collective-permute-start.16 = (bf16[1,4096,128]{2,1,0:T(8,128)(2,1)S(1)}, bf16[1,4096,128]{2,1,0:T(8,128)(2,1)S(1)}, u32[]{:S(2)}, u32[]{:S(2)}) collective-permute-start(bf16[1,4096,128]{2,1,0:T(8,128)(2,1)S(1)} %fusion.12), channel_id=1, source_target_pairs={{0,2},{1,3},{2,0},{3,1},{4,6},{5,7},{6,4},{7,5},{8,10},{9,11},{10,... | collective-permute-start | bytes 3145736 | tf_op jit(solution)/shard_map/ppermute | solution.py:44
  141.9 4.4 %collective-permute-start.17 = (bf16[2,4096,128]{2,1,0:T(8,128)(2,1)S(1)}, bf16[2,4096,128]{2,1,0:T(8,128)(2,1)}, u32[]{:S(2)}, u32[]{:S(2)}) collective-permute-start(bf16[2,4096,128]{2,1,0:T(8,128)(2,1)S(1)} %pad_maximum_fusion.1), channel_id=1, source_target_pairs={{0,1},{1,0},{2,3},{3,2},{4,5},{5,4},{6,7},{7,6},{8,9},{9,8},{10,11... | collective-permute-start | bytes 6291464 | tf_op jit(solution)/shard_map/ppermute | solution.py:44
  149.1 16.5 %copy-start.1 = (bf16[256,128]{1,0:T(8,128)(2,1)S(1)}, bf16[256,128]{1,0:T(8,128)(2,1)}, u32[]{:S(2)}) copy-start(bf16[256,128]{1,0:T(8,128)(2,1)} %param.6) | copy-start | bytes 196612
  150.4 9.4 %collective-permute-start.18 = (f32[256,128]{1,0:T(8,128)S(1)}, f32[256,128]{1,0:T(8,128)S(1)}, u32[]{:S(2)}, u32[]{:S(2)}) collective-permute-start(f32[256,128]{1,0:T(8,128)S(1)} %convolution_add_fusion), channel_id=1, source_target_pairs={{0,8},{4,12},{8,0},{12,4},{1,9},{5,13},{9,1},{13,5},{2,10},{6,14},... | collective-permute-start | bytes 393224 | tf_op jit(solution)/shard_map/ppermute | solution.py:44
  159.9 5.0 %collective-permute-start.19 = (f32[256,128]{1,0:T(8,128)S(1)}, f32[256,128]{1,0:T(8,128)S(1)}, u32[]{:S(2)}, u32[]{:S(2)}) collective-permute-start(f32[256,128]{1,0:T(8,128)S(1)} %add.304), channel_id=1, source_target_pairs={{0,4},{4,0},{8,12},{12,8},{1,5},{5,1},{9,13},{13,9},{2,6},{6,2},{1... | collective-permute-start | bytes 393224 | tf_op jit(solution)/shard_map/ppermute | solution.py:44
